TPU v7x, 32 devices: a whole 2x2x4 slice. The times are simulated.
32 devices in a mesh: grp: 2 (over y), row: 8 (over z, x), chan: 2 (over core).
Axes of the slice: x: 2, y: 2, z: 4, core: 2. Of those that a mesh axis runs over, the one named last changes fastest.
Arguments:
- band_strip: bfloat16 [424, 64, 128], P('chan', ('grp', 'row')), parts along dimension 1, may hold values from -6 to 6
- conv_weight: bfloat16 [1024, 9, 424], P('row', None, 'chan'), may hold values from -0.09375 to 0.09375
- gdn_gamma: bfloat16 [1024, 1024], P('chan'), as said below
- gdn_beta: float32 [1024], P('chan'), may hold values from 0.5 to 2
- cotangent: bfloat16 [1024, 64, 128], P('chan', ('grp', 'row')), parts along dimension 1, may hold values from -6 to 6
Outputs:
- latent: bfloat16 [1024, 64, 128], P('chan', ('grp', 'row')), parts along dimension 1
- grad_strip: float32 [424, 64, 128], P('chan', ('grp', 'row')), parts along dimension 1
- grad_gamma: float32 [2048, 1024], P(('grp', 'chan')), parts along dimension 0
- grad_beta: float32 [2048], P(('grp', 'chan')), parts along dimension 0
There are 2 independent parts, one for each index of `grp`. A program takes and returns all parts, laid end to end along the dimension named above; an argument that names none is the same for every part. Nothing has to cross between parts.
Inputs may be any that keep to these rules, and one draw needn't show every extreme that they name: `gdn_gamma`: gamma's entries are non-negative.
All inputs are finite; a program needn't handle non-finite values.
Results may differ from a plain program's by a relative error of at most 0.0054.
Values may be sent and summed in bfloat16 or wider, within the bound.
No kernel may reach another device: no remote copies, remote signals or barrier semaphores. Data moves between devices by JAX's collectives and lax.ppermute only.
A program may use at most 64 MiB of HBM per device.

v0:
```python
import math

import jax
import jax.numpy as jnp
from jax import lax
from jax.sharding import PartitionSpec as P

TAPS = ((-1, -1), (-1, 0), (-1, 1), (0, -1), (0, 0), (0, 1), (1, -1), (1, 0), (1, 1))


def extended(shard, sides, width):
    for axis, dim in sides:
        count, length = (lax.axis_size(axis), shard.shape[dim])
        up = [(i, (i + 1) % count) for i in range(count - 1)]
        down = [(j, i) for i, j in up]
        last = lax.slice_in_dim(shard, length - width, length, axis=dim)
        leading = lax.slice_in_dim(shard, 0, width, axis=dim)
        before = lax.ppermute(last, axis, up)
        after = lax.ppermute(leading, axis, down)
        shard = jnp.concatenate([before, shard, after], axis=dim)
    return shard


def tap_columns(rimmed, row_count, col_count):
    padded = jnp.pad(rimmed, ((0, 0), (0, 0), (1, 1)))
    stacked = jnp.stack(
        [
            padded[
                :,
                1 + row_shift : 1 + row_shift + row_count,
                1 + col_shift : 1 + col_shift + col_count,
            ]
            for row_shift, col_shift in TAPS
        ],
        axis=0,
    )
    return stacked.reshape(9 * rimmed.shape[0], row_count * col_count)


def per_device(band_strip, conv_weight, gdn_gamma, gdn_beta, cotangent):
    in_local = band_strip.shape[0]
    row_count = band_strip.shape[1]
    col_count = band_strip.shape[2]
    pixels = row_count * col_count
    lat_local = gdn_gamma.shape[0]
    rimmed = extended(band_strip, (("row", 1),), 1)
    columns = tap_columns(rimmed, row_count, col_count)
    shard_piece = lax.all_gather(conv_weight, "row", axis=0, tiled=True)
    flat = shard_piece.reshape(shard_piece.shape[0], 9 * in_local)
    partial_value = jnp.dot(flat, columns, preferred_element_type=jnp.float32)
    pre = lax.psum_scatter(partial_value, "chan", scatter_dimension=0, tiled=True)
    squares_own = (pre * pre).astype(jnp.bfloat16)
    squares = lax.all_gather(squares_own, "chan", axis=0, tiled=True)
    norm_value = gdn_beta[:, None] + jnp.dot(gdn_gamma, squares, preferred_element_type=jnp.float32)
    inverse = lax.rsqrt(norm_value)
    latent = (pre * inverse).astype(jnp.bfloat16)
    upstream = cotangent.reshape(lat_local, pixels).astype(jnp.float32)
    shares = (-0.5 * upstream * pre * inverse * inverse * inverse).astype(jnp.bfloat16)
    gamma_cols = lax.all_to_all(gdn_gamma, "chan", split_axis=1, concat_axis=0, tiled=True)
    shares_all = lax.all_gather(shares, "chan", axis=0, tiled=True)
    back_sum = lax.dot_general(
        gamma_cols, shares_all, (((0,), (0,)), ((), ())), preferred_element_type=jnp.float32
    )
    latent_grad = (upstream * inverse + 2.0 * pre * back_sum).astype(jnp.bfloat16)
    gamma_terms = lax.dot_general(
        shares, squares, (((1,), (1,)), ((), ())), preferred_element_type=jnp.float32
    )
    beta_terms = jnp.sum(shares.astype(jnp.float32), axis=1)
    gamma_total, beta_total = lax.psum((gamma_terms, beta_terms), "row")
    scale_factor = 1.0 / math.sqrt(pixels * lax.axis_size("row"))
    grad_gamma = gamma_total * scale_factor
    grad_beta = beta_total * scale_factor
    grad_all = lax.all_gather(
        latent_grad.reshape(lat_local, row_count, col_count), "chan", axis=0, tiled=True
    )
    grad_rimmed = extended(grad_all, (("row", 1),), 1)
    grad_padded = jnp.pad(grad_rimmed, ((0, 0), (0, 0), (1, 1)))
    initial = jnp.zeros((in_local, pixels), jnp.float32)
    running = initial
    shard_piece = lax.all_gather(conv_weight, "row", axis=0, tiled=True)
    count_rows = shard_piece.shape[0]
    for tap_index, (row_shift, col_shift) in enumerate(TAPS):
        window = grad_padded[
            :, 1 - row_shift : 1 - row_shift + row_count, 1 - col_shift : 1 - col_shift + col_count
        ].reshape(count_rows, pixels)
        running = running + lax.dot_general(
            shard_piece[:, tap_index, :],
            window,
            (((0,), (0,)), ((), ())),
            preferred_element_type=jnp.float32,
        )
    return (
        latent.reshape(lat_local, row_count, col_count),
        running.reshape(in_local, row_count, col_count),
        grad_gamma,
        grad_beta,
    )


def solution(mesh):
    return jax.shard_map(
        per_device,
        mesh=mesh,
        in_specs=(
            P("chan", ("grp", "row"), None),
            P("row", None, "chan"),
            P("chan", None),
            P("chan"),
            P("chan", ("grp", "row"), None),
        ),
        out_specs=(
            P("chan", ("grp", "row"), None),
            P("chan", ("grp", "row"), None),
            P(("grp", "chan"), None),
            P(("grp", "chan")),
        ),
        check_vma=False,
    )
```

profile of v0, /device:TPU:0, one launch (start us, length us, event | category | flops | bytes accessed | tf_op | source)
XLA Modules:
  0.0 275.5 jit_solution(17126695772306795772)
XLA Ops:
  7.2 0.7 all-gather.5.cloned.1.call-update
  8.0 1.2 fusion.48
  9.2 1.3 collective-permute-start.1
  10.5 5.5 %collective-permute-start = (bf16[212,1,128]{2,1,0:T(2,128)(2,1)S(1)}, bf16[212,1,128]{2,1,0:T(2,128)(2,1)S(1)}, u32[]{:S(2)}, u32[]{:S(2)}) collective-permute-start(bf16[212,1,128]{2,1,0:T(2,128)(2,1)S(1)} %get-tuple-element.30), channel_id=1, source_target_pairs={{0,2},{2,4},{4,6},{6,8},{8,10},{10,12},{12,14},{1,3},{3,5},{5,7},{... | collective-permute-start | bytes 162824 | tf_op jit(solution)/shard_map/ppermute | solution.py:18
  16.0 1.1 collective-permute-done.1
  17.1 2.5 collective-permute-done
  19.5 2.1 fusion.22
  23.6 0.8 pad.38
  24.8 60.2 %all-gather.5.cloned.1.call-done = bf16[1024,9,212]{0,2,1:T(8,128)(2,1)} async-done(((bf16[128,9,212]{0,2,1:T(8,128)(2,1)}), bf16[1024,9,212]{0,2,1:T(8,128)(2,1)}) %all-gather.5.cloned.1.call-update) | async-done | bytes 3907600 | tf_op jit(solution)/shard_map/all_gather | solution.py:48
  85.0 5.5 %reshape.58 = bf16[1024,1908]{0,1:T(8,128)(2,1)} reshape(bf16[1024,9,212]{0,2,1:T(8,128)(2,1)} %all-gather.5.cloned.1.call-done) | data formatting | bytes 7815168 | tf_op jit(solution)/shard_map/reshape | solution.py:49
  90.5 5.8 %convolution_bitcast_fusion = f32[1024,512]{0,1:T(8,128)} fusion(bf16[1908,512]{1,0:T(8,128)(2,1)S(1)} %bitcast.144, bf16[1024,1908]{0,1:T(8,128)(2,1)} %reshape.58), kind=kOutput, calls=%fused_computation.11 | convolution fusion | flops 2000683008 | bytes 7958528 | tf_op jit(solution)/shard_map/dot_general | solution.py:50
  96.4 7.9 %reduce-scatter.2.cloned.1.call-done = f32[512,512]{0,1:T(8,128)} async-done(((f32[1024,512]{0,1:T(8,128)}), f32[512,512]{0,1:T(8,128)}) %reduce-scatter.2.cloned.1.call-update) | async-done | bytes 1048592 | tf_op jit(solution)/shard_map/reduce_scatter | solution.py:51
  104.3 2.2 multiply_convert_fusion.1
  106.6 1.4 copy.13
  108.0 9.0 %all-gather.7.cloned.1.call-done = bf16[1024,512]{0,1:T(8,128)(2,1)} async-done(((bf16[512,512]{0,1:T(8,128)(2,1)}), bf16[1024,512]{0,1:T(8,128)(2,1)}) %all-gather.7.cloned.1.call-update) | async-done | bytes 1048592 | tf_op jit(solution)/shard_map/all_gather | solution.py:53
  117.0 3.5 %convert_reduce_fusion = (f32[512]{0:T(512)S(1)}, bf16[512,512]{0,1:T(8,128)(2,1)}, f32[512,512]{0,1:T(8,128)}, bf16[512,512]{0,1:T(8,128)(2,1)}) fusion(f32[512,512]{0,1:T(8,128)S(1)} %copy-done.2, f32[512,4,128]{0,2,1:T(8,128)S(1)} %copy.13, bf16[1024,512]{0,1:T(8,128)(2,1)} %all-gather.7.cloned.1.call-done, bf16[512,1024]{1,0:T(8,128)(2,1)S(1)} %copy-done.6, ...), kind=kOutput, calls=%fused_computation.31 | convolution fusion | flops 540016128 | bytes 6295552 | tf_op jit(solution)/shard_map/dot_general | solution.py:54
  121.2 4.6 %all_to_all.19 = bf16[512,2,512]{0,2,1:T(8,128)(2,1)S(1)} all-to-all(bf16[512,2,512]{0,2,1:T(8,128)(2,1)S(1)} %bitcast.139), channel_id=1, replica_groups=mesh['grp'=2,'row'=8,'chan'=2] {'chan'}, dimensions={1} | all-to-all | bytes 2097152 | tf_op jit(solution)/shard_map/all_to_all | solution.py:59
  125.7 1.3 copy.15
  127.1 3.9 %all-gather.9.cloned.1.call-done = bf16[1024,512]{0,1:T(8,128)(2,1)} async-done(((bf16[512,512]{0,1:T(8,128)(2,1)}), bf16[1024,512]{0,1:T(8,128)(2,1)}) %all-gather.9.cloned.1.call-update) | async-done | bytes 1048592 | tf_op jit(solution)/shard_map/all_gather | solution.py:60
  130.9 3.5 %fusion.11 = bf16[512,512]{0,1:T(8,128)(2,1)} fusion(f32[512,512]{0,1:T(8,128)} %get-tuple-element.18, bf16[1024,512]{0,1:T(8,128)(2,1)} %all-gather.9.cloned.1.call-done, bf16[1024,512]{1,0:T(8,128)(2,1)} %bitcast.140, f32[512,512]{0,1:T(8,128)S(1)} %copy-done.2), kind=kOutput, calls=%fused_computation.19 | convolution fusion | flops 537919488 | bytes 4718592 | tf_op jit(solution)/shard_map/dot_general | solution.py:61
  134.6 2.0 fusion.49
  136.6 1.0 copy-done.7
  137.6 1.1 copy.16
  138.7 21.8 %psum.15 = f32[512]{0:T(512)S(1)} all-reduce(f32[512]{0:T(512)S(1)} %get-tuple-element.16), channel_id=1, replica_groups=mesh['grp'=2,'row'=8,'chan'=2] {'row'}, use_global_device_ids=true, to_apply=%region_3.4 | all-reduce | flops 512 | bytes 4096 | tf_op jit(solution)/shard_map/psum | solution.py:69
  160.5 0.6 broadcast_multiply_fusion.1
  161.1 1.2 fusion.47
  162.3 1.3 collective-permute-start.3
  163.6 4.7 %collective-permute-start.2 = (bf16[1024,1,128]{0,2,1:T(8,128)(2,1)S(1)}, bf16[1024,1,128]{0,2,1:T(8,128)(2,1)S(1)}, u32[]{:S(2)}, u32[]{:S(2)}) collective-permute-start(bf16[1024,1,128]{0,2,1:T(8,128)(2,1)S(1)} %get-tuple-element.28), channel_id=1, source_target_pairs={{0,2},{2,4},{4,6},{6,8},{8,10},{10,12},{12,14},{1,3},{3,5},{5,7},{... | collective-permute-start | bytes 786440 | tf_op jit(solution)/shard_map/ppermute | solution.py:18
  168.3 89.7 %all-reduce.4.cloned.1.call-done = f32[512,1024]{1,0:T(8,128)} async-done(((f32[512,1024]{1,0:T(8,128)}), f32[512,1024]{1,0:T(8,128)}) %all-reduce.4.cloned.1.call-update) | async-done | bytes 2097168 | tf_op jit(solution)/shard_map/psum | solution.py:69
  258.0 3.4 %broadcast_multiply_fusion = f32[512,1024]{1,0:T(8,128)} fusion(f32[512,1024]{1,0:T(8,128)} %all-reduce.4.cloned.1.call-done), kind=kLoop, calls=%fused_computation.32 | loop fusion | flops 524288 | bytes 4194304 | tf_op jit(solution)/shard_map/mul | solution.py:71
  262.4 1.1 fusion.46
  267.8 0.9 reshape.70
  (53 shorter events, 8.4 us)
Async XLA Ops:
  7.2 14.6 %copy-start.3 = (bf16[212,4,128]{2,1,0:T(4,128)(2,1)S(1)}, bf16[212,4,128]{2,1,0:T(4,128)(2,1)}, u32[]{:S(2)}) copy-start(bf16[212,4,128]{2,1,0:T(4,128)(2,1)} %param.5) | copy-start | bytes 651268
  7.2 77.8 %all-gather.5.cloned.1.call-start = ((), (), s32[]{:S(2)}) async-start(), calls=%async_computation.2 | async-start | bytes 4478976 | tf_op jit(solution)/shard_map/all_gather | solution.py:48
  7.9 96.4 %reduce-scatter.2.cloned.1.call-start = ((), (), s32[]{:S(2)}) async-start(), calls=%async_computation.3 | async-start | bytes 3145728 | tf_op jit(solution)/shard_map/reduce_scatter | solution.py:51
  9.2 7.9 %collective-permute-start.1 = (bf16[212,1,128]{2,1,0:T(2,128)(2,1)S(1)}, bf16[212,1,128]{2,1,0:T(2,128)(2,1)S(1)}, u32[]{:S(2)}, u32[]{:S(2)}) collective-permute-start(bf16[212,1,128]{2,1,0:T(2,128)(2,1)S(1)} %get-tuple-element.31), channel_id=1, source_target_pairs={{2,0},{4,2},{6,4},{8,6},{10,8},{12,10},{14,12},{3,1},{5,3},{7,5},{... | collective-permute-start | bytes 162824 | tf_op jit(solution)/shard_map/ppermute | solution.py:19
  10.5 9.1 %collective-permute-start = (bf16[212,1,128]{2,1,0:T(2,128)(2,1)S(1)}, bf16[212,1,128]{2,1,0:T(2,128)(2,1)S(1)}, u32[]{:S(2)}, u32[]{:S(2)}) collective-permute-start(bf16[212,1,128]{2,1,0:T(2,128)(2,1)S(1)} %get-tuple-element.30), channel_id=1, source_target_pairs={{0,2},{2,4},{4,6},{6,8},{8,10},{10,12},{12,14},{1,3},{3,5},{5,7},{... | collective-permute-start | bytes 162824 | tf_op jit(solution)/shard_map/ppermute | solution.py:18
  96.3 20.7 %copy-start.6 = (bf16[512,1024]{1,0:T(8,128)(2,1)S(1)}, bf16[512,1024]{1,0:T(8,128)(2,1)}, u32[]{:S(2)}) copy-start(bf16[512,1024]{1,0:T(8,128)(2,1)} %param.7) | copy-start | bytes 3145732
  96.4 20.7 %copy-start.8 = (f32[512]{0:T(512)S(1)}, f32[512]{0:T(512)}, u32[]{:S(2)}) copy-start(f32[512]{0:T(512)} %param.8) | copy-start | bytes 6148
  96.4 20.6 %all-gather.7.cloned.1.call-start = ((), (), s32[]{:S(2)}) async-start(), calls=%async_computation.4 | async-start | bytes 1572864 | tf_op jit(solution)/shard_map/all_gather | solution.py:53
  104.3 12.7 %copy-start.2 = (f32[512,512]{0,1:T(8,128)S(1)}, f32[512,512]{0,1:T(8,128)}, u32[]{:S(2)}) copy-start(f32[512,512]{0,1:T(8,128)} %reduce-scatter.2.cloned.1.call-done) | copy-start | bytes 3145732
  106.6 24.4 %all-gather.9.cloned.1.call-start = ((), (), s32[]{:S(2)}) async-start(), calls=%async_computation.5 | async-start | bytes 1572864 | tf_op jit(solution)/shard_map/all_gather | solution.py:60
  120.6 40.5 %all-gather.11.cloned.1.call-start = ((), (), s32[]{:S(2)}) async-start(), calls=%async_computation.6 | async-start | bytes 1572864 | tf_op jit(solution)/shard_map/all_gather | solution.py:73
  130.9 3.6 %copy-start.4 = (bf16[512,512]{0,1:T(8,128)(2,1)S(1)}, bf16[512,512]{0,1:T(8,128)(2,1)}, u32[]{:S(2)}) copy-start(bf16[512,512]{0,1:T(8,128)(2,1)} %get-tuple-element.17) | copy-start | bytes 1572868
  130.9 3.6 %copy-start.5 = (bf16[1024,512]{0,1:T(8,128)(2,1)S(1)}, bf16[1024,512]{0,1:T(8,128)(2,1)}, u32[]{:S(2)}) copy-start(bf16[1024,512]{0,1:T(8,128)(2,1)} %all-gather.7.cloned.1.call-done) | copy-start | bytes 3145732
  134.5 123.5 %all-reduce.4.cloned.1.call-start = ((), (), s32[]{:S(2)}) async-start(), calls=%async_computation.7 | async-start | bytes 4194304 | tf_op jit(solution)/shard_map/psum | solution.py:69
  136.6 1.0 copy-start.7
  161.1 100.2 %copy-start.1 = (bf16[1024,4,128]{0,2,1:T(8,128)(2,1)S(1)}, bf16[1024,4,128]{0,2,1:T(8,128)(2,1)}, u32[]{:S(2)}) copy-start(bf16[1024,4,128]{0,2,1:T(8,128)(2,1)} %all-gather.11.cloned.1.call-done) | copy-start | bytes 3145732
  162.3 99.6 %collective-permute-start.3 = (bf16[1024,1,128]{0,2,1:T(8,128)(2,1)S(1)}, bf16[1024,1,128]{0,2,1:T(8,128)(2,1)S(1)}, u32[]{:S(2)}, u32[]{:S(2)}) collective-permute-start(bf16[1024,1,128]{0,2,1:T(8,128)(2,1)S(1)} %get-tuple-element.29), channel_id=1, source_target_pairs={{2,0},{4,2},{6,4},{8,6},{10,8},{12,10},{14,12},{3,1},{5,3},{7,5},{... | collective-permute-start | bytes 786440 | tf_op jit(solution)/shard_map/ppermute | solution.py:19
  163.6 98.3 %collective-permute-start.2 = (bf16[1024,1,128]{0,2,1:T(8,128)(2,1)S(1)}, bf16[1024,1,128]{0,2,1:T(8,128)(2,1)S(1)}, u32[]{:S(2)}, u32[]{:S(2)}) collective-permute-start(bf16[1024,1,128]{0,2,1:T(8,128)(2,1)S(1)} %get-tuple-element.28), channel_id=1, source_target_pairs={{0,2},{2,4},{4,6},{6,8},{8,10},{10,12},{12,14},{1,3},{3,5},{5,7},{... | collective-permute-start | bytes 786440 | tf_op jit(solution)/shard_map/ppermute | solution.py:18
  258.0 3.4 %copy-start = (bf16[1024,9,212]{0,2,1:T(8,128)(2,1)S(1)}, bf16[1024,9,212]{0,2,1:T(8,128)(2,1)}, u32[]{:S(2)}) copy-start(bf16[1024,9,212]{0,2,1:T(8,128)(2,1)} %all-gather.5.cloned.1.call-done) | copy-start | bytes 11722756
Sparse Core Ops, SparseCore 0:
  10.0 74.9 all-gather.4
  96.5 7.7 reduce-scatter.1
  106.7 10.2 all-gather.6
  120.7 10.1 all-gather.8
  134.6 10.1 all-gather.10
  148.9 109.0 all-reduce.3
where the time goes:
time: 276 us
  waiting for transfers between devices  175 us (63%)
  blocking collectives  26.4 us (10%)
  matrix products  19.4 us (7%)
  local copies, waits for them, and re-layouts  17.9 us (6%)
  between operations  14.4 us (5%)
  starting transfers between devices  13.1 us (5%)
  other arithmetic  9.48 us (3%)
    psum x1, waiting for transfers between devices, per_device(): gamma_total, beta_total = lax.psum((gamma_terms, beta_terms), 'row')  89.7 us
    all_gather x1, waiting for transfers between devices, per_device(): shard_piece = lax.all_gather(conv_weight, 'row', axis=0, tiled=True)  60.2 us
    psum x1, blocking collectives, per_device(): gamma_total, beta_total = lax.psum((gamma_terms, beta_terms), 'row')  21.8 us
    ppermute x2, starting transfers between devices, extended(): before = lax.ppermute(last, axis, up)  10.2 us
    all_gather x1, waiting for transfers between devices, per_device(): squares = lax.all_gather(squares_own, 'chan', axis=0, tiled=True)  8.99 us
    reduce_scatter x1, waiting for transfers between devices, per_device(): lax.psum_scatter(partial_value, 'chan', scatter_dimension=0, tiled=True)  7.88 us
    dot_general x1, matrix products, per_device(): partial_value = jnp.dot(flat, columns, preferred_element_type=jnp.float32)  5.78 us
    reshape x1, local copies, waits for them, and re-layouts, per_device(): flat = shard_piece.reshape(shard_piece.shape[0], 9 * in_local)  5.54 us
  transfers between devices with their start and end apart: 10, of which 7 were waited for; matrix products, arithmetic and copies ran while one was open for 7% of the time, Pallas kernels for 0%

commit v1 on v0

v1 whole, which is shorter than its diff:
```python
import math

import jax
import jax.numpy as jnp
from jax import lax
from jax.sharding import PartitionSpec as P

TAPS = ((-1, -1), (-1, 0), (-1, 1), (0, -1), (0, 0), (0, 1), (1, -1), (1, 0), (1, 1))
SWAP = [(0, 1), (1, 0)]


def extended(shard, sides, width):
    for axis, dim in sides:
        count, length = (lax.axis_size(axis), shard.shape[dim])
        up = [(i, (i + 1) % count) for i in range(count - 1)]
        down = [(j, i) for i, j in up]
        last = lax.slice_in_dim(shard, length - width, length, axis=dim)
        leading = lax.slice_in_dim(shard, 0, width, axis=dim)
        before = lax.ppermute(last, axis, up)
        after = lax.ppermute(leading, axis, down)
        shard = jnp.concatenate([before, shard, after], axis=dim)
    return shard


def tap_columns(rimmed, row_count, col_count):
    padded = jnp.pad(rimmed, ((0, 0), (0, 0), (1, 1)))
    stacked = jnp.stack(
        [
            padded[
                :,
                1 + row_shift : 1 + row_shift + row_count,
                1 + col_shift : 1 + col_shift + col_count,
            ]
            for row_shift, col_shift in TAPS
        ],
        axis=0,
    )
    return stacked.reshape(9 * rimmed.shape[0], row_count * col_count)


def chan_gather(x):
    other = lax.ppermute(x, "chan", SWAP)
    first = lax.axis_index("chan") == 0
    return jnp.where(first, jnp.concatenate([x, other], 0), jnp.concatenate([other, x], 0))


def chan_scatter_sum(x):
    half = x.shape[0] // 2
    first = lax.axis_index("chan") == 0
    top, bottom = x[:half], x[half:]
    mine = jnp.where(first, top, bottom)
    theirs = jnp.where(first, bottom, top)
    return mine + lax.ppermute(theirs, "chan", SWAP)


def ring_order(mesh):
    count = mesh.shape["row"]
    try:
        coords = [tuple(d.coords) for d in mesh.devices[0, :, 0]]
    except Exception:
        return list(range(count))
    xs = sorted({c[0] for c in coords})
    zs = sorted({c[2] for c in coords})
    if len(xs) * len(zs) != count or len(zs) % 2:
        return list(range(count))
    where = {(c[0], c[2]): i for i, c in enumerate(coords)}
    path = [where[(xs[0], zs[0])]]
    for k, z in enumerate(zs):
        cols = xs[1:] if k % 2 == 0 else xs[:0:-1]
        path += [where[(x, z)] for x in cols]
    path += [where[(xs[0], z)] for z in zs[:0:-1]]
    return path if len(set(path)) == count else list(range(count))


def ring_sum(blocks, ring):
    count = len(ring)
    forward = [(ring[i], ring[(i + 1) % count]) for i in range(count)]
    backward = [(b, a) for a, b in forward]
    position = jnp.asarray([ring.index(i) for i in range(count)], jnp.int32)[lax.axis_index("row")]

    def chunks(x, part):
        half = x.shape[0] // 2
        piece = x[part * half : (part + 1) * half]
        return piece.reshape((count, half // count) + x.shape[1:])

    split = [[chunks(x, part) for x in blocks] for part in range(2)]
    moves = (forward, backward)
    signs = (1, -1)

    def pick(part, step):
        index = (position - signs[part] * (1 + step)) % count
        return [jnp.take(c, index, axis=0) for c in split[part]]

    carry = [pick(part, 0) for part in range(2)]
    for step in range(1, count):
        for part in range(2):
            got = lax.ppermute(carry[part], "row", moves[part])
            carry[part] = [g + o for g, o in zip(got, pick(part, step))]
    gathered = [[c] for c in carry]
    for step in range(1, count):
        for part in range(2):
            gathered[part].append(lax.ppermute(gathered[part][-1], "row", moves[part]))
    results = []
    for leaf in range(len(blocks)):
        halves = []
        for part in range(2):
            stacked = jnp.stack([g[leaf] for g in gathered[part]], 0)
            order = (signs[part] * (position - jnp.arange(count))) % count
            halves.append(jnp.take(stacked, order, axis=0).reshape((-1,) + stacked.shape[2:]))
        results.append(jnp.concatenate(halves, 0))
    return results


def make_per_device(ring):
    def per_device(band_strip, conv_weight, gdn_gamma, gdn_beta, cotangent):
        in_local = band_strip.shape[0]
        row_count = band_strip.shape[1]
        col_count = band_strip.shape[2]
        pixels = row_count * col_count
        lat_local = gdn_gamma.shape[0]
        first = lax.axis_index("chan") == 0
        rimmed = extended(band_strip, (("row", 1),), 1)
        columns = tap_columns(rimmed, row_count, col_count)
        shard_piece = lax.all_gather(conv_weight, "row", axis=0, tiled=True)
        flat = shard_piece.reshape(shard_piece.shape[0], 9 * in_local)
        partial_value = jnp.dot(flat, columns, preferred_element_type=jnp.float32)
        pre = chan_scatter_sum(partial_value)
        squares_own = (pre * pre).astype(jnp.bfloat16)
        squares = chan_gather(squares_own)
        norm_value = gdn_beta[:, None] + jnp.dot(gdn_gamma, squares, preferred_element_type=jnp.float32)
        inverse = lax.rsqrt(norm_value)
        latent = (pre * inverse).astype(jnp.bfloat16)
        upstream = cotangent.reshape(lat_local, pixels).astype(jnp.float32)
        shares = (-0.5 * upstream * pre * inverse * inverse * inverse).astype(jnp.bfloat16)
        gamma_left, gamma_right = gdn_gamma[:, :lat_local], gdn_gamma[:, lat_local:]
        gamma_mine = jnp.where(first, gamma_left, gamma_right)
        gamma_theirs = lax.ppermute(jnp.where(first, gamma_right, gamma_left), "chan", SWAP)
        gamma_cols = jnp.where(
            first,
            jnp.concatenate([gamma_mine, gamma_theirs], 0),
            jnp.concatenate([gamma_theirs, gamma_mine], 0),
        )
        shares_all = chan_gather(shares)
        back_sum = lax.dot_general(
            gamma_cols, shares_all, (((0,), (0,)), ((), ())), preferred_element_type=jnp.float32
        )
        latent_grad = (upstream * inverse + 2.0 * pre * back_sum).astype(jnp.bfloat16)
        gamma_terms = lax.dot_general(
            shares, squares, (((1,), (1,)), ((), ())), preferred_element_type=jnp.float32
        )
        beta_terms = jnp.sum(shares.astype(jnp.float32), axis=1)
        if len(ring) <= 16:
            gamma_total, beta_total = ring_sum([gamma_terms, beta_terms], ring)
        else:
            gamma_total, beta_total = lax.psum((gamma_terms, beta_terms), "row")
        scale_factor = 1.0 / math.sqrt(pixels * lax.axis_size("row"))
        grad_gamma = gamma_total * scale_factor
        grad_beta = beta_total * scale_factor
        grad_all = chan_gather(latent_grad.reshape(lat_local, row_count, col_count))
        grad_rimmed = extended(grad_all, (("row", 1),), 1)
        grad_padded = jnp.pad(grad_rimmed, ((0, 0), (0, 0), (1, 1)))
        running = jnp.zeros((in_local, pixels), jnp.float32)
        count_rows = shard_piece.shape[0]
        for tap_index, (row_shift, col_shift) in enumerate(TAPS):
            window = grad_padded[
                :, 1 - row_shift : 1 - row_shift + row_count, 1 - col_shift : 1 - col_shift + col_count
            ].reshape(count_rows, pixels)
            running = running + lax.dot_general(
                shard_piece[:, tap_index, :],
                window,
                (((0,), (0,)), ((), ())),
                preferred_element_type=jnp.float32,
            )
        return (
            latent.reshape(lat_local, row_count, col_count),
            running.reshape(in_local, row_count, col_count),
            grad_gamma,
            grad_beta,
        )

    return per_device


def solution(mesh):
    return jax.shard_map(
        make_per_device(ring_order(mesh)),
        mesh=mesh,
        in_specs=(
            P("chan", ("grp", "row"), None),
            P("row", None, "chan"),
            P("chan", None),
            P("chan"),
            P("chan", ("grp", "row"), None),
        ),
        out_specs=(
            P("chan", ("grp", "row"), None),
            P("chan", ("grp", "row"), None),
            P(("grp", "chan"), None),
            P(("grp", "chan")),
        ),
        check_vma=False,
    )
```

time: 276 us -> 276 us (level)
  starting transfers between devices: 13.1 us -> 69.1 us
  waiting for transfers between devices: 175 us -> 122 us
  blocking collectives: 26.4 us -> 0 us
  between operations: 14.4 us -> 25.5 us
  other arithmetic: 9.48 us -> 17.1 us
  local copies, waits for them, and re-layouts: 17.9 us -> 24.9 us
  matrix products: 19.4 us -> 16.6 us
    psum x1 -> x0, waiting for transfers between devices: 89.7 us -> none  [per_device(): gamma_total, beta_total = lax.psum((gamma_terms, beta_terms), 'row')]
    ppermute x0 -> x61, starting transfers between devices: none -> 59.2 us  [the longest x28 29.6 us: ring_sum(): gathered[part].append(lax.ppermute(gathered[part][-1], 'row', moves[part]))]
    ppermute x0 -> x61, waiting for transfers between devices: none -> 58.6 us  [the longest x28 33.7 us: ring_sum(): gathered[part].append(lax.ppermute(gathered[part][-1], 'row', moves[part]))]
    psum x1 -> x0, blocking collectives: 21.8 us -> none  [per_device(): gamma_total, beta_total = lax.psum((gamma_terms, beta_terms), 'row')]
    all_gather x3 -> x0, waiting for transfers between devices: 12.8 us -> none  [the longest x1 8.99 us: per_device(): squares = lax.all_gather(squares_own, 'chan', axis=0, tiled=True)]
    reduce_scatter x1 -> x0, waiting for transfers between devices: 7.88 us -> none  [per_device(): lax.psum_scatter(partial_value, 'chan', scatter_dimension=0, tiled=True)]
    select_n x0 -> x13, other arithmetic: none -> 6.46 us  [the longest x6 3.15 us: ring_sum(): jnp.take(stacked, order, axis=0).reshape((-1,) + stacked.shape[2:])]
    all_to_all x1 -> x0, blocking collectives: 4.58 us -> none  [per_device(): lax.all_to_all(gdn_gamma, 'chan', split_axis=1, concat_axis=0, tiled=True)]
  transfers between devices with their start and end apart: 10 -> 66, of which waited for: 7 -> 43; matrix products, arithmetic and copies ran while one was open for 7% -> 16% of each run, Pallas kernels for 0% -> 0%
where the time goes in v1:
time: 276 us
  waiting for transfers between devices  122 us (44%)
  starting transfers between devices  69.1 us (25%)
  between operations  25.5 us (9%)
  local copies, waits for them, and re-layouts  24.9 us (9%)
  other arithmetic  17.1 us (6%)
  matrix products  16.6 us (6%)
    all_gather x1, waiting for transfers between devices, per_device(): shard_piece = lax.all_gather(conv_weight, 'row', axis=0, tiled=True)  57.8 us
    ppermute x28, waiting for transfers between devices, ring_sum(): gathered[part].append(lax.ppermute(gathered[part][-1], 'row', moves[part]))  33.7 us
    ppermute x28, starting transfers between devices, ring_sum(): gathered[part].append(lax.ppermute(gathered[part][-1], 'row', moves[part]))  29.6 us
    ppermute x28, starting transfers between devices, ring_sum(): got = lax.ppermute(carry[part], 'row', moves[part])  28.9 us
    ppermute x28, waiting for transfers between devices, ring_sum(): got = lax.ppermute(carry[part], 'row', moves[part])  24.9 us
    ppermute x2, starting transfers between devices, extended(): before = lax.ppermute(last, axis, up)  7.28 us
    unnamed x79, local copies, waits for them, and re-layouts  7.24 us
    reshape x1, local copies, waits for them, and re-layouts, per_device(): flat = shard_piece.reshape(shard_piece.shape[0], 9 * in_local)  5.57 us
  transfers between devices with their start and end apart: 66, of which 43 were waited for; matrix products, arithmetic and copies ran while one was open for 16% of the time, Pallas kernels for 0%

profile of v1, /device:TPU:0, one launch (start us, length us, event | category | flops | bytes accessed | tf_op | source)
XLA Modules:
  0.0 275.6 jit_solution(1936061474365692763)
XLA Ops:
  9.1 4.9 %collective-permute-start = (bf16[212,1,128]{2,1,0:T(2,128)(2,1)S(1)}, bf16[212,1,128]{2,1,0:T(2,128)(2,1)S(1)}, u32[]{:S(2)}, u32[]{:S(2)}) collective-permute-start(bf16[212,1,128]{2,1,0:T(2,128)(2,1)S(1)} %get-tuple-element.59), channel_id=1, source_target_pairs={{0,2},{2,4},{4,6},{6,8},{8,10},{10,12},{12,14},{1,3},{3,5},{5,7},{... | collective-permute-start | bytes 162824 | tf_op jit(solution)/shard_map/ppermute | solution.py:19
  16.3 4.3 %collective-permute-done.1 = bf16[212,1,128]{2,1,0:T(2,128)(2,1)S(1)} collective-permute-done((bf16[212,1,128]{2,1,0:T(2,128)(2,1)S(1)}, bf16[212,1,128]{2,1,0:T(2,128)(2,1)S(1)}, u32[]{:S(2)}, u32[]{:S(2)}) %collective-permute-start.1) | collective-permute-done | bytes 54304 | tf_op jit(solution)/shard_map/ppermute | solution.py:20
  20.6 2.1 fusion.40
  27.2 57.8 %all-gather.2.cloned.1.call-done = bf16[1024,9,212]{0,2,1:T(8,128)(2,1)} async-done(((bf16[128,9,212]{0,2,1:T(8,128)(2,1)}), bf16[1024,9,212]{0,2,1:T(8,128)(2,1)}) %all-gather.2.cloned.1.call-update) | async-done | bytes 3907600 | tf_op jit(solution)/shard_map/all_gather | solution.py:124
  85.0 5.6 %reshape.111 = bf16[1024,1908]{0,1:T(8,128)(2,1)} reshape(bf16[1024,9,212]{0,2,1:T(8,128)(2,1)} %all-gather.2.cloned.1.call-done) | data formatting | bytes 7815168 | tf_op jit(solution)/shard_map/reshape | solution.py:125
  90.6 5.1 %convolution_bitcast_fusion = f32[1024,512]{0,1:T(8,128)S(1)} fusion(bf16[1908,512]{1,0:T(8,128)(2,1)} %bitcast.291, bf16[1024,1908]{0,1:T(8,128)(2,1)} %reshape.111), kind=kOutput, calls=%fused_computation.16 | convolution fusion | flops 2000683008 | bytes 7958528 | tf_op jit(solution)/shard_map/dot_general | solution.py:126
  112.1 2.4 copy.10
  121.0 2.2 convert_reduce_fusion
  124.4 2.0 collective-permute-start.37
  126.4 2.1 fusion.62
  175.4 2.2 collective-permute-done.64
  184.2 2.0 collective-permute-start.24
  186.2 2.9 %collective-permute-done.10 = f32[32,1024]{1,0:T(8,128)S(1)} collective-permute-done((f32[32,1024]{1,0:T(8,128)S(1)}, f32[32,1024]{1,0:T(8,128)S(1)}, u32[]{:S(2)}, u32[]{:S(2)}) %collective-permute-start.10) | collective-permute-done | bytes 131104 | tf_op jit(solution)/shard_map/ppermute | solution.py:97
  189.2 2.0 collective-permute-start.25
  191.2 2.9 %collective-permute-done.11 = f32[32,1024]{1,0:T(8,128)S(1)} collective-permute-done((f32[32,1024]{1,0:T(8,128)S(1)}, f32[32,1024]{1,0:T(8,128)S(1)}, u32[]{:S(2)}, u32[]{:S(2)}) %collective-permute-start.11) | collective-permute-done | bytes 131104 | tf_op jit(solution)/shard_map/ppermute | solution.py:97
  194.3 2.0 collective-permute-start.26
  196.2 2.9 %collective-permute-done.12 = f32[32,1024]{1,0:T(8,128)S(1)} collective-permute-done((f32[32,1024]{1,0:T(8,128)S(1)}, f32[32,1024]{1,0:T(8,128)S(1)}, u32[]{:S(2)}, u32[]{:S(2)}) %collective-permute-start.12) | collective-permute-done | bytes 131104 | tf_op jit(solution)/shard_map/ppermute | solution.py:97
  199.3 2.0 collective-permute-start.27
  201.3 2.7 fusion.32
  204.3 2.0 collective-permute-start.28
  206.3 3.8 %collective-permute-done.14 = f32[32,1024]{1,0:T(8,128)S(1)} collective-permute-done((f32[32,1024]{1,0:T(8,128)S(1)}, f32[32,1024]{1,0:T(8,128)S(1)}, u32[]{:S(2)}, u32[]{:S(2)}) %collective-permute-start.14) | collective-permute-done | bytes 131104 | tf_op jit(solution)/shard_map/ppermute | solution.py:97
  212.3 2.9 %collective-permute-done.15 = f32[32,1024]{1,0:T(8,128)S(1)} collective-permute-done((f32[32,1024]{1,0:T(8,128)S(1)}, f32[32,1024]{1,0:T(8,128)S(1)}, u32[]{:S(2)}, u32[]{:S(2)}) %collective-permute-start.15) | collective-permute-done | bytes 131104 | tf_op jit(solution)/shard_map/ppermute | solution.py:97
  217.8 2.4 collective-permute-start.7
  221.5 2.7 collective-permute-start.17
  225.8 6.9 %collective-permute-done.17 = f32[32,1024]{1,0:T(8,128)S(1)} collective-permute-done((f32[32,1024]{1,0:T(8,128)S(1)}, f32[32,1024]{1,0:T(8,128)S(1)}, u32[]{:S(2)}, u32[]{:S(2)}) %collective-permute-start.17) | collective-permute-done | bytes 131104 | tf_op jit(solution)/shard_map/ppermute | solution.py:102
  232.7 2.5 collective-permute-start.18
  242.1 2.0 collective-permute-start.19
  244.3 3.5 %collective-permute-done.19 = f32[32,1024]{1,0:T(8,128)S(1)} collective-permute-done((f32[32,1024]{1,0:T(8,128)S(1)}, f32[32,1024]{1,0:T(8,128)S(1)}, u32[]{:S(2)}, u32[]{:S(2)}) %collective-permute-start.19) | collective-permute-done | bytes 131104 | tf_op jit(solution)/shard_map/ppermute | solution.py:102
  247.8 2.5 collective-permute-start.20
  250.6 3.4 %collective-permute-done.20 = f32[32,1024]{1,0:T(8,128)S(1)} collective-permute-done((f32[32,1024]{1,0:T(8,128)S(1)}, f32[32,1024]{1,0:T(8,128)S(1)}, u32[]{:S(2)}, u32[]{:S(2)}) %collective-permute-start.20) | collective-permute-done | bytes 131104 | tf_op jit(solution)/shard_map/ppermute | solution.py:102
  256.4 3.1 %collective-permute-done.21 = f32[32,1024]{1,0:T(8,128)S(1)} collective-permute-done((f32[32,1024]{1,0:T(8,128)S(1)}, f32[32,1024]{1,0:T(8,128)S(1)}, u32[]{:S(2)}, u32[]{:S(2)}) %collective-permute-start.21) | collective-permute-done | bytes 131104 | tf_op jit(solution)/shard_map/ppermute | solution.py:102
  261.6 2.8 %collective-permute-done.22 = f32[32,1024]{1,0:T(8,128)S(1)} collective-permute-done((f32[32,1024]{1,0:T(8,128)S(1)}, f32[32,1024]{1,0:T(8,128)S(1)}, u32[]{:S(2)}, u32[]{:S(2)}) %collective-permute-start.22) | collective-permute-done | bytes 131104 | tf_op jit(solution)/shard_map/ppermute | solution.py:102
  (269 shorter events, 99.9 us)
Async XLA Ops:
  7.2 77.8 %all-gather.2.cloned.1.call-start = ((), (), s32[]{:S(2)}) async-start(), calls=%async_computation | async-start | bytes 4478976 | tf_op jit(solution)/shard_map/all_gather | solution.py:124
  9.1 7.2 %collective-permute-start = (bf16[212,1,128]{2,1,0:T(2,128)(2,1)S(1)}, bf16[212,1,128]{2,1,0:T(2,128)(2,1)S(1)}, u32[]{:S(2)}, u32[]{:S(2)}) collective-permute-start(bf16[212,1,128]{2,1,0:T(2,128)(2,1)S(1)} %get-tuple-element.59), channel_id=1, source_target_pairs={{0,2},{2,4},{4,6},{6,8},{8,10},{10,12},{12,14},{1,3},{3,5},{5,7},{... | collective-permute-start | bytes 162824 | tf_op jit(solution)/shard_map/ppermute | solution.py:19
  14.0 6.6 %collective-permute-start.1 = (bf16[212,1,128]{2,1,0:T(2,128)(2,1)S(1)}, bf16[212,1,128]{2,1,0:T(2,128)(2,1)S(1)}, u32[]{:S(2)}, u32[]{:S(2)}) collective-permute-start(bf16[212,1,128]{2,1,0:T(2,128)(2,1)S(1)} %get-tuple-element.60), channel_id=1, source_target_pairs={{2,0},{4,2},{6,4},{8,6},{10,8},{12,10},{14,12},{3,1},{5,3},{7,5},{... | collective-permute-start | bytes 162824 | tf_op jit(solution)/shard_map/ppermute | solution.py:20
  96.8 18.9 %collective-permute-start.2 = (f32[512,512]{0,1:T(8,128)}, f32[512,512]{0,1:T(8,128)}, u32[]{:S(2)}, u32[]{:S(2)}) collective-permute-start(f32[512,512]{0,1:T(8,128)} %slice_select_fusion), channel_id=1, source_target_pairs={{0,1},{1,0},{2,3},{3,2},{4,5},{5,4},{6,7},{7,6},{8,9},{9,8},{10,11... | collective-permute-start | bytes 3145736 | tf_op jit(solution)/shard_map/ppermute | solution.py:53
  100.5 100.8 %collective-permute-start.4 = (bf16[512,512]{0,1:T(8,128)(2,1)}, bf16[512,512]{0,1:T(8,128)(2,1)}, u32[]{:S(2)}, u32[]{:S(2)}) collective-permute-start(bf16[512,512]{0,1:T(8,128)(2,1)} %get-tuple-element.56), channel_id=1, source_target_pairs={{0,1},{1,0},{2,3},{3,2},{4,5},{5,4},{6,7},{7,6},{8,9},{9,8},{10,11... | collective-permute-start | bytes 1572872 | tf_op jit(solution)/shard_map/ppermute | solution.py:137
  124.4 6.6 %collective-permute-start.51 = (f32[32]{0:T(128)S(1)}, f32[32]{0:T(128)S(1)}, u32[]{:S(2)}, u32[]{:S(2)}) collective-permute-start(f32[32]{0:T(128)S(1)} %fusion.78), channel_id=1, source_target_pairs={{2,0},{6,2},{10,6},{14,10},{12,14},{8,12},{4,8},{0,4},{3,1},{7,3},... | collective-permute-start | bytes 392 | tf_op jit(solution)/shard_map/ppermute | solution.py:97
  124.4 7.2 %collective-permute-start.37 = (f32[32]{0:T(128)S(1)}, f32[32]{0:T(128)S(1)}, u32[]{:S(2)}, u32[]{:S(2)}) collective-permute-start(f32[32]{0:T(128)S(1)} %fusion.63), channel_id=1, source_target_pairs={{0,2},{2,6},{6,10},{10,14},{14,12},{12,8},{8,4},{4,0},{1,3},{3,7},... | collective-permute-start | bytes 392 | tf_op jit(solution)/shard_map/ppermute | solution.py:97
  126.4 74.8 %collective-permute-start.5 = (bf16[512,512]{0,1:T(8,128)(2,1)}, bf16[512,512]{0,1:T(8,128)(2,1)}, u32[]{:S(2)}, u32[]{:S(2)}) collective-permute-start(bf16[512,512]{0,1:T(8,128)(2,1)} %get-tuple-element.35), channel_id=1, source_target_pairs={{0,1},{1,0},{2,3},{3,2},{4,5},{5,4},{6,7},{7,6},{8,9},{9,8},{10,11... | collective-permute-start | bytes 1572872 | tf_op jit(solution)/shard_map/ppermute | solution.py:42
  129.5 54.5 %collective-permute-start.9 = (f32[32,1024]{1,0:T(8,128)}, f32[32,1024]{1,0:T(8,128)S(1)}, u32[]{:S(2)}, u32[]{:S(2)}) collective-permute-start(f32[32,1024]{1,0:T(8,128)} %select_bitcast_fusion.1), channel_id=1, source_target_pairs={{0,2},{2,6},{6,10},{10,14},{14,12},{12,8},{8,4},{4,0},{1,3},{3,7},... | collective-permute-start | bytes 393224 | tf_op jit(solution)/shard_map/ppermute | solution.py:97
  175.1 9.1 %collective-permute-start.23 = (f32[32,1024]{1,0:T(8,128)S(1)}, f32[32,1024]{1,0:T(8,128)S(1)}, u32[]{:S(2)}, u32[]{:S(2)}) collective-permute-start(f32[32,1024]{1,0:T(8,128)S(1)} %select_bitcast_fusion), channel_id=1, source_target_pairs={{2,0},{6,2},{10,6},{14,10},{12,14},{8,12},{4,8},{0,4},{3,1},{7,3},... | collective-permute-start | bytes 393224 | tf_op jit(solution)/shard_map/ppermute | solution.py:97
  184.0 5.0 %collective-permute-start.10 = (f32[32,1024]{1,0:T(8,128)S(1)}, f32[32,1024]{1,0:T(8,128)S(1)}, u32[]{:S(2)}, u32[]{:S(2)}) collective-permute-start(f32[32,1024]{1,0:T(8,128)S(1)} %bitcast_add_fusion.13), channel_id=1, source_target_pairs={{0,2},{2,6},{6,10},{10,14},{14,12},{12,8},{8,4},{4,0},{1,3},{3,7},... | collective-permute-start | bytes 393224 | tf_op jit(solution)/shard_map/ppermute | solution.py:97
  184.2 5.0 %collective-permute-start.24 = (f32[32,1024]{1,0:T(8,128)S(1)}, f32[32,1024]{1,0:T(8,128)S(1)}, u32[]{:S(2)}, u32[]{:S(2)}) collective-permute-start(f32[32,1024]{1,0:T(8,128)S(1)} %bitcast_add_fusion.6), channel_id=1, source_target_pairs={{2,0},{6,2},{10,6},{14,10},{12,14},{8,12},{4,8},{0,4},{3,1},{7,3},... | collective-permute-start | bytes 393224 | tf_op jit(solution)/shard_map/ppermute | solution.py:97
  189.0 5.0 %collective-permute-start.11 = (f32[32,1024]{1,0:T(8,128)S(1)}, f32[32,1024]{1,0:T(8,128)S(1)}, u32[]{:S(2)}, u32[]{:S(2)}) collective-permute-start(f32[32,1024]{1,0:T(8,128)S(1)} %bitcast_add_fusion.12), channel_id=1, source_target_pairs={{0,2},{2,6},{6,10},{10,14},{14,12},{12,8},{8,4},{4,0},{1,3},{3,7},... | collective-permute-start | bytes 393224 | tf_op jit(solution)/shard_map/ppermute | solution.py:97
  199.3 5.0 %collective-permute-start.27 = (f32[32,1024]{1,0:T(8,128)S(1)}, f32[32,1024]{1,0:T(8,128)S(1)}, u32[]{:S(2)}, u32[]{:S(2)}) collective-permute-start(f32[32,1024]{1,0:T(8,128)S(1)} %bitcast_add_fusion.3), channel_id=1, source_target_pairs={{2,0},{6,2},{10,6},{14,10},{12,14},{8,12},{4,8},{0,4},{3,1},{7,3},... | collective-permute-start | bytes 393224 | tf_op jit(solution)/shard_map/ppermute | solution.py:97
  204.1 13.3 %collective-permute-start.6 = (bf16[512,4,128]{0,2,1:T(8,128)(2,1)S(1)}, bf16[512,4,128]{0,2,1:T(8,128)(2,1)S(1)}, u32[]{:S(2)}, u32[]{:S(2)}) collective-permute-start(bf16[512,4,128]{0,2,1:T(8,128)(2,1)S(1)} %bitcast.292), channel_id=1, source_target_pairs={{0,1},{1,0},{2,3},{3,2},{4,5},{5,4},{6,7},{7,6},{8,9},{9,8},{10,11... | collective-permute-start | bytes 1572872 | tf_op jit(solution)/shard_map/ppermute | solution.py:42
  204.2 5.9 %collective-permute-start.14 = (f32[32,1024]{1,0:T(8,128)S(1)}, f32[32,1024]{1,0:T(8,128)S(1)}, u32[]{:S(2)}, u32[]{:S(2)}) collective-permute-start(f32[32,1024]{1,0:T(8,128)S(1)} %bitcast_add_fusion.9), channel_id=1, source_target_pairs={{0,2},{2,6},{6,10},{10,14},{14,12},{12,8},{8,4},{4,0},{1,3},{3,7},... | collective-permute-start | bytes 393224 | tf_op jit(solution)/shard_map/ppermute | solution.py:97
  204.3 6.1 %collective-permute-start.28 = (f32[32,1024]{1,0:T(8,128)S(1)}, f32[32,1024]{1,0:T(8,128)S(1)}, u32[]{:S(2)}, u32[]{:S(2)}) collective-permute-start(f32[32,1024]{1,0:T(8,128)S(1)} %bitcast_add_fusion.2), channel_id=1, source_target_pairs={{2,0},{6,2},{10,6},{14,10},{12,14},{8,12},{4,8},{0,4},{3,1},{7,3},... | collective-permute-start | bytes 393224 | tf_op jit(solution)/shard_map/ppermute | solution.py:97
  210.1 5.1 %collective-permute-start.15 = (f32[32,1024]{1,0:T(8,128)S(1)}, f32[32,1024]{1,0:T(8,128)S(1)}, u32[]{:S(2)}, u32[]{:S(2)}) collective-permute-start(f32[32,1024]{1,0:T(8,128)S(1)} %bitcast_add_fusion.8), channel_id=1, source_target_pairs={{0,2},{2,6},{6,10},{10,14},{14,12},{12,8},{8,4},{4,0},{1,3},{3,7},... | collective-permute-start | bytes 393224 | tf_op jit(solution)/shard_map/ppermute | solution.py:97
  210.5 5.3 %collective-permute-start.29 = (f32[32,1024]{1,0:T(8,128)S(1)}, f32[32,1024]{1,0:T(8,128)S(1)}, u32[]{:S(2)}, u32[]{:S(2)}) collective-permute-start(f32[32,1024]{1,0:T(8,128)S(1)} %bitcast_add_fusion.1), channel_id=1, source_target_pairs={{2,0},{6,2},{10,6},{14,10},{12,14},{8,12},{4,8},{0,4},{3,1},{7,3},... | collective-permute-start | bytes 393224 | tf_op jit(solution)/shard_map/ppermute | solution.py:97
  215.2 6.2 %collective-permute-start.16 = (f32[32,1024]{1,0:T(8,128)S(1)}, f32[32,1024]{1,0:T(8,128)S(1)}, u32[]{:S(2)}, u32[]{:S(2)}) collective-permute-start(f32[32,1024]{1,0:T(8,128)S(1)} %get-tuple-element.37), channel_id=1, source_target_pairs={{0,2},{2,6},{6,10},{10,14},{14,12},{12,8},{8,4},{4,0},{1,3},{3,7},... | collective-permute-start | bytes 393224 | tf_op jit(solution)/shard_map/ppermute | solution.py:102
  215.8 8.4 %collective-permute-start.30 = (f32[32,1024]{1,0:T(8,128)S(1)}, f32[32,1024]{1,0:T(8,128)S(1)}, u32[]{:S(2)}, u32[]{:S(2)}) collective-permute-start(f32[32,1024]{1,0:T(8,128)S(1)} %get-tuple-element.39), channel_id=1, source_target_pairs={{2,0},{6,2},{10,6},{14,10},{12,14},{8,12},{4,8},{0,4},{3,1},{7,3},... | collective-permute-start | bytes 393224 | tf_op jit(solution)/shard_map/ppermute | solution.py:102
  217.8 17.5 %collective-permute-start.7 = (bf16[1024,1,128]{0,2,1:T(8,128)(2,1)S(1)}, bf16[1024,1,128]{0,2,1:T(8,128)(2,1)S(1)}, u32[]{:S(2)}, u32[]{:S(2)}) collective-permute-start(bf16[1024,1,128]{0,2,1:T(8,128)(2,1)S(1)} %get-tuple-element.53), channel_id=1, source_target_pairs={{0,2},{2,4},{4,6},{6,8},{8,10},{10,12},{12,14},{1,3},{3,5},{5,7},{... | collective-permute-start | bytes 786440 | tf_op jit(solution)/shard_map/ppermute | solution.py:19
  220.2 15.1 %collective-permute-start.8 = (bf16[1024,1,128]{0,2,1:T(8,128)(2,1)S(1)}, bf16[1024,1,128]{0,2,1:T(8,128)(2,1)S(1)}, u32[]{:S(2)}, u32[]{:S(2)}) collective-permute-start(bf16[1024,1,128]{0,2,1:T(8,128)(2,1)S(1)} %get-tuple-element.54), channel_id=1, source_target_pairs={{2,0},{4,2},{6,4},{8,6},{10,8},{12,10},{14,12},{3,1},{5,3},{7,5},{... | collective-permute-start | bytes 786440 | tf_op jit(solution)/shard_map/ppermute | solution.py:20
  221.5 11.2 %collective-permute-start.17 = (f32[32,1024]{1,0:T(8,128)S(1)}, f32[32,1024]{1,0:T(8,128)S(1)}, u32[]{:S(2)}, u32[]{:S(2)}) collective-permute-start(f32[32,1024]{1,0:T(8,128)S(1)} %collective-permute-done.16), channel_id=1, source_target_pairs={{0,2},{2,6},{6,10},{10,14},{14,12},{12,8},{8,4},{4,0},{1,3},{3,7},... | collective-permute-start | bytes 393224 | tf_op jit(solution)/shard_map/ppermute | solution.py:102
  224.2 11.0 %collective-permute-start.31 = (f32[32,1024]{1,0:T(8,128)S(1)}, f32[32,1024]{1,0:T(8,128)S(1)}, u32[]{:S(2)}, u32[]{:S(2)}) collective-permute-start(f32[32,1024]{1,0:T(8,128)S(1)} %collective-permute-done.30), channel_id=1, source_target_pairs={{2,0},{6,2},{10,6},{14,10},{12,14},{8,12},{4,8},{0,4},{3,1},{7,3},... | collective-permute-start | bytes 393224 | tf_op jit(solution)/shard_map/ppermute | solution.py:102
  232.7 9.4 %collective-permute-start.18 = (f32[32,1024]{1,0:T(8,128)S(1)}, f32[32,1024]{1,0:T(8,128)S(1)}, u32[]{:S(2)}, u32[]{:S(2)}) collective-permute-start(f32[32,1024]{1,0:T(8,128)S(1)} %collective-permute-done.17), channel_id=1, source_target_pairs={{0,2},{2,6},{6,10},{10,14},{14,12},{12,8},{8,4},{4,0},{1,3},{3,7},... | collective-permute-start | bytes 393224 | tf_op jit(solution)/shard_map/ppermute | solution.py:102
  235.2 9.0 %collective-permute-start.32 = (f32[32,1024]{1,0:T(8,128)S(1)}, f32[32,1024]{1,0:T(8,128)S(1)}, u32[]{:S(2)}, u32[]{:S(2)}) collective-permute-start(f32[32,1024]{1,0:T(8,128)S(1)} %collective-permute-done.31), channel_id=1, source_target_pairs={{2,0},{6,2},{10,6},{14,10},{12,14},{8,12},{4,8},{0,4},{3,1},{7,3},... | collective-permute-start | bytes 393224 | tf_op jit(solution)/shard_map/ppermute | solution.py:102
  242.1 5.6 %collective-permute-start.19 = (f32[32,1024]{1,0:T(8,128)S(1)}, f32[32,1024]{1,0:T(8,128)S(1)}, u32[]{:S(2)}, u32[]{:S(2)}) collective-permute-start(f32[32,1024]{1,0:T(8,128)S(1)} %collective-permute-done.18), channel_id=1, source_target_pairs={{0,2},{2,6},{6,10},{10,14},{14,12},{12,8},{8,4},{4,0},{1,3},{3,7},... | collective-permute-start | bytes 393224 | tf_op jit(solution)/shard_map/ppermute | solution.py:102
  244.2 6.4 %collective-permute-start.33 = (f32[32,1024]{1,0:T(8,128)S(1)}, f32[32,1024]{1,0:T(8,128)S(1)}, u32[]{:S(2)}, u32[]{:S(2)}) collective-permute-start(f32[32,1024]{1,0:T(8,128)S(1)} %collective-permute-done.32), channel_id=1, source_target_pairs={{2,0},{6,2},{10,6},{14,10},{12,14},{8,12},{4,8},{0,4},{3,1},{7,3},... | collective-permute-start | bytes 393224 | tf_op jit(solution)/shard_map/ppermute | solution.py:102
  247.8 6.3 %collective-permute-start.20 = (f32[32,1024]{1,0:T(8,128)S(1)}, f32[32,1024]{1,0:T(8,128)S(1)}, u32[]{:S(2)}, u32[]{:S(2)}) collective-permute-start(f32[32,1024]{1,0:T(8,128)S(1)} %collective-permute-done.19), channel_id=1, source_target_pairs={{0,2},{2,6},{6,10},{10,14},{14,12},{12,8},{8,4},{4,0},{1,3},{3,7},... | collective-permute-start | bytes 393224 | tf_op jit(solution)/shard_map/ppermute | solution.py:102
  250.6 5.5 %collective-permute-start.34 = (f32[32,1024]{1,0:T(8,128)S(1)}, f32[32,1024]{1,0:T(8,128)S(1)}, u32[]{:S(2)}, u32[]{:S(2)}) collective-permute-start(f32[32,1024]{1,0:T(8,128)S(1)} %collective-permute-done.33), channel_id=1, source_target_pairs={{2,0},{6,2},{10,6},{14,10},{12,14},{8,12},{4,8},{0,4},{3,1},{7,3},... | collective-permute-start | bytes 393224 | tf_op jit(solution)/shard_map/ppermute | solution.py:102
  254.0 5.4 %collective-permute-start.21 = (f32[32,1024]{1,0:T(8,128)S(1)}, f32[32,1024]{1,0:T(8,128)S(1)}, u32[]{:S(2)}, u32[]{:S(2)}) collective-permute-start(f32[32,1024]{1,0:T(8,128)S(1)} %collective-permute-done.20), channel_id=1, source_target_pairs={{0,2},{2,6},{6,10},{10,14},{14,12},{12,8},{8,4},{4,0},{1,3},{3,7},... | collective-permute-start | bytes 393224 | tf_op jit(solution)/shard_map/ppermute | solution.py:102
  (62 other events, 418.4 us)
Sparse Core Ops, SparseCore 0:
  10.0 74.9 all-gather.1

commit v2 on v1

--- a/solution.py
+++ b/solution.py
@@ -40,16 +40,20 @@
 
 def chan_gather(x):
     other = lax.ppermute(x, "chan", SWAP)
-    first = lax.axis_index("chan") == 0
-    return jnp.where(first, jnp.concatenate([x, other], 0), jnp.concatenate([other, x], 0))
+    both = jnp.concatenate([x, other], 0)
+    return jnp.roll(both, lax.axis_index("chan") * x.shape[0], axis=0)
+
+
+def chan_gather_into(mine, other):
+    both = jnp.concatenate([mine, other], 0)
+    return jnp.roll(both, lax.axis_index("chan") * mine.shape[0], axis=0)
 
 
 def chan_scatter_sum(x):
     half = x.shape[0] // 2
-    first = lax.axis_index("chan") == 0
-    top, bottom = x[:half], x[half:]
-    mine = jnp.where(first, top, bottom)
-    theirs = jnp.where(first, bottom, top)
+    index = lax.axis_index("chan")
+    mine = lax.dynamic_slice_in_dim(x, index * half, half, 0)
+    theirs = lax.dynamic_slice_in_dim(x, (1 - index) * half, half, 0)
     return mine + lax.ppermute(theirs, "chan", SWAP)
 
 
@@ -118,7 +122,6 @@
         col_count = band_strip.shape[2]
         pixels = row_count * col_count
         lat_local = gdn_gamma.shape[0]
-        first = lax.axis_index("chan") == 0
         rimmed = extended(band_strip, (("row", 1),), 1)
         columns = tap_columns(rimmed, row_count, col_count)
         shard_piece = lax.all_gather(conv_weight, "row", axis=0, tiled=True)
@@ -132,14 +135,10 @@
         latent = (pre * inverse).astype(jnp.bfloat16)
         upstream = cotangent.reshape(lat_local, pixels).astype(jnp.float32)
         shares = (-0.5 * upstream * pre * inverse * inverse * inverse).astype(jnp.bfloat16)
-        gamma_left, gamma_right = gdn_gamma[:, :lat_local], gdn_gamma[:, lat_local:]
-        gamma_mine = jnp.where(first, gamma_left, gamma_right)
-        gamma_theirs = lax.ppermute(jnp.where(first, gamma_right, gamma_left), "chan", SWAP)
-        gamma_cols = jnp.where(
-            first,
-            jnp.concatenate([gamma_mine, gamma_theirs], 0),
-            jnp.concatenate([gamma_theirs, gamma_mine], 0),
-        )
+        index = lax.axis_index("chan")
+        gamma_mine = lax.dynamic_slice_in_dim(gdn_gamma, index * lat_local, lat_local, 1)
+        gamma_theirs = lax.dynamic_slice_in_dim(gdn_gamma, (1 - index) * lat_local, lat_local, 1)
+        gamma_cols = chan_gather_into(gamma_mine, lax.ppermute(gamma_theirs, "chan", SWAP))
         shares_all = chan_gather(shares)
         back_sum = lax.dot_general(
             gamma_cols, shares_all, (((0,), (0,)), ((), ())), preferred_element_type=jnp.float32
@@ -149,10 +148,15 @@
             shares, squares, (((1,), (1,)), ((), ())), preferred_element_type=jnp.float32
         )
         beta_terms = jnp.sum(shares.astype(jnp.float32), axis=1)
+        joined = jnp.concatenate(
+            [gamma_terms, jnp.broadcast_to(beta_terms[:, None], (lat_local, 128))], 1
+        )
         if len(ring) <= 16:
-            gamma_total, beta_total = ring_sum([gamma_terms, beta_terms], ring)
+            (joined_total,) = ring_sum([joined], ring)
         else:
-            gamma_total, beta_total = lax.psum((gamma_terms, beta_terms), "row")
+            joined_total = lax.psum(joined, "row")
+        gamma_total = joined_total[:, : gamma_terms.shape[1]]
+        beta_total = joined_total[:, gamma_terms.shape[1]]
         scale_factor = 1.0 / math.sqrt(pixels * lax.axis_size("row"))
         grad_gamma = gamma_total * scale_factor
         grad_beta = beta_total * scale_factor

time: 276 us -> 232 us (0.84)
  starting transfers between devices: 69.1 us -> 46.8 us
  waiting for transfers between devices: 122 us -> 104 us
  other arithmetic: 17.1 us -> 12.4 us
    ppermute x28 -> x14, waiting for transfers between devices: 33.7 us -> 14 us  [ring_sum(): gathered[part].append(lax.ppermute(gathered[part][-1], 'row', moves[part]))]
    ppermute x28 -> x14, starting transfers between devices: 28.9 us -> 15.1 us  [ring_sum(): got = lax.ppermute(carry[part], 'row', moves[part])]
    ppermute x28 -> x14, starting transfers between devices: 29.6 us -> 17.9 us  [ring_sum(): gathered[part].append(lax.ppermute(gathered[part][-1], 'row', moves[part]))]
    ppermute x2, waiting for transfers between devices: 0.98 us -> 7.17 us  [extended(): before = lax.ppermute(last, axis, up)]
    ppermute x28 -> x14, waiting for transfers between devices: 24.9 us -> 20.7 us  [ring_sum(): got = lax.ppermute(carry[part], 'row', moves[part])]
    ppermute x2, waiting for transfers between devices: 4.34 us -> 1.06 us  [extended(): after = lax.ppermute(leading, axis, down)]
    ppermute x2, starting transfers between devices: 7.28 us -> 10.1 us  [extended(): before = lax.ppermute(last, axis, up)]
    unnamed x79 -> x43, local copies, waits for them, and re-layouts: 7.24 us -> 9.18 us
  transfers between devices with their start and end apart: 66 -> 38, of which waited for: 43 -> 20; matrix products, arithmetic and copies ran while one was open for 16% -> 16% of each run, Pallas kernels for 0% -> 0%
where the time goes in v2:
time: 232 us; the launch traced here: 231 us
  waiting for transfers between devices  104 us (45%)
  starting transfers between devices  46.8 us (20%)
  between operations  25.5 us (11%)
  local copies, waits for them, and re-layouts  25.1 us (11%)
  matrix products  17.8 us (8%)
  other arithmetic  12.4 us (5%)
    all_gather x1, waiting for transfers between devices, per_device(): shard_piece = lax.all_gather(conv_weight, 'row', axis=0, tiled=True)  60.2 us
    ppermute x14, waiting for transfers between devices, ring_sum(): got = lax.ppermute(carry[part], 'row', moves[part])  20.7 us
    ppermute x14, starting transfers between devices, ring_sum(): gathered[part].append(lax.ppermute(gathered[part][-1], 'row', moves[part]))  17.9 us
    ppermute x14, starting transfers between devices, ring_sum(): got = lax.ppermute(carry[part], 'row', moves[part])  15.1 us
    ppermute x14, waiting for transfers between devices, ring_sum(): gathered[part].append(lax.ppermute(gathered[part][-1], 'row', moves[part]))  14 us
    ppermute x2, starting transfers between devices, extended(): before = lax.ppermute(last, axis, up)  10.1 us
    unnamed x43, local copies, waits for them, and re-layouts  9.18 us
    ppermute x2, waiting for transfers between devices, extended(): before = lax.ppermute(last, axis, up)  7.17 us
  transfers between devices with their start and end apart: 38, of which 20 were waited for; matrix products, arithmetic and copies ran while one was open for 16% of the time, Pallas kernels for 0%

profile of v2, /device:TPU:0, one launch (start us, length us, event | category | flops | bytes accessed | tf_op | source)
XLA Modules:
  0.0 231.5 jit_solution(3176500248424967050)
XLA Ops:
  10.4 5.5 %collective-permute-start = (bf16[212,1,128]{2,1,0:T(2,128)(2,1)S(1)}, bf16[212,1,128]{2,1,0:T(2,128)(2,1)S(1)}, u32[]{:S(2)}, u32[]{:S(2)}) collective-permute-start(bf16[212,1,128]{2,1,0:T(2,128)(2,1)S(1)} %get-tuple-element.49), channel_id=1, source_target_pairs={{0,2},{2,4},{4,6},{6,8},{8,10},{10,12},{12,14},{1,3},{3,5},{5,7},{... | collective-permute-start | bytes 162824 | tf_op jit(solution)/shard_map/ppermute | solution.py:19
  17.0 2.5 %collective-permute-done = bf16[212,1,128]{2,1,0:T(2,128)(2,1)S(1)} collective-permute-done((bf16[212,1,128]{2,1,0:T(2,128)(2,1)S(1)}, bf16[212,1,128]{2,1,0:T(2,128)(2,1)S(1)}, u32[]{:S(2)}, u32[]{:S(2)}) %collective-permute-start) | collective-permute-done | bytes 54304 | tf_op jit(solution)/shard_map/ppermute | solution.py:19
  19.5 2.1 fusion.37
  24.8 60.2 %all-gather.2.cloned.1.call-done = bf16[1024,9,212]{0,2,1:T(8,128)(2,1)} async-done(((bf16[128,9,212]{0,2,1:T(8,128)(2,1)}), bf16[1024,9,212]{0,2,1:T(8,128)(2,1)}) %all-gather.2.cloned.1.call-update) | async-done | bytes 3907600 | tf_op jit(solution)/shard_map/all_gather | solution.py:127
  85.0 5.6 %reshape.76 = bf16[1024,1908]{0,1:T(8,128)(2,1)} reshape(bf16[1024,9,212]{0,2,1:T(8,128)(2,1)} %all-gather.2.cloned.1.call-done) | data formatting | bytes 7815168 | tf_op jit(solution)/shard_map/reshape | solution.py:128
  90.6 5.8 %fusion.80 = f32[512,1024]{1,0:T(8,128)} fusion(bf16[1908,512]{1,0:T(8,128)(2,1)S(1)} %bitcast.235, bf16[1024,1908]{0,1:T(8,128)(2,1)} %reshape.76), kind=kOutput, calls=%fused_computation.177 | convolution fusion | flops 2000683008 | bytes 7958528 | tf_op jit(solution)/shard_map/dot_general | solution.py:129
  112.9 1.8 multiply_convert_fusion.1
  117.7 2.3 %convert_reduce_fusion = (f32[512]{0:T(512)S(1)}, bf16[512,512]{0,1:T(8,128)(2,1)}, bf16[512,512]{0,1:T(8,128)(2,1)}, f32[512,512]{0,1:T(8,128)}) fusion(f32[512,512]{0,1:T(8,128)S(1)} %get-tuple-element.33, f32[512,4,128]{0,2,1:T(8,128)S(1)} %copy.12, bf16[1024,512]{0,1:T(8,128)(2,1)S(1)} %fusion.28, bf16[512,1024]{1,0:T(8,128)(2,1)S(1)} %copy-done.2, ...), kind=kOutput, calls=%fused_computation.63 | convolution fusion | flops 539753984 | bytes 6295552 | tf_op jit(solution)/shard_map/dot_general | solution.py:133
  120.4 1.8 fusion.81
  122.2 2.1 copy.13
  126.8 3.8 %collective-permute-done.9 = f32[32,1152]{1,0:T(8,128)S(1)} collective-permute-done((f32[32,1152]{1,0:T(8,128)S(1)}, f32[32,1152]{1,0:T(8,128)S(1)}, u32[]{:S(2)}, u32[]{:S(2)}) %collective-permute-start.9) | collective-permute-done | bytes 147488 | tf_op jit(solution)/shard_map/ppermute | solution.py:101
  130.6 1.5 collective-permute-start.10
  132.8 3.0 %collective-permute-done.10 = f32[32,1152]{1,0:T(8,128)S(1)} collective-permute-done((f32[32,1152]{1,0:T(8,128)S(1)}, f32[32,1152]{1,0:T(8,128)S(1)}, u32[]{:S(2)}, u32[]{:S(2)}) %collective-permute-start.10) | collective-permute-done | bytes 147488 | tf_op jit(solution)/shard_map/ppermute | solution.py:101
  135.8 1.5 collective-permute-start.11
  138.0 3.4 %collective-permute-done.11 = f32[32,1152]{1,0:T(8,128)S(1)} collective-permute-done((f32[32,1152]{1,0:T(8,128)S(1)}, f32[32,1152]{1,0:T(8,128)S(1)}, u32[]{:S(2)}, u32[]{:S(2)}) %collective-permute-start.11) | collective-permute-done | bytes 147488 | tf_op jit(solution)/shard_map/ppermute | solution.py:101
  143.8 3.3 %fusion.31 = bf16[512,512]{0,1:T(8,128)(2,1)S(1)} fusion(f32[512,512]{0,1:T(8,128)S(1)} %copy-done.7, f32[512,4,128]{0,2,1:T(8,128)S(1)} %copy.12, f32[512,512]{0,1:T(8,128)S(1)} %copy-done.4, s32[]{:T(128)S(6)} %select_n.196, bf16[512,512]{1,0:T(8,128)(2,1)S(1)} %copy-done.8, bf16[512,512]{1,0:T(8,128)(2,1)} %collective-permute-done.4, ...), kind=kOutput, calls=%fused_computation.60 | convolution fusion | flops 546570240 | bytes 5768192 | tf_op jit(solution)/shard_map/dot_general | solution.py:143
  147.2 1.5 collective-permute-start.13
  149.4 4.1 %collective-permute-done.13 = f32[32,1152]{1,0:T(8,128)S(1)} collective-permute-done((f32[32,1152]{1,0:T(8,128)S(1)}, f32[32,1152]{1,0:T(8,128)S(1)}, u32[]{:S(2)}, u32[]{:S(2)}) %collective-permute-start.13) | collective-permute-done | bytes 147488 | tf_op jit(solution)/shard_map/ppermute | solution.py:101
  155.7 3.3 %collective-permute-done.14 = f32[32,1152]{1,0:T(8,128)S(1)} collective-permute-done((f32[32,1152]{1,0:T(8,128)S(1)}, f32[32,1152]{1,0:T(8,128)S(1)}, u32[]{:S(2)}, u32[]{:S(2)}) %collective-permute-start.14) | collective-permute-done | bytes 147488 | tf_op jit(solution)/shard_map/ppermute | solution.py:101
  161.2 3.0 %collective-permute-done.15 = f32[32,1152]{1,0:T(8,128)S(1)} collective-permute-done((f32[32,1152]{1,0:T(8,128)S(1)}, f32[32,1152]{1,0:T(8,128)S(1)}, u32[]{:S(2)}, u32[]{:S(2)}) %collective-permute-start.15) | collective-permute-done | bytes 147488 | tf_op jit(solution)/shard_map/ppermute | solution.py:101
  168.4 4.6 %collective-permute-start.7 = (bf16[1024,1,128]{0,2,1:T(8,128)(2,1)S(1)}, bf16[1024,1,128]{0,2,1:T(8,128)(2,1)S(1)}, u32[]{:S(2)}, u32[]{:S(2)}) collective-permute-start(bf16[1024,1,128]{0,2,1:T(8,128)(2,1)S(1)} %get-tuple-element.45), channel_id=1, source_target_pairs={{0,2},{2,4},{4,6},{6,8},{8,10},{10,12},{12,14},{1,3},{3,5},{5,7},{... | collective-permute-start | bytes 786440 | tf_op jit(solution)/shard_map/ppermute | solution.py:19
  173.5 2.4 %collective-permute-start.17 = (f32[32,1152]{1,0:T(8,128)}, f32[32,1152]{1,0:T(8,128)}, u32[]{:S(2)}, u32[]{:S(2)}) collective-permute-start(f32[32,1152]{1,0:T(8,128)} %collective-permute-done.16), channel_id=1, source_target_pairs={{0,2},{2,6},{6,10},{10,14},{14,12},{12,8},{8,4},{4,0},{1,3},{3,7},... | collective-permute-start | bytes 442376 | tf_op jit(solution)/shard_map/ppermute | solution.py:106
  177.0 4.7 %collective-permute-done.7 = bf16[1024,1,128]{0,2,1:T(8,128)(2,1)S(1)} collective-permute-done((bf16[1024,1,128]{0,2,1:T(8,128)(2,1)S(1)}, bf16[1024,1,128]{0,2,1:T(8,128)(2,1)S(1)}, u32[]{:S(2)}, u32[]{:S(2)}) %collective-permute-start.7) | collective-permute-done | bytes 262176 | tf_op jit(solution)/shard_map/ppermute | solution.py:19
  188.5 2.4 %collective-permute-start.18 = (f32[32,1152]{1,0:T(8,128)}, f32[32,1152]{1,0:T(8,128)S(1)}, u32[]{:S(2)}, u32[]{:S(2)}) collective-permute-start(f32[32,1152]{1,0:T(8,128)} %collective-permute-done.17), channel_id=1, source_target_pairs={{0,2},{2,6},{6,10},{10,14},{14,12},{12,8},{8,4},{4,0},{1,3},{3,7},... | collective-permute-start | bytes 442376 | tf_op jit(solution)/shard_map/ppermute | solution.py:106
  193.0 2.5 %collective-permute-done.18 = f32[32,1152]{1,0:T(8,128)S(1)} collective-permute-done((f32[32,1152]{1,0:T(8,128)}, f32[32,1152]{1,0:T(8,128)S(1)}, u32[]{:S(2)}, u32[]{:S(2)}) %collective-permute-start.18) | collective-permute-done | bytes 147488 | tf_op jit(solution)/shard_map/ppermute | solution.py:106
  195.5 2.4 %collective-permute-start.19 = (f32[32,1152]{1,0:T(8,128)S(1)}, f32[32,1152]{1,0:T(8,128)S(1)}, u32[]{:S(2)}, u32[]{:S(2)}) collective-permute-start(f32[32,1152]{1,0:T(8,128)S(1)} %collective-permute-done.18), channel_id=1, source_target_pairs={{0,2},{2,6},{6,10},{10,14},{14,12},{12,8},{8,4},{4,0},{1,3},{3,7},... | collective-permute-start | bytes 442376 | tf_op jit(solution)/shard_map/ppermute | solution.py:106
  198.9 2.3 collective-permute-done.19
  201.2 2.5 %collective-permute-start.20 = (f32[32,1152]{1,0:T(8,128)S(1)}, f32[32,1152]{1,0:T(8,128)S(1)}, u32[]{:S(2)}, u32[]{:S(2)}) collective-permute-start(f32[32,1152]{1,0:T(8,128)S(1)} %collective-permute-done.19), channel_id=1, source_target_pairs={{0,2},{2,6},{6,10},{10,14},{14,12},{12,8},{8,4},{4,0},{1,3},{3,7},... | collective-permute-start | bytes 442376 | tf_op jit(solution)/shard_map/ppermute | solution.py:106
  206.3 2.5 %collective-permute-start.21 = (f32[32,1152]{1,0:T(8,128)S(1)}, f32[32,1152]{1,0:T(8,128)S(1)}, u32[]{:S(2)}, u32[]{:S(2)}) collective-permute-start(f32[32,1152]{1,0:T(8,128)S(1)} %collective-permute-done.20), channel_id=1, source_target_pairs={{0,2},{2,6},{6,10},{10,14},{14,12},{12,8},{8,4},{4,0},{1,3},{3,7},... | collective-permute-start | bytes 442376 | tf_op jit(solution)/shard_map/ppermute | solution.py:106
  211.5 2.5 %collective-permute-start.22 = (f32[32,1152]{1,0:T(8,128)S(1)}, f32[32,1152]{1,0:T(8,128)S(1)}, u32[]{:S(2)}, u32[]{:S(2)}) collective-permute-start(f32[32,1152]{1,0:T(8,128)S(1)} %collective-permute-done.21), channel_id=1, source_target_pairs={{0,2},{2,6},{6,10},{10,14},{14,12},{12,8},{8,4},{4,0},{1,3},{3,7},... | collective-permute-start | bytes 442376 | tf_op jit(solution)/shard_map/ppermute | solution.py:106
  218.3 2.3 collective-permute-done.36
  222.3 1.6 fusion.2
  (151 shorter events, 55.2 us)
Async XLA Ops:
  7.2 77.8 %all-gather.2.cloned.1.call-start = ((), (), s32[]{:S(2)}) async-start(), calls=%async_computation | async-start | bytes 4478976 | tf_op jit(solution)/shard_map/all_gather | solution.py:127
  9.1 7.9 %collective-permute-start.1 = (bf16[212,1,128]{2,1,0:T(2,128)(2,1)S(1)}, bf16[212,1,128]{2,1,0:T(2,128)(2,1)S(1)}, u32[]{:S(2)}, u32[]{:S(2)}) collective-permute-start(bf16[212,1,128]{2,1,0:T(2,128)(2,1)S(1)} %get-tuple-element.50), channel_id=1, source_target_pairs={{2,0},{4,2},{6,4},{8,6},{10,8},{12,10},{14,12},{3,1},{5,3},{7,5},{... | collective-permute-start | bytes 162824 | tf_op jit(solution)/shard_map/ppermute | solution.py:20
  10.4 9.1 %collective-permute-start = (bf16[212,1,128]{2,1,0:T(2,128)(2,1)S(1)}, bf16[212,1,128]{2,1,0:T(2,128)(2,1)S(1)}, u32[]{:S(2)}, u32[]{:S(2)}) collective-permute-start(bf16[212,1,128]{2,1,0:T(2,128)(2,1)S(1)} %get-tuple-element.49), channel_id=1, source_target_pairs={{0,2},{2,4},{4,6},{6,8},{8,10},{10,12},{12,14},{1,3},{3,5},{5,7},{... | collective-permute-start | bytes 162824 | tf_op jit(solution)/shard_map/ppermute | solution.py:19
  97.8 15.1 %collective-permute-start.2 = (f32[512,512]{0,1:T(8,128)S(1)}, f32[512,512]{0,1:T(8,128)}, u32[]{:S(2)}, u32[]{:S(2)}) collective-permute-start(f32[512,512]{0,1:T(8,128)S(1)} %dynamic-slice_bitcast_fusion), channel_id=1, source_target_pairs={{0,1},{1,0},{2,3},{3,2},{4,5},{5,4},{6,7},{7,6},{8,9},{9,8},{10,11... | collective-permute-start | bytes 3145736 | tf_op jit(solution)/shard_map/ppermute | solution.py:57
  99.0 44.7 %collective-permute-start.4 = (bf16[512,512]{1,0:T(8,128)(2,1)}, bf16[512,512]{1,0:T(8,128)(2,1)}, u32[]{:S(2)}, u32[]{:S(2)}) collective-permute-start(bf16[512,512]{1,0:T(8,128)(2,1)} %get-tuple-element.47), channel_id=1, source_target_pairs={{0,1},{1,0},{2,3},{3,2},{4,5},{5,4},{6,7},{7,6},{8,9},{9,8},{10,11... | collective-permute-start | bytes 1572872 | tf_op jit(solution)/shard_map/ppermute | solution.py:141
  120.0 23.7 %collective-permute-start.5 = (bf16[512,512]{0,1:T(8,128)(2,1)}, bf16[512,512]{0,1:T(8,128)(2,1)}, u32[]{:S(2)}, u32[]{:S(2)}) collective-permute-start(bf16[512,512]{0,1:T(8,128)(2,1)} %get-tuple-element.31), channel_id=1, source_target_pairs={{0,1},{1,0},{2,3},{3,2},{4,5},{5,4},{6,7},{7,6},{8,9},{9,8},{10,11... | collective-permute-start | bytes 1572872 | tf_op jit(solution)/shard_map/ppermute | solution.py:42
  124.7 5.9 %collective-permute-start.9 = (f32[32,1152]{1,0:T(8,128)S(1)}, f32[32,1152]{1,0:T(8,128)S(1)}, u32[]{:S(2)}, u32[]{:S(2)}) collective-permute-start(f32[32,1152]{1,0:T(8,128)S(1)} %select_bitcast_fusion.1), channel_id=1, source_target_pairs={{0,2},{2,6},{6,10},{10,14},{14,12},{12,8},{8,4},{4,0},{1,3},{3,7},... | collective-permute-start | bytes 442376 | tf_op jit(solution)/shard_map/ppermute | solution.py:101
  126.2 5.9 %collective-permute-start.23 = (f32[32,1152]{1,0:T(8,128)S(1)}, f32[32,1152]{1,0:T(8,128)S(1)}, u32[]{:S(2)}, u32[]{:S(2)}) collective-permute-start(f32[32,1152]{1,0:T(8,128)S(1)} %select_bitcast_fusion), channel_id=1, source_target_pairs={{2,0},{6,2},{10,6},{14,10},{12,14},{8,12},{4,8},{0,4},{3,1},{7,3},... | collective-permute-start | bytes 442376 | tf_op jit(solution)/shard_map/ppermute | solution.py:101
  132.1 5.2 %collective-permute-start.24 = (f32[32,1152]{1,0:T(8,128)S(1)}, f32[32,1152]{1,0:T(8,128)S(1)}, u32[]{:S(2)}, u32[]{:S(2)}) collective-permute-start(f32[32,1152]{1,0:T(8,128)S(1)} %bitcast_add_fusion.7), channel_id=1, source_target_pairs={{2,0},{6,2},{10,6},{14,10},{12,14},{8,12},{4,8},{0,4},{3,1},{7,3},... | collective-permute-start | bytes 442376 | tf_op jit(solution)/shard_map/ppermute | solution.py:101
  135.8 5.6 %collective-permute-start.11 = (f32[32,1152]{1,0:T(8,128)S(1)}, f32[32,1152]{1,0:T(8,128)S(1)}, u32[]{:S(2)}, u32[]{:S(2)}) collective-permute-start(f32[32,1152]{1,0:T(8,128)S(1)} %bitcast_add_fusion.13), channel_id=1, source_target_pairs={{0,2},{2,6},{6,10},{10,14},{14,12},{12,8},{8,4},{4,0},{1,3},{3,7},... | collective-permute-start | bytes 442376 | tf_op jit(solution)/shard_map/ppermute | solution.py:101
  137.4 5.6 %collective-permute-start.25 = (f32[32,1152]{1,0:T(8,128)S(1)}, f32[32,1152]{1,0:T(8,128)S(1)}, u32[]{:S(2)}, u32[]{:S(2)}) collective-permute-start(f32[32,1152]{1,0:T(8,128)S(1)} %bitcast_add_fusion.6), channel_id=1, source_target_pairs={{2,0},{6,2},{10,6},{14,10},{12,14},{8,12},{4,8},{0,4},{3,1},{7,3},... | collective-permute-start | bytes 442376 | tf_op jit(solution)/shard_map/ppermute | solution.py:101
  141.4 5.8 %collective-permute-start.12 = (f32[32,1152]{1,0:T(8,128)S(1)}, f32[32,1152]{1,0:T(8,128)S(1)}, u32[]{:S(2)}, u32[]{:S(2)}) collective-permute-start(f32[32,1152]{1,0:T(8,128)S(1)} %bitcast_add_fusion.12), channel_id=1, source_target_pairs={{0,2},{2,6},{6,10},{10,14},{14,12},{12,8},{8,4},{4,0},{1,3},{3,7},... | collective-permute-start | bytes 442376 | tf_op jit(solution)/shard_map/ppermute | solution.py:101
  142.9 5.8 %collective-permute-start.26 = (f32[32,1152]{1,0:T(8,128)S(1)}, f32[32,1152]{1,0:T(8,128)S(1)}, u32[]{:S(2)}, u32[]{:S(2)}) collective-permute-start(f32[32,1152]{1,0:T(8,128)S(1)} %bitcast_add_fusion.5), channel_id=1, source_target_pairs={{2,0},{6,2},{10,6},{14,10},{12,14},{8,12},{4,8},{0,4},{3,1},{7,3},... | collective-permute-start | bytes 442376 | tf_op jit(solution)/shard_map/ppermute | solution.py:101
  147.1 19.3 %collective-permute-start.6 = (bf16[512,4,128]{0,2,1:T(8,128)(2,1)S(1)}, bf16[512,4,128]{0,2,1:T(8,128)(2,1)S(1)}, u32[]{:S(2)}, u32[]{:S(2)}) collective-permute-start(bf16[512,4,128]{0,2,1:T(8,128)(2,1)S(1)} %bitcast.236), channel_id=1, source_target_pairs={{0,1},{1,0},{2,3},{3,2},{4,5},{5,4},{6,7},{7,6},{8,9},{9,8},{10,11... | collective-permute-start | bytes 1572872 | tf_op jit(solution)/shard_map/ppermute | solution.py:42
  147.2 6.3 %collective-permute-start.13 = (f32[32,1152]{1,0:T(8,128)S(1)}, f32[32,1152]{1,0:T(8,128)S(1)}, u32[]{:S(2)}, u32[]{:S(2)}) collective-permute-start(f32[32,1152]{1,0:T(8,128)S(1)} %bitcast_add_fusion.11), channel_id=1, source_target_pairs={{0,2},{2,6},{6,10},{10,14},{14,12},{12,8},{8,4},{4,0},{1,3},{3,7},... | collective-permute-start | bytes 442376 | tf_op jit(solution)/shard_map/ppermute | solution.py:101
  148.8 6.3 %collective-permute-start.27 = (f32[32,1152]{1,0:T(8,128)S(1)}, f32[32,1152]{1,0:T(8,128)S(1)}, u32[]{:S(2)}, u32[]{:S(2)}) collective-permute-start(f32[32,1152]{1,0:T(8,128)S(1)} %bitcast_add_fusion.4), channel_id=1, source_target_pairs={{2,0},{6,2},{10,6},{14,10},{12,14},{8,12},{4,8},{0,4},{3,1},{7,3},... | collective-permute-start | bytes 442376 | tf_op jit(solution)/shard_map/ppermute | solution.py:101
  153.5 5.4 %collective-permute-start.14 = (f32[32,1152]{1,0:T(8,128)S(1)}, f32[32,1152]{1,0:T(8,128)S(1)}, u32[]{:S(2)}, u32[]{:S(2)}) collective-permute-start(f32[32,1152]{1,0:T(8,128)S(1)} %bitcast_add_fusion.10), channel_id=1, source_target_pairs={{0,2},{2,6},{6,10},{10,14},{14,12},{12,8},{8,4},{4,0},{1,3},{3,7},... | collective-permute-start | bytes 442376 | tf_op jit(solution)/shard_map/ppermute | solution.py:101
  155.1 5.4 %collective-permute-start.28 = (f32[32,1152]{1,0:T(8,128)S(1)}, f32[32,1152]{1,0:T(8,128)S(1)}, u32[]{:S(2)}, u32[]{:S(2)}) collective-permute-start(f32[32,1152]{1,0:T(8,128)S(1)} %bitcast_add_fusion.3), channel_id=1, source_target_pairs={{2,0},{6,2},{10,6},{14,10},{12,14},{8,12},{4,8},{0,4},{3,1},{7,3},... | collective-permute-start | bytes 442376 | tf_op jit(solution)/shard_map/ppermute | solution.py:101
  159.0 5.2 %collective-permute-start.15 = (f32[32,1152]{1,0:T(8,128)S(1)}, f32[32,1152]{1,0:T(8,128)S(1)}, u32[]{:S(2)}, u32[]{:S(2)}) collective-permute-start(f32[32,1152]{1,0:T(8,128)S(1)} %bitcast_add_fusion.9), channel_id=1, source_target_pairs={{0,2},{2,6},{6,10},{10,14},{14,12},{12,8},{8,4},{4,0},{1,3},{3,7},... | collective-permute-start | bytes 442376 | tf_op jit(solution)/shard_map/ppermute | solution.py:101
  160.5 5.2 %collective-permute-start.29 = (f32[32,1152]{1,0:T(8,128)S(1)}, f32[32,1152]{1,0:T(8,128)S(1)}, u32[]{:S(2)}, u32[]{:S(2)}) collective-permute-start(f32[32,1152]{1,0:T(8,128)S(1)} %bitcast_add_fusion.2), channel_id=1, source_target_pairs={{2,0},{6,2},{10,6},{14,10},{12,14},{8,12},{4,8},{0,4},{3,1},{7,3},... | collective-permute-start | bytes 442376 | tf_op jit(solution)/shard_map/ppermute | solution.py:101
  164.2 9.3 %collective-permute-start.16 = (f32[32,1152]{1,0:T(8,128)S(1)}, f32[32,1152]{1,0:T(8,128)}, u32[]{:S(2)}, u32[]{:S(2)}) collective-permute-start(f32[32,1152]{1,0:T(8,128)S(1)} %get-tuple-element.29), channel_id=1, source_target_pairs={{0,2},{2,6},{6,10},{10,14},{14,12},{12,8},{8,4},{4,0},{1,3},{3,7},... | collective-permute-start | bytes 442376 | tf_op jit(solution)/shard_map/ppermute | solution.py:106
  165.8 11.1 %collective-permute-start.30 = (f32[32,1152]{1,0:T(8,128)S(1)}, f32[32,1152]{1,0:T(8,128)S(1)}, u32[]{:S(2)}, u32[]{:S(2)}) collective-permute-start(f32[32,1152]{1,0:T(8,128)S(1)} %get-tuple-element.27), channel_id=1, source_target_pairs={{2,0},{6,2},{10,6},{14,10},{12,14},{8,12},{4,8},{0,4},{3,1},{7,3},... | collective-permute-start | bytes 442376 | tf_op jit(solution)/shard_map/ppermute | solution.py:106
  167.1 9.8 %collective-permute-start.8 = (bf16[1024,1,128]{0,2,1:T(8,128)(2,1)S(1)}, bf16[1024,1,128]{0,2,1:T(8,128)(2,1)S(1)}, u32[]{:S(2)}, u32[]{:S(2)}) collective-permute-start(bf16[1024,1,128]{0,2,1:T(8,128)(2,1)S(1)} %get-tuple-element.46), channel_id=1, source_target_pairs={{2,0},{4,2},{6,4},{8,6},{10,8},{12,10},{14,12},{3,1},{5,3},{7,5},{... | collective-permute-start | bytes 786440 | tf_op jit(solution)/shard_map/ppermute | solution.py:20
  168.4 13.2 %collective-permute-start.7 = (bf16[1024,1,128]{0,2,1:T(8,128)(2,1)S(1)}, bf16[1024,1,128]{0,2,1:T(8,128)(2,1)S(1)}, u32[]{:S(2)}, u32[]{:S(2)}) collective-permute-start(bf16[1024,1,128]{0,2,1:T(8,128)(2,1)S(1)} %get-tuple-element.45), channel_id=1, source_target_pairs={{0,2},{2,4},{4,6},{6,8},{8,10},{10,12},{12,14},{1,3},{3,5},{5,7},{... | collective-permute-start | bytes 786440 | tf_op jit(solution)/shard_map/ppermute | solution.py:19
  173.5 15.0 %collective-permute-start.17 = (f32[32,1152]{1,0:T(8,128)}, f32[32,1152]{1,0:T(8,128)}, u32[]{:S(2)}, u32[]{:S(2)}) collective-permute-start(f32[32,1152]{1,0:T(8,128)} %collective-permute-done.16), channel_id=1, source_target_pairs={{0,2},{2,6},{6,10},{10,14},{14,12},{12,8},{8,4},{4,0},{1,3},{3,7},... | collective-permute-start | bytes 442376 | tf_op jit(solution)/shard_map/ppermute | solution.py:106
  176.9 15.0 %collective-permute-start.31 = (f32[32,1152]{1,0:T(8,128)S(1)}, f32[32,1152]{1,0:T(8,128)}, u32[]{:S(2)}, u32[]{:S(2)}) collective-permute-start(f32[32,1152]{1,0:T(8,128)S(1)} %collective-permute-done.30), channel_id=1, source_target_pairs={{2,0},{6,2},{10,6},{14,10},{12,14},{8,12},{4,8},{0,4},{3,1},{7,3},... | collective-permute-start | bytes 442376 | tf_op jit(solution)/shard_map/ppermute | solution.py:106
  188.5 7.0 %collective-permute-start.18 = (f32[32,1152]{1,0:T(8,128)}, f32[32,1152]{1,0:T(8,128)S(1)}, u32[]{:S(2)}, u32[]{:S(2)}) collective-permute-start(f32[32,1152]{1,0:T(8,128)} %collective-permute-done.17), channel_id=1, source_target_pairs={{0,2},{2,6},{6,10},{10,14},{14,12},{12,8},{8,4},{4,0},{1,3},{3,7},... | collective-permute-start | bytes 442376 | tf_op jit(solution)/shard_map/ppermute | solution.py:106
  191.9 6.9 %collective-permute-start.32 = (f32[32,1152]{1,0:T(8,128)}, f32[32,1152]{1,0:T(8,128)S(1)}, u32[]{:S(2)}, u32[]{:S(2)}) collective-permute-start(f32[32,1152]{1,0:T(8,128)} %collective-permute-done.31), channel_id=1, source_target_pairs={{2,0},{6,2},{10,6},{14,10},{12,14},{8,12},{4,8},{0,4},{3,1},{7,3},... | collective-permute-start | bytes 442376 | tf_op jit(solution)/shard_map/ppermute | solution.py:106
  195.5 5.7 %collective-permute-start.19 = (f32[32,1152]{1,0:T(8,128)S(1)}, f32[32,1152]{1,0:T(8,128)S(1)}, u32[]{:S(2)}, u32[]{:S(2)}) collective-permute-start(f32[32,1152]{1,0:T(8,128)S(1)} %collective-permute-done.18), channel_id=1, source_target_pairs={{0,2},{2,6},{6,10},{10,14},{14,12},{12,8},{8,4},{4,0},{1,3},{3,7},... | collective-permute-start | bytes 442376 | tf_op jit(solution)/shard_map/ppermute | solution.py:106
  198.9 5.8 %collective-permute-start.33 = (f32[32,1152]{1,0:T(8,128)S(1)}, f32[32,1152]{1,0:T(8,128)S(1)}, u32[]{:S(2)}, u32[]{:S(2)}) collective-permute-start(f32[32,1152]{1,0:T(8,128)S(1)} %collective-permute-done.32), channel_id=1, source_target_pairs={{2,0},{6,2},{10,6},{14,10},{12,14},{8,12},{4,8},{0,4},{3,1},{7,3},... | collective-permute-start | bytes 442376 | tf_op jit(solution)/shard_map/ppermute | solution.py:106
  209.9 5.2 %collective-permute-start.35 = (f32[32,1152]{1,0:T(8,128)S(1)}, f32[32,1152]{1,0:T(8,128)}, u32[]{:S(2)}, u32[]{:S(2)}) collective-permute-start(f32[32,1152]{1,0:T(8,128)S(1)} %collective-permute-done.34), channel_id=1, source_target_pairs={{2,0},{6,2},{10,6},{14,10},{12,14},{8,12},{4,8},{0,4},{3,1},{7,3},... | collective-permute-start | bytes 442376 | tf_op jit(solution)/shard_map/ppermute | solution.py:106
  215.1 5.5 %collective-permute-start.36 = (f32[32,1152]{1,0:T(8,128)}, f32[32,1152]{1,0:T(8,128)}, u32[]{:S(2)}, u32[]{:S(2)}) collective-permute-start(f32[32,1152]{1,0:T(8,128)} %collective-permute-done.35), channel_id=1, source_target_pairs={{2,0},{6,2},{10,6},{14,10},{12,14},{8,12},{4,8},{0,4},{3,1},{7,3},... | collective-permute-start | bytes 442376 | tf_op jit(solution)/shard_map/ppermute | solution.py:106
  (17 other events, 125.0 us)
Sparse Core Ops, SparseCore 0:
  10.0 74.9 all-gather.1

commit v3 on v2

--- a/solution.py
+++ b/solution.py
@@ -20,22 +20,6 @@
         after = lax.ppermute(leading, axis, down)
         shard = jnp.concatenate([before, shard, after], axis=dim)
     return shard
-
-
-def tap_columns(rimmed, row_count, col_count):
-    padded = jnp.pad(rimmed, ((0, 0), (0, 0), (1, 1)))
-    stacked = jnp.stack(
-        [
-            padded[
-                :,
-                1 + row_shift : 1 + row_shift + row_count,
-                1 + col_shift : 1 + col_shift + col_count,
-            ]
-            for row_shift, col_shift in TAPS
-        ],
-        axis=0,
-    )
-    return stacked.reshape(9 * rimmed.shape[0], row_count * col_count)
 
 
 def chan_gather(x):
@@ -123,10 +107,16 @@
         pixels = row_count * col_count
         lat_local = gdn_gamma.shape[0]
         rimmed = extended(band_strip, (("row", 1),), 1)
-        columns = tap_columns(rimmed, row_count, col_count)
+        strip_padded = jnp.pad(rimmed, ((0, 0), (0, 0), (1, 1)))
         shard_piece = lax.all_gather(conv_weight, "row", axis=0, tiled=True)
-        flat = shard_piece.reshape(shard_piece.shape[0], 9 * in_local)
-        partial_value = jnp.dot(flat, columns, preferred_element_type=jnp.float32)
+        partial_value = jnp.zeros((shard_piece.shape[0], pixels), jnp.float32)
+        for tap_index, (row_shift, col_shift) in enumerate(TAPS):
+            window = strip_padded[
+                :, 1 + row_shift : 1 + row_shift + row_count, 1 + col_shift : 1 + col_shift + col_count
+            ].reshape(in_local, pixels)
+            partial_value = partial_value + jnp.dot(
+                shard_piece[:, tap_index, :], window, preferred_element_type=jnp.float32
+            )
         pre = chan_scatter_sum(partial_value)
         squares_own = (pre * pre).astype(jnp.bfloat16)
         squares = chan_gather(squares_own)

time: 232 us -> 227 us (0.978)
  local copies, waits for them, and re-layouts: 25.1 us -> 19.9 us
    reshape x1 -> x0, local copies, waits for them, and re-layouts: 5.61 us -> none  [per_device(): flat = shard_piece.reshape(shard_piece.shape[0], 9 * in_local)]
    ppermute x2, waiting for transfers between devices: 1.06 us -> 4.23 us  [extended(): after = lax.ppermute(leading, axis, down)]
    ppermute x2, waiting for transfers between devices: 7.17 us -> 4.7 us  [extended(): before = lax.ppermute(last, axis, up)]
    dot_general x1 -> x9, matrix products: 5.78 us -> 6.92 us  [per_device(): jnp.dot(shard_piece[:, tap_index, :], window, preferred_element_type=jnp....]
    unnamed x43 -> x57, local copies, waits for them, and re-layouts: 9.18 us -> 9.45 us
  transfers between devices with their start and end apart: 38 -> 38, of which waited for: 20 -> 19; matrix products, arithmetic and copies ran while one was open for 16% -> 17% of each run, Pallas kernels for 0% -> 0%
where the time goes in v3:
time: 227 us; the launch traced here: 226 us
  waiting for transfers between devices  104 us (46%)
  starting transfers between devices  45.8 us (20%)
  between operations  25.7 us (11%)
  local copies, waits for them, and re-layouts  19.9 us (9%)
  matrix products  18.9 us (8%)
  other arithmetic  12.1 us (5%)
    all_gather x1, waiting for transfers between devices, per_device(): shard_piece = lax.all_gather(conv_weight, 'row', axis=0, tiled=True)  59.8 us
    ppermute x14, waiting for transfers between devices, ring_sum(): got = lax.ppermute(carry[part], 'row', moves[part])  20.7 us
    ppermute x14, starting transfers between devices, ring_sum(): gathered[part].append(lax.ppermute(gathered[part][-1], 'row', moves[part]))  17.9 us
    ppermute x14, starting transfers between devices, ring_sum(): got = lax.ppermute(carry[part], 'row', moves[part])  15.1 us
    ppermute x14, waiting for transfers between devices, ring_sum(): gathered[part].append(lax.ppermute(gathered[part][-1], 'row', moves[part]))  14 us
    unnamed x57, local copies, waits for them, and re-layouts  9.45 us
    ppermute x2, starting transfers between devices, extended(): before = lax.ppermute(last, axis, up)  9.44 us
    dot_general x9, matrix products, per_device(): jnp.dot(shard_piece[:, tap_index, :], window, preferred_element_type=jnp....  6.92 us
  transfers between devices with their start and end apart: 38, of which 19 were waited for; matrix products, arithmetic and copies ran while one was open for 17% of the time, Pallas kernels for 0%

profile of v3, /device:TPU:0, one launch (start us, length us, event | category | flops | bytes accessed | tf_op | source)
XLA Modules:
  0.0 226.4 jit_solution(512044424073770313)
XLA Ops:
  9.1 4.9 %collective-permute-start = (bf16[212,1,128]{2,1,0:T(2,128)(2,1)S(1)}, bf16[212,1,128]{2,1,0:T(2,128)(2,1)S(1)}, u32[]{:S(2)}, u32[]{:S(2)}) collective-permute-start(bf16[212,1,128]{2,1,0:T(2,128)(2,1)S(1)} %get-tuple-element.57), channel_id=1, source_target_pairs={{0,2},{2,4},{4,6},{6,8},{8,10},{10,12},{12,14},{1,3},{3,5},{5,7},{... | collective-permute-start | bytes 162824 | tf_op jit(solution)/shard_map/ppermute | solution.py:19
  16.4 4.2 %collective-permute-done.1 = bf16[212,1,128]{2,1,0:T(2,128)(2,1)S(1)} collective-permute-done((bf16[212,1,128]{2,1,0:T(2,128)(2,1)S(1)}, bf16[212,1,128]{2,1,0:T(2,128)(2,1)S(1)}, u32[]{:S(2)}, u32[]{:S(2)}) %collective-permute-start.1) | collective-permute-done | bytes 54304 | tf_op jit(solution)/shard_map/ppermute | solution.py:20
  20.7 1.6 pad_maximum_fusion.5
  25.2 59.8 %all-gather.2.cloned.1.call-done = bf16[1024,9,212]{0,2,1:T(8,128)(2,1)} async-done(((bf16[128,9,212]{0,2,1:T(8,128)(2,1)}), bf16[1024,9,212]{0,2,1:T(8,128)(2,1)}) %all-gather.2.cloned.1.call-update) | async-done | bytes 3907600 | tf_op jit(solution)/shard_map/all_gather | solution.py:111
  85.0 1.6 fusion.53
  108.2 1.6 multiply_convert_fusion.1
  113.1 2.3 %convert_reduce_fusion = (f32[512]{0:T(512)S(1)}, bf16[512,512]{0,1:T(8,128)(2,1)}, bf16[512,512]{0,1:T(8,128)(2,1)}, f32[512,512]{0,1:T(8,128)}) fusion(f32[512,512]{0,1:T(8,128)S(1)} %get-tuple-element.33, f32[512,4,128]{0,2,1:T(8,128)S(1)} %copy.12, bf16[1024,512]{0,1:T(8,128)(2,1)S(1)} %fusion.28, bf16[512,1024]{1,0:T(8,128)(2,1)S(1)} %copy-done.3, ...), kind=kOutput, calls=%fused_computation.67 | convolution fusion | flops 539753984 | bytes 6295552 | tf_op jit(solution)/shard_map/dot_general | solution.py:123
  115.5 1.8 fusion.70
  117.2 2.1 copy.13
  119.7 1.5 collective-permute-start.9
  122.1 3.9 %collective-permute-done.9 = f32[32,1152]{1,0:T(8,128)S(1)} collective-permute-done((f32[32,1152]{1,0:T(8,128)S(1)}, f32[32,1152]{1,0:T(8,128)S(1)}, u32[]{:S(2)}, u32[]{:S(2)}) %collective-permute-start.9) | collective-permute-done | bytes 147488 | tf_op jit(solution)/shard_map/ppermute | solution.py:85
  126.0 1.5 collective-permute-start.10
  128.2 3.2 %collective-permute-done.10 = f32[32,1152]{1,0:T(8,128)S(1)} collective-permute-done((f32[32,1152]{1,0:T(8,128)S(1)}, f32[32,1152]{1,0:T(8,128)S(1)}, u32[]{:S(2)}, u32[]{:S(2)}) %collective-permute-start.10) | collective-permute-done | bytes 147488 | tf_op jit(solution)/shard_map/ppermute | solution.py:85
  133.6 3.0 %collective-permute-done.11 = f32[32,1152]{1,0:T(8,128)S(1)} collective-permute-done((f32[32,1152]{1,0:T(8,128)S(1)}, f32[32,1152]{1,0:T(8,128)S(1)}, u32[]{:S(2)}, u32[]{:S(2)}) %collective-permute-start.11) | collective-permute-done | bytes 147488 | tf_op jit(solution)/shard_map/ppermute | solution.py:85
  138.8 3.3 %fusion.31 = bf16[512,512]{0,1:T(8,128)(2,1)S(1)} fusion(f32[512,512]{0,1:T(8,128)S(1)} %copy-done.9, f32[512,4,128]{0,2,1:T(8,128)S(1)} %copy.12, f32[512,512]{0,1:T(8,128)S(1)} %copy-done.5, s32[]{:T(128)S(6)} %select_n.196, bf16[512,512]{1,0:T(8,128)(2,1)S(1)} %copy-done.10, bf16[512,512]{1,0:T(8,128)(2,1)} %collective-permute-done.4, ...), kind=kOutput, calls=%fused_computation.65 | convolution fusion | flops 546570240 | bytes 5768192 | tf_op jit(solution)/shard_map/dot_general | solution.py:133
  142.3 1.5 collective-permute-start.13
  144.5 4.1 %collective-permute-done.13 = f32[32,1152]{1,0:T(8,128)S(1)} collective-permute-done((f32[32,1152]{1,0:T(8,128)S(1)}, f32[32,1152]{1,0:T(8,128)S(1)}, u32[]{:S(2)}, u32[]{:S(2)}) %collective-permute-start.13) | collective-permute-done | bytes 147488 | tf_op jit(solution)/shard_map/ppermute | solution.py:85
  148.6 1.5 collective-permute-start.14
  150.8 3.3 %collective-permute-done.14 = f32[32,1152]{1,0:T(8,128)S(1)} collective-permute-done((f32[32,1152]{1,0:T(8,128)S(1)}, f32[32,1152]{1,0:T(8,128)S(1)}, u32[]{:S(2)}, u32[]{:S(2)}) %collective-permute-start.14) | collective-permute-done | bytes 147488 | tf_op jit(solution)/shard_map/ppermute | solution.py:85
  156.2 3.0 %collective-permute-done.15 = f32[32,1152]{1,0:T(8,128)S(1)} collective-permute-done((f32[32,1152]{1,0:T(8,128)S(1)}, f32[32,1152]{1,0:T(8,128)S(1)}, u32[]{:S(2)}, u32[]{:S(2)}) %collective-permute-start.15) | collective-permute-done | bytes 147488 | tf_op jit(solution)/shard_map/ppermute | solution.py:85
  163.5 4.6 %collective-permute-start.7 = (bf16[1024,1,128]{0,2,1:T(8,128)(2,1)S(1)}, bf16[1024,1,128]{0,2,1:T(8,128)(2,1)S(1)}, u32[]{:S(2)}, u32[]{:S(2)}) collective-permute-start(bf16[1024,1,128]{0,2,1:T(8,128)(2,1)S(1)} %get-tuple-element.46), channel_id=1, source_target_pairs={{0,2},{2,4},{4,6},{6,8},{8,10},{10,12},{12,14},{1,3},{3,5},{5,7},{... | collective-permute-start | bytes 786440 | tf_op jit(solution)/shard_map/ppermute | solution.py:19
  168.6 2.4 %collective-permute-start.17 = (f32[32,1152]{1,0:T(8,128)}, f32[32,1152]{1,0:T(8,128)}, u32[]{:S(2)}, u32[]{:S(2)}) collective-permute-start(f32[32,1152]{1,0:T(8,128)} %collective-permute-done.16), channel_id=1, source_target_pairs={{0,2},{2,6},{6,10},{10,14},{14,12},{12,8},{8,4},{4,0},{1,3},{3,7},... | collective-permute-start | bytes 442376 | tf_op jit(solution)/shard_map/ppermute | solution.py:90
  172.0 4.7 %collective-permute-done.7 = bf16[1024,1,128]{0,2,1:T(8,128)(2,1)S(1)} collective-permute-done((bf16[1024,1,128]{0,2,1:T(8,128)(2,1)S(1)}, bf16[1024,1,128]{0,2,1:T(8,128)(2,1)S(1)}, u32[]{:S(2)}, u32[]{:S(2)}) %collective-permute-start.7) | collective-permute-done | bytes 262176 | tf_op jit(solution)/shard_map/ppermute | solution.py:19
  183.5 2.4 %collective-permute-start.18 = (f32[32,1152]{1,0:T(8,128)}, f32[32,1152]{1,0:T(8,128)S(1)}, u32[]{:S(2)}, u32[]{:S(2)}) collective-permute-start(f32[32,1152]{1,0:T(8,128)} %collective-permute-done.17), channel_id=1, source_target_pairs={{0,2},{2,6},{6,10},{10,14},{14,12},{12,8},{8,4},{4,0},{1,3},{3,7},... | collective-permute-start | bytes 442376 | tf_op jit(solution)/shard_map/ppermute | solution.py:90
  187.9 2.5 %collective-permute-done.18 = f32[32,1152]{1,0:T(8,128)S(1)} collective-permute-done((f32[32,1152]{1,0:T(8,128)}, f32[32,1152]{1,0:T(8,128)S(1)}, u32[]{:S(2)}, u32[]{:S(2)}) %collective-permute-start.18) | collective-permute-done | bytes 147488 | tf_op jit(solution)/shard_map/ppermute | solution.py:90
  190.5 2.4 %collective-permute-start.19 = (f32[32,1152]{1,0:T(8,128)S(1)}, f32[32,1152]{1,0:T(8,128)S(1)}, u32[]{:S(2)}, u32[]{:S(2)}) collective-permute-start(f32[32,1152]{1,0:T(8,128)S(1)} %collective-permute-done.18), channel_id=1, source_target_pairs={{0,2},{2,6},{6,10},{10,14},{14,12},{12,8},{8,4},{4,0},{1,3},{3,7},... | collective-permute-start | bytes 442376 | tf_op jit(solution)/shard_map/ppermute | solution.py:90
  193.9 2.3 %collective-permute-done.19 = f32[32,1152]{1,0:T(8,128)S(1)} collective-permute-done((f32[32,1152]{1,0:T(8,128)S(1)}, f32[32,1152]{1,0:T(8,128)S(1)}, u32[]{:S(2)}, u32[]{:S(2)}) %collective-permute-start.19) | collective-permute-done | bytes 147488 | tf_op jit(solution)/shard_map/ppermute | solution.py:90
  196.2 2.5 %collective-permute-start.20 = (f32[32,1152]{1,0:T(8,128)S(1)}, f32[32,1152]{1,0:T(8,128)S(1)}, u32[]{:S(2)}, u32[]{:S(2)}) collective-permute-start(f32[32,1152]{1,0:T(8,128)S(1)} %collective-permute-done.19), channel_id=1, source_target_pairs={{0,2},{2,6},{6,10},{10,14},{14,12},{12,8},{8,4},{4,0},{1,3},{3,7},... | collective-permute-start | bytes 442376 | tf_op jit(solution)/shard_map/ppermute | solution.py:90
  201.3 2.5 %collective-permute-start.21 = (f32[32,1152]{1,0:T(8,128)S(1)}, f32[32,1152]{1,0:T(8,128)S(1)}, u32[]{:S(2)}, u32[]{:S(2)}) collective-permute-start(f32[32,1152]{1,0:T(8,128)S(1)} %collective-permute-done.20), channel_id=1, source_target_pairs={{0,2},{2,6},{6,10},{10,14},{14,12},{12,8},{8,4},{4,0},{1,3},{3,7},... | collective-permute-start | bytes 442376 | tf_op jit(solution)/shard_map/ppermute | solution.py:90
  206.5 2.5 %collective-permute-start.22 = (f32[32,1152]{1,0:T(8,128)S(1)}, f32[32,1152]{1,0:T(8,128)S(1)}, u32[]{:S(2)}, u32[]{:S(2)}) collective-permute-start(f32[32,1152]{1,0:T(8,128)S(1)} %collective-permute-done.21), channel_id=1, source_target_pairs={{0,2},{2,6},{6,10},{10,14},{14,12},{12,8},{8,4},{4,0},{1,3},{3,7},... | collective-permute-start | bytes 442376 | tf_op jit(solution)/shard_map/ppermute | solution.py:90
  213.3 2.3 %collective-permute-done.36 = f32[32,1152]{1,0:T(8,128)} collective-permute-done((f32[32,1152]{1,0:T(8,128)}, f32[32,1152]{1,0:T(8,128)}, u32[]{:S(2)}, u32[]{:S(2)}) %collective-permute-start.36) | collective-permute-done | bytes 147488 | tf_op jit(solution)/shard_map/ppermute | solution.py:90
  217.3 1.6 fusion.2
  (171 shorter events, 58.4 us)
Async XLA Ops:
  7.2 77.8 %all-gather.2.cloned.1.call-start = ((), (), s32[]{:S(2)}) async-start(), calls=%async_computation | async-start | bytes 4478976 | tf_op jit(solution)/shard_map/all_gather | solution.py:111
  9.1 7.3 %collective-permute-start = (bf16[212,1,128]{2,1,0:T(2,128)(2,1)S(1)}, bf16[212,1,128]{2,1,0:T(2,128)(2,1)S(1)}, u32[]{:S(2)}, u32[]{:S(2)}) collective-permute-start(bf16[212,1,128]{2,1,0:T(2,128)(2,1)S(1)} %get-tuple-element.57), channel_id=1, source_target_pairs={{0,2},{2,4},{4,6},{6,8},{8,10},{10,12},{12,14},{1,3},{3,5},{5,7},{... | collective-permute-start | bytes 162824 | tf_op jit(solution)/shard_map/ppermute | solution.py:19
  14.0 6.6 %collective-permute-start.1 = (bf16[212,1,128]{2,1,0:T(2,128)(2,1)S(1)}, bf16[212,1,128]{2,1,0:T(2,128)(2,1)S(1)}, u32[]{:S(2)}, u32[]{:S(2)}) collective-permute-start(bf16[212,1,128]{2,1,0:T(2,128)(2,1)S(1)} %get-tuple-element.58), channel_id=1, source_target_pairs={{2,0},{4,2},{6,4},{8,6},{10,8},{12,10},{14,12},{3,1},{5,3},{7,5},{... | collective-permute-start | bytes 162824 | tf_op jit(solution)/shard_map/ppermute | solution.py:20
  93.1 15.1 %collective-permute-start.2 = (f32[512,512]{0,1:T(8,128)}, f32[512,512]{0,1:T(8,128)}, u32[]{:S(2)}, u32[]{:S(2)}) collective-permute-start(f32[512,512]{0,1:T(8,128)} %constant_dynamic-slice_fusion.2), channel_id=1, source_target_pairs={{0,1},{1,0},{2,3},{3,2},{4,5},{5,4},{6,7},{7,6},{8,9},{9,8},{10,11... | collective-permute-start | bytes 3145736 | tf_op jit(solution)/shard_map/ppermute | solution.py:41
  94.7 44.1 %collective-permute-start.4 = (bf16[512,512]{1,0:T(8,128)(2,1)}, bf16[512,512]{1,0:T(8,128)(2,1)}, u32[]{:S(2)}, u32[]{:S(2)}) collective-permute-start(bf16[512,512]{1,0:T(8,128)(2,1)} %get-tuple-element.47), channel_id=1, source_target_pairs={{0,1},{1,0},{2,3},{3,2},{4,5},{5,4},{6,7},{7,6},{8,9},{9,8},{10,11... | collective-permute-start | bytes 1572872 | tf_op jit(solution)/shard_map/ppermute | solution.py:131
  115.4 23.4 %collective-permute-start.5 = (bf16[512,512]{0,1:T(8,128)(2,1)}, bf16[512,512]{0,1:T(8,128)(2,1)}, u32[]{:S(2)}, u32[]{:S(2)}) collective-permute-start(bf16[512,512]{0,1:T(8,128)(2,1)} %get-tuple-element.31), channel_id=1, source_target_pairs={{0,1},{1,0},{2,3},{3,2},{4,5},{5,4},{6,7},{7,6},{8,9},{9,8},{10,11... | collective-permute-start | bytes 1572872 | tf_op jit(solution)/shard_map/ppermute | solution.py:26
  119.7 6.3 %collective-permute-start.9 = (f32[32,1152]{1,0:T(8,128)S(1)}, f32[32,1152]{1,0:T(8,128)S(1)}, u32[]{:S(2)}, u32[]{:S(2)}) collective-permute-start(f32[32,1152]{1,0:T(8,128)S(1)} %select_bitcast_fusion.1), channel_id=1, source_target_pairs={{0,2},{2,6},{6,10},{10,14},{14,12},{12,8},{8,4},{4,0},{1,3},{3,7},... | collective-permute-start | bytes 442376 | tf_op jit(solution)/shard_map/ppermute | solution.py:85
  121.3 6.3 %collective-permute-start.23 = (f32[32,1152]{1,0:T(8,128)S(1)}, f32[32,1152]{1,0:T(8,128)S(1)}, u32[]{:S(2)}, u32[]{:S(2)}) collective-permute-start(f32[32,1152]{1,0:T(8,128)S(1)} %select_bitcast_fusion), channel_id=1, source_target_pairs={{2,0},{6,2},{10,6},{14,10},{12,14},{8,12},{4,8},{0,4},{3,1},{7,3},... | collective-permute-start | bytes 442376 | tf_op jit(solution)/shard_map/ppermute | solution.py:85
  126.0 5.4 %collective-permute-start.10 = (f32[32,1152]{1,0:T(8,128)S(1)}, f32[32,1152]{1,0:T(8,128)S(1)}, u32[]{:S(2)}, u32[]{:S(2)}) collective-permute-start(f32[32,1152]{1,0:T(8,128)S(1)} %bitcast_add_fusion.18), channel_id=1, source_target_pairs={{0,2},{2,6},{6,10},{10,14},{14,12},{12,8},{8,4},{4,0},{1,3},{3,7},... | collective-permute-start | bytes 442376 | tf_op jit(solution)/shard_map/ppermute | solution.py:85
  127.5 5.4 %collective-permute-start.24 = (f32[32,1152]{1,0:T(8,128)S(1)}, f32[32,1152]{1,0:T(8,128)S(1)}, u32[]{:S(2)}, u32[]{:S(2)}) collective-permute-start(f32[32,1152]{1,0:T(8,128)S(1)} %bitcast_add_fusion.11), channel_id=1, source_target_pairs={{2,0},{6,2},{10,6},{14,10},{12,14},{8,12},{4,8},{0,4},{3,1},{7,3},... | collective-permute-start | bytes 442376 | tf_op jit(solution)/shard_map/ppermute | solution.py:85
  131.4 5.2 %collective-permute-start.11 = (f32[32,1152]{1,0:T(8,128)S(1)}, f32[32,1152]{1,0:T(8,128)S(1)}, u32[]{:S(2)}, u32[]{:S(2)}) collective-permute-start(f32[32,1152]{1,0:T(8,128)S(1)} %bitcast_add_fusion.17), channel_id=1, source_target_pairs={{0,2},{2,6},{6,10},{10,14},{14,12},{12,8},{8,4},{4,0},{1,3},{3,7},... | collective-permute-start | bytes 442376 | tf_op jit(solution)/shard_map/ppermute | solution.py:85
  133.0 5.2 %collective-permute-start.25 = (f32[32,1152]{1,0:T(8,128)S(1)}, f32[32,1152]{1,0:T(8,128)S(1)}, u32[]{:S(2)}, u32[]{:S(2)}) collective-permute-start(f32[32,1152]{1,0:T(8,128)S(1)} %bitcast_add_fusion.10), channel_id=1, source_target_pairs={{2,0},{6,2},{10,6},{14,10},{12,14},{8,12},{4,8},{0,4},{3,1},{7,3},... | collective-permute-start | bytes 442376 | tf_op jit(solution)/shard_map/ppermute | solution.py:85
  136.7 5.6 %collective-permute-start.12 = (f32[32,1152]{1,0:T(8,128)S(1)}, f32[32,1152]{1,0:T(8,128)S(1)}, u32[]{:S(2)}, u32[]{:S(2)}) collective-permute-start(f32[32,1152]{1,0:T(8,128)S(1)} %bitcast_add_fusion.16), channel_id=1, source_target_pairs={{0,2},{2,6},{6,10},{10,14},{14,12},{12,8},{8,4},{4,0},{1,3},{3,7},... | collective-permute-start | bytes 442376 | tf_op jit(solution)/shard_map/ppermute | solution.py:85
  138.2 5.6 %collective-permute-start.26 = (f32[32,1152]{1,0:T(8,128)S(1)}, f32[32,1152]{1,0:T(8,128)S(1)}, u32[]{:S(2)}, u32[]{:S(2)}) collective-permute-start(f32[32,1152]{1,0:T(8,128)S(1)} %bitcast_add_fusion.9), channel_id=1, source_target_pairs={{2,0},{6,2},{10,6},{14,10},{12,14},{8,12},{4,8},{0,4},{3,1},{7,3},... | collective-permute-start | bytes 442376 | tf_op jit(solution)/shard_map/ppermute | solution.py:85
  142.2 19.3 %collective-permute-start.6 = (bf16[512,4,128]{0,2,1:T(8,128)(2,1)S(1)}, bf16[512,4,128]{0,2,1:T(8,128)(2,1)S(1)}, u32[]{:S(2)}, u32[]{:S(2)}) collective-permute-start(bf16[512,4,128]{0,2,1:T(8,128)(2,1)S(1)} %bitcast.251), channel_id=1, source_target_pairs={{0,1},{1,0},{2,3},{3,2},{4,5},{5,4},{6,7},{7,6},{8,9},{9,8},{10,11... | collective-permute-start | bytes 1572872 | tf_op jit(solution)/shard_map/ppermute | solution.py:26
  142.3 6.3 %collective-permute-start.13 = (f32[32,1152]{1,0:T(8,128)S(1)}, f32[32,1152]{1,0:T(8,128)S(1)}, u32[]{:S(2)}, u32[]{:S(2)}) collective-permute-start(f32[32,1152]{1,0:T(8,128)S(1)} %bitcast_add_fusion.15), channel_id=1, source_target_pairs={{0,2},{2,6},{6,10},{10,14},{14,12},{12,8},{8,4},{4,0},{1,3},{3,7},... | collective-permute-start | bytes 442376 | tf_op jit(solution)/shard_map/ppermute | solution.py:85
  143.8 6.3 %collective-permute-start.27 = (f32[32,1152]{1,0:T(8,128)S(1)}, f32[32,1152]{1,0:T(8,128)S(1)}, u32[]{:S(2)}, u32[]{:S(2)}) collective-permute-start(f32[32,1152]{1,0:T(8,128)S(1)} %bitcast_add_fusion.8), channel_id=1, source_target_pairs={{2,0},{6,2},{10,6},{14,10},{12,14},{8,12},{4,8},{0,4},{3,1},{7,3},... | collective-permute-start | bytes 442376 | tf_op jit(solution)/shard_map/ppermute | solution.py:85
  148.6 5.4 %collective-permute-start.14 = (f32[32,1152]{1,0:T(8,128)S(1)}, f32[32,1152]{1,0:T(8,128)S(1)}, u32[]{:S(2)}, u32[]{:S(2)}) collective-permute-start(f32[32,1152]{1,0:T(8,128)S(1)} %bitcast_add_fusion.14), channel_id=1, source_target_pairs={{0,2},{2,6},{6,10},{10,14},{14,12},{12,8},{8,4},{4,0},{1,3},{3,7},... | collective-permute-start | bytes 442376 | tf_op jit(solution)/shard_map/ppermute | solution.py:85
  150.1 5.4 %collective-permute-start.28 = (f32[32,1152]{1,0:T(8,128)S(1)}, f32[32,1152]{1,0:T(8,128)S(1)}, u32[]{:S(2)}, u32[]{:S(2)}) collective-permute-start(f32[32,1152]{1,0:T(8,128)S(1)} %bitcast_add_fusion.7), channel_id=1, source_target_pairs={{2,0},{6,2},{10,6},{14,10},{12,14},{8,12},{4,8},{0,4},{3,1},{7,3},... | collective-permute-start | bytes 442376 | tf_op jit(solution)/shard_map/ppermute | solution.py:85
  155.6 5.2 %collective-permute-start.29 = (f32[32,1152]{1,0:T(8,128)S(1)}, f32[32,1152]{1,0:T(8,128)S(1)}, u32[]{:S(2)}, u32[]{:S(2)}) collective-permute-start(f32[32,1152]{1,0:T(8,128)S(1)} %bitcast_add_fusion.6), channel_id=1, source_target_pairs={{2,0},{6,2},{10,6},{14,10},{12,14},{8,12},{4,8},{0,4},{3,1},{7,3},... | collective-permute-start | bytes 442376 | tf_op jit(solution)/shard_map/ppermute | solution.py:85
  159.3 9.3 %collective-permute-start.16 = (f32[32,1152]{1,0:T(8,128)S(1)}, f32[32,1152]{1,0:T(8,128)}, u32[]{:S(2)}, u32[]{:S(2)}) collective-permute-start(f32[32,1152]{1,0:T(8,128)S(1)} %get-tuple-element.29), channel_id=1, source_target_pairs={{0,2},{2,6},{6,10},{10,14},{14,12},{12,8},{8,4},{4,0},{1,3},{3,7},... | collective-permute-start | bytes 442376 | tf_op jit(solution)/shard_map/ppermute | solution.py:90
  160.8 11.1 %collective-permute-start.30 = (f32[32,1152]{1,0:T(8,128)S(1)}, f32[32,1152]{1,0:T(8,128)S(1)}, u32[]{:S(2)}, u32[]{:S(2)}) collective-permute-start(f32[32,1152]{1,0:T(8,128)S(1)} %get-tuple-element.27), channel_id=1, source_target_pairs={{2,0},{6,2},{10,6},{14,10},{12,14},{8,12},{4,8},{0,4},{3,1},{7,3},... | collective-permute-start | bytes 442376 | tf_op jit(solution)/shard_map/ppermute | solution.py:90
  162.2 9.8 %collective-permute-start.8 = (bf16[1024,1,128]{0,2,1:T(8,128)(2,1)S(1)}, bf16[1024,1,128]{0,2,1:T(8,128)(2,1)S(1)}, u32[]{:S(2)}, u32[]{:S(2)}) collective-permute-start(bf16[1024,1,128]{0,2,1:T(8,128)(2,1)S(1)} %get-tuple-element.45), channel_id=1, source_target_pairs={{2,0},{4,2},{6,4},{8,6},{10,8},{12,10},{14,12},{3,1},{5,3},{7,5},{... | collective-permute-start | bytes 786440 | tf_op jit(solution)/shard_map/ppermute | solution.py:20
  163.5 13.2 %collective-permute-start.7 = (bf16[1024,1,128]{0,2,1:T(8,128)(2,1)S(1)}, bf16[1024,1,128]{0,2,1:T(8,128)(2,1)S(1)}, u32[]{:S(2)}, u32[]{:S(2)}) collective-permute-start(bf16[1024,1,128]{0,2,1:T(8,128)(2,1)S(1)} %get-tuple-element.46), channel_id=1, source_target_pairs={{0,2},{2,4},{4,6},{6,8},{8,10},{10,12},{12,14},{1,3},{3,5},{5,7},{... | collective-permute-start | bytes 786440 | tf_op jit(solution)/shard_map/ppermute | solution.py:19
  168.6 14.9 %collective-permute-start.17 = (f32[32,1152]{1,0:T(8,128)}, f32[32,1152]{1,0:T(8,128)}, u32[]{:S(2)}, u32[]{:S(2)}) collective-permute-start(f32[32,1152]{1,0:T(8,128)} %collective-permute-done.16), channel_id=1, source_target_pairs={{0,2},{2,6},{6,10},{10,14},{14,12},{12,8},{8,4},{4,0},{1,3},{3,7},... | collective-permute-start | bytes 442376 | tf_op jit(solution)/shard_map/ppermute | solution.py:90
  172.0 15.0 %collective-permute-start.31 = (f32[32,1152]{1,0:T(8,128)S(1)}, f32[32,1152]{1,0:T(8,128)}, u32[]{:S(2)}, u32[]{:S(2)}) collective-permute-start(f32[32,1152]{1,0:T(8,128)S(1)} %collective-permute-done.30), channel_id=1, source_target_pairs={{2,0},{6,2},{10,6},{14,10},{12,14},{8,12},{4,8},{0,4},{3,1},{7,3},... | collective-permute-start | bytes 442376 | tf_op jit(solution)/shard_map/ppermute | solution.py:90
  183.5 7.0 %collective-permute-start.18 = (f32[32,1152]{1,0:T(8,128)}, f32[32,1152]{1,0:T(8,128)S(1)}, u32[]{:S(2)}, u32[]{:S(2)}) collective-permute-start(f32[32,1152]{1,0:T(8,128)} %collective-permute-done.17), channel_id=1, source_target_pairs={{0,2},{2,6},{6,10},{10,14},{14,12},{12,8},{8,4},{4,0},{1,3},{3,7},... | collective-permute-start | bytes 442376 | tf_op jit(solution)/shard_map/ppermute | solution.py:90
  186.9 6.9 %collective-permute-start.32 = (f32[32,1152]{1,0:T(8,128)}, f32[32,1152]{1,0:T(8,128)S(1)}, u32[]{:S(2)}, u32[]{:S(2)}) collective-permute-start(f32[32,1152]{1,0:T(8,128)} %collective-permute-done.31), channel_id=1, source_target_pairs={{2,0},{6,2},{10,6},{14,10},{12,14},{8,12},{4,8},{0,4},{3,1},{7,3},... | collective-permute-start | bytes 442376 | tf_op jit(solution)/shard_map/ppermute | solution.py:90
  190.5 5.7 %collective-permute-start.19 = (f32[32,1152]{1,0:T(8,128)S(1)}, f32[32,1152]{1,0:T(8,128)S(1)}, u32[]{:S(2)}, u32[]{:S(2)}) collective-permute-start(f32[32,1152]{1,0:T(8,128)S(1)} %collective-permute-done.18), channel_id=1, source_target_pairs={{0,2},{2,6},{6,10},{10,14},{14,12},{12,8},{8,4},{4,0},{1,3},{3,7},... | collective-permute-start | bytes 442376 | tf_op jit(solution)/shard_map/ppermute | solution.py:90
  193.9 5.8 %collective-permute-start.33 = (f32[32,1152]{1,0:T(8,128)S(1)}, f32[32,1152]{1,0:T(8,128)S(1)}, u32[]{:S(2)}, u32[]{:S(2)}) collective-permute-start(f32[32,1152]{1,0:T(8,128)S(1)} %collective-permute-done.32), channel_id=1, source_target_pairs={{2,0},{6,2},{10,6},{14,10},{12,14},{8,12},{4,8},{0,4},{3,1},{7,3},... | collective-permute-start | bytes 442376 | tf_op jit(solution)/shard_map/ppermute | solution.py:90
  204.8 5.2 %collective-permute-start.35 = (f32[32,1152]{1,0:T(8,128)S(1)}, f32[32,1152]{1,0:T(8,128)}, u32[]{:S(2)}, u32[]{:S(2)}) collective-permute-start(f32[32,1152]{1,0:T(8,128)S(1)} %collective-permute-done.34), channel_id=1, source_target_pairs={{2,0},{6,2},{10,6},{14,10},{12,14},{8,12},{4,8},{0,4},{3,1},{7,3},... | collective-permute-start | bytes 442376 | tf_op jit(solution)/shard_map/ppermute | solution.py:90
  210.1 5.5 %collective-permute-start.36 = (f32[32,1152]{1,0:T(8,128)}, f32[32,1152]{1,0:T(8,128)}, u32[]{:S(2)}, u32[]{:S(2)}) collective-permute-start(f32[32,1152]{1,0:T(8,128)} %collective-permute-done.35), channel_id=1, source_target_pairs={{2,0},{6,2},{10,6},{14,10},{12,14},{8,12},{4,8},{0,4},{3,1},{7,3},... | collective-permute-start | bytes 442376 | tf_op jit(solution)/shard_map/ppermute | solution.py:90
  (19 other events, 139.9 us)
Sparse Core Ops, SparseCore 0:
  10.0 74.9 all-gather.1

commit v4 on v3

--- a/solution.py
+++ b/solution.py
@@ -84,7 +84,8 @@
         for part in range(2):
             got = lax.ppermute(carry[part], "row", moves[part])
             carry[part] = [g + o for g, o in zip(got, pick(part, step))]
-    gathered = [[c] for c in carry]
+    gathered = [[c.astype(jnp.bfloat16) for c in part] for part in carry]
+    gathered = [[c] for c in gathered]
     for step in range(1, count):
         for part in range(2):
             gathered[part].append(lax.ppermute(gathered[part][-1], "row", moves[part]))
@@ -95,7 +96,7 @@
             stacked = jnp.stack([g[leaf] for g in gathered[part]], 0)
             order = (signs[part] * (position - jnp.arange(count))) % count
             halves.append(jnp.take(stacked, order, axis=0).reshape((-1,) + stacked.shape[2:]))
-        results.append(jnp.concatenate(halves, 0))
+        results.append(jnp.concatenate(halves, 0).astype(jnp.float32))
     return results
 
 

time: 227 us -> 215 us (0.947)
  local copies, waits for them, and re-layouts: 19.9 us -> 14.4 us
  waiting for transfers between devices: 104 us -> 99.1 us
    ppermute x2, waiting for transfers between devices: 4.7 us -> 0.01 us  [extended(): before = lax.ppermute(last, axis, up)]
    unnamed x57 -> x53, local copies, waits for them, and re-layouts: 9.45 us -> 4.86 us
  transfers between devices with their start and end apart: 38 -> 38, of which waited for: 19 -> 15; matrix products, arithmetic and copies ran while one was open for 17% -> 16% of each run, Pallas kernels for 0% -> 0%
where the time goes in v4:
time: 215 us
  waiting for transfers between devices  99.1 us (46%)
  starting transfers between devices  44.4 us (21%)
  between operations  25.7 us (12%)
  matrix products  18.9 us (9%)
  local copies, waits for them, and re-layouts  14.4 us (7%)
  other arithmetic  12.2 us (6%)
    all_gather x1, waiting for transfers between devices, per_device(): shard_piece = lax.all_gather(conv_weight, 'row', axis=0, tiled=True)  59.8 us
    ppermute x14, waiting for transfers between devices, ring_sum(): got = lax.ppermute(carry[part], 'row', moves[part])  20.7 us
    ppermute x14, starting transfers between devices, ring_sum(): gathered[part].append(lax.ppermute(gathered[part][-1], 'row', moves[part]))  16.5 us
    ppermute x14, starting transfers between devices, ring_sum(): got = lax.ppermute(carry[part], 'row', moves[part])  15.1 us
    ppermute x14, waiting for transfers between devices, ring_sum(): gathered[part].append(lax.ppermute(gathered[part][-1], 'row', moves[part]))  13.7 us
    ppermute x2, starting transfers between devices, extended(): before = lax.ppermute(last, axis, up)  9.44 us
    dot_general x9, matrix products, per_device(): jnp.dot(shard_piece[:, tap_index, :], window, preferred_element_type=jnp....  6.92 us
    unnamed x53, local copies, waits for them, and re-layouts  4.86 us
  transfers between devices with their start and end apart: 38, of which 15 were waited for; matrix products, arithmetic and copies ran while one was open for 16% of the time, Pallas kernels for 0%

profile of v4, /device:TPU:0, one launch (start us, length us, event | category | flops | bytes accessed | tf_op | source)
XLA Modules:
  0.0 214.7 jit_solution(395757181845759559)
XLA Ops:
  9.1 4.9 %collective-permute-start = (bf16[212,1,128]{2,1,0:T(2,128)(2,1)S(1)}, bf16[212,1,128]{2,1,0:T(2,128)(2,1)S(1)}, u32[]{:S(2)}, u32[]{:S(2)}) collective-permute-start(bf16[212,1,128]{2,1,0:T(2,128)(2,1)S(1)} %get-tuple-element.57), channel_id=1, source_target_pairs={{0,2},{2,4},{4,6},{6,8},{8,10},{10,12},{12,14},{1,3},{3,5},{5,7},{... | collective-permute-start | bytes 162824 | tf_op jit(solution)/shard_map/ppermute | solution.py:19
  16.4 4.2 %collective-permute-done.1 = bf16[212,1,128]{2,1,0:T(2,128)(2,1)S(1)} collective-permute-done((bf16[212,1,128]{2,1,0:T(2,128)(2,1)S(1)}, bf16[212,1,128]{2,1,0:T(2,128)(2,1)S(1)}, u32[]{:S(2)}, u32[]{:S(2)}) %collective-permute-start.1) | collective-permute-done | bytes 54304 | tf_op jit(solution)/shard_map/ppermute | solution.py:20
  20.7 1.6 pad_maximum_fusion.4
  25.2 59.8 %all-gather.2.cloned.1.call-done = bf16[1024,9,212]{0,2,1:T(8,128)(2,1)} async-done(((bf16[128,9,212]{0,2,1:T(8,128)(2,1)}), bf16[1024,9,212]{0,2,1:T(8,128)(2,1)}) %all-gather.2.cloned.1.call-update) | async-done | bytes 3907600 | tf_op jit(solution)/shard_map/all_gather | solution.py:112
  85.0 1.6 fusion.51
  108.2 1.6 multiply_convert_fusion.1
  113.1 2.3 %convert_reduce_fusion = (f32[512]{0:T(512)S(1)}, bf16[512,512]{0,1:T(8,128)(2,1)}, bf16[512,512]{0,1:T(8,128)(2,1)}, f32[512,512]{0,1:T(8,128)}) fusion(f32[512,512]{0,1:T(8,128)S(1)} %get-tuple-element.33, f32[512,4,128]{0,2,1:T(8,128)S(1)} %copy.12, bf16[1024,512]{0,1:T(8,128)(2,1)S(1)} %fusion.26, bf16[512,1024]{1,0:T(8,128)(2,1)S(1)} %copy-done.3, ...), kind=kOutput, calls=%fused_computation.65 | convolution fusion | flops 539753984 | bytes 6295552 | tf_op jit(solution)/shard_map/dot_general | solution.py:124
  115.4 1.8 fusion.71
  117.2 2.1 copy.13
  119.8 2.2 %collective-permute-start.9 = (f32[32,1152]{1,0:T(8,128)S(1)}, f32[32,1152]{1,0:T(8,128)S(1)}, u32[]{:S(2)}, u32[]{:S(2)}) collective-permute-start(f32[32,1152]{1,0:T(8,128)S(1)} %select_bitcast_fusion.1), channel_id=1, source_target_pairs={{0,2},{2,6},{6,10},{10,14},{14,12},{12,8},{8,4},{4,0},{1,3},{3,7},... | collective-permute-start | bytes 442376 | tf_op jit(solution)/shard_map/ppermute | solution.py:85
  122.0 3.9 %collective-permute-done.23 = f32[32,1152]{1,0:T(8,128)S(1)} collective-permute-done((f32[32,1152]{1,0:T(8,128)S(1)}, f32[32,1152]{1,0:T(8,128)S(1)}, u32[]{:S(2)}, u32[]{:S(2)}) %collective-permute-start.23) | collective-permute-done | bytes 147488 | tf_op jit(solution)/shard_map/ppermute | solution.py:85
  126.4 1.8 collective-permute-start.10
  128.1 3.2 %collective-permute-done.24 = f32[32,1152]{1,0:T(8,128)S(1)} collective-permute-done((f32[32,1152]{1,0:T(8,128)S(1)}, f32[32,1152]{1,0:T(8,128)S(1)}, u32[]{:S(2)}, u32[]{:S(2)}) %collective-permute-start.24) | collective-permute-done | bytes 147488 | tf_op jit(solution)/shard_map/ppermute | solution.py:85
  133.6 3.0 %collective-permute-done.25 = f32[32,1152]{1,0:T(8,128)S(1)} collective-permute-done((f32[32,1152]{1,0:T(8,128)S(1)}, f32[32,1152]{1,0:T(8,128)S(1)}, u32[]{:S(2)}, u32[]{:S(2)}) %collective-permute-start.25) | collective-permute-done | bytes 147488 | tf_op jit(solution)/shard_map/ppermute | solution.py:85
  138.8 3.3 %fusion.29 = bf16[512,512]{0,1:T(8,128)(2,1)S(1)} fusion(f32[512,512]{0,1:T(8,128)S(1)} %copy-done.7, f32[512,4,128]{0,2,1:T(8,128)S(1)} %copy.12, f32[512,512]{0,1:T(8,128)S(1)} %copy-done.5, s32[]{:T(128)S(6)} %select_n.196, bf16[512,512]{1,0:T(8,128)(2,1)S(1)} %copy-done.8, bf16[512,512]{1,0:T(8,128)(2,1)} %collective-permute-done.4, ...), kind=kOutput, calls=%fused_computation.63 | convolution fusion | flops 546570240 | bytes 5768192 | tf_op jit(solution)/shard_map/dot_general | solution.py:134
  142.9 1.5 collective-permute-start.13
  144.5 4.1 %collective-permute-done.27 = f32[32,1152]{1,0:T(8,128)S(1)} collective-permute-done((f32[32,1152]{1,0:T(8,128)S(1)}, f32[32,1152]{1,0:T(8,128)S(1)}, u32[]{:S(2)}, u32[]{:S(2)}) %collective-permute-start.27) | collective-permute-done | bytes 147488 | tf_op jit(solution)/shard_map/ppermute | solution.py:85
  150.8 3.3 %collective-permute-done.28 = f32[32,1152]{1,0:T(8,128)S(1)} collective-permute-done((f32[32,1152]{1,0:T(8,128)S(1)}, f32[32,1152]{1,0:T(8,128)S(1)}, u32[]{:S(2)}, u32[]{:S(2)}) %collective-permute-start.28) | collective-permute-done | bytes 147488 | tf_op jit(solution)/shard_map/ppermute | solution.py:85
  156.2 3.0 %collective-permute-done.29 = f32[32,1152]{1,0:T(8,128)S(1)} collective-permute-done((f32[32,1152]{1,0:T(8,128)S(1)}, f32[32,1152]{1,0:T(8,128)S(1)}, u32[]{:S(2)}, u32[]{:S(2)}) %collective-permute-start.29) | collective-permute-done | bytes 147488 | tf_op jit(solution)/shard_map/ppermute | solution.py:85
  163.5 4.6 %collective-permute-start.7 = (bf16[1024,1,128]{0,2,1:T(8,128)(2,1)S(1)}, bf16[1024,1,128]{0,2,1:T(8,128)(2,1)S(1)}, u32[]{:S(2)}, u32[]{:S(2)}) collective-permute-start(bf16[1024,1,128]{0,2,1:T(8,128)(2,1)S(1)} %get-tuple-element.46), channel_id=1, source_target_pairs={{0,2},{2,4},{4,6},{6,8},{8,10},{10,12},{12,14},{1,3},{3,5},{5,7},{... | collective-permute-start | bytes 786440 | tf_op jit(solution)/shard_map/ppermute | solution.py:19
  171.1 2.6 %collective-permute-done.31 = bf16[32,1152]{1,0:T(8,128)(2,1)S(1)} collective-permute-done((bf16[32,1152]{1,0:T(8,128)(2,1)S(1)}, bf16[32,1152]{1,0:T(8,128)(2,1)S(1)}, u32[]{:S(2)}, u32[]{:S(2)}) %collective-permute-start.31) | collective-permute-done | bytes 73760 | tf_op jit(solution)/shard_map/ppermute | solution.py:91
  174.6 2.1 collective-permute-done.17
  176.7 2.5 %collective-permute-start.18 = (bf16[32,1152]{1,0:T(8,128)(2,1)S(1)}, bf16[32,1152]{1,0:T(8,128)(2,1)S(1)}, u32[]{:S(2)}, u32[]{:S(2)}) collective-permute-start(bf16[32,1152]{1,0:T(8,128)(2,1)S(1)} %collective-permute-done.17), channel_id=1, source_target_pairs={{0,2},{2,6},{6,10},{10,14},{14,12},{12,8},{8,4},{4,0},{1,3},{3,7},... | collective-permute-start | bytes 221192 | tf_op jit(solution)/shard_map/ppermute | solution.py:91
  179.3 1.9 collective-permute-done.18
  181.2 2.4 %collective-permute-start.19 = (bf16[32,1152]{1,0:T(8,128)(2,1)S(1)}, bf16[32,1152]{1,0:T(8,128)(2,1)S(1)}, u32[]{:S(2)}, u32[]{:S(2)}) collective-permute-start(bf16[32,1152]{1,0:T(8,128)(2,1)S(1)} %collective-permute-done.18), channel_id=1, source_target_pairs={{0,2},{2,6},{6,10},{10,14},{14,12},{12,8},{8,4},{4,0},{1,3},{3,7},... | collective-permute-start | bytes 221192 | tf_op jit(solution)/shard_map/ppermute | solution.py:91
  190.4 2.1 collective-permute-start.20
  192.4 2.5 %collective-permute-done.34 = bf16[32,1152]{1,0:T(8,128)(2,1)S(1)} collective-permute-done((bf16[32,1152]{1,0:T(8,128)(2,1)S(1)}, bf16[32,1152]{1,0:T(8,128)(2,1)S(1)}, u32[]{:S(2)}, u32[]{:S(2)}) %collective-permute-start.34) | collective-permute-done | bytes 73760 | tf_op jit(solution)/shard_map/ppermute | solution.py:91
  195.3 1.8 collective-permute-start.21
  197.1 2.2 %collective-permute-done.35 = bf16[32,1152]{1,0:T(8,128)(2,1)S(1)} collective-permute-done((bf16[32,1152]{1,0:T(8,128)(2,1)S(1)}, bf16[32,1152]{1,0:T(8,128)(2,1)S(1)}, u32[]{:S(2)}, u32[]{:S(2)}) %collective-permute-start.35) | collective-permute-done | bytes 73760 | tf_op jit(solution)/shard_map/ppermute | solution.py:91
  199.7 1.7 collective-permute-start.22
  201.5 2.2 %collective-permute-done.36 = bf16[32,1152]{1,0:T(8,128)(2,1)S(1)} collective-permute-done((bf16[32,1152]{1,0:T(8,128)(2,1)S(1)}, bf16[32,1152]{1,0:T(8,128)(2,1)S(1)}, u32[]{:S(2)}, u32[]{:S(2)}) %collective-permute-start.36) | collective-permute-done | bytes 73760 | tf_op jit(solution)/shard_map/ppermute | solution.py:91
  206.2 1.6 slice_multiply_fusion
  (168 shorter events, 49.4 us)
Async XLA Ops:
  7.2 77.8 %all-gather.2.cloned.1.call-start = ((), (), s32[]{:S(2)}) async-start(), calls=%async_computation | async-start | bytes 4478976 | tf_op jit(solution)/shard_map/all_gather | solution.py:112
  9.1 7.3 %collective-permute-start = (bf16[212,1,128]{2,1,0:T(2,128)(2,1)S(1)}, bf16[212,1,128]{2,1,0:T(2,128)(2,1)S(1)}, u32[]{:S(2)}, u32[]{:S(2)}) collective-permute-start(bf16[212,1,128]{2,1,0:T(2,128)(2,1)S(1)} %get-tuple-element.57), channel_id=1, source_target_pairs={{0,2},{2,4},{4,6},{6,8},{8,10},{10,12},{12,14},{1,3},{3,5},{5,7},{... | collective-permute-start | bytes 162824 | tf_op jit(solution)/shard_map/ppermute | solution.py:19
  14.0 6.6 %collective-permute-start.1 = (bf16[212,1,128]{2,1,0:T(2,128)(2,1)S(1)}, bf16[212,1,128]{2,1,0:T(2,128)(2,1)S(1)}, u32[]{:S(2)}, u32[]{:S(2)}) collective-permute-start(bf16[212,1,128]{2,1,0:T(2,128)(2,1)S(1)} %get-tuple-element.58), channel_id=1, source_target_pairs={{2,0},{4,2},{6,4},{8,6},{10,8},{12,10},{14,12},{3,1},{5,3},{7,5},{... | collective-permute-start | bytes 162824 | tf_op jit(solution)/shard_map/ppermute | solution.py:20
  93.1 15.1 %collective-permute-start.2 = (f32[512,512]{0,1:T(8,128)}, f32[512,512]{0,1:T(8,128)}, u32[]{:S(2)}, u32[]{:S(2)}) collective-permute-start(f32[512,512]{0,1:T(8,128)} %constant_dynamic-slice_fusion.2), channel_id=1, source_target_pairs={{0,1},{1,0},{2,3},{3,2},{4,5},{5,4},{6,7},{7,6},{8,9},{9,8},{10,11... | collective-permute-start | bytes 3145736 | tf_op jit(solution)/shard_map/ppermute | solution.py:41
  94.6 44.2 %collective-permute-start.4 = (bf16[512,512]{1,0:T(8,128)(2,1)}, bf16[512,512]{1,0:T(8,128)(2,1)}, u32[]{:S(2)}, u32[]{:S(2)}) collective-permute-start(bf16[512,512]{1,0:T(8,128)(2,1)} %get-tuple-element.47), channel_id=1, source_target_pairs={{0,1},{1,0},{2,3},{3,2},{4,5},{5,4},{6,7},{7,6},{8,9},{9,8},{10,11... | collective-permute-start | bytes 1572872 | tf_op jit(solution)/shard_map/ppermute | solution.py:132
  115.4 23.4 %collective-permute-start.5 = (bf16[512,512]{0,1:T(8,128)(2,1)}, bf16[512,512]{0,1:T(8,128)(2,1)}, u32[]{:S(2)}, u32[]{:S(2)}) collective-permute-start(bf16[512,512]{0,1:T(8,128)(2,1)} %get-tuple-element.31), channel_id=1, source_target_pairs={{0,1},{1,0},{2,3},{3,2},{4,5},{5,4},{6,7},{7,6},{8,9},{9,8},{10,11... | collective-permute-start | bytes 1572872 | tf_op jit(solution)/shard_map/ppermute | solution.py:26
  119.7 6.3 %collective-permute-start.23 = (f32[32,1152]{1,0:T(8,128)S(1)}, f32[32,1152]{1,0:T(8,128)S(1)}, u32[]{:S(2)}, u32[]{:S(2)}) collective-permute-start(f32[32,1152]{1,0:T(8,128)S(1)} %select_bitcast_fusion), channel_id=1, source_target_pairs={{2,0},{6,2},{10,6},{14,10},{12,14},{8,12},{4,8},{0,4},{3,1},{7,3},... | collective-permute-start | bytes 442376 | tf_op jit(solution)/shard_map/ppermute | solution.py:85
  119.8 6.5 %collective-permute-start.9 = (f32[32,1152]{1,0:T(8,128)S(1)}, f32[32,1152]{1,0:T(8,128)S(1)}, u32[]{:S(2)}, u32[]{:S(2)}) collective-permute-start(f32[32,1152]{1,0:T(8,128)S(1)} %select_bitcast_fusion.1), channel_id=1, source_target_pairs={{0,2},{2,6},{6,10},{10,14},{14,12},{12,8},{8,4},{4,0},{1,3},{3,7},... | collective-permute-start | bytes 442376 | tf_op jit(solution)/shard_map/ppermute | solution.py:85
  126.0 5.4 %collective-permute-start.24 = (f32[32,1152]{1,0:T(8,128)S(1)}, f32[32,1152]{1,0:T(8,128)S(1)}, u32[]{:S(2)}, u32[]{:S(2)}) collective-permute-start(f32[32,1152]{1,0:T(8,128)S(1)} %bitcast_add_fusion.11), channel_id=1, source_target_pairs={{2,0},{6,2},{10,6},{14,10},{12,14},{8,12},{4,8},{0,4},{3,1},{7,3},... | collective-permute-start | bytes 442376 | tf_op jit(solution)/shard_map/ppermute | solution.py:85
  126.4 5.7 %collective-permute-start.10 = (f32[32,1152]{1,0:T(8,128)S(1)}, f32[32,1152]{1,0:T(8,128)S(1)}, u32[]{:S(2)}, u32[]{:S(2)}) collective-permute-start(f32[32,1152]{1,0:T(8,128)S(1)} %bitcast_add_fusion.18), channel_id=1, source_target_pairs={{0,2},{2,6},{6,10},{10,14},{14,12},{12,8},{8,4},{4,0},{1,3},{3,7},... | collective-permute-start | bytes 442376 | tf_op jit(solution)/shard_map/ppermute | solution.py:85
  131.4 5.2 %collective-permute-start.25 = (f32[32,1152]{1,0:T(8,128)S(1)}, f32[32,1152]{1,0:T(8,128)S(1)}, u32[]{:S(2)}, u32[]{:S(2)}) collective-permute-start(f32[32,1152]{1,0:T(8,128)S(1)} %bitcast_add_fusion.10), channel_id=1, source_target_pairs={{2,0},{6,2},{10,6},{14,10},{12,14},{8,12},{4,8},{0,4},{3,1},{7,3},... | collective-permute-start | bytes 442376 | tf_op jit(solution)/shard_map/ppermute | solution.py:85
  132.1 5.2 %collective-permute-start.11 = (f32[32,1152]{1,0:T(8,128)S(1)}, f32[32,1152]{1,0:T(8,128)S(1)}, u32[]{:S(2)}, u32[]{:S(2)}) collective-permute-start(f32[32,1152]{1,0:T(8,128)S(1)} %bitcast_add_fusion.17), channel_id=1, source_target_pairs={{0,2},{2,6},{6,10},{10,14},{14,12},{12,8},{8,4},{4,0},{1,3},{3,7},... | collective-permute-start | bytes 442376 | tf_op jit(solution)/shard_map/ppermute | solution.py:85
  136.6 5.6 %collective-permute-start.26 = (f32[32,1152]{1,0:T(8,128)S(1)}, f32[32,1152]{1,0:T(8,128)S(1)}, u32[]{:S(2)}, u32[]{:S(2)}) collective-permute-start(f32[32,1152]{1,0:T(8,128)S(1)} %bitcast_add_fusion.9), channel_id=1, source_target_pairs={{2,0},{6,2},{10,6},{14,10},{12,14},{8,12},{4,8},{0,4},{3,1},{7,3},... | collective-permute-start | bytes 442376 | tf_op jit(solution)/shard_map/ppermute | solution.py:85
  137.3 5.6 %collective-permute-start.12 = (f32[32,1152]{1,0:T(8,128)S(1)}, f32[32,1152]{1,0:T(8,128)S(1)}, u32[]{:S(2)}, u32[]{:S(2)}) collective-permute-start(f32[32,1152]{1,0:T(8,128)S(1)} %bitcast_add_fusion.16), channel_id=1, source_target_pairs={{0,2},{2,6},{6,10},{10,14},{14,12},{12,8},{8,4},{4,0},{1,3},{3,7},... | collective-permute-start | bytes 442376 | tf_op jit(solution)/shard_map/ppermute | solution.py:85
  142.2 19.3 %collective-permute-start.6 = (bf16[512,4,128]{0,2,1:T(8,128)(2,1)S(1)}, bf16[512,4,128]{0,2,1:T(8,128)(2,1)S(1)}, u32[]{:S(2)}, u32[]{:S(2)}) collective-permute-start(bf16[512,4,128]{0,2,1:T(8,128)(2,1)S(1)} %bitcast.255), channel_id=1, source_target_pairs={{0,1},{1,0},{2,3},{3,2},{4,5},{5,4},{6,7},{7,6},{8,9},{9,8},{10,11... | collective-permute-start | bytes 1572872 | tf_op jit(solution)/shard_map/ppermute | solution.py:26
  142.3 6.3 %collective-permute-start.27 = (f32[32,1152]{1,0:T(8,128)S(1)}, f32[32,1152]{1,0:T(8,128)S(1)}, u32[]{:S(2)}, u32[]{:S(2)}) collective-permute-start(f32[32,1152]{1,0:T(8,128)S(1)} %bitcast_add_fusion.8), channel_id=1, source_target_pairs={{2,0},{6,2},{10,6},{14,10},{12,14},{8,12},{4,8},{0,4},{3,1},{7,3},... | collective-permute-start | bytes 442376 | tf_op jit(solution)/shard_map/ppermute | solution.py:85
  142.9 6.3 %collective-permute-start.13 = (f32[32,1152]{1,0:T(8,128)S(1)}, f32[32,1152]{1,0:T(8,128)S(1)}, u32[]{:S(2)}, u32[]{:S(2)}) collective-permute-start(f32[32,1152]{1,0:T(8,128)S(1)} %bitcast_add_fusion.15), channel_id=1, source_target_pairs={{0,2},{2,6},{6,10},{10,14},{14,12},{12,8},{8,4},{4,0},{1,3},{3,7},... | collective-permute-start | bytes 442376 | tf_op jit(solution)/shard_map/ppermute | solution.py:85
  148.6 5.4 %collective-permute-start.28 = (f32[32,1152]{1,0:T(8,128)S(1)}, f32[32,1152]{1,0:T(8,128)S(1)}, u32[]{:S(2)}, u32[]{:S(2)}) collective-permute-start(f32[32,1152]{1,0:T(8,128)S(1)} %bitcast_add_fusion.7), channel_id=1, source_target_pairs={{2,0},{6,2},{10,6},{14,10},{12,14},{8,12},{4,8},{0,4},{3,1},{7,3},... | collective-permute-start | bytes 442376 | tf_op jit(solution)/shard_map/ppermute | solution.py:85
  149.2 5.4 %collective-permute-start.14 = (f32[32,1152]{1,0:T(8,128)S(1)}, f32[32,1152]{1,0:T(8,128)S(1)}, u32[]{:S(2)}, u32[]{:S(2)}) collective-permute-start(f32[32,1152]{1,0:T(8,128)S(1)} %bitcast_add_fusion.14), channel_id=1, source_target_pairs={{0,2},{2,6},{6,10},{10,14},{14,12},{12,8},{8,4},{4,0},{1,3},{3,7},... | collective-permute-start | bytes 442376 | tf_op jit(solution)/shard_map/ppermute | solution.py:85
  154.1 5.2 %collective-permute-start.29 = (f32[32,1152]{1,0:T(8,128)S(1)}, f32[32,1152]{1,0:T(8,128)S(1)}, u32[]{:S(2)}, u32[]{:S(2)}) collective-permute-start(f32[32,1152]{1,0:T(8,128)S(1)} %bitcast_add_fusion.6), channel_id=1, source_target_pairs={{2,0},{6,2},{10,6},{14,10},{12,14},{8,12},{4,8},{0,4},{3,1},{7,3},... | collective-permute-start | bytes 442376 | tf_op jit(solution)/shard_map/ppermute | solution.py:85
  154.7 5.2 %collective-permute-start.15 = (f32[32,1152]{1,0:T(8,128)S(1)}, f32[32,1152]{1,0:T(8,128)S(1)}, u32[]{:S(2)}, u32[]{:S(2)}) collective-permute-start(f32[32,1152]{1,0:T(8,128)S(1)} %bitcast_add_fusion.13), channel_id=1, source_target_pairs={{0,2},{2,6},{6,10},{10,14},{14,12},{12,8},{8,4},{4,0},{1,3},{3,7},... | collective-permute-start | bytes 442376 | tf_op jit(solution)/shard_map/ppermute | solution.py:85
  159.3 9.3 %collective-permute-start.30 = (bf16[32,1152]{1,0:T(8,128)(2,1)S(1)}, bf16[32,1152]{1,0:T(8,128)(2,1)S(1)}, u32[]{:S(2)}, u32[]{:S(2)}) collective-permute-start(bf16[32,1152]{1,0:T(8,128)(2,1)S(1)} %get-tuple-element.29), channel_id=1, source_target_pairs={{2,0},{6,2},{10,6},{14,10},{12,14},{8,12},{4,8},{0,4},{3,1},{7,3},... | collective-permute-start | bytes 221192 | tf_op jit(solution)/shard_map/ppermute | solution.py:91
  159.9 9.6 %collective-permute-start.16 = (bf16[32,1152]{1,0:T(8,128)(2,1)S(1)}, bf16[32,1152]{1,0:T(8,128)(2,1)S(1)}, u32[]{:S(2)}, u32[]{:S(2)}) collective-permute-start(bf16[32,1152]{1,0:T(8,128)(2,1)S(1)} %get-tuple-element.27), channel_id=1, source_target_pairs={{0,2},{2,6},{6,10},{10,14},{14,12},{12,8},{8,4},{4,0},{1,3},{3,7},... | collective-permute-start | bytes 221192 | tf_op jit(solution)/shard_map/ppermute | solution.py:91
  162.2 21.3 %collective-permute-start.8 = (bf16[1024,1,128]{0,2,1:T(8,128)(2,1)S(1)}, bf16[1024,1,128]{0,2,1:T(8,128)(2,1)S(1)}, u32[]{:S(2)}, u32[]{:S(2)}) collective-permute-start(bf16[1024,1,128]{0,2,1:T(8,128)(2,1)S(1)} %get-tuple-element.45), channel_id=1, source_target_pairs={{2,0},{4,2},{6,4},{8,6},{10,8},{12,10},{14,12},{3,1},{5,3},{7,5},{... | collective-permute-start | bytes 786440 | tf_op jit(solution)/shard_map/ppermute | solution.py:20
  163.5 20.1 %collective-permute-start.7 = (bf16[1024,1,128]{0,2,1:T(8,128)(2,1)S(1)}, bf16[1024,1,128]{0,2,1:T(8,128)(2,1)S(1)}, u32[]{:S(2)}, u32[]{:S(2)}) collective-permute-start(bf16[1024,1,128]{0,2,1:T(8,128)(2,1)S(1)} %get-tuple-element.46), channel_id=1, source_target_pairs={{0,2},{2,4},{4,6},{6,8},{8,10},{10,12},{12,14},{1,3},{3,5},{5,7},{... | collective-permute-start | bytes 786440 | tf_op jit(solution)/shard_map/ppermute | solution.py:19
  168.6 5.1 %collective-permute-start.31 = (bf16[32,1152]{1,0:T(8,128)(2,1)S(1)}, bf16[32,1152]{1,0:T(8,128)(2,1)S(1)}, u32[]{:S(2)}, u32[]{:S(2)}) collective-permute-start(bf16[32,1152]{1,0:T(8,128)(2,1)S(1)} %collective-permute-done.30), channel_id=1, source_target_pairs={{2,0},{6,2},{10,6},{14,10},{12,14},{8,12},{4,8},{0,4},{3,1},{7,3},... | collective-permute-start | bytes 221192 | tf_op jit(solution)/shard_map/ppermute | solution.py:91
  169.5 7.2 %collective-permute-start.17 = (bf16[32,1152]{1,0:T(8,128)(2,1)S(1)}, bf16[32,1152]{1,0:T(8,128)(2,1)S(1)}, u32[]{:S(2)}, u32[]{:S(2)}) collective-permute-start(bf16[32,1152]{1,0:T(8,128)(2,1)S(1)} %collective-permute-done.16), channel_id=1, source_target_pairs={{0,2},{2,6},{6,10},{10,14},{14,12},{12,8},{8,4},{4,0},{1,3},{3,7},... | collective-permute-start | bytes 221192 | tf_op jit(solution)/shard_map/ppermute | solution.py:91
  173.7 5.5 %collective-permute-start.32 = (bf16[32,1152]{1,0:T(8,128)(2,1)S(1)}, bf16[32,1152]{1,0:T(8,128)(2,1)S(1)}, u32[]{:S(2)}, u32[]{:S(2)}) collective-permute-start(bf16[32,1152]{1,0:T(8,128)(2,1)S(1)} %collective-permute-done.31), channel_id=1, source_target_pairs={{2,0},{6,2},{10,6},{14,10},{12,14},{8,12},{4,8},{0,4},{3,1},{7,3},... | collective-permute-start | bytes 221192 | tf_op jit(solution)/shard_map/ppermute | solution.py:91
  179.2 11.1 %collective-permute-start.33 = (bf16[32,1152]{1,0:T(8,128)(2,1)S(1)}, bf16[32,1152]{1,0:T(8,128)(2,1)S(1)}, u32[]{:S(2)}, u32[]{:S(2)}) collective-permute-start(bf16[32,1152]{1,0:T(8,128)(2,1)S(1)} %collective-permute-done.32), channel_id=1, source_target_pairs={{2,0},{6,2},{10,6},{14,10},{12,14},{8,12},{4,8},{0,4},{3,1},{7,3},... | collective-permute-start | bytes 221192 | tf_op jit(solution)/shard_map/ppermute | solution.py:91
  181.2 9.2 %collective-permute-start.19 = (bf16[32,1152]{1,0:T(8,128)(2,1)S(1)}, bf16[32,1152]{1,0:T(8,128)(2,1)S(1)}, u32[]{:S(2)}, u32[]{:S(2)}) collective-permute-start(bf16[32,1152]{1,0:T(8,128)(2,1)S(1)} %collective-permute-done.18), channel_id=1, source_target_pairs={{0,2},{2,6},{6,10},{10,14},{14,12},{12,8},{8,4},{4,0},{1,3},{3,7},... | collective-permute-start | bytes 221192 | tf_op jit(solution)/shard_map/ppermute | solution.py:91
  190.4 4.9 %collective-permute-start.20 = (bf16[32,1152]{1,0:T(8,128)(2,1)S(1)}, bf16[32,1152]{1,0:T(8,128)(2,1)S(1)}, u32[]{:S(2)}, u32[]{:S(2)}) collective-permute-start(bf16[32,1152]{1,0:T(8,128)(2,1)S(1)} %collective-permute-done.19), channel_id=1, source_target_pairs={{0,2},{2,6},{6,10},{10,14},{14,12},{12,8},{8,4},{4,0},{1,3},{3,7},... | collective-permute-start | bytes 221192 | tf_op jit(solution)/shard_map/ppermute | solution.py:91
  199.7 4.8 %collective-permute-start.22 = (bf16[32,1152]{1,0:T(8,128)(2,1)S(1)}, bf16[32,1152]{1,0:T(8,128)(2,1)S(1)}, u32[]{:S(2)}, u32[]{:S(2)}) collective-permute-start(bf16[32,1152]{1,0:T(8,128)(2,1)S(1)} %collective-permute-done.21), channel_id=1, source_target_pairs={{0,2},{2,6},{6,10},{10,14},{14,12},{12,8},{8,4},{4,0},{1,3},{3,7},... | collective-permute-start | bytes 221192 | tf_op jit(solution)/shard_map/ppermute | solution.py:91
  (17 other events, 133.8 us)
Sparse Core Ops, SparseCore 0:
  10.0 74.9 all-gather.1

commit v5 on v4

--- a/solution.py
+++ b/solution.py
@@ -118,7 +118,7 @@
             partial_value = partial_value + jnp.dot(
                 shard_piece[:, tap_index, :], window, preferred_element_type=jnp.float32
             )
-        pre = chan_scatter_sum(partial_value)
+        pre = lax.psum_scatter(partial_value, "chan", scatter_dimension=0, tiled=True)
         squares_own = (pre * pre).astype(jnp.bfloat16)
         squares = chan_gather(squares_own)
         norm_value = gdn_beta[:, None] + jnp.dot(gdn_gamma, squares, preferred_element_type=jnp.float32)

time: 215 us -> 215 us (level)
    unnamed x53 -> x51, local copies, waits for them, and re-layouts: 4.86 us -> 5.53 us
  transfers between devices with their start and end apart: 38 -> 38, of which waited for: 15 -> 15; matrix products, arithmetic and copies ran while one was open for 16% -> 15% of each run, Pallas kernels for 0% -> 0%
where the time goes in v5:
time: 215 us; the launch traced here: 214 us
  waiting for transfers between devices  99.2 us (46%)
  starting transfers between devices  44.4 us (21%)
  between operations  25.7 us (12%)
  matrix products  20.1 us (9%)
  local copies, waits for them, and re-layouts  13 us (6%)
  other arithmetic  12.1 us (6%)
    all_gather x1, waiting for transfers between devices, per_device(): shard_piece = lax.all_gather(conv_weight, 'row', axis=0, tiled=True)  59.7 us
    ppermute x14, waiting for transfers between devices, ring_sum(): got = lax.ppermute(carry[part], 'row', moves[part])  20.8 us
    ppermute x14, starting transfers between devices, ring_sum(): gathered[part].append(lax.ppermute(gathered[part][-1], 'row', moves[part]))  16.5 us
    ppermute x14, starting transfers between devices, ring_sum(): got = lax.ppermute(carry[part], 'row', moves[part])  15.1 us
    ppermute x14, waiting for transfers between devices, ring_sum(): gathered[part].append(lax.ppermute(gathered[part][-1], 'row', moves[part]))  13.7 us
    ppermute x2, starting transfers between devices, extended(): before = lax.ppermute(last, axis, up)  9.44 us
    dot_general x9, matrix products, per_device(): jnp.dot(shard_piece[:, tap_index, :], window, preferred_element_type=jnp....  8.27 us
    unnamed x51, local copies, waits for them, and re-layouts  5.53 us
  transfers between devices with their start and end apart: 38, of which 15 were waited for; matrix products, arithmetic and copies ran while one was open for 15% of the time, Pallas kernels for 0%

profile of v5, /device:TPU:0, one launch (start us, length us, event | category | flops | bytes accessed | tf_op | source)
XLA Modules:
  0.0 214.5 jit_solution(478686455616075633)
XLA Ops:
  9.2 4.9 %collective-permute-start = (bf16[212,1,128]{2,1,0:T(2,128)(2,1)S(1)}, bf16[212,1,128]{2,1,0:T(2,128)(2,1)S(1)}, u32[]{:S(2)}, u32[]{:S(2)}) collective-permute-start(bf16[212,1,128]{2,1,0:T(2,128)(2,1)S(1)} %get-tuple-element.56), channel_id=1, source_target_pairs={{0,2},{2,4},{4,6},{6,8},{8,10},{10,12},{12,14},{1,3},{3,5},{5,7},{... | collective-permute-start | bytes 162824 | tf_op jit(solution)/shard_map/ppermute | solution.py:19
  16.5 4.2 %collective-permute-done.1 = bf16[212,1,128]{2,1,0:T(2,128)(2,1)S(1)} collective-permute-done((bf16[212,1,128]{2,1,0:T(2,128)(2,1)S(1)}, bf16[212,1,128]{2,1,0:T(2,128)(2,1)S(1)}, u32[]{:S(2)}, u32[]{:S(2)}) %collective-permute-start.1) | collective-permute-done | bytes 54304 | tf_op jit(solution)/shard_map/ppermute | solution.py:20
  20.7 1.6 pad_maximum_fusion.4
  25.3 59.7 %all-gather.2.cloned.1.call-done = bf16[1024,9,212]{0,2,1:T(8,128)(2,1)} async-done(((bf16[128,9,212]{0,2,1:T(8,128)(2,1)}), bf16[1024,9,212]{0,2,1:T(8,128)(2,1)}) %all-gather.2.cloned.1.call-update) | async-done | bytes 3907600 | tf_op jit(solution)/shard_map/all_gather | solution.py:112
  85.0 1.6 fusion.50
  91.0 2.3 %bitcast_add_fusion = f32[1024,512]{0,1:T(8,128)} fusion(f32[512,1024]{1,0:T(8,128)S(1)} %fusion.50, f32[512,1024]{1,0:T(8,128)S(1)} %fusion.48, f32[512,1024]{1,0:T(8,128)S(1)} %fusion.46, f32[1024,512]{0,1:T(8,128)S(1)} %fusion.44, f32[512,1024]{1,0:T(8,128)S(1)} %fusion.42, f32[512,1024]{1,0:T(8,128)S(1)} %fusion.40, f32[512,1024]{1,0:T(8,128)S(1)} %fusion.36, ...), kind=kOutput, calls=%fused_computation.26 | convolution fusion | flops 226492416 | bytes 19537920 | tf_op jit(solution)/shard_map/dot_general | solution.py:118
  112.9 2.3 %convert_reduce_fusion = (f32[512]{0:T(512)S(1)}, bf16[512,512]{0,1:T(8,128)(2,1)}, f32[512,512]{0,1:T(8,128)}, bf16[512,512]{0,1:T(8,128)(2,1)}) fusion(f32[512,512]{0,1:T(8,128)S(1)} %copy-done.2, f32[512,4,128]{0,2,1:T(8,128)S(1)} %copy.14, bf16[1024,512]{0,1:T(8,128)(2,1)S(1)} %fusion.27, bf16[512,1024]{1,0:T(8,128)(2,1)S(1)} %copy-done.3, ...), kind=kOutput, calls=%fused_computation.65 | convolution fusion | flops 540016128 | bytes 6295552 | tf_op jit(solution)/shard_map/dot_general | solution.py:124
  115.2 1.8 fusion.66
  117.0 2.1 copy.15
  119.6 2.1 collective-permute-start.8
  121.6 4.2 %collective-permute-done.22 = f32[32,1152]{1,0:T(8,128)S(1)} collective-permute-done((f32[32,1152]{1,0:T(8,128)S(1)}, f32[32,1152]{1,0:T(8,128)S(1)}, u32[]{:S(2)}, u32[]{:S(2)}) %collective-permute-start.22) | collective-permute-done | bytes 147488 | tf_op jit(solution)/shard_map/ppermute | solution.py:85
  126.1 2.0 collective-permute-start.9
  128.1 3.1 %collective-permute-done.23 = f32[32,1152]{1,0:T(8,128)S(1)} collective-permute-done((f32[32,1152]{1,0:T(8,128)S(1)}, f32[32,1152]{1,0:T(8,128)S(1)}, u32[]{:S(2)}, u32[]{:S(2)}) %collective-permute-start.23) | collective-permute-done | bytes 147488 | tf_op jit(solution)/shard_map/ppermute | solution.py:85
  133.4 3.0 %collective-permute-done.24 = f32[32,1152]{1,0:T(8,128)S(1)} collective-permute-done((f32[32,1152]{1,0:T(8,128)S(1)}, f32[32,1152]{1,0:T(8,128)S(1)}, u32[]{:S(2)}, u32[]{:S(2)}) %collective-permute-start.24) | collective-permute-done | bytes 147488 | tf_op jit(solution)/shard_map/ppermute | solution.py:85
  138.6 3.3 %fusion.10 = bf16[512,512]{0,1:T(8,128)(2,1)S(1)} fusion(f32[512,512]{0,1:T(8,128)S(1)} %copy-done.5, s32[]{:T(128)S(6)} %select_n.194, bf16[512,512]{1,0:T(8,128)(2,1)S(1)} %copy-done.7, bf16[512,512]{1,0:T(8,128)(2,1)} %collective-permute-done.3, bf16[512,512]{0,1:T(8,128)(2,1)} %get-tuple-element.31, bf16[512,512]{0,1:T(8,128)(2,1)} %collective-permute-done.4, ...), kind=kOutput, calls=%fused_computation.43 | convolution fusion | flops 546308096 | bytes 4719616 | tf_op jit(solution)/shard_map/dot_general | solution.py:134
  142.7 1.5 collective-permute-start.12
  144.2 4.1 %collective-permute-done.26 = f32[32,1152]{1,0:T(8,128)S(1)} collective-permute-done((f32[32,1152]{1,0:T(8,128)S(1)}, f32[32,1152]{1,0:T(8,128)S(1)}, u32[]{:S(2)}, u32[]{:S(2)}) %collective-permute-start.26) | collective-permute-done | bytes 147488 | tf_op jit(solution)/shard_map/ppermute | solution.py:85
  150.5 3.3 %collective-permute-done.27 = f32[32,1152]{1,0:T(8,128)S(1)} collective-permute-done((f32[32,1152]{1,0:T(8,128)S(1)}, f32[32,1152]{1,0:T(8,128)S(1)}, u32[]{:S(2)}, u32[]{:S(2)}) %collective-permute-start.27) | collective-permute-done | bytes 147488 | tf_op jit(solution)/shard_map/ppermute | solution.py:85
  156.0 3.0 %collective-permute-done.28 = f32[32,1152]{1,0:T(8,128)S(1)} collective-permute-done((f32[32,1152]{1,0:T(8,128)S(1)}, f32[32,1152]{1,0:T(8,128)S(1)}, u32[]{:S(2)}, u32[]{:S(2)}) %collective-permute-start.28) | collective-permute-done | bytes 147488 | tf_op jit(solution)/shard_map/ppermute | solution.py:85
  163.2 4.6 %collective-permute-start.6 = (bf16[1024,1,128]{0,2,1:T(8,128)(2,1)S(1)}, bf16[1024,1,128]{0,2,1:T(8,128)(2,1)S(1)}, u32[]{:S(2)}, u32[]{:S(2)}) collective-permute-start(bf16[1024,1,128]{0,2,1:T(8,128)(2,1)S(1)} %get-tuple-element.45), channel_id=1, source_target_pairs={{0,2},{2,4},{4,6},{6,8},{8,10},{10,12},{12,14},{1,3},{3,5},{5,7},{... | collective-permute-start | bytes 786440 | tf_op jit(solution)/shard_map/ppermute | solution.py:19
  170.8 2.6 %collective-permute-done.30 = bf16[32,1152]{1,0:T(8,128)(2,1)S(1)} collective-permute-done((bf16[32,1152]{1,0:T(8,128)(2,1)S(1)}, bf16[32,1152]{1,0:T(8,128)(2,1)S(1)}, u32[]{:S(2)}, u32[]{:S(2)}) %collective-permute-start.30) | collective-permute-done | bytes 73760 | tf_op jit(solution)/shard_map/ppermute | solution.py:91
  174.3 2.1 collective-permute-done.16
  176.5 2.5 %collective-permute-start.17 = (bf16[32,1152]{1,0:T(8,128)(2,1)S(1)}, bf16[32,1152]{1,0:T(8,128)(2,1)S(1)}, u32[]{:S(2)}, u32[]{:S(2)}) collective-permute-start(bf16[32,1152]{1,0:T(8,128)(2,1)S(1)} %collective-permute-done.16), channel_id=1, source_target_pairs={{0,2},{2,6},{6,10},{10,14},{14,12},{12,8},{8,4},{4,0},{1,3},{3,7},... | collective-permute-start | bytes 221192 | tf_op jit(solution)/shard_map/ppermute | solution.py:91
  179.0 1.9 collective-permute-done.17
  180.9 2.4 %collective-permute-start.18 = (bf16[32,1152]{1,0:T(8,128)(2,1)S(1)}, bf16[32,1152]{1,0:T(8,128)(2,1)S(1)}, u32[]{:S(2)}, u32[]{:S(2)}) collective-permute-start(bf16[32,1152]{1,0:T(8,128)(2,1)S(1)} %collective-permute-done.17), channel_id=1, source_target_pairs={{0,2},{2,6},{6,10},{10,14},{14,12},{12,8},{8,4},{4,0},{1,3},{3,7},... | collective-permute-start | bytes 221192 | tf_op jit(solution)/shard_map/ppermute | solution.py:91
  190.1 2.1 collective-permute-start.19
  192.2 2.6 %collective-permute-done.33 = bf16[32,1152]{1,0:T(8,128)(2,1)S(1)} collective-permute-done((bf16[32,1152]{1,0:T(8,128)(2,1)S(1)}, bf16[32,1152]{1,0:T(8,128)(2,1)S(1)}, u32[]{:S(2)}, u32[]{:S(2)}) %collective-permute-start.33) | collective-permute-done | bytes 73760 | tf_op jit(solution)/shard_map/ppermute | solution.py:91
  195.1 1.8 collective-permute-start.20
  196.9 2.2 %collective-permute-done.34 = bf16[32,1152]{1,0:T(8,128)(2,1)S(1)} collective-permute-done((bf16[32,1152]{1,0:T(8,128)(2,1)S(1)}, bf16[32,1152]{1,0:T(8,128)(2,1)S(1)}, u32[]{:S(2)}, u32[]{:S(2)}) %collective-permute-start.34) | collective-permute-done | bytes 73760 | tf_op jit(solution)/shard_map/ppermute | solution.py:91
  199.5 1.7 collective-permute-start.21
  201.3 2.2 %collective-permute-done.35 = bf16[32,1152]{1,0:T(8,128)(2,1)S(1)} collective-permute-done((bf16[32,1152]{1,0:T(8,128)(2,1)S(1)}, bf16[32,1152]{1,0:T(8,128)(2,1)S(1)}, u32[]{:S(2)}, u32[]{:S(2)}) %collective-permute-start.35) | collective-permute-done | bytes 73760 | tf_op jit(solution)/shard_map/ppermute | solution.py:91
  206.0 1.6 slice_multiply_fusion
  (166 shorter events, 48.5 us)
Async XLA Ops:
  7.2 77.8 %all-gather.2.cloned.1.call-start = ((), (), s32[]{:S(2)}) async-start(), calls=%async_computation.1 | async-start | bytes 4478976 | tf_op jit(solution)/shard_map/all_gather | solution.py:112
  7.9 100.2 %reduce-scatter.2.cloned.1.call-start = ((), (), s32[]{:S(2)}) async-start(), calls=%async_computation.2 | async-start | bytes 3145728 | tf_op jit(solution)/shard_map/reduce_scatter | solution.py:121
  9.2 7.3 %collective-permute-start = (bf16[212,1,128]{2,1,0:T(2,128)(2,1)S(1)}, bf16[212,1,128]{2,1,0:T(2,128)(2,1)S(1)}, u32[]{:S(2)}, u32[]{:S(2)}) collective-permute-start(bf16[212,1,128]{2,1,0:T(2,128)(2,1)S(1)} %get-tuple-element.56), channel_id=1, source_target_pairs={{0,2},{2,4},{4,6},{6,8},{8,10},{10,12},{12,14},{1,3},{3,5},{5,7},{... | collective-permute-start | bytes 162824 | tf_op jit(solution)/shard_map/ppermute | solution.py:19
  14.1 6.6 %collective-permute-start.1 = (bf16[212,1,128]{2,1,0:T(2,128)(2,1)S(1)}, bf16[212,1,128]{2,1,0:T(2,128)(2,1)S(1)}, u32[]{:S(2)}, u32[]{:S(2)}) collective-permute-start(bf16[212,1,128]{2,1,0:T(2,128)(2,1)S(1)} %get-tuple-element.57), channel_id=1, source_target_pairs={{2,0},{4,2},{6,4},{8,6},{10,8},{12,10},{14,12},{3,1},{5,3},{7,5},{... | collective-permute-start | bytes 162824 | tf_op jit(solution)/shard_map/ppermute | solution.py:20
  95.6 43.0 %collective-permute-start.3 = (bf16[512,512]{1,0:T(8,128)(2,1)}, bf16[512,512]{1,0:T(8,128)(2,1)}, u32[]{:S(2)}, u32[]{:S(2)}) collective-permute-start(bf16[512,512]{1,0:T(8,128)(2,1)} %get-tuple-element.46), channel_id=1, source_target_pairs={{0,1},{1,0},{2,3},{3,2},{4,5},{5,4},{6,7},{7,6},{8,9},{9,8},{10,11... | collective-permute-start | bytes 1572872 | tf_op jit(solution)/shard_map/ppermute | solution.py:132
  115.2 23.4 %collective-permute-start.4 = (bf16[512,512]{0,1:T(8,128)(2,1)}, bf16[512,512]{0,1:T(8,128)(2,1)}, u32[]{:S(2)}, u32[]{:S(2)}) collective-permute-start(bf16[512,512]{0,1:T(8,128)(2,1)} %get-tuple-element.31), channel_id=1, source_target_pairs={{0,1},{1,0},{2,3},{3,2},{4,5},{5,4},{6,7},{7,6},{8,9},{9,8},{10,11... | collective-permute-start | bytes 1572872 | tf_op jit(solution)/shard_map/ppermute | solution.py:26
  119.5 6.3 %collective-permute-start.22 = (f32[32,1152]{1,0:T(8,128)S(1)}, f32[32,1152]{1,0:T(8,128)S(1)}, u32[]{:S(2)}, u32[]{:S(2)}) collective-permute-start(f32[32,1152]{1,0:T(8,128)S(1)} %select_bitcast_fusion), channel_id=1, source_target_pairs={{2,0},{6,2},{10,6},{14,10},{12,14},{8,12},{4,8},{0,4},{3,1},{7,3},... | collective-permute-start | bytes 442376 | tf_op jit(solution)/shard_map/ppermute | solution.py:85
  119.6 6.6 %collective-permute-start.8 = (f32[32,1152]{1,0:T(8,128)S(1)}, f32[32,1152]{1,0:T(8,128)S(1)}, u32[]{:S(2)}, u32[]{:S(2)}) collective-permute-start(f32[32,1152]{1,0:T(8,128)S(1)} %select_bitcast_fusion.1), channel_id=1, source_target_pairs={{0,2},{2,6},{6,10},{10,14},{14,12},{12,8},{8,4},{4,0},{1,3},{3,7},... | collective-permute-start | bytes 442376 | tf_op jit(solution)/shard_map/ppermute | solution.py:85
  125.8 5.4 %collective-permute-start.23 = (f32[32,1152]{1,0:T(8,128)S(1)}, f32[32,1152]{1,0:T(8,128)S(1)}, u32[]{:S(2)}, u32[]{:S(2)}) collective-permute-start(f32[32,1152]{1,0:T(8,128)S(1)} %bitcast_add_fusion.11), channel_id=1, source_target_pairs={{2,0},{6,2},{10,6},{14,10},{12,14},{8,12},{4,8},{0,4},{3,1},{7,3},... | collective-permute-start | bytes 442376 | tf_op jit(solution)/shard_map/ppermute | solution.py:85
  126.1 5.7 %collective-permute-start.9 = (f32[32,1152]{1,0:T(8,128)S(1)}, f32[32,1152]{1,0:T(8,128)S(1)}, u32[]{:S(2)}, u32[]{:S(2)}) collective-permute-start(f32[32,1152]{1,0:T(8,128)S(1)} %bitcast_add_fusion.18), channel_id=1, source_target_pairs={{0,2},{2,6},{6,10},{10,14},{14,12},{12,8},{8,4},{4,0},{1,3},{3,7},... | collective-permute-start | bytes 442376 | tf_op jit(solution)/shard_map/ppermute | solution.py:85
  131.2 5.2 %collective-permute-start.24 = (f32[32,1152]{1,0:T(8,128)S(1)}, f32[32,1152]{1,0:T(8,128)S(1)}, u32[]{:S(2)}, u32[]{:S(2)}) collective-permute-start(f32[32,1152]{1,0:T(8,128)S(1)} %bitcast_add_fusion.10), channel_id=1, source_target_pairs={{2,0},{6,2},{10,6},{14,10},{12,14},{8,12},{4,8},{0,4},{3,1},{7,3},... | collective-permute-start | bytes 442376 | tf_op jit(solution)/shard_map/ppermute | solution.py:85
  131.9 5.2 %collective-permute-start.10 = (f32[32,1152]{1,0:T(8,128)S(1)}, f32[32,1152]{1,0:T(8,128)S(1)}, u32[]{:S(2)}, u32[]{:S(2)}) collective-permute-start(f32[32,1152]{1,0:T(8,128)S(1)} %bitcast_add_fusion.17), channel_id=1, source_target_pairs={{0,2},{2,6},{6,10},{10,14},{14,12},{12,8},{8,4},{4,0},{1,3},{3,7},... | collective-permute-start | bytes 442376 | tf_op jit(solution)/shard_map/ppermute | solution.py:85
  136.5 5.5 %collective-permute-start.25 = (f32[32,1152]{1,0:T(8,128)S(1)}, f32[32,1152]{1,0:T(8,128)S(1)}, u32[]{:S(2)}, u32[]{:S(2)}) collective-permute-start(f32[32,1152]{1,0:T(8,128)S(1)} %bitcast_add_fusion.9), channel_id=1, source_target_pairs={{2,0},{6,2},{10,6},{14,10},{12,14},{8,12},{4,8},{0,4},{3,1},{7,3},... | collective-permute-start | bytes 442376 | tf_op jit(solution)/shard_map/ppermute | solution.py:85
  137.1 5.5 %collective-permute-start.11 = (f32[32,1152]{1,0:T(8,128)S(1)}, f32[32,1152]{1,0:T(8,128)S(1)}, u32[]{:S(2)}, u32[]{:S(2)}) collective-permute-start(f32[32,1152]{1,0:T(8,128)S(1)} %bitcast_add_fusion.16), channel_id=1, source_target_pairs={{0,2},{2,6},{6,10},{10,14},{14,12},{12,8},{8,4},{4,0},{1,3},{3,7},... | collective-permute-start | bytes 442376 | tf_op jit(solution)/shard_map/ppermute | solution.py:85
  141.9 19.3 %collective-permute-start.5 = (bf16[512,4,128]{0,2,1:T(8,128)(2,1)S(1)}, bf16[512,4,128]{0,2,1:T(8,128)(2,1)S(1)}, u32[]{:S(2)}, u32[]{:S(2)}) collective-permute-start(bf16[512,4,128]{0,2,1:T(8,128)(2,1)S(1)} %bitcast.251), channel_id=1, source_target_pairs={{0,1},{1,0},{2,3},{3,2},{4,5},{5,4},{6,7},{7,6},{8,9},{9,8},{10,11... | collective-permute-start | bytes 1572872 | tf_op jit(solution)/shard_map/ppermute | solution.py:26
  142.0 6.3 %collective-permute-start.26 = (f32[32,1152]{1,0:T(8,128)S(1)}, f32[32,1152]{1,0:T(8,128)S(1)}, u32[]{:S(2)}, u32[]{:S(2)}) collective-permute-start(f32[32,1152]{1,0:T(8,128)S(1)} %bitcast_add_fusion.8), channel_id=1, source_target_pairs={{2,0},{6,2},{10,6},{14,10},{12,14},{8,12},{4,8},{0,4},{3,1},{7,3},... | collective-permute-start | bytes 442376 | tf_op jit(solution)/shard_map/ppermute | solution.py:85
  142.7 6.3 %collective-permute-start.12 = (f32[32,1152]{1,0:T(8,128)S(1)}, f32[32,1152]{1,0:T(8,128)S(1)}, u32[]{:S(2)}, u32[]{:S(2)}) collective-permute-start(f32[32,1152]{1,0:T(8,128)S(1)} %bitcast_add_fusion.15), channel_id=1, source_target_pairs={{0,2},{2,6},{6,10},{10,14},{14,12},{12,8},{8,4},{4,0},{1,3},{3,7},... | collective-permute-start | bytes 442376 | tf_op jit(solution)/shard_map/ppermute | solution.py:85
  148.3 5.4 %collective-permute-start.27 = (f32[32,1152]{1,0:T(8,128)S(1)}, f32[32,1152]{1,0:T(8,128)S(1)}, u32[]{:S(2)}, u32[]{:S(2)}) collective-permute-start(f32[32,1152]{1,0:T(8,128)S(1)} %bitcast_add_fusion.7), channel_id=1, source_target_pairs={{2,0},{6,2},{10,6},{14,10},{12,14},{8,12},{4,8},{0,4},{3,1},{7,3},... | collective-permute-start | bytes 442376 | tf_op jit(solution)/shard_map/ppermute | solution.py:85
  149.0 5.4 %collective-permute-start.13 = (f32[32,1152]{1,0:T(8,128)S(1)}, f32[32,1152]{1,0:T(8,128)S(1)}, u32[]{:S(2)}, u32[]{:S(2)}) collective-permute-start(f32[32,1152]{1,0:T(8,128)S(1)} %bitcast_add_fusion.14), channel_id=1, source_target_pairs={{0,2},{2,6},{6,10},{10,14},{14,12},{12,8},{8,4},{4,0},{1,3},{3,7},... | collective-permute-start | bytes 442376 | tf_op jit(solution)/shard_map/ppermute | solution.py:85
  153.8 5.2 %collective-permute-start.28 = (f32[32,1152]{1,0:T(8,128)S(1)}, f32[32,1152]{1,0:T(8,128)S(1)}, u32[]{:S(2)}, u32[]{:S(2)}) collective-permute-start(f32[32,1152]{1,0:T(8,128)S(1)} %bitcast_add_fusion.6), channel_id=1, source_target_pairs={{2,0},{6,2},{10,6},{14,10},{12,14},{8,12},{4,8},{0,4},{3,1},{7,3},... | collective-permute-start | bytes 442376 | tf_op jit(solution)/shard_map/ppermute | solution.py:85
  154.4 5.2 %collective-permute-start.14 = (f32[32,1152]{1,0:T(8,128)S(1)}, f32[32,1152]{1,0:T(8,128)S(1)}, u32[]{:S(2)}, u32[]{:S(2)}) collective-permute-start(f32[32,1152]{1,0:T(8,128)S(1)} %bitcast_add_fusion.13), channel_id=1, source_target_pairs={{0,2},{2,6},{6,10},{10,14},{14,12},{12,8},{8,4},{4,0},{1,3},{3,7},... | collective-permute-start | bytes 442376 | tf_op jit(solution)/shard_map/ppermute | solution.py:85
  159.0 9.3 %collective-permute-start.29 = (bf16[32,1152]{1,0:T(8,128)(2,1)S(1)}, bf16[32,1152]{1,0:T(8,128)(2,1)S(1)}, u32[]{:S(2)}, u32[]{:S(2)}) collective-permute-start(bf16[32,1152]{1,0:T(8,128)(2,1)S(1)} %get-tuple-element.29), channel_id=1, source_target_pairs={{2,0},{6,2},{10,6},{14,10},{12,14},{8,12},{4,8},{0,4},{3,1},{7,3},... | collective-permute-start | bytes 221192 | tf_op jit(solution)/shard_map/ppermute | solution.py:91
  159.7 9.6 %collective-permute-start.15 = (bf16[32,1152]{1,0:T(8,128)(2,1)S(1)}, bf16[32,1152]{1,0:T(8,128)(2,1)S(1)}, u32[]{:S(2)}, u32[]{:S(2)}) collective-permute-start(bf16[32,1152]{1,0:T(8,128)(2,1)S(1)} %get-tuple-element.27), channel_id=1, source_target_pairs={{0,2},{2,6},{6,10},{10,14},{14,12},{12,8},{8,4},{4,0},{1,3},{3,7},... | collective-permute-start | bytes 221192 | tf_op jit(solution)/shard_map/ppermute | solution.py:91
  161.9 21.4 %collective-permute-start.7 = (bf16[1024,1,128]{0,2,1:T(8,128)(2,1)S(1)}, bf16[1024,1,128]{0,2,1:T(8,128)(2,1)S(1)}, u32[]{:S(2)}, u32[]{:S(2)}) collective-permute-start(bf16[1024,1,128]{0,2,1:T(8,128)(2,1)S(1)} %get-tuple-element.44), channel_id=1, source_target_pairs={{2,0},{4,2},{6,4},{8,6},{10,8},{12,10},{14,12},{3,1},{5,3},{7,5},{... | collective-permute-start | bytes 786440 | tf_op jit(solution)/shard_map/ppermute | solution.py:20
  163.2 20.1 %collective-permute-start.6 = (bf16[1024,1,128]{0,2,1:T(8,128)(2,1)S(1)}, bf16[1024,1,128]{0,2,1:T(8,128)(2,1)S(1)}, u32[]{:S(2)}, u32[]{:S(2)}) collective-permute-start(bf16[1024,1,128]{0,2,1:T(8,128)(2,1)S(1)} %get-tuple-element.45), channel_id=1, source_target_pairs={{0,2},{2,4},{4,6},{6,8},{8,10},{10,12},{12,14},{1,3},{3,5},{5,7},{... | collective-permute-start | bytes 786440 | tf_op jit(solution)/shard_map/ppermute | solution.py:19
  168.3 5.1 %collective-permute-start.30 = (bf16[32,1152]{1,0:T(8,128)(2,1)S(1)}, bf16[32,1152]{1,0:T(8,128)(2,1)S(1)}, u32[]{:S(2)}, u32[]{:S(2)}) collective-permute-start(bf16[32,1152]{1,0:T(8,128)(2,1)S(1)} %collective-permute-done.29), channel_id=1, source_target_pairs={{2,0},{6,2},{10,6},{14,10},{12,14},{8,12},{4,8},{0,4},{3,1},{7,3},... | collective-permute-start | bytes 221192 | tf_op jit(solution)/shard_map/ppermute | solution.py:91
  169.3 7.2 %collective-permute-start.16 = (bf16[32,1152]{1,0:T(8,128)(2,1)S(1)}, bf16[32,1152]{1,0:T(8,128)(2,1)S(1)}, u32[]{:S(2)}, u32[]{:S(2)}) collective-permute-start(bf16[32,1152]{1,0:T(8,128)(2,1)S(1)} %collective-permute-done.15), channel_id=1, source_target_pairs={{0,2},{2,6},{6,10},{10,14},{14,12},{12,8},{8,4},{4,0},{1,3},{3,7},... | collective-permute-start | bytes 221192 | tf_op jit(solution)/shard_map/ppermute | solution.py:91
  173.4 5.5 %collective-permute-start.31 = (bf16[32,1152]{1,0:T(8,128)(2,1)S(1)}, bf16[32,1152]{1,0:T(8,128)(2,1)S(1)}, u32[]{:S(2)}, u32[]{:S(2)}) collective-permute-start(bf16[32,1152]{1,0:T(8,128)(2,1)S(1)} %collective-permute-done.30), channel_id=1, source_target_pairs={{2,0},{6,2},{10,6},{14,10},{12,14},{8,12},{4,8},{0,4},{3,1},{7,3},... | collective-permute-start | bytes 221192 | tf_op jit(solution)/shard_map/ppermute | solution.py:91
  179.0 11.2 %collective-permute-start.32 = (bf16[32,1152]{1,0:T(8,128)(2,1)S(1)}, bf16[32,1152]{1,0:T(8,128)(2,1)S(1)}, u32[]{:S(2)}, u32[]{:S(2)}) collective-permute-start(bf16[32,1152]{1,0:T(8,128)(2,1)S(1)} %collective-permute-done.31), channel_id=1, source_target_pairs={{2,0},{6,2},{10,6},{14,10},{12,14},{8,12},{4,8},{0,4},{3,1},{7,3},... | collective-permute-start | bytes 221192 | tf_op jit(solution)/shard_map/ppermute | solution.py:91
  180.9 9.2 %collective-permute-start.18 = (bf16[32,1152]{1,0:T(8,128)(2,1)S(1)}, bf16[32,1152]{1,0:T(8,128)(2,1)S(1)}, u32[]{:S(2)}, u32[]{:S(2)}) collective-permute-start(bf16[32,1152]{1,0:T(8,128)(2,1)S(1)} %collective-permute-done.17), channel_id=1, source_target_pairs={{0,2},{2,6},{6,10},{10,14},{14,12},{12,8},{8,4},{4,0},{1,3},{3,7},... | collective-permute-start | bytes 221192 | tf_op jit(solution)/shard_map/ppermute | solution.py:91
  190.1 5.0 %collective-permute-start.19 = (bf16[32,1152]{1,0:T(8,128)(2,1)S(1)}, bf16[32,1152]{1,0:T(8,128)(2,1)S(1)}, u32[]{:S(2)}, u32[]{:S(2)}) collective-permute-start(bf16[32,1152]{1,0:T(8,128)(2,1)S(1)} %collective-permute-done.18), channel_id=1, source_target_pairs={{0,2},{2,6},{6,10},{10,14},{14,12},{12,8},{8,4},{4,0},{1,3},{3,7},... | collective-permute-start | bytes 221192 | tf_op jit(solution)/shard_map/ppermute | solution.py:91
  199.5 4.8 %collective-permute-start.21 = (bf16[32,1152]{1,0:T(8,128)(2,1)S(1)}, bf16[32,1152]{1,0:T(8,128)(2,1)S(1)}, u32[]{:S(2)}, u32[]{:S(2)}) collective-permute-start(bf16[32,1152]{1,0:T(8,128)(2,1)S(1)} %collective-permute-done.20), channel_id=1, source_target_pairs={{0,2},{2,6},{6,10},{10,14},{14,12},{12,8},{8,4},{4,0},{1,3},{3,7},... | collective-permute-start | bytes 221192 | tf_op jit(solution)/shard_map/ppermute | solution.py:91
  (16 other events, 122.6 us)
Sparse Core Ops, SparseCore 0:
  10.0 74.9 all-gather.1
  93.5 7.7 reduce-scatter.1

commit v6 on v5

--- a/solution.py
+++ b/solution.py
@@ -139,15 +139,12 @@
             shares, squares, (((1,), (1,)), ((), ())), preferred_element_type=jnp.float32
         )
         beta_terms = jnp.sum(shares.astype(jnp.float32), axis=1)
-        joined = jnp.concatenate(
-            [gamma_terms, jnp.broadcast_to(beta_terms[:, None], (lat_local, 128))], 1
-        )
+        beta_wide = jnp.broadcast_to(beta_terms[None, :], (32, lat_local))
+        beta_total = lax.psum(beta_wide, "row")[0]
         if len(ring) <= 16:
-            (joined_total,) = ring_sum([joined], ring)
+            (gamma_total,) = ring_sum([gamma_terms], ring)
         else:
-            joined_total = lax.psum(joined, "row")
-        gamma_total = joined_total[:, : gamma_terms.shape[1]]
-        beta_total = joined_total[:, gamma_terms.shape[1]]
+            gamma_total = lax.psum(gamma_terms, "row")
         scale_factor = 1.0 / math.sqrt(pixels * lax.axis_size("row"))
         grad_gamma = gamma_total * scale_factor
         grad_beta = beta_total * scale_factor

time: 215 us -> 253 us (1.18)
  waiting for transfers between devices: 99.2 us -> 125 us
  local copies, waits for them, and re-layouts: 13 us -> 18.7 us
  other arithmetic: 12.1 us -> 14.9 us
    psum x0 -> x1, waiting for transfers between devices: none -> 32 us  [per_device(): beta_total = lax.psum(beta_wide, 'row')[0]]
    ppermute x14, waiting for transfers between devices: 13.7 us -> 8.12 us  [ring_sum(): gathered[part].append(lax.ppermute(gathered[part][-1], 'row', moves[part]))]
    unnamed x51 -> x75, local copies, waits for them, and re-layouts: 5.53 us -> 10.9 us
    reduce_scatter x1, waiting for transfers between devices: 0.02 us -> 4.05 us  [per_device(): lax.psum_scatter(partial_value, 'chan', scatter_dimension=0, tiled=True)]
    all_gather x1, waiting for transfers between devices: 59.7 us -> 56.3 us  [per_device(): shard_piece = lax.all_gather(conv_weight, 'row', axis=0, tiled=True)]
  transfers between devices with their start and end apart: 38 -> 39, of which waited for: 15 -> 18; matrix products, arithmetic and copies ran while one was open for 15% -> 17% of each run, Pallas kernels for 0% -> 0%
where the time goes in v6:
time: 253 us; the launch traced here: 252 us
  waiting for transfers between devices  125 us (49%)
  starting transfers between devices  45.7 us (18%)
  between operations  25.3 us (10%)
  matrix products  22.1 us (9%)
  local copies, waits for them, and re-layouts  18.7 us (7%)
  other arithmetic  14.9 us (6%)
    all_gather x1, waiting for transfers between devices, per_device(): shard_piece = lax.all_gather(conv_weight, 'row', axis=0, tiled=True)  56.3 us
    psum x1, waiting for transfers between devices, per_device(): beta_total = lax.psum(beta_wide, 'row')[0]  32 us
    ppermute x14, waiting for transfers between devices, ring_sum(): got = lax.ppermute(carry[part], 'row', moves[part])  19.9 us
    ppermute x14, starting transfers between devices, ring_sum(): gathered[part].append(lax.ppermute(gathered[part][-1], 'row', moves[part]))  18.4 us
    ppermute x14, starting transfers between devices, ring_sum(): got = lax.ppermute(carry[part], 'row', moves[part])  14.6 us
    unnamed x75, local copies, waits for them, and re-layouts  10.9 us
    ppermute x2, starting transfers between devices, extended(): before = lax.ppermute(last, axis, up)  9.44 us
    dot_general x9, matrix products, per_device(): jnp.dot(shard_piece[:, tap_index, :], window, preferred_element_type=jnp....  8.39 us
  transfers between devices with their start and end apart: 39, of which 18 were waited for; matrix products, arithmetic and copies ran while one was open for 17% of the time, Pallas kernels for 0%

profile of v6, /device:TPU:0, one launch (start us, length us, event | category | flops | bytes accessed | tf_op | source)
XLA Modules:
  0.0 251.9 jit_solution(8465417475353522214)
XLA Ops:
  9.2 4.9 %collective-permute-start = (bf16[212,1,128]{2,1,0:T(2,128)(2,1)S(1)}, bf16[212,1,128]{2,1,0:T(2,128)(2,1)S(1)}, u32[]{:S(2)}, u32[]{:S(2)}) collective-permute-start(bf16[212,1,128]{2,1,0:T(2,128)(2,1)S(1)} %get-tuple-element.52), channel_id=1, source_target_pairs={{0,2},{2,4},{4,6},{6,8},{8,10},{10,12},{12,14},{1,3},{3,5},{5,7},{... | collective-permute-start | bytes 162824 | tf_op jit(solution)/shard_map/ppermute | solution.py:19
  16.5 4.2 %collective-permute-done.1 = bf16[212,1,128]{2,1,0:T(2,128)(2,1)S(1)} collective-permute-done((bf16[212,1,128]{2,1,0:T(2,128)(2,1)S(1)}, bf16[212,1,128]{2,1,0:T(2,128)(2,1)S(1)}, u32[]{:S(2)}, u32[]{:S(2)}) %collective-permute-start.1) | collective-permute-done | bytes 54304 | tf_op jit(solution)/shard_map/ppermute | solution.py:20
  28.6 56.3 %all-gather.2.cloned.1.call-done = bf16[1024,9,212]{0,2,1:T(8,128)(2,1)} async-done(((bf16[128,9,212]{0,2,1:T(8,128)(2,1)}), bf16[1024,9,212]{0,2,1:T(8,128)(2,1)}) %all-gather.2.cloned.1.call-update) | async-done | bytes 3907600 | tf_op jit(solution)/shard_map/all_gather | solution.py:112
  91.1 2.4 bitcast_add_fusion
  97.5 4.1 %reduce-scatter.2.cloned.1.call-done = f32[512,512]{0,1:T(8,128)} async-done(((f32[1024,512]{0,1:T(8,128)}), f32[512,512]{0,1:T(8,128)}) %reduce-scatter.2.cloned.1.call-update) | async-done | bytes 1048592 | tf_op jit(solution)/shard_map/reduce_scatter | solution.py:121
  106.1 3.4 %convert_reduce_fusion = (f32[512]{0:T(512)S(1)}, bf16[512,512]{0,1:T(8,128)(2,1)S(1)}, f32[512,512]{0,1:T(8,128)}, bf16[512,512]{0,1:T(8,128)(2,1)}) fusion(f32[512,512]{0,1:T(8,128)S(1)} %copy-done.2, f32[512,4,128]{0,2,1:T(8,128)S(1)} %copy.11, bf16[1024,512]{0,1:T(8,128)(2,1)S(1)} %fusion.26, bf16[512,1024]{1,0:T(8,128)(2,1)} %param.14, ...), kind=kOutput, calls=%fused_computation.60 | convolution fusion | flops 540016128 | bytes 6295552 | tf_op jit(solution)/shard_map/dot_general | solution.py:124
  111.2 1.9 collective-permute-start.22
  124.6 2.1 copy.12
  128.3 1.8 collective-permute-start.23
  130.1 3.3 %collective-permute-done.8 = f32[32,1024]{1,0:T(8,128)S(1)} collective-permute-done((f32[32,1024]{1,0:T(8,128)}, f32[32,1024]{1,0:T(8,128)S(1)}, u32[]{:S(2)}, u32[]{:S(2)}) %collective-permute-start.8) | collective-permute-done | bytes 131104 | tf_op jit(solution)/shard_map/ppermute | solution.py:85
  134.0 1.8 collective-permute-start.24
  135.8 2.9 %collective-permute-done.9 = f32[32,1024]{1,0:T(8,128)S(1)} collective-permute-done((f32[32,1024]{1,0:T(8,128)S(1)}, f32[32,1024]{1,0:T(8,128)S(1)}, u32[]{:S(2)}, u32[]{:S(2)}) %collective-permute-start.9) | collective-permute-done | bytes 131104 | tf_op jit(solution)/shard_map/ppermute | solution.py:85
  139.2 1.7 collective-permute-start.25
  140.9 3.1 %collective-permute-done.10 = f32[32,1024]{1,0:T(8,128)S(1)} collective-permute-done((f32[32,1024]{1,0:T(8,128)S(1)}, f32[32,1024]{1,0:T(8,128)S(1)}, u32[]{:S(2)}, u32[]{:S(2)}) %collective-permute-start.10) | collective-permute-done | bytes 131104 | tf_op jit(solution)/shard_map/ppermute | solution.py:85
  144.1 4.0 %fusion.10 = bf16[512,512]{0,1:T(8,128)(2,1)} fusion(f32[512,512]{0,1:T(8,128)S(1)} %copy-done.7, s32[]{:T(128)S(6)} %select_n.194, bf16[512,512]{1,0:T(8,128)(2,1)S(1)} %copy-done.18, bf16[512,512]{1,0:T(8,128)(2,1)} %collective-permute-done.3, bf16[512,512]{0,1:T(8,128)(2,1)S(1)} %copy-done.6, bf16[512,512]{0,1:T(8,128)(2,1)} %collective-permute-done.4, ...), kind=kOutput, calls=%fused_computation.41 | convolution fusion | flops 546308096 | bytes 4719616 | tf_op jit(solution)/shard_map/dot_general | solution.py:134
  148.1 2.1 collective-permute-start.26
  150.3 4.1 %collective-permute-done.26 = f32[32,1024]{1,0:T(8,128)S(1)} collective-permute-done((f32[32,1024]{1,0:T(8,128)S(1)}, f32[32,1024]{1,0:T(8,128)S(1)}, u32[]{:S(2)}, u32[]{:S(2)}) %collective-permute-start.26) | collective-permute-done | bytes 131104 | tf_op jit(solution)/shard_map/ppermute | solution.py:85
  154.5 1.8 collective-permute-start.27
  156.6 3.2 %collective-permute-done.27 = f32[32,1024]{1,0:T(8,128)S(1)} collective-permute-done((f32[32,1024]{1,0:T(8,128)S(1)}, f32[32,1024]{1,0:T(8,128)S(1)}, u32[]{:S(2)}, u32[]{:S(2)}) %collective-permute-start.27) | collective-permute-done | bytes 131104 | tf_op jit(solution)/shard_map/ppermute | solution.py:85
  162.0 2.9 %collective-permute-done.28 = f32[32,1024]{1,0:T(8,128)S(1)} collective-permute-done((f32[32,1024]{1,0:T(8,128)S(1)}, f32[32,1024]{1,0:T(8,128)S(1)}, u32[]{:S(2)}, u32[]{:S(2)}) %collective-permute-start.28) | collective-permute-done | bytes 131104 | tf_op jit(solution)/shard_map/ppermute | solution.py:85
  164.9 1.6 collective-permute-start.29
  167.0 32.0 %all-reduce.4.cloned.1.call-done = f32[32,512]{1,0:T(8,128)} async-done(((f32[32,512]{1,0:T(8,128)}), f32[32,512]{1,0:T(8,128)}) %all-reduce.4.cloned.1.call-update) | async-done | bytes 65552 | tf_op jit(solution)/shard_map/psum | solution.py:143
  200.3 1.7 collective-permute-start.30
  202.4 2.0 fusion.14
  205.8 4.6 %collective-permute-start.6 = (bf16[1024,1,128]{0,2,1:T(8,128)(2,1)S(1)}, bf16[1024,1,128]{0,2,1:T(8,128)(2,1)S(1)}, u32[]{:S(2)}, u32[]{:S(2)}) collective-permute-start(bf16[1024,1,128]{0,2,1:T(8,128)(2,1)S(1)} %get-tuple-element.41), channel_id=1, source_target_pairs={{0,2},{2,4},{4,6},{6,8},{8,10},{10,12},{12,14},{1,3},{3,5},{5,7},{... | collective-permute-start | bytes 786440 | tf_op jit(solution)/shard_map/ppermute | solution.py:19
  211.9 1.8 collective-permute-start.31
  214.4 2.6 %collective-permute-done.31 = bf16[32,1024]{1,0:T(8,128)(2,1)S(1)} collective-permute-done((bf16[32,1024]{1,0:T(8,128)(2,1)S(1)}, bf16[32,1024]{1,0:T(8,128)(2,1)S(1)}, u32[]{:S(2)}, u32[]{:S(2)}) %collective-permute-start.31) | collective-permute-done | bytes 65568 | tf_op jit(solution)/shard_map/ppermute | solution.py:91
  218.9 2.5 collective-permute-start.18
  223.2 2.4 collective-permute-start.19
  227.7 2.4 collective-permute-start.20
  238.1 2.1 collective-permute-start.21
  240.2 2.2 collective-permute-done.35
  (192 shorter events, 57.0 us)
Async XLA Ops:
  7.2 77.8 %all-gather.2.cloned.1.call-start = ((), (), s32[]{:S(2)}) async-start(), calls=%async_computation.1 | async-start | bytes 4478976 | tf_op jit(solution)/shard_map/all_gather | solution.py:112
  7.9 93.6 %reduce-scatter.2.cloned.1.call-start = ((), (), s32[]{:S(2)}) async-start(), calls=%async_computation.2 | async-start | bytes 3145728 | tf_op jit(solution)/shard_map/reduce_scatter | solution.py:121
  9.2 7.3 %collective-permute-start = (bf16[212,1,128]{2,1,0:T(2,128)(2,1)S(1)}, bf16[212,1,128]{2,1,0:T(2,128)(2,1)S(1)}, u32[]{:S(2)}, u32[]{:S(2)}) collective-permute-start(bf16[212,1,128]{2,1,0:T(2,128)(2,1)S(1)} %get-tuple-element.52), channel_id=1, source_target_pairs={{0,2},{2,4},{4,6},{6,8},{8,10},{10,12},{12,14},{1,3},{3,5},{5,7},{... | collective-permute-start | bytes 162824 | tf_op jit(solution)/shard_map/ppermute | solution.py:19
  14.1 6.6 %collective-permute-start.1 = (bf16[212,1,128]{2,1,0:T(2,128)(2,1)S(1)}, bf16[212,1,128]{2,1,0:T(2,128)(2,1)S(1)}, u32[]{:S(2)}, u32[]{:S(2)}) collective-permute-start(bf16[212,1,128]{2,1,0:T(2,128)(2,1)S(1)} %get-tuple-element.53), channel_id=1, source_target_pairs={{2,0},{4,2},{6,4},{8,6},{10,8},{12,10},{14,12},{3,1},{5,3},{7,5},{... | collective-permute-start | bytes 162824 | tf_op jit(solution)/shard_map/ppermute | solution.py:20
  93.6 105.5 %all-reduce.4.cloned.1.call-start = ((), (), s32[]{:S(2)}) async-start(), calls=%async_computation.3 | async-start | bytes 131072 | tf_op jit(solution)/shard_map/psum | solution.py:143
  95.8 48.2 %collective-permute-start.3 = (bf16[512,512]{1,0:T(8,128)(2,1)}, bf16[512,512]{1,0:T(8,128)(2,1)}, u32[]{:S(2)}, u32[]{:S(2)}) collective-permute-start(bf16[512,512]{1,0:T(8,128)(2,1)} %get-tuple-element.42), channel_id=1, source_target_pairs={{0,1},{1,0},{2,3},{3,2},{4,5},{5,4},{6,7},{7,6},{8,9},{9,8},{10,11... | collective-permute-start | bytes 1572872 | tf_op jit(solution)/shard_map/ppermute | solution.py:132
  111.2 17.1 %collective-permute-start.22 = (f32[32,1024]{1,0:T(8,128)S(1)}, f32[32,1024]{1,0:T(8,128)S(1)}, u32[]{:S(2)}, u32[]{:S(2)}) collective-permute-start(f32[32,1024]{1,0:T(8,128)S(1)} %select_bitcast_fusion), channel_id=1, source_target_pairs={{2,0},{6,2},{10,6},{14,10},{12,14},{8,12},{4,8},{0,4},{3,1},{7,3},... | collective-permute-start | bytes 393224 | tf_op jit(solution)/shard_map/ppermute | solution.py:85
  124.4 19.6 %collective-permute-start.4 = (bf16[512,512]{0,1:T(8,128)(2,1)}, bf16[512,512]{0,1:T(8,128)(2,1)}, u32[]{:S(2)}, u32[]{:S(2)}) collective-permute-start(bf16[512,512]{0,1:T(8,128)(2,1)} %copy-done.5), channel_id=1, source_target_pairs={{0,1},{1,0},{2,3},{3,2},{4,5},{5,4},{6,7},{7,6},{8,9},{9,8},{10,11... | collective-permute-start | bytes 1572872 | tf_op jit(solution)/shard_map/ppermute | solution.py:26
  127.3 6.1 %collective-permute-start.8 = (f32[32,1024]{1,0:T(8,128)}, f32[32,1024]{1,0:T(8,128)S(1)}, u32[]{:S(2)}, u32[]{:S(2)}) collective-permute-start(f32[32,1024]{1,0:T(8,128)} %select_bitcast_fusion.1), channel_id=1, source_target_pairs={{0,2},{2,6},{6,10},{10,14},{14,12},{12,8},{8,4},{4,0},{1,3},{3,7},... | collective-permute-start | bytes 393224 | tf_op jit(solution)/shard_map/ppermute | solution.py:85
  128.3 5.6 %collective-permute-start.23 = (f32[32,1024]{1,0:T(8,128)S(1)}, f32[32,1024]{1,0:T(8,128)S(1)}, u32[]{:S(2)}, u32[]{:S(2)}) collective-permute-start(f32[32,1024]{1,0:T(8,128)S(1)} %bitcast_add_fusion.11), channel_id=1, source_target_pairs={{2,0},{6,2},{10,6},{14,10},{12,14},{8,12},{4,8},{0,4},{3,1},{7,3},... | collective-permute-start | bytes 393224 | tf_op jit(solution)/shard_map/ppermute | solution.py:85
  133.4 5.3 %collective-permute-start.9 = (f32[32,1024]{1,0:T(8,128)S(1)}, f32[32,1024]{1,0:T(8,128)S(1)}, u32[]{:S(2)}, u32[]{:S(2)}) collective-permute-start(f32[32,1024]{1,0:T(8,128)S(1)} %bitcast_add_fusion.18), channel_id=1, source_target_pairs={{0,2},{2,6},{6,10},{10,14},{14,12},{12,8},{8,4},{4,0},{1,3},{3,7},... | collective-permute-start | bytes 393224 | tf_op jit(solution)/shard_map/ppermute | solution.py:85
  134.0 5.1 %collective-permute-start.24 = (f32[32,1024]{1,0:T(8,128)S(1)}, f32[32,1024]{1,0:T(8,128)S(1)}, u32[]{:S(2)}, u32[]{:S(2)}) collective-permute-start(f32[32,1024]{1,0:T(8,128)S(1)} %bitcast_add_fusion.10), channel_id=1, source_target_pairs={{2,0},{6,2},{10,6},{14,10},{12,14},{8,12},{4,8},{0,4},{3,1},{7,3},... | collective-permute-start | bytes 393224 | tf_op jit(solution)/shard_map/ppermute | solution.py:85
  138.7 5.2 %collective-permute-start.10 = (f32[32,1024]{1,0:T(8,128)S(1)}, f32[32,1024]{1,0:T(8,128)S(1)}, u32[]{:S(2)}, u32[]{:S(2)}) collective-permute-start(f32[32,1024]{1,0:T(8,128)S(1)} %bitcast_add_fusion.17), channel_id=1, source_target_pairs={{0,2},{2,6},{6,10},{10,14},{14,12},{12,8},{8,4},{4,0},{1,3},{3,7},... | collective-permute-start | bytes 393224 | tf_op jit(solution)/shard_map/ppermute | solution.py:85
  139.2 8.9 %collective-permute-start.25 = (f32[32,1024]{1,0:T(8,128)S(1)}, f32[32,1024]{1,0:T(8,128)S(1)}, u32[]{:S(2)}, u32[]{:S(2)}) collective-permute-start(f32[32,1024]{1,0:T(8,128)S(1)} %bitcast_add_fusion.9), channel_id=1, source_target_pairs={{2,0},{6,2},{10,6},{14,10},{12,14},{8,12},{4,8},{0,4},{3,1},{7,3},... | collective-permute-start | bytes 393224 | tf_op jit(solution)/shard_map/ppermute | solution.py:85
  143.9 6.2 %collective-permute-start.11 = (f32[32,1024]{1,0:T(8,128)S(1)}, f32[32,1024]{1,0:T(8,128)S(1)}, u32[]{:S(2)}, u32[]{:S(2)}) collective-permute-start(f32[32,1024]{1,0:T(8,128)S(1)} %bitcast_add_fusion.16), channel_id=1, source_target_pairs={{0,2},{2,6},{6,10},{10,14},{14,12},{12,8},{8,4},{4,0},{1,3},{3,7},... | collective-permute-start | bytes 393224 | tf_op jit(solution)/shard_map/ppermute | solution.py:85
  148.1 54.3 %collective-permute-start.5 = (bf16[512,4,128]{0,2,1:T(8,128)(2,1)}, bf16[512,4,128]{0,2,1:T(8,128)(2,1)}, u32[]{:S(2)}, u32[]{:S(2)}) collective-permute-start(bf16[512,4,128]{0,2,1:T(8,128)(2,1)} %bitcast.17), channel_id=1, source_target_pairs={{0,1},{1,0},{2,3},{3,2},{4,5},{5,4},{6,7},{7,6},{8,9},{9,8},{10,11... | collective-permute-start | bytes 1572872 | tf_op jit(solution)/shard_map/ppermute | solution.py:26
  148.1 6.3 %collective-permute-start.26 = (f32[32,1024]{1,0:T(8,128)S(1)}, f32[32,1024]{1,0:T(8,128)S(1)}, u32[]{:S(2)}, u32[]{:S(2)}) collective-permute-start(f32[32,1024]{1,0:T(8,128)S(1)} %bitcast_add_fusion.8), channel_id=1, source_target_pairs={{2,0},{6,2},{10,6},{14,10},{12,14},{8,12},{4,8},{0,4},{3,1},{7,3},... | collective-permute-start | bytes 393224 | tf_op jit(solution)/shard_map/ppermute | solution.py:85
  150.2 6.0 %collective-permute-start.12 = (f32[32,1024]{1,0:T(8,128)S(1)}, f32[32,1024]{1,0:T(8,128)S(1)}, u32[]{:S(2)}, u32[]{:S(2)}) collective-permute-start(f32[32,1024]{1,0:T(8,128)S(1)} %bitcast_add_fusion.15), channel_id=1, source_target_pairs={{0,2},{2,6},{6,10},{10,14},{14,12},{12,8},{8,4},{4,0},{1,3},{3,7},... | collective-permute-start | bytes 393224 | tf_op jit(solution)/shard_map/ppermute | solution.py:85
  154.5 5.4 %collective-permute-start.27 = (f32[32,1024]{1,0:T(8,128)S(1)}, f32[32,1024]{1,0:T(8,128)S(1)}, u32[]{:S(2)}, u32[]{:S(2)}) collective-permute-start(f32[32,1024]{1,0:T(8,128)S(1)} %bitcast_add_fusion.7), channel_id=1, source_target_pairs={{2,0},{6,2},{10,6},{14,10},{12,14},{8,12},{4,8},{0,4},{3,1},{7,3},... | collective-permute-start | bytes 393224 | tf_op jit(solution)/shard_map/ppermute | solution.py:85
  156.3 5.2 %collective-permute-start.13 = (f32[32,1024]{1,0:T(8,128)S(1)}, f32[32,1024]{1,0:T(8,128)S(1)}, u32[]{:S(2)}, u32[]{:S(2)}) collective-permute-start(f32[32,1024]{1,0:T(8,128)S(1)} %bitcast_add_fusion.14), channel_id=1, source_target_pairs={{0,2},{2,6},{6,10},{10,14},{14,12},{12,8},{8,4},{4,0},{1,3},{3,7},... | collective-permute-start | bytes 393224 | tf_op jit(solution)/shard_map/ppermute | solution.py:85
  159.8 5.0 %collective-permute-start.28 = (f32[32,1024]{1,0:T(8,128)S(1)}, f32[32,1024]{1,0:T(8,128)S(1)}, u32[]{:S(2)}, u32[]{:S(2)}) collective-permute-start(f32[32,1024]{1,0:T(8,128)S(1)} %bitcast_add_fusion.6), channel_id=1, source_target_pairs={{2,0},{6,2},{10,6},{14,10},{12,14},{8,12},{4,8},{0,4},{3,1},{7,3},... | collective-permute-start | bytes 393224 | tf_op jit(solution)/shard_map/ppermute | solution.py:85
  161.5 5.0 %collective-permute-start.14 = (f32[32,1024]{1,0:T(8,128)S(1)}, f32[32,1024]{1,0:T(8,128)S(1)}, u32[]{:S(2)}, u32[]{:S(2)}) collective-permute-start(f32[32,1024]{1,0:T(8,128)S(1)} %bitcast_add_fusion.13), channel_id=1, source_target_pairs={{0,2},{2,6},{6,10},{10,14},{14,12},{12,8},{8,4},{4,0},{1,3},{3,7},... | collective-permute-start | bytes 393224 | tf_op jit(solution)/shard_map/ppermute | solution.py:85
  164.9 35.4 %collective-permute-start.29 = (bf16[32,1024]{1,0:T(8,128)(2,1)S(1)}, bf16[32,1024]{1,0:T(8,128)(2,1)S(1)}, u32[]{:S(2)}, u32[]{:S(2)}) collective-permute-start(bf16[32,1024]{1,0:T(8,128)(2,1)S(1)} %get-tuple-element.27), channel_id=1, source_target_pairs={{2,0},{6,2},{10,6},{14,10},{12,14},{8,12},{4,8},{0,4},{3,1},{7,3},... | collective-permute-start | bytes 196616 | tf_op jit(solution)/shard_map/ppermute | solution.py:91
  166.6 35.5 %collective-permute-start.15 = (bf16[32,1024]{1,0:T(8,128)(2,1)S(1)}, bf16[32,1024]{1,0:T(8,128)(2,1)S(1)}, u32[]{:S(2)}, u32[]{:S(2)}) collective-permute-start(bf16[32,1024]{1,0:T(8,128)(2,1)S(1)} %get-tuple-element.25), channel_id=1, source_target_pairs={{0,2},{2,6},{6,10},{10,14},{14,12},{12,8},{8,4},{4,0},{1,3},{3,7},... | collective-permute-start | bytes 196616 | tf_op jit(solution)/shard_map/ppermute | solution.py:91
  200.3 11.5 %collective-permute-start.30 = (bf16[32,1024]{1,0:T(8,128)(2,1)S(1)}, bf16[32,1024]{1,0:T(8,128)(2,1)S(1)}, u32[]{:S(2)}, u32[]{:S(2)}) collective-permute-start(bf16[32,1024]{1,0:T(8,128)(2,1)S(1)} %collective-permute-done.29), channel_id=1, source_target_pairs={{2,0},{6,2},{10,6},{14,10},{12,14},{8,12},{4,8},{0,4},{3,1},{7,3},... | collective-permute-start | bytes 196616 | tf_op jit(solution)/shard_map/ppermute | solution.py:91
  202.0 11.6 %collective-permute-start.16 = (bf16[32,1024]{1,0:T(8,128)(2,1)S(1)}, bf16[32,1024]{1,0:T(8,128)(2,1)S(1)}, u32[]{:S(2)}, u32[]{:S(2)}) collective-permute-start(bf16[32,1024]{1,0:T(8,128)(2,1)S(1)} %collective-permute-done.15), channel_id=1, source_target_pairs={{0,2},{2,6},{6,10},{10,14},{14,12},{12,8},{8,4},{4,0},{1,3},{3,7},... | collective-permute-start | bytes 196616 | tf_op jit(solution)/shard_map/ppermute | solution.py:91
  204.5 25.6 %collective-permute-start.7 = (bf16[1024,1,128]{0,2,1:T(8,128)(2,1)S(1)}, bf16[1024,1,128]{0,2,1:T(8,128)(2,1)S(1)}, u32[]{:S(2)}, u32[]{:S(2)}) collective-permute-start(bf16[1024,1,128]{0,2,1:T(8,128)(2,1)S(1)} %get-tuple-element.40), channel_id=1, source_target_pairs={{2,0},{4,2},{6,4},{8,6},{10,8},{12,10},{14,12},{3,1},{5,3},{7,5},{... | collective-permute-start | bytes 786440 | tf_op jit(solution)/shard_map/ppermute | solution.py:20
  205.8 24.3 %collective-permute-start.6 = (bf16[1024,1,128]{0,2,1:T(8,128)(2,1)S(1)}, bf16[1024,1,128]{0,2,1:T(8,128)(2,1)S(1)}, u32[]{:S(2)}, u32[]{:S(2)}) collective-permute-start(bf16[1024,1,128]{0,2,1:T(8,128)(2,1)S(1)} %get-tuple-element.41), channel_id=1, source_target_pairs={{0,2},{2,4},{4,6},{6,8},{8,10},{10,12},{12,14},{1,3},{3,5},{5,7},{... | collective-permute-start | bytes 786440 | tf_op jit(solution)/shard_map/ppermute | solution.py:19
  211.9 5.1 %collective-permute-start.31 = (bf16[32,1024]{1,0:T(8,128)(2,1)S(1)}, bf16[32,1024]{1,0:T(8,128)(2,1)S(1)}, u32[]{:S(2)}, u32[]{:S(2)}) collective-permute-start(bf16[32,1024]{1,0:T(8,128)(2,1)S(1)} %collective-permute-done.30), channel_id=1, source_target_pairs={{2,0},{6,2},{10,6},{14,10},{12,14},{8,12},{4,8},{0,4},{3,1},{7,3},... | collective-permute-start | bytes 196616 | tf_op jit(solution)/shard_map/ppermute | solution.py:91
  213.6 5.2 %collective-permute-start.17 = (bf16[32,1024]{1,0:T(8,128)(2,1)S(1)}, bf16[32,1024]{1,0:T(8,128)(2,1)S(1)}, u32[]{:S(2)}, u32[]{:S(2)}) collective-permute-start(bf16[32,1024]{1,0:T(8,128)(2,1)S(1)} %collective-permute-done.16), channel_id=1, source_target_pairs={{0,2},{2,6},{6,10},{10,14},{14,12},{12,8},{8,4},{4,0},{1,3},{3,7},... | collective-permute-start | bytes 196616 | tf_op jit(solution)/shard_map/ppermute | solution.py:91
  225.7 12.4 %collective-permute-start.34 = (bf16[32,1024]{1,0:T(8,128)(2,1)S(1)}, bf16[32,1024]{1,0:T(8,128)(2,1)S(1)}, u32[]{:S(2)}, u32[]{:S(2)}) collective-permute-start(bf16[32,1024]{1,0:T(8,128)(2,1)S(1)} %collective-permute-done.33), channel_id=1, source_target_pairs={{2,0},{6,2},{10,6},{14,10},{12,14},{8,12},{4,8},{0,4},{3,1},{7,3},... | collective-permute-start | bytes 196616 | tf_op jit(solution)/shard_map/ppermute | solution.py:91
  227.7 10.4 %collective-permute-start.20 = (bf16[32,1024]{1,0:T(8,128)(2,1)S(1)}, bf16[32,1024]{1,0:T(8,128)(2,1)S(1)}, u32[]{:S(2)}, u32[]{:S(2)}) collective-permute-start(bf16[32,1024]{1,0:T(8,128)(2,1)S(1)} %collective-permute-done.19), channel_id=1, source_target_pairs={{0,2},{2,6},{6,10},{10,14},{14,12},{12,8},{8,4},{4,0},{1,3},{3,7},... | collective-permute-start | bytes 196616 | tf_op jit(solution)/shard_map/ppermute | solution.py:91
  (29 other events, 141.7 us)
Sparse Core Ops, SparseCore 0:
  10.0 74.9 all-gather.1
  93.7 7.7 reduce-scatter.1
  128.4 70.5 all-reduce.3

commit v7 on v5

--- a/solution.py
+++ b/solution.py
@@ -135,19 +135,17 @@
             gamma_cols, shares_all, (((0,), (0,)), ((), ())), preferred_element_type=jnp.float32
         )
         latent_grad = (upstream * inverse + 2.0 * pre * back_sum).astype(jnp.bfloat16)
-        gamma_terms = lax.dot_general(
-            shares, squares, (((1,), (1,)), ((), ())), preferred_element_type=jnp.float32
-        )
-        beta_terms = jnp.sum(shares.astype(jnp.float32), axis=1)
-        joined = jnp.concatenate(
-            [gamma_terms, jnp.broadcast_to(beta_terms[:, None], (lat_local, 128))], 1
+        lat_all = squares.shape[0]
+        squares_ones = jnp.concatenate([squares, jnp.ones((128, pixels), squares.dtype)], 0)
+        joined = lax.dot_general(
+            shares, squares_ones, (((1,), (1,)), ((), ())), preferred_element_type=jnp.float32
         )
         if len(ring) <= 16:
             (joined_total,) = ring_sum([joined], ring)
         else:
             joined_total = lax.psum(joined, "row")
-        gamma_total = joined_total[:, : gamma_terms.shape[1]]
-        beta_total = joined_total[:, gamma_terms.shape[1]]
+        gamma_total = joined_total[:, :lat_all]
+        beta_total = joined_total[:, lat_all]
         scale_factor = 1.0 / math.sqrt(pixels * lax.axis_size("row"))
         grad_gamma = gamma_total * scale_factor
         grad_beta = beta_total * scale_factor

time: 215 us -> 215 us (level)
  no operation moved by 1% of the time
where the time goes in v7:
time: 215 us
  waiting for transfers between devices  99.4 us (46%)
  starting transfers between devices  44.3 us (21%)
  between operations  25.6 us (12%)
  matrix products  20.2 us (9%)
  local copies, waits for them, and re-layouts  13 us (6%)
  other arithmetic  11.9 us (6%)
    all_gather x1, waiting for transfers between devices, per_device(): shard_piece = lax.all_gather(conv_weight, 'row', axis=0, tiled=True)  59.7 us
    ppermute x14, waiting for transfers between devices, ring_sum(): got = lax.ppermute(carry[part], 'row', moves[part])  20.9 us
    ppermute x14, starting transfers between devices, ring_sum(): gathered[part].append(lax.ppermute(gathered[part][-1], 'row', moves[part]))  16.5 us
    ppermute x14, starting transfers between devices, ring_sum(): got = lax.ppermute(carry[part], 'row', moves[part])  15.1 us
    ppermute x14, waiting for transfers between devices, ring_sum(): gathered[part].append(lax.ppermute(gathered[part][-1], 'row', moves[part]))  13.8 us
    ppermute x2, starting transfers between devices, extended(): before = lax.ppermute(last, axis, up)  9.44 us
    dot_general x9, matrix products, per_device(): jnp.dot(shard_piece[:, tap_index, :], window, preferred_element_type=jnp....  8.27 us
    unnamed x51, local copies, waits for them, and re-layouts  5.53 us
  transfers between devices with their start and end apart: 38, of which 15 were waited for; matrix products, arithmetic and copies ran while one was open for 15% of the time, Pallas kernels for 0%

profile of v7, /device:TPU:0, one launch (start us, length us, event | category | flops | bytes accessed | tf_op | source)
XLA Modules:
  0.0 214.5 jit_solution(15883814567892855439)
XLA Ops:
  9.2 4.9 %collective-permute-start = (bf16[212,1,128]{2,1,0:T(2,128)(2,1)S(1)}, bf16[212,1,128]{2,1,0:T(2,128)(2,1)S(1)}, u32[]{:S(2)}, u32[]{:S(2)}) collective-permute-start(bf16[212,1,128]{2,1,0:T(2,128)(2,1)S(1)} %get-tuple-element.55), channel_id=1, source_target_pairs={{0,2},{2,4},{4,6},{6,8},{8,10},{10,12},{12,14},{1,3},{3,5},{5,7},{... | collective-permute-start | bytes 162824 | tf_op jit(solution)/shard_map/ppermute | solution.py:19
  16.5 4.2 %collective-permute-done.1 = bf16[212,1,128]{2,1,0:T(2,128)(2,1)S(1)} collective-permute-done((bf16[212,1,128]{2,1,0:T(2,128)(2,1)S(1)}, bf16[212,1,128]{2,1,0:T(2,128)(2,1)S(1)}, u32[]{:S(2)}, u32[]{:S(2)}) %collective-permute-start.1) | collective-permute-done | bytes 54304 | tf_op jit(solution)/shard_map/ppermute | solution.py:20
  20.7 1.6 pad_maximum_fusion.3
  25.3 59.7 %all-gather.2.cloned.1.call-done = bf16[1024,9,212]{0,2,1:T(8,128)(2,1)} async-done(((bf16[128,9,212]{0,2,1:T(8,128)(2,1)}), bf16[1024,9,212]{0,2,1:T(8,128)(2,1)}) %all-gather.2.cloned.1.call-update) | async-done | bytes 3907600 | tf_op jit(solution)/shard_map/all_gather | solution.py:112
  85.0 1.6 fusion.51
  91.0 2.3 %bitcast_add_fusion = f32[1024,512]{0,1:T(8,128)} fusion(f32[512,1024]{1,0:T(8,128)S(1)} %fusion.51, f32[512,1024]{1,0:T(8,128)S(1)} %fusion.49, f32[512,1024]{1,0:T(8,128)S(1)} %fusion.47, f32[1024,512]{0,1:T(8,128)S(1)} %fusion.45, f32[512,1024]{1,0:T(8,128)S(1)} %fusion.43, f32[512,1024]{1,0:T(8,128)S(1)} %fusion.41, f32[512,1024]{1,0:T(8,128)S(1)} %fusion.37, ...), kind=kOutput, calls=%fused_computation.24 | convolution fusion | flops 226492416 | bytes 19537920 | tf_op jit(solution)/shard_map/dot_general | solution.py:118
  112.9 2.3 %fusion.13 = (bf16[512,512]{0,1:T(8,128)(2,1)}, f32[512,512]{0,1:T(8,128)}, bf16[512,512]{0,1:T(8,128)(2,1)}) fusion(f32[512,512]{0,1:T(8,128)S(1)} %copy-done.2, f32[512,4,128]{0,2,1:T(8,128)S(1)} %copy.14, bf16[1024,512]{0,1:T(8,128)(2,1)S(1)} %fusion.28, bf16[512,1024]{1,0:T(8,128)(2,1)S(1)} %copy-done.3, f32[512]{0:T(512)S(1)} %copy-done.8), kind=kOutput, calls=%fused_computation.45 | convolution fusion | flops 539492352 | bytes 6293504 | tf_op jit(solution)/shard_map/dot_general | solution.py:124
  115.2 1.9 fusion.11
  117.1 2.1 copy.15
  119.5 2.1 collective-permute-start.8
  121.5 4.2 %collective-permute-done.22 = f32[32,1152]{1,0:T(8,128)S(1)} collective-permute-done((f32[32,1152]{1,0:T(8,128)S(1)}, f32[32,1152]{1,0:T(8,128)S(1)}, u32[]{:S(2)}, u32[]{:S(2)}) %collective-permute-start.22) | collective-permute-done | bytes 147488 | tf_op jit(solution)/shard_map/ppermute | solution.py:85
  126.3 1.8 collective-permute-start.9
  128.0 3.3 %collective-permute-done.23 = f32[32,1152]{1,0:T(8,128)S(1)} collective-permute-done((f32[32,1152]{1,0:T(8,128)S(1)}, f32[32,1152]{1,0:T(8,128)S(1)}, u32[]{:S(2)}, u32[]{:S(2)}) %collective-permute-start.23) | collective-permute-done | bytes 147488 | tf_op jit(solution)/shard_map/ppermute | solution.py:85
  133.5 3.0 %collective-permute-done.24 = f32[32,1152]{1,0:T(8,128)S(1)} collective-permute-done((f32[32,1152]{1,0:T(8,128)S(1)}, f32[32,1152]{1,0:T(8,128)S(1)}, u32[]{:S(2)}, u32[]{:S(2)}) %collective-permute-start.24) | collective-permute-done | bytes 147488 | tf_op jit(solution)/shard_map/ppermute | solution.py:85
  138.8 3.3 %fusion.10 = bf16[512,512]{0,1:T(8,128)(2,1)S(1)} fusion(f32[512,512]{0,1:T(8,128)S(1)} %copy-done.5, s32[]{:T(128)S(6)} %select_n.194, bf16[512,512]{1,0:T(8,128)(2,1)S(1)} %copy-done.7, bf16[512,512]{1,0:T(8,128)(2,1)} %collective-permute-done.3, bf16[512,512]{0,1:T(8,128)(2,1)} %get-tuple-element.32, bf16[512,512]{0,1:T(8,128)(2,1)} %collective-permute-done.4, ...), kind=kOutput, calls=%fused_computation.41 | convolution fusion | flops 546308096 | bytes 4719616 | tf_op jit(solution)/shard_map/dot_general | solution.py:134
  144.3 4.1 %collective-permute-done.26 = f32[32,1152]{1,0:T(8,128)S(1)} collective-permute-done((f32[32,1152]{1,0:T(8,128)S(1)}, f32[32,1152]{1,0:T(8,128)S(1)}, u32[]{:S(2)}, u32[]{:S(2)}) %collective-permute-start.26) | collective-permute-done | bytes 147488 | tf_op jit(solution)/shard_map/ppermute | solution.py:85
  150.6 3.3 %collective-permute-done.27 = f32[32,1152]{1,0:T(8,128)S(1)} collective-permute-done((f32[32,1152]{1,0:T(8,128)S(1)}, f32[32,1152]{1,0:T(8,128)S(1)}, u32[]{:S(2)}, u32[]{:S(2)}) %collective-permute-start.27) | collective-permute-done | bytes 147488 | tf_op jit(solution)/shard_map/ppermute | solution.py:85
  156.1 3.0 %collective-permute-done.28 = f32[32,1152]{1,0:T(8,128)S(1)} collective-permute-done((f32[32,1152]{1,0:T(8,128)S(1)}, f32[32,1152]{1,0:T(8,128)S(1)}, u32[]{:S(2)}, u32[]{:S(2)}) %collective-permute-start.28) | collective-permute-done | bytes 147488 | tf_op jit(solution)/shard_map/ppermute | solution.py:85
  163.3 4.6 %collective-permute-start.6 = (bf16[1024,1,128]{0,2,1:T(8,128)(2,1)S(1)}, bf16[1024,1,128]{0,2,1:T(8,128)(2,1)S(1)}, u32[]{:S(2)}, u32[]{:S(2)}) collective-permute-start(bf16[1024,1,128]{0,2,1:T(8,128)(2,1)S(1)} %get-tuple-element.44), channel_id=1, source_target_pairs={{0,2},{2,4},{4,6},{6,8},{8,10},{10,12},{12,14},{1,3},{3,5},{5,7},{... | collective-permute-start | bytes 786440 | tf_op jit(solution)/shard_map/ppermute | solution.py:19
  169.4 1.5 collective-permute-start.16
  170.9 2.6 %collective-permute-done.30 = bf16[32,1152]{1,0:T(8,128)(2,1)S(1)} collective-permute-done((bf16[32,1152]{1,0:T(8,128)(2,1)S(1)}, bf16[32,1152]{1,0:T(8,128)(2,1)S(1)}, u32[]{:S(2)}, u32[]{:S(2)}) %collective-permute-start.30) | collective-permute-done | bytes 73760 | tf_op jit(solution)/shard_map/ppermute | solution.py:91
  174.4 2.1 %collective-permute-done.16 = bf16[32,1152]{1,0:T(8,128)(2,1)S(1)} collective-permute-done((bf16[32,1152]{1,0:T(8,128)(2,1)S(1)}, bf16[32,1152]{1,0:T(8,128)(2,1)S(1)}, u32[]{:S(2)}, u32[]{:S(2)}) %collective-permute-start.16) | collective-permute-done | bytes 73760 | tf_op jit(solution)/shard_map/ppermute | solution.py:91
  176.6 2.5 %collective-permute-start.17 = (bf16[32,1152]{1,0:T(8,128)(2,1)S(1)}, bf16[32,1152]{1,0:T(8,128)(2,1)S(1)}, u32[]{:S(2)}, u32[]{:S(2)}) collective-permute-start(bf16[32,1152]{1,0:T(8,128)(2,1)S(1)} %collective-permute-done.16), channel_id=1, source_target_pairs={{0,2},{2,6},{6,10},{10,14},{14,12},{12,8},{8,4},{4,0},{1,3},{3,7},... | collective-permute-start | bytes 221192 | tf_op jit(solution)/shard_map/ppermute | solution.py:91
  179.1 1.9 collective-permute-done.17
  181.0 2.4 %collective-permute-start.18 = (bf16[32,1152]{1,0:T(8,128)(2,1)S(1)}, bf16[32,1152]{1,0:T(8,128)(2,1)S(1)}, u32[]{:S(2)}, u32[]{:S(2)}) collective-permute-start(bf16[32,1152]{1,0:T(8,128)(2,1)S(1)} %collective-permute-done.17), channel_id=1, source_target_pairs={{0,2},{2,6},{6,10},{10,14},{14,12},{12,8},{8,4},{4,0},{1,3},{3,7},... | collective-permute-start | bytes 221192 | tf_op jit(solution)/shard_map/ppermute | solution.py:91
  190.2 2.1 collective-permute-start.19
  192.3 2.6 %collective-permute-done.33 = bf16[32,1152]{1,0:T(8,128)(2,1)S(1)} collective-permute-done((bf16[32,1152]{1,0:T(8,128)(2,1)S(1)}, bf16[32,1152]{1,0:T(8,128)(2,1)S(1)}, u32[]{:S(2)}, u32[]{:S(2)}) %collective-permute-start.33) | collective-permute-done | bytes 73760 | tf_op jit(solution)/shard_map/ppermute | solution.py:91
  195.2 1.8 collective-permute-start.20
  197.0 2.2 %collective-permute-done.34 = bf16[32,1152]{1,0:T(8,128)(2,1)S(1)} collective-permute-done((bf16[32,1152]{1,0:T(8,128)(2,1)S(1)}, bf16[32,1152]{1,0:T(8,128)(2,1)S(1)}, u32[]{:S(2)}, u32[]{:S(2)}) %collective-permute-start.34) | collective-permute-done | bytes 73760 | tf_op jit(solution)/shard_map/ppermute | solution.py:91
  199.6 1.7 collective-permute-start.21
  201.4 2.2 %collective-permute-done.35 = bf16[32,1152]{1,0:T(8,128)(2,1)S(1)} collective-permute-done((bf16[32,1152]{1,0:T(8,128)(2,1)S(1)}, bf16[32,1152]{1,0:T(8,128)(2,1)S(1)}, u32[]{:S(2)}, u32[]{:S(2)}) %collective-permute-start.35) | collective-permute-done | bytes 73760 | tf_op jit(solution)/shard_map/ppermute | solution.py:91
  206.1 1.6 slice_multiply_fusion
  (165 shorter events, 48.5 us)
Async XLA Ops:
  7.2 77.8 %all-gather.2.cloned.1.call-start = ((), (), s32[]{:S(2)}) async-start(), calls=%async_computation.1 | async-start | bytes 4478976 | tf_op jit(solution)/shard_map/all_gather | solution.py:112
  7.9 100.2 %reduce-scatter.2.cloned.1.call-start = ((), (), s32[]{:S(2)}) async-start(), calls=%async_computation.2 | async-start | bytes 3145728 | tf_op jit(solution)/shard_map/reduce_scatter | solution.py:121
  9.2 7.3 %collective-permute-start = (bf16[212,1,128]{2,1,0:T(2,128)(2,1)S(1)}, bf16[212,1,128]{2,1,0:T(2,128)(2,1)S(1)}, u32[]{:S(2)}, u32[]{:S(2)}) collective-permute-start(bf16[212,1,128]{2,1,0:T(2,128)(2,1)S(1)} %get-tuple-element.55), channel_id=1, source_target_pairs={{0,2},{2,4},{4,6},{6,8},{8,10},{10,12},{12,14},{1,3},{3,5},{5,7},{... | collective-permute-start | bytes 162824 | tf_op jit(solution)/shard_map/ppermute | solution.py:19
  14.1 6.6 %collective-permute-start.1 = (bf16[212,1,128]{2,1,0:T(2,128)(2,1)S(1)}, bf16[212,1,128]{2,1,0:T(2,128)(2,1)S(1)}, u32[]{:S(2)}, u32[]{:S(2)}) collective-permute-start(bf16[212,1,128]{2,1,0:T(2,128)(2,1)S(1)} %get-tuple-element.56), channel_id=1, source_target_pairs={{2,0},{4,2},{6,4},{8,6},{10,8},{12,10},{14,12},{3,1},{5,3},{7,5},{... | collective-permute-start | bytes 162824 | tf_op jit(solution)/shard_map/ppermute | solution.py:20
  95.6 43.1 %collective-permute-start.3 = (bf16[512,512]{1,0:T(8,128)(2,1)}, bf16[512,512]{1,0:T(8,128)(2,1)}, u32[]{:S(2)}, u32[]{:S(2)}) collective-permute-start(bf16[512,512]{1,0:T(8,128)(2,1)} %get-tuple-element.45), channel_id=1, source_target_pairs={{0,1},{1,0},{2,3},{3,2},{4,5},{5,4},{6,7},{7,6},{8,9},{9,8},{10,11... | collective-permute-start | bytes 1572872 | tf_op jit(solution)/shard_map/ppermute | solution.py:132
  115.1 23.6 %collective-permute-start.4 = (bf16[512,512]{0,1:T(8,128)(2,1)}, bf16[512,512]{0,1:T(8,128)(2,1)}, u32[]{:S(2)}, u32[]{:S(2)}) collective-permute-start(bf16[512,512]{0,1:T(8,128)(2,1)} %get-tuple-element.32), channel_id=1, source_target_pairs={{0,1},{1,0},{2,3},{3,2},{4,5},{5,4},{6,7},{7,6},{8,9},{9,8},{10,11... | collective-permute-start | bytes 1572872 | tf_op jit(solution)/shard_map/ppermute | solution.py:26
  119.4 6.3 %collective-permute-start.22 = (f32[32,1152]{1,0:T(8,128)S(1)}, f32[32,1152]{1,0:T(8,128)S(1)}, u32[]{:S(2)}, u32[]{:S(2)}) collective-permute-start(f32[32,1152]{1,0:T(8,128)S(1)} %select_bitcast_fusion), channel_id=1, source_target_pairs={{2,0},{6,2},{10,6},{14,10},{12,14},{8,12},{4,8},{0,4},{3,1},{7,3},... | collective-permute-start | bytes 442376 | tf_op jit(solution)/shard_map/ppermute | solution.py:85
  119.5 6.8 %collective-permute-start.8 = (f32[32,1152]{1,0:T(8,128)S(1)}, f32[32,1152]{1,0:T(8,128)S(1)}, u32[]{:S(2)}, u32[]{:S(2)}) collective-permute-start(f32[32,1152]{1,0:T(8,128)S(1)} %select_bitcast_fusion.1), channel_id=1, source_target_pairs={{0,2},{2,6},{6,10},{10,14},{14,12},{12,8},{8,4},{4,0},{1,3},{3,7},... | collective-permute-start | bytes 442376 | tf_op jit(solution)/shard_map/ppermute | solution.py:85
  125.7 5.6 %collective-permute-start.23 = (f32[32,1152]{1,0:T(8,128)S(1)}, f32[32,1152]{1,0:T(8,128)S(1)}, u32[]{:S(2)}, u32[]{:S(2)}) collective-permute-start(f32[32,1152]{1,0:T(8,128)S(1)} %bitcast_add_fusion.11), channel_id=1, source_target_pairs={{2,0},{6,2},{10,6},{14,10},{12,14},{8,12},{4,8},{0,4},{3,1},{7,3},... | collective-permute-start | bytes 442376 | tf_op jit(solution)/shard_map/ppermute | solution.py:85
  126.3 5.7 %collective-permute-start.9 = (f32[32,1152]{1,0:T(8,128)S(1)}, f32[32,1152]{1,0:T(8,128)S(1)}, u32[]{:S(2)}, u32[]{:S(2)}) collective-permute-start(f32[32,1152]{1,0:T(8,128)S(1)} %bitcast_add_fusion.18), channel_id=1, source_target_pairs={{0,2},{2,6},{6,10},{10,14},{14,12},{12,8},{8,4},{4,0},{1,3},{3,7},... | collective-permute-start | bytes 442376 | tf_op jit(solution)/shard_map/ppermute | solution.py:85
  131.4 5.2 %collective-permute-start.24 = (f32[32,1152]{1,0:T(8,128)S(1)}, f32[32,1152]{1,0:T(8,128)S(1)}, u32[]{:S(2)}, u32[]{:S(2)}) collective-permute-start(f32[32,1152]{1,0:T(8,128)S(1)} %bitcast_add_fusion.10), channel_id=1, source_target_pairs={{2,0},{6,2},{10,6},{14,10},{12,14},{8,12},{4,8},{0,4},{3,1},{7,3},... | collective-permute-start | bytes 442376 | tf_op jit(solution)/shard_map/ppermute | solution.py:85
  132.0 5.2 %collective-permute-start.10 = (f32[32,1152]{1,0:T(8,128)S(1)}, f32[32,1152]{1,0:T(8,128)S(1)}, u32[]{:S(2)}, u32[]{:S(2)}) collective-permute-start(f32[32,1152]{1,0:T(8,128)S(1)} %bitcast_add_fusion.17), channel_id=1, source_target_pairs={{0,2},{2,6},{6,10},{10,14},{14,12},{12,8},{8,4},{4,0},{1,3},{3,7},... | collective-permute-start | bytes 442376 | tf_op jit(solution)/shard_map/ppermute | solution.py:85
  136.6 5.5 %collective-permute-start.25 = (f32[32,1152]{1,0:T(8,128)S(1)}, f32[32,1152]{1,0:T(8,128)S(1)}, u32[]{:S(2)}, u32[]{:S(2)}) collective-permute-start(f32[32,1152]{1,0:T(8,128)S(1)} %bitcast_add_fusion.9), channel_id=1, source_target_pairs={{2,0},{6,2},{10,6},{14,10},{12,14},{8,12},{4,8},{0,4},{3,1},{7,3},... | collective-permute-start | bytes 442376 | tf_op jit(solution)/shard_map/ppermute | solution.py:85
  137.2 5.5 %collective-permute-start.11 = (f32[32,1152]{1,0:T(8,128)S(1)}, f32[32,1152]{1,0:T(8,128)S(1)}, u32[]{:S(2)}, u32[]{:S(2)}) collective-permute-start(f32[32,1152]{1,0:T(8,128)S(1)} %bitcast_add_fusion.16), channel_id=1, source_target_pairs={{0,2},{2,6},{6,10},{10,14},{14,12},{12,8},{8,4},{4,0},{1,3},{3,7},... | collective-permute-start | bytes 442376 | tf_op jit(solution)/shard_map/ppermute | solution.py:85
  142.0 19.3 %collective-permute-start.5 = (bf16[512,4,128]{0,2,1:T(8,128)(2,1)S(1)}, bf16[512,4,128]{0,2,1:T(8,128)(2,1)S(1)}, u32[]{:S(2)}, u32[]{:S(2)}) collective-permute-start(bf16[512,4,128]{0,2,1:T(8,128)(2,1)S(1)} %bitcast.249), channel_id=1, source_target_pairs={{0,1},{1,0},{2,3},{3,2},{4,5},{5,4},{6,7},{7,6},{8,9},{9,8},{10,11... | collective-permute-start | bytes 1572872 | tf_op jit(solution)/shard_map/ppermute | solution.py:26
  142.1 6.3 %collective-permute-start.26 = (f32[32,1152]{1,0:T(8,128)S(1)}, f32[32,1152]{1,0:T(8,128)S(1)}, u32[]{:S(2)}, u32[]{:S(2)}) collective-permute-start(f32[32,1152]{1,0:T(8,128)S(1)} %bitcast_add_fusion.8), channel_id=1, source_target_pairs={{2,0},{6,2},{10,6},{14,10},{12,14},{8,12},{4,8},{0,4},{3,1},{7,3},... | collective-permute-start | bytes 442376 | tf_op jit(solution)/shard_map/ppermute | solution.py:85
  142.8 6.3 %collective-permute-start.12 = (f32[32,1152]{1,0:T(8,128)S(1)}, f32[32,1152]{1,0:T(8,128)S(1)}, u32[]{:S(2)}, u32[]{:S(2)}) collective-permute-start(f32[32,1152]{1,0:T(8,128)S(1)} %bitcast_add_fusion.15), channel_id=1, source_target_pairs={{0,2},{2,6},{6,10},{10,14},{14,12},{12,8},{8,4},{4,0},{1,3},{3,7},... | collective-permute-start | bytes 442376 | tf_op jit(solution)/shard_map/ppermute | solution.py:85
  148.5 5.4 %collective-permute-start.27 = (f32[32,1152]{1,0:T(8,128)S(1)}, f32[32,1152]{1,0:T(8,128)S(1)}, u32[]{:S(2)}, u32[]{:S(2)}) collective-permute-start(f32[32,1152]{1,0:T(8,128)S(1)} %bitcast_add_fusion.7), channel_id=1, source_target_pairs={{2,0},{6,2},{10,6},{14,10},{12,14},{8,12},{4,8},{0,4},{3,1},{7,3},... | collective-permute-start | bytes 442376 | tf_op jit(solution)/shard_map/ppermute | solution.py:85
  149.1 5.4 %collective-permute-start.13 = (f32[32,1152]{1,0:T(8,128)S(1)}, f32[32,1152]{1,0:T(8,128)S(1)}, u32[]{:S(2)}, u32[]{:S(2)}) collective-permute-start(f32[32,1152]{1,0:T(8,128)S(1)} %bitcast_add_fusion.14), channel_id=1, source_target_pairs={{0,2},{2,6},{6,10},{10,14},{14,12},{12,8},{8,4},{4,0},{1,3},{3,7},... | collective-permute-start | bytes 442376 | tf_op jit(solution)/shard_map/ppermute | solution.py:85
  153.9 5.2 %collective-permute-start.28 = (f32[32,1152]{1,0:T(8,128)S(1)}, f32[32,1152]{1,0:T(8,128)S(1)}, u32[]{:S(2)}, u32[]{:S(2)}) collective-permute-start(f32[32,1152]{1,0:T(8,128)S(1)} %bitcast_add_fusion.6), channel_id=1, source_target_pairs={{2,0},{6,2},{10,6},{14,10},{12,14},{8,12},{4,8},{0,4},{3,1},{7,3},... | collective-permute-start | bytes 442376 | tf_op jit(solution)/shard_map/ppermute | solution.py:85
  154.6 5.2 %collective-permute-start.14 = (f32[32,1152]{1,0:T(8,128)S(1)}, f32[32,1152]{1,0:T(8,128)S(1)}, u32[]{:S(2)}, u32[]{:S(2)}) collective-permute-start(f32[32,1152]{1,0:T(8,128)S(1)} %bitcast_add_fusion.13), channel_id=1, source_target_pairs={{0,2},{2,6},{6,10},{10,14},{14,12},{12,8},{8,4},{4,0},{1,3},{3,7},... | collective-permute-start | bytes 442376 | tf_op jit(solution)/shard_map/ppermute | solution.py:85
  159.1 9.3 %collective-permute-start.29 = (bf16[32,1152]{1,0:T(8,128)(2,1)S(1)}, bf16[32,1152]{1,0:T(8,128)(2,1)S(1)}, u32[]{:S(2)}, u32[]{:S(2)}) collective-permute-start(bf16[32,1152]{1,0:T(8,128)(2,1)S(1)} %get-tuple-element.29), channel_id=1, source_target_pairs={{2,0},{6,2},{10,6},{14,10},{12,14},{8,12},{4,8},{0,4},{3,1},{7,3},... | collective-permute-start | bytes 221192 | tf_op jit(solution)/shard_map/ppermute | solution.py:91
  159.8 9.6 %collective-permute-start.15 = (bf16[32,1152]{1,0:T(8,128)(2,1)S(1)}, bf16[32,1152]{1,0:T(8,128)(2,1)S(1)}, u32[]{:S(2)}, u32[]{:S(2)}) collective-permute-start(bf16[32,1152]{1,0:T(8,128)(2,1)S(1)} %get-tuple-element.27), channel_id=1, source_target_pairs={{0,2},{2,6},{6,10},{10,14},{14,12},{12,8},{8,4},{4,0},{1,3},{3,7},... | collective-permute-start | bytes 221192 | tf_op jit(solution)/shard_map/ppermute | solution.py:91
  162.0 21.4 %collective-permute-start.7 = (bf16[1024,1,128]{0,2,1:T(8,128)(2,1)S(1)}, bf16[1024,1,128]{0,2,1:T(8,128)(2,1)S(1)}, u32[]{:S(2)}, u32[]{:S(2)}) collective-permute-start(bf16[1024,1,128]{0,2,1:T(8,128)(2,1)S(1)} %get-tuple-element.43), channel_id=1, source_target_pairs={{2,0},{4,2},{6,4},{8,6},{10,8},{12,10},{14,12},{3,1},{5,3},{7,5},{... | collective-permute-start | bytes 786440 | tf_op jit(solution)/shard_map/ppermute | solution.py:20
  163.3 20.1 %collective-permute-start.6 = (bf16[1024,1,128]{0,2,1:T(8,128)(2,1)S(1)}, bf16[1024,1,128]{0,2,1:T(8,128)(2,1)S(1)}, u32[]{:S(2)}, u32[]{:S(2)}) collective-permute-start(bf16[1024,1,128]{0,2,1:T(8,128)(2,1)S(1)} %get-tuple-element.44), channel_id=1, source_target_pairs={{0,2},{2,4},{4,6},{6,8},{8,10},{10,12},{12,14},{1,3},{3,5},{5,7},{... | collective-permute-start | bytes 786440 | tf_op jit(solution)/shard_map/ppermute | solution.py:19
  168.4 5.1 %collective-permute-start.30 = (bf16[32,1152]{1,0:T(8,128)(2,1)S(1)}, bf16[32,1152]{1,0:T(8,128)(2,1)S(1)}, u32[]{:S(2)}, u32[]{:S(2)}) collective-permute-start(bf16[32,1152]{1,0:T(8,128)(2,1)S(1)} %collective-permute-done.29), channel_id=1, source_target_pairs={{2,0},{6,2},{10,6},{14,10},{12,14},{8,12},{4,8},{0,4},{3,1},{7,3},... | collective-permute-start | bytes 221192 | tf_op jit(solution)/shard_map/ppermute | solution.py:91
  169.4 7.2 %collective-permute-start.16 = (bf16[32,1152]{1,0:T(8,128)(2,1)S(1)}, bf16[32,1152]{1,0:T(8,128)(2,1)S(1)}, u32[]{:S(2)}, u32[]{:S(2)}) collective-permute-start(bf16[32,1152]{1,0:T(8,128)(2,1)S(1)} %collective-permute-done.15), channel_id=1, source_target_pairs={{0,2},{2,6},{6,10},{10,14},{14,12},{12,8},{8,4},{4,0},{1,3},{3,7},... | collective-permute-start | bytes 221192 | tf_op jit(solution)/shard_map/ppermute | solution.py:91
  173.5 5.5 %collective-permute-start.31 = (bf16[32,1152]{1,0:T(8,128)(2,1)S(1)}, bf16[32,1152]{1,0:T(8,128)(2,1)S(1)}, u32[]{:S(2)}, u32[]{:S(2)}) collective-permute-start(bf16[32,1152]{1,0:T(8,128)(2,1)S(1)} %collective-permute-done.30), channel_id=1, source_target_pairs={{2,0},{6,2},{10,6},{14,10},{12,14},{8,12},{4,8},{0,4},{3,1},{7,3},... | collective-permute-start | bytes 221192 | tf_op jit(solution)/shard_map/ppermute | solution.py:91
  179.1 11.2 %collective-permute-start.32 = (bf16[32,1152]{1,0:T(8,128)(2,1)S(1)}, bf16[32,1152]{1,0:T(8,128)(2,1)S(1)}, u32[]{:S(2)}, u32[]{:S(2)}) collective-permute-start(bf16[32,1152]{1,0:T(8,128)(2,1)S(1)} %collective-permute-done.31), channel_id=1, source_target_pairs={{2,0},{6,2},{10,6},{14,10},{12,14},{8,12},{4,8},{0,4},{3,1},{7,3},... | collective-permute-start | bytes 221192 | tf_op jit(solution)/shard_map/ppermute | solution.py:91
  181.0 9.2 %collective-permute-start.18 = (bf16[32,1152]{1,0:T(8,128)(2,1)S(1)}, bf16[32,1152]{1,0:T(8,128)(2,1)S(1)}, u32[]{:S(2)}, u32[]{:S(2)}) collective-permute-start(bf16[32,1152]{1,0:T(8,128)(2,1)S(1)} %collective-permute-done.17), channel_id=1, source_target_pairs={{0,2},{2,6},{6,10},{10,14},{14,12},{12,8},{8,4},{4,0},{1,3},{3,7},... | collective-permute-start | bytes 221192 | tf_op jit(solution)/shard_map/ppermute | solution.py:91
  190.2 4.9 %collective-permute-start.19 = (bf16[32,1152]{1,0:T(8,128)(2,1)S(1)}, bf16[32,1152]{1,0:T(8,128)(2,1)S(1)}, u32[]{:S(2)}, u32[]{:S(2)}) collective-permute-start(bf16[32,1152]{1,0:T(8,128)(2,1)S(1)} %collective-permute-done.18), channel_id=1, source_target_pairs={{0,2},{2,6},{6,10},{10,14},{14,12},{12,8},{8,4},{4,0},{1,3},{3,7},... | collective-permute-start | bytes 221192 | tf_op jit(solution)/shard_map/ppermute | solution.py:91
  199.6 4.8 %collective-permute-start.21 = (bf16[32,1152]{1,0:T(8,128)(2,1)S(1)}, bf16[32,1152]{1,0:T(8,128)(2,1)S(1)}, u32[]{:S(2)}, u32[]{:S(2)}) collective-permute-start(bf16[32,1152]{1,0:T(8,128)(2,1)S(1)} %collective-permute-done.20), channel_id=1, source_target_pairs={{0,2},{2,6},{6,10},{10,14},{14,12},{12,8},{8,4},{4,0},{1,3},{3,7},... | collective-permute-start | bytes 221192 | tf_op jit(solution)/shard_map/ppermute | solution.py:91
  (16 other events, 122.9 us)
Sparse Core Ops, SparseCore 0:
  10.0 74.9 all-gather.1
  93.5 7.7 reduce-scatter.1

commit v8 on v7

--- a/solution.py
+++ b/solution.py
@@ -60,44 +60,27 @@
     return path if len(set(path)) == count else list(range(count))
 
 
-def ring_sum(blocks, ring):
+def ring_sum(x, ring):
     count = len(ring)
     forward = [(ring[i], ring[(i + 1) % count]) for i in range(count)]
     backward = [(b, a) for a, b in forward]
+    ring_index = jnp.asarray(ring, jnp.int32)
     position = jnp.asarray([ring.index(i) for i in range(count)], jnp.int32)[lax.axis_index("row")]
-
-    def chunks(x, part):
-        half = x.shape[0] // 2
-        piece = x[part * half : (part + 1) * half]
-        return piece.reshape((count, half // count) + x.shape[1:])
-
-    split = [[chunks(x, part) for x in blocks] for part in range(2)]
+    rows = x.shape[0] // (2 * count)
+    blocks = x.reshape((count, 2, rows) + x.shape[1:])
     moves = (forward, backward)
     signs = (1, -1)
 
     def pick(part, step):
-        index = (position - signs[part] * (1 + step)) % count
-        return [jnp.take(c, index, axis=0) for c in split[part]]
+        index = ring_index[(position - signs[part] * (1 + step)) % count]
+        return lax.dynamic_index_in_dim(blocks, index, 0, keepdims=False)[part]
 
     carry = [pick(part, 0) for part in range(2)]
     for step in range(1, count):
         for part in range(2):
-            got = lax.ppermute(carry[part], "row", moves[part])
-            carry[part] = [g + o for g, o in zip(got, pick(part, step))]
-    gathered = [[c.astype(jnp.bfloat16) for c in part] for part in carry]
-    gathered = [[c] for c in gathered]
-    for step in range(1, count):
-        for part in range(2):
-            gathered[part].append(lax.ppermute(gathered[part][-1], "row", moves[part]))
-    results = []
-    for leaf in range(len(blocks)):
-        halves = []
-        for part in range(2):
-            stacked = jnp.stack([g[leaf] for g in gathered[part]], 0)
-            order = (signs[part] * (position - jnp.arange(count))) % count
-            halves.append(jnp.take(stacked, order, axis=0).reshape((-1,) + stacked.shape[2:]))
-        results.append(jnp.concatenate(halves, 0).astype(jnp.float32))
-    return results
+            carry[part] = lax.ppermute(carry[part], "row", moves[part]) + pick(part, step)
+    own = jnp.concatenate(carry, 0).astype(jnp.bfloat16)
+    return lax.all_gather(own, "row", axis=0, tiled=True).astype(jnp.float32)
 
 
 def make_per_device(ring):
@@ -141,7 +124,7 @@
             shares, squares_ones, (((1,), (1,)), ((), ())), preferred_element_type=jnp.float32
         )
         if len(ring) <= 16:
-            (joined_total,) = ring_sum([joined], ring)
+            joined_total = ring_sum(joined, ring)
         else:
             joined_total = lax.psum(joined, "row")
         gamma_total = joined_total[:, :lat_all]

time: 215 us -> 251 us (1.17)
  between operations: 25.6 us -> 55.2 us
  starting transfers between devices: 44.3 us -> 27.3 us
  other arithmetic: 11.9 us -> 23.2 us
  waiting for transfers between devices: 99.4 us -> 107 us
    ppermute x28 -> x14, waiting for transfers between devices: 34.7 us -> 4.9 us  [ring_sum(): lax.ppermute(carry[part], 'row', moves[part]) + pick(part, step)]
    all_gather x0 -> x1, waiting for transfers between devices: none -> 19 us  [ring_sum(): return lax.all_gather(own, 'row', axis=0, tiled=True).astype(jnp.float32)]
    ppermute x28 -> x14, starting transfers between devices: 31.6 us -> 14.3 us  [ring_sum(): lax.ppermute(carry[part], 'row', moves[part]) + pick(part, step)]
    add x12 -> x6, other arithmetic: 0.22 us -> 9.38 us  [ring_sum(): lax.ppermute(carry[part], 'row', moves[part]) + pick(part, step)]
    reduce_scatter x1, waiting for transfers between devices: 0.02 us -> 7.93 us  [per_device(): lax.psum_scatter(partial_value, 'chan', scatter_dimension=0, tiled=True)]
    ppermute x2, waiting for transfers between devices: 0.01 us -> 4.84 us  [extended(): before = lax.ppermute(last, axis, up)]
    ppermute x2, waiting for transfers between devices: 4.24 us -> 8.64 us  [extended(): after = lax.ppermute(leading, axis, down)]
    unnamed x51 -> x35, local copies, waits for them, and re-layouts: 5.53 us -> 5.14 us
  transfers between devices with their start and end apart: 38 -> 25, of which waited for: 15 -> 13; matrix products, arithmetic and copies ran while one was open for 15% -> 12% of each run, Pallas kernels for 0% -> 0%
where the time goes in v8:
time: 251 us; the launch traced here: 250 us
  waiting for transfers between devices  107 us (43%)
  between operations  55.2 us (22%)
  starting transfers between devices  27.3 us (11%)
  other arithmetic  23.2 us (9%)
  matrix products  22.4 us (9%)
  local copies, waits for them, and re-layouts  14.8 us (6%)
    all_gather x1, waiting for transfers between devices, per_device(): shard_piece = lax.all_gather(conv_weight, 'row', axis=0, tiled=True)  59.7 us
    all_gather x1, waiting for transfers between devices, ring_sum(): return lax.all_gather(own, 'row', axis=0, tiled=True).astype(jnp.float32)  19 us
    ppermute x14, starting transfers between devices, ring_sum(): lax.ppermute(carry[part], 'row', moves[part]) + pick(part, step)  14.3 us
    ppermute x2, starting transfers between devices, extended(): before = lax.ppermute(last, axis, up)  9.44 us
    add x6, other arithmetic, ring_sum(): lax.ppermute(carry[part], 'row', moves[part]) + pick(part, step)  9.38 us
    ppermute x2, waiting for transfers between devices, extended(): after = lax.ppermute(leading, axis, down)  8.64 us
    dot_general x9, matrix products, per_device(): jnp.dot(shard_piece[:, tap_index, :], window, preferred_element_type=jnp....  8.26 us
    reduce_scatter x1, waiting for transfers between devices, per_device(): lax.psum_scatter(partial_value, 'chan', scatter_dimension=0, tiled=True)  7.93 us
  transfers between devices with their start and end apart: 25, of which 13 were waited for; matrix products, arithmetic and copies ran while one was open for 12% of the time, Pallas kernels for 0%

profile of v8, /device:TPU:0, one launch (start us, length us, event | category | flops | bytes accessed | tf_op | source)
XLA Modules:
  0.0 249.8 jit_solution(12192685188022226994)
XLA Ops:
  9.2 4.9 %collective-permute-start = (bf16[212,1,128]{2,1,0:T(2,128)(2,1)S(1)}, bf16[212,1,128]{2,1,0:T(2,128)(2,1)S(1)}, u32[]{:S(2)}, u32[]{:S(2)}) collective-permute-start(bf16[212,1,128]{2,1,0:T(2,128)(2,1)S(1)} %get-tuple-element.52), channel_id=1, source_target_pairs={{0,2},{2,4},{4,6},{6,8},{8,10},{10,12},{12,14},{1,3},{3,5},{5,7},{... | collective-permute-start | bytes 162824 | tf_op jit(solution)/shard_map/ppermute | solution.py:19
  16.5 4.2 %collective-permute-done.1 = bf16[212,1,128]{2,1,0:T(2,128)(2,1)S(1)} collective-permute-done((bf16[212,1,128]{2,1,0:T(2,128)(2,1)S(1)}, bf16[212,1,128]{2,1,0:T(2,128)(2,1)S(1)}, u32[]{:S(2)}, u32[]{:S(2)}) %collective-permute-start.1) | collective-permute-done | bytes 54304 | tf_op jit(solution)/shard_map/ppermute | solution.py:20
  20.7 1.6 pad_maximum_fusion.3
  25.3 59.7 %all-gather.3.cloned.1.call-done = bf16[1024,9,212]{0,2,1:T(8,128)(2,1)} async-done(((bf16[128,9,212]{0,2,1:T(8,128)(2,1)}), bf16[1024,9,212]{0,2,1:T(8,128)(2,1)}) %all-gather.3.cloned.1.call-update) | async-done | bytes 3907600 | tf_op jit(solution)/shard_map/all_gather | solution.py:95
  85.0 1.6 fusion.51
  86.6 1.5 fusion.49
  91.0 2.3 bitcast_add_fusion
  93.4 7.9 %reduce-scatter.2.cloned.1.call-done = f32[512,512]{0,1:T(8,128)} async-done(((f32[1024,512]{0,1:T(8,128)}), f32[512,512]{0,1:T(8,128)}) %reduce-scatter.2.cloned.1.call-update) | async-done | bytes 1048592 | tf_op jit(solution)/shard_map/reduce_scatter | solution.py:104
  101.3 2.1 multiply_convert_fusion.1
  121.3 2.0 fusion.28
  123.4 2.3 fusion.13
  125.6 1.9 fusion.11
  128.2 1.7 collective-permute-start.8
  135.8 1.7 fusion.69
  137.5 1.5 collective-permute-start.9
  144.3 1.7 fusion.68
  145.9 1.5 collective-permute-start.10
  152.7 1.7 fusion.67
  154.3 1.5 collective-permute-start.11
  161.1 1.7 fusion.66
  168.6 1.7 fusion.65
  172.3 2.2 constant_dynamic-slice_fusion
  182.7 2.1 copy.16
  186.4 1.5 collective-permute-start.21
  187.9 4.5 %fusion.10 = bf16[512,512]{0,1:T(8,128)(2,1)} fusion(f32[512,512]{0,1:T(8,128)} %get-tuple-element.30, s32[]{:T(128)S(6)} %select_n.250, bf16[512,512]{1,0:T(8,128)(2,1)} %get-tuple-element.43, bf16[512,512]{1,0:T(8,128)(2,1)} %collective-permute-done.3, bf16[512,512]{0,1:T(8,128)(2,1)} %get-tuple-element.29, bf16[512,512]{0,1:T(8,128)(2,1)} %collective-permute-done.4, ...), kind=kOutput, calls=%fused_computation.39 | convolution fusion | flops 546308096 | bytes 4719616 | tf_op jit(solution)/shard_map/dot_general | solution.py:117
  194.5 1.8 fusion.16
  197.6 4.6 %collective-permute-start.6 = (bf16[1024,1,128]{0,2,1:T(8,128)(2,1)S(1)}, bf16[1024,1,128]{0,2,1:T(8,128)(2,1)S(1)}, u32[]{:S(2)}, u32[]{:S(2)}) collective-permute-start(bf16[1024,1,128]{0,2,1:T(8,128)(2,1)S(1)} %get-tuple-element.41), channel_id=1, source_target_pairs={{0,2},{2,4},{4,6},{6,8},{8,10},{10,12},{12,14},{1,3},{3,5},{5,7},{... | collective-permute-start | bytes 786440 | tf_op jit(solution)/shard_map/ppermute | solution.py:19
  202.2 1.5 fusion.44
  203.7 4.4 %collective-permute-done.7 = bf16[1024,1,128]{0,2,1:T(8,128)(2,1)S(1)} collective-permute-done((bf16[1024,1,128]{0,2,1:T(8,128)(2,1)S(1)}, bf16[1024,1,128]{0,2,1:T(8,128)(2,1)S(1)}, u32[]{:S(2)}, u32[]{:S(2)}) %collective-permute-start.7) | collective-permute-done | bytes 262176 | tf_op jit(solution)/shard_map/ppermute | solution.py:20
  208.1 4.8 %collective-permute-done.6 = bf16[1024,1,128]{0,2,1:T(8,128)(2,1)S(1)} collective-permute-done((bf16[1024,1,128]{0,2,1:T(8,128)(2,1)S(1)}, bf16[1024,1,128]{0,2,1:T(8,128)(2,1)S(1)}, u32[]{:S(2)}, u32[]{:S(2)}) %collective-permute-start.6) | collective-permute-done | bytes 262176 | tf_op jit(solution)/shard_map/ppermute | solution.py:19
  220.6 19.0 %all-gather.5.cloned.1.call-done = bf16[512,1152]{1,0:T(8,128)(2,1)} async-done(((bf16[64,1152]{1,0:T(8,128)(2,1)}), bf16[512,1152]{1,0:T(8,128)(2,1)}) %all-gather.5.cloned.1.call-update) | async-done | bytes 1179664 | tf_op jit(solution)/shard_map/all_gather | solution.py:83
  241.0 1.6 slice_multiply_fusion
  (105 shorter events, 40.2 us)
Async XLA Ops:
  7.2 15.3 %copy-start.4 = (bf16[212,4,128]{2,1,0:T(4,128)(2,1)S(1)}, bf16[212,4,128]{2,1,0:T(4,128)(2,1)}, u32[]{:S(2)}) copy-start(bf16[212,4,128]{2,1,0:T(4,128)(2,1)} %param.9) | copy-start | bytes 651268
  7.2 77.8 %all-gather.3.cloned.1.call-start = ((), (), s32[]{:S(2)}) async-start(), calls=%async_computation.1 | async-start | bytes 4478976 | tf_op jit(solution)/shard_map/all_gather | solution.py:95
  7.9 93.4 %reduce-scatter.2.cloned.1.call-start = ((), (), s32[]{:S(2)}) async-start(), calls=%async_computation.2 | async-start | bytes 3145728 | tf_op jit(solution)/shard_map/reduce_scatter | solution.py:104
  9.2 7.3 %collective-permute-start = (bf16[212,1,128]{2,1,0:T(2,128)(2,1)S(1)}, bf16[212,1,128]{2,1,0:T(2,128)(2,1)S(1)}, u32[]{:S(2)}, u32[]{:S(2)}) collective-permute-start(bf16[212,1,128]{2,1,0:T(2,128)(2,1)S(1)} %get-tuple-element.52), channel_id=1, source_target_pairs={{0,2},{2,4},{4,6},{6,8},{8,10},{10,12},{12,14},{1,3},{3,5},{5,7},{... | collective-permute-start | bytes 162824 | tf_op jit(solution)/shard_map/ppermute | solution.py:19
  14.1 6.6 %collective-permute-start.1 = (bf16[212,1,128]{2,1,0:T(2,128)(2,1)S(1)}, bf16[212,1,128]{2,1,0:T(2,128)(2,1)S(1)}, u32[]{:S(2)}, u32[]{:S(2)}) collective-permute-start(bf16[212,1,128]{2,1,0:T(2,128)(2,1)S(1)} %get-tuple-element.53), channel_id=1, source_target_pairs={{2,0},{4,2},{6,4},{8,6},{10,8},{12,10},{14,12},{3,1},{5,3},{7,5},{... | collective-permute-start | bytes 162824 | tf_op jit(solution)/shard_map/ppermute | solution.py:20
  85.0 3.1 %copy-start = (bf16[1024,9,212]{0,2,1:T(8,128)(2,1)S(1)}, bf16[1024,9,212]{0,2,1:T(8,128)(2,1)}, u32[]{:S(2)}) copy-start(bf16[1024,9,212]{0,2,1:T(8,128)(2,1)} %all-gather.3.cloned.1.call-done) | copy-start | bytes 11722756
  93.3 10.5 %copy-start.7 = (s32[8]{0:T(128)S(1)}, s32[8]{0:T(128)}, u32[]{:S(2)}) copy-start(s32[8]{0:T(128)} %constant.235.clone) | copy-start | bytes 100
  93.3 21.9 %copy-start.5 = (s32[8]{0:T(128)S(1)}, s32[8]{0:T(128)}, u32[]{:S(2)}) copy-start(s32[8]{0:T(128)} %constant.234.clone) | copy-start | bytes 100
  93.3 146.2 %all-gather.5.cloned.1.call-start = ((), (), s32[]{:S(2)}) async-start(), calls=%async_computation.3 | async-start | bytes 1327104 | tf_op jit(solution)/shard_map/all_gather | solution.py:83
  103.4 17.8 %collective-permute-start.2 = (bf16[512,512]{0,1:T(8,128)(2,1)}, bf16[512,512]{0,1:T(8,128)(2,1)}, u32[]{:S(2)}, u32[]{:S(2)}) collective-permute-start(bf16[512,512]{0,1:T(8,128)(2,1)} %multiply_convert_fusion.1), channel_id=1, source_target_pairs={{0,1},{1,0},{2,3},{3,2},{4,5},{5,4},{6,7},{7,6},{8,9},{9,8},{10,11... | collective-permute-start | bytes 1572872 | tf_op jit(solution)/shard_map/ppermute | solution.py:26
  105.7 17.6 %copy-start.2 = (f32[512,512]{0,1:T(8,128)S(1)}, f32[512,512]{0,1:T(8,128)}, u32[]{:S(2)}) copy-start(f32[512,512]{0,1:T(8,128)} %reduce-scatter.2.cloned.1.call-done) | copy-start | bytes 3145732
  105.7 17.6 %copy-start.3 = (bf16[512,1024]{1,0:T(8,128)(2,1)S(1)}, bf16[512,1024]{1,0:T(8,128)(2,1)}, u32[]{:S(2)}) copy-start(bf16[512,1024]{1,0:T(8,128)(2,1)} %param.11) | copy-start | bytes 3145732
  105.7 17.6 %copy-start.6 = (f32[512]{0:T(512)S(1)}, f32[512]{0:T(512)}, u32[]{:S(2)}) copy-start(f32[512]{0:T(512)} %param.12) | copy-start | bytes 6148
  128.2 6.4 %collective-permute-start.8 = (f32[32,1152]{1,0:T(8,128)}, f32[32,1152]{1,0:T(8,128)}, u32[]{:S(2)}, u32[]{:S(2)}) collective-permute-start(f32[32,1152]{1,0:T(8,128)} %get-tuple-element.27), channel_id=1, source_target_pairs={{0,2},{2,6},{6,10},{10,14},{14,12},{12,8},{8,4},{4,0},{1,3},{3,7},... | collective-permute-start | bytes 442376 | tf_op jit(solution)/shard_map/ppermute | solution.py:81
  129.9 5.9 %collective-permute-start.15 = (f32[32,1152]{1,0:T(8,128)S(1)}, f32[32,1152]{1,0:T(8,128)}, u32[]{:S(2)}, u32[]{:S(2)}) collective-permute-start(f32[32,1152]{1,0:T(8,128)S(1)} %get-tuple-element.28), channel_id=1, source_target_pairs={{2,0},{6,2},{10,6},{14,10},{12,14},{8,12},{4,8},{0,4},{3,1},{7,3},... | collective-permute-start | bytes 442376 | tf_op jit(solution)/shard_map/ppermute | solution.py:81
  137.5 5.8 %collective-permute-start.9 = (f32[32,1152]{1,0:T(8,128)}, f32[32,1152]{1,0:T(8,128)}, u32[]{:S(2)}, u32[]{:S(2)}) collective-permute-start(f32[32,1152]{1,0:T(8,128)} %get-tuple-element.25), channel_id=1, source_target_pairs={{0,2},{2,6},{6,10},{10,14},{14,12},{12,8},{8,4},{4,0},{1,3},{3,7},... | collective-permute-start | bytes 442376 | tf_op jit(solution)/shard_map/ppermute | solution.py:81
  139.0 5.2 %collective-permute-start.16 = (f32[32,1152]{1,0:T(8,128)S(1)}, f32[32,1152]{1,0:T(8,128)}, u32[]{:S(2)}, u32[]{:S(2)}) collective-permute-start(f32[32,1152]{1,0:T(8,128)S(1)} %get-tuple-element.26), channel_id=1, source_target_pairs={{2,0},{6,2},{10,6},{14,10},{12,14},{8,12},{4,8},{0,4},{3,1},{7,3},... | collective-permute-start | bytes 442376 | tf_op jit(solution)/shard_map/ppermute | solution.py:81
  145.9 5.8 %collective-permute-start.10 = (f32[32,1152]{1,0:T(8,128)}, f32[32,1152]{1,0:T(8,128)}, u32[]{:S(2)}, u32[]{:S(2)}) collective-permute-start(f32[32,1152]{1,0:T(8,128)} %get-tuple-element.23), channel_id=1, source_target_pairs={{0,2},{2,6},{6,10},{10,14},{14,12},{12,8},{8,4},{4,0},{1,3},{3,7},... | collective-permute-start | bytes 442376 | tf_op jit(solution)/shard_map/ppermute | solution.py:81
  147.4 5.2 %collective-permute-start.17 = (f32[32,1152]{1,0:T(8,128)S(1)}, f32[32,1152]{1,0:T(8,128)}, u32[]{:S(2)}, u32[]{:S(2)}) collective-permute-start(f32[32,1152]{1,0:T(8,128)S(1)} %get-tuple-element.24), channel_id=1, source_target_pairs={{2,0},{6,2},{10,6},{14,10},{12,14},{8,12},{4,8},{0,4},{3,1},{7,3},... | collective-permute-start | bytes 442376 | tf_op jit(solution)/shard_map/ppermute | solution.py:81
  154.3 5.5 %collective-permute-start.11 = (f32[32,1152]{1,0:T(8,128)}, f32[32,1152]{1,0:T(8,128)}, u32[]{:S(2)}, u32[]{:S(2)}) collective-permute-start(f32[32,1152]{1,0:T(8,128)} %get-tuple-element.21), channel_id=1, source_target_pairs={{0,2},{2,6},{6,10},{10,14},{14,12},{12,8},{8,4},{4,0},{1,3},{3,7},... | collective-permute-start | bytes 442376 | tf_op jit(solution)/shard_map/ppermute | solution.py:81
  155.8 5.2 %collective-permute-start.18 = (f32[32,1152]{1,0:T(8,128)S(1)}, f32[32,1152]{1,0:T(8,128)}, u32[]{:S(2)}, u32[]{:S(2)}) collective-permute-start(f32[32,1152]{1,0:T(8,128)S(1)} %get-tuple-element.22), channel_id=1, source_target_pairs={{2,0},{6,2},{10,6},{14,10},{12,14},{8,12},{4,8},{0,4},{3,1},{7,3},... | collective-permute-start | bytes 442376 | tf_op jit(solution)/shard_map/ppermute | solution.py:81
  162.8 5.8 %collective-permute-start.12 = (f32[32,1152]{1,0:T(8,128)}, f32[32,1152]{1,0:T(8,128)}, u32[]{:S(2)}, u32[]{:S(2)}) collective-permute-start(f32[32,1152]{1,0:T(8,128)} %get-tuple-element.19), channel_id=1, source_target_pairs={{0,2},{2,6},{6,10},{10,14},{14,12},{12,8},{8,4},{4,0},{1,3},{3,7},... | collective-permute-start | bytes 442376 | tf_op jit(solution)/shard_map/ppermute | solution.py:81
  163.4 5.2 %collective-permute-start.19 = (f32[32,1152]{1,0:T(8,128)S(1)}, f32[32,1152]{1,0:T(8,128)}, u32[]{:S(2)}, u32[]{:S(2)}) collective-permute-start(f32[32,1152]{1,0:T(8,128)S(1)} %get-tuple-element.20), channel_id=1, source_target_pairs={{2,0},{6,2},{10,6},{14,10},{12,14},{8,12},{4,8},{0,4},{3,1},{7,3},... | collective-permute-start | bytes 442376 | tf_op jit(solution)/shard_map/ppermute | solution.py:81
  170.3 14.5 %collective-permute-start.13 = (f32[32,1152]{1,0:T(8,128)}, f32[32,1152]{1,0:T(8,128)}, u32[]{:S(2)}, u32[]{:S(2)}) collective-permute-start(f32[32,1152]{1,0:T(8,128)} %get-tuple-element.17), channel_id=1, source_target_pairs={{0,2},{2,6},{6,10},{10,14},{14,12},{12,8},{8,4},{4,0},{1,3},{3,7},... | collective-permute-start | bytes 442376 | tf_op jit(solution)/shard_map/ppermute | solution.py:81
  170.9 13.9 %collective-permute-start.20 = (f32[32,1152]{1,0:T(8,128)S(1)}, f32[32,1152]{1,0:T(8,128)}, u32[]{:S(2)}, u32[]{:S(2)}) collective-permute-start(f32[32,1152]{1,0:T(8,128)S(1)} %get-tuple-element.18), channel_id=1, source_target_pairs={{2,0},{6,2},{10,6},{14,10},{12,14},{8,12},{4,8},{0,4},{3,1},{7,3},... | collective-permute-start | bytes 442376 | tf_op jit(solution)/shard_map/ppermute | solution.py:81
  174.6 13.4 %collective-permute-start.3 = (bf16[512,512]{1,0:T(8,128)(2,1)}, bf16[512,512]{1,0:T(8,128)(2,1)}, u32[]{:S(2)}, u32[]{:S(2)}) collective-permute-start(bf16[512,512]{1,0:T(8,128)(2,1)} %get-tuple-element.42), channel_id=1, source_target_pairs={{0,1},{1,0},{2,3},{3,2},{4,5},{5,4},{6,7},{7,6},{8,9},{9,8},{10,11... | collective-permute-start | bytes 1572872 | tf_op jit(solution)/shard_map/ppermute | solution.py:115
  174.6 13.4 %collective-permute-start.4 = (bf16[512,512]{0,1:T(8,128)(2,1)}, bf16[512,512]{0,1:T(8,128)(2,1)}, u32[]{:S(2)}, u32[]{:S(2)}) collective-permute-start(bf16[512,512]{0,1:T(8,128)(2,1)} %get-tuple-element.29), channel_id=1, source_target_pairs={{0,1},{1,0},{2,3},{3,2},{4,5},{5,4},{6,7},{7,6},{8,9},{9,8},{10,11... | collective-permute-start | bytes 1572872 | tf_op jit(solution)/shard_map/ppermute | solution.py:26
  185.8 6.6 %collective-permute-start.14 = (f32[32,1152]{1,0:T(8,128)S(1)}, f32[32,1152]{1,0:T(8,128)S(1)}, u32[]{:S(2)}, u32[]{:S(2)}) collective-permute-start(f32[32,1152]{1,0:T(8,128)S(1)} %get-tuple-element.15), channel_id=1, source_target_pairs={{0,2},{2,6},{6,10},{10,14},{14,12},{12,8},{8,4},{4,0},{1,3},{3,7},... | collective-permute-start | bytes 442376 | tf_op jit(solution)/shard_map/ppermute | solution.py:81
  186.4 6.0 %collective-permute-start.21 = (f32[32,1152]{1,0:T(8,128)S(1)}, f32[32,1152]{1,0:T(8,128)S(1)}, u32[]{:S(2)}, u32[]{:S(2)}) collective-permute-start(f32[32,1152]{1,0:T(8,128)S(1)} %get-tuple-element.16), channel_id=1, source_target_pairs={{2,0},{6,2},{10,6},{14,10},{12,14},{8,12},{4,8},{0,4},{3,1},{7,3},... | collective-permute-start | bytes 442376 | tf_op jit(solution)/shard_map/ppermute | solution.py:81
  192.4 2.1 collective-permute-start.5
  196.3 11.8 %collective-permute-start.7 = (bf16[1024,1,128]{0,2,1:T(8,128)(2,1)S(1)}, bf16[1024,1,128]{0,2,1:T(8,128)(2,1)S(1)}, u32[]{:S(2)}, u32[]{:S(2)}) collective-permute-start(bf16[1024,1,128]{0,2,1:T(8,128)(2,1)S(1)} %get-tuple-element.40), channel_id=1, source_target_pairs={{2,0},{4,2},{6,4},{8,6},{10,8},{12,10},{14,12},{3,1},{5,3},{7,5},{... | collective-permute-start | bytes 786440 | tf_op jit(solution)/shard_map/ppermute | solution.py:20
  197.6 15.3 %collective-permute-start.6 = (bf16[1024,1,128]{0,2,1:T(8,128)(2,1)S(1)}, bf16[1024,1,128]{0,2,1:T(8,128)(2,1)S(1)}, u32[]{:S(2)}, u32[]{:S(2)}) collective-permute-start(bf16[1024,1,128]{0,2,1:T(8,128)(2,1)S(1)} %get-tuple-element.41), channel_id=1, source_target_pairs={{0,2},{2,4},{4,6},{6,8},{8,10},{10,12},{12,14},{1,3},{3,5},{5,7},{... | collective-permute-start | bytes 786440 | tf_op jit(solution)/shard_map/ppermute | solution.py:19
  (1 other events, 2.1 us)
Sparse Core Ops, SparseCore 0:
  10.0 74.9 all-gather.2
  93.4 7.8 reduce-scatter.1
  193.3 46.2 all-gather.4

commit v9 on v7

--- a/solution.py
+++ b/solution.py
@@ -60,7 +60,7 @@
     return path if len(set(path)) == count else list(range(count))
 
 
-def ring_sum(blocks, ring):
+def ring_sum(blocks, ring, hold):
     count = len(ring)
     forward = [(ring[i], ring[(i + 1) % count]) for i in range(count)]
     backward = [(b, a) for a, b in forward]
@@ -84,6 +84,8 @@
         for part in range(2):
             got = lax.ppermute(carry[part], "row", moves[part])
             carry[part] = [g + o for g, o in zip(got, pick(part, step))]
+        if step == 1:
+            hold, carry = lax.optimization_barrier((hold, carry))
     gathered = [[c.astype(jnp.bfloat16) for c in part] for part in carry]
     gathered = [[c] for c in gathered]
     for step in range(1, count):
@@ -97,7 +99,7 @@
             order = (signs[part] * (position - jnp.arange(count))) % count
             halves.append(jnp.take(stacked, order, axis=0).reshape((-1,) + stacked.shape[2:]))
         results.append(jnp.concatenate(halves, 0).astype(jnp.float32))
-    return results
+    return results, hold
 
 
 def make_per_device(ring):
@@ -123,7 +125,7 @@
         squares = chan_gather(squares_own)
         norm_value = gdn_beta[:, None] + jnp.dot(gdn_gamma, squares, preferred_element_type=jnp.float32)
         inverse = lax.rsqrt(norm_value)
-        latent = (pre * inverse).astype(jnp.bfloat16)
+        scaled = pre * inverse
         upstream = cotangent.reshape(lat_local, pixels).astype(jnp.float32)
         shares = (-0.5 * upstream * pre * inverse * inverse * inverse).astype(jnp.bfloat16)
         index = lax.axis_index("chan")
@@ -141,9 +143,10 @@
             shares, squares_ones, (((1,), (1,)), ((), ())), preferred_element_type=jnp.float32
         )
         if len(ring) <= 16:
-            (joined_total,) = ring_sum([joined], ring)
+            (joined_total,), scaled = ring_sum([joined], ring, scaled)
         else:
             joined_total = lax.psum(joined, "row")
+        latent = scaled.astype(jnp.bfloat16)
         gamma_total = joined_total[:, :lat_all]
         beta_total = joined_total[:, lat_all]
         scale_factor = 1.0 / math.sqrt(pixels * lax.axis_size("row"))

time: 215 us -> 231 us (1.074)
  waiting for transfers between devices: 99.4 us -> 109 us
  other arithmetic: 11.9 us -> 20.3 us
    reduce_scatter x1, waiting for transfers between devices: 0.02 us -> 7.96 us  [per_device(): lax.psum_scatter(partial_value, 'chan', scatter_dimension=0, tiled=True)]
    unnamed x51 -> x55, local copies, waits for them, and re-layouts: 5.53 us -> 4.36 us
  transfers between devices with their start and end apart: 38 -> 38, of which waited for: 15 -> 19; matrix products, arithmetic and copies ran while one was open for 15% -> 17% of each run, Pallas kernels for 0% -> 0%
where the time goes in v9:
time: 231 us; the launch traced here: 230 us
  waiting for transfers between devices  109 us (47%)
  starting transfers between devices  43.7 us (19%)
  between operations  25.5 us (11%)
  other arithmetic  20.3 us (9%)
  matrix products  19 us (8%)
  local copies, waits for them, and re-layouts  13.2 us (6%)
    all_gather x1, waiting for transfers between devices, per_device(): shard_piece = lax.all_gather(conv_weight, 'row', axis=0, tiled=True)  59.7 us
    ppermute x14, waiting for transfers between devices, ring_sum(): got = lax.ppermute(carry[part], 'row', moves[part])  22.4 us
    ppermute x14, starting transfers between devices, ring_sum(): gathered[part].append(lax.ppermute(gathered[part][-1], 'row', moves[part]))  16.2 us
    ppermute x14, starting transfers between devices, ring_sum(): got = lax.ppermute(carry[part], 'row', moves[part])  14.8 us
    ppermute x14, waiting for transfers between devices, ring_sum(): gathered[part].append(lax.ppermute(gathered[part][-1], 'row', moves[part]))  13.7 us
    ppermute x2, starting transfers between devices, extended(): before = lax.ppermute(last, axis, up)  9.44 us
    dot_general x9, matrix products, per_device(): jnp.dot(shard_piece[:, tap_index, :], window, preferred_element_type=jnp....  8.26 us
    reduce_scatter x1, waiting for transfers between devices, per_device(): lax.psum_scatter(partial_value, 'chan', scatter_dimension=0, tiled=True)  7.96 us
  transfers between devices with their start and end apart: 38, of which 19 were waited for; matrix products, arithmetic and copies ran while one was open for 17% of the time, Pallas kernels for 0%

profile of v9, /device:TPU:0, one launch (start us, length us, event | category | flops | bytes accessed | tf_op | source)
XLA Modules:
  0.0 230.3 jit_solution(9657726107465671437)
XLA Ops:
  9.2 4.9 %collective-permute-start = (bf16[212,1,128]{2,1,0:T(2,128)(2,1)S(1)}, bf16[212,1,128]{2,1,0:T(2,128)(2,1)S(1)}, u32[]{:S(2)}, u32[]{:S(2)}) collective-permute-start(bf16[212,1,128]{2,1,0:T(2,128)(2,1)S(1)} %get-tuple-element.60), channel_id=1, source_target_pairs={{0,2},{2,4},{4,6},{6,8},{8,10},{10,12},{12,14},{1,3},{3,5},{5,7},{... | collective-permute-start | bytes 162824 | tf_op jit(solution)/shard_map/ppermute | solution.py:19
  16.5 4.2 %collective-permute-done.1 = bf16[212,1,128]{2,1,0:T(2,128)(2,1)S(1)} collective-permute-done((bf16[212,1,128]{2,1,0:T(2,128)(2,1)S(1)}, bf16[212,1,128]{2,1,0:T(2,128)(2,1)S(1)}, u32[]{:S(2)}, u32[]{:S(2)}) %collective-permute-start.1) | collective-permute-done | bytes 54304 | tf_op jit(solution)/shard_map/ppermute | solution.py:20
  25.3 59.7 %all-gather.2.cloned.1.call-done = bf16[1024,9,212]{0,2,1:T(8,128)(2,1)} async-done(((bf16[128,9,212]{0,2,1:T(8,128)(2,1)}), bf16[1024,9,212]{0,2,1:T(8,128)(2,1)}) %all-gather.2.cloned.1.call-update) | async-done | bytes 3907600 | tf_op jit(solution)/shard_map/all_gather | solution.py:114
  91.0 2.3 bitcast_add_fusion
  93.3 8.0 %reduce-scatter.2.cloned.1.call-done = f32[512,512]{0,1:T(8,128)} async-done(((f32[1024,512]{0,1:T(8,128)}), f32[512,512]{0,1:T(8,128)}) %reduce-scatter.2.cloned.1.call-update) | async-done | bytes 1048592 | tf_op jit(solution)/shard_map/reduce_scatter | solution.py:123
  101.3 2.1 multiply_convert_fusion
  113.4 2.0 fusion.28
  119.5 1.9 collective-permute-start.3
  121.6 4.0 %collective-permute-done.3 = f32[32,1152]{1,0:T(8,128)S(1)} collective-permute-done((f32[32,1152]{1,0:T(8,128)S(1)}, f32[32,1152]{1,0:T(8,128)S(1)}, u32[]{:S(2)}, u32[]{:S(2)}) %collective-permute-start.3) | collective-permute-done | bytes 147488 | tf_op jit(solution)/shard_map/ppermute | solution.py:85
  138.6 2.1 copy.15
  143.7 3.2 %collective-permute-done.10 = f32[32,1152]{1,0:T(8,128)S(1)} collective-permute-done((f32[32,1152]{1,0:T(8,128)S(1)}, f32[32,1152]{1,0:T(8,128)S(1)}, u32[]{:S(2)}, u32[]{:S(2)}) %collective-permute-start.10) | collective-permute-done | bytes 147488 | tf_op jit(solution)/shard_map/ppermute | solution.py:85
  146.9 1.7 collective-permute-start.11
  149.7 2.7 %collective-permute-done.11 = f32[32,1152]{1,0:T(8,128)S(1)} collective-permute-done((f32[32,1152]{1,0:T(8,128)S(1)}, f32[32,1152]{1,0:T(8,128)S(1)}, u32[]{:S(2)}, u32[]{:S(2)}) %collective-permute-start.11) | collective-permute-done | bytes 147488 | tf_op jit(solution)/shard_map/ppermute | solution.py:85
  152.4 1.7 collective-permute-start.12
  154.2 3.7 %fusion.10 = bf16[512,512]{0,1:T(8,128)(2,1)S(1)} fusion(f32[512,512]{0,1:T(8,128)} %get-tuple-element.38, s32[]{:T(128)S(6)} %select_n.194, bf16[512,512]{1,0:T(8,128)(2,1)} %get-tuple-element.51, bf16[512,512]{1,0:T(8,128)(2,1)} %collective-permute-done.5, bf16[512,512]{0,1:T(8,128)(2,1)} %copy-done.5, bf16[512,512]{0,1:T(8,128)(2,1)} %collective-permute-done.6, ...), kind=kOutput, calls=%fused_computation.41 | convolution fusion | flops 546308096 | bytes 4719616 | tf_op jit(solution)/shard_map/dot_general | solution.py:136
  160.1 4.1 %collective-permute-done.26 = f32[32,1152]{1,0:T(8,128)S(1)} collective-permute-done((f32[32,1152]{1,0:T(8,128)S(1)}, f32[32,1152]{1,0:T(8,128)S(1)}, u32[]{:S(2)}, u32[]{:S(2)}) %collective-permute-start.26) | collective-permute-done | bytes 147488 | tf_op jit(solution)/shard_map/ppermute | solution.py:85
  164.7 1.7 collective-permute-start.14
  166.4 3.3 %collective-permute-done.27 = f32[32,1152]{1,0:T(8,128)S(1)} collective-permute-done((f32[32,1152]{1,0:T(8,128)S(1)}, f32[32,1152]{1,0:T(8,128)S(1)}, u32[]{:S(2)}, u32[]{:S(2)}) %collective-permute-start.27) | collective-permute-done | bytes 147488 | tf_op jit(solution)/shard_map/ppermute | solution.py:85
  170.2 1.7 collective-permute-start.15
  171.9 3.0 %collective-permute-done.28 = f32[32,1152]{1,0:T(8,128)S(1)} collective-permute-done((f32[32,1152]{1,0:T(8,128)S(1)}, f32[32,1152]{1,0:T(8,128)S(1)}, u32[]{:S(2)}, u32[]{:S(2)}) %collective-permute-start.28) | collective-permute-done | bytes 147488 | tf_op jit(solution)/shard_map/ppermute | solution.py:85
  179.2 4.6 %collective-permute-start.8 = (bf16[1024,1,128]{0,2,1:T(8,128)(2,1)S(1)}, bf16[1024,1,128]{0,2,1:T(8,128)(2,1)S(1)}, u32[]{:S(2)}, u32[]{:S(2)}) collective-permute-start(bf16[1024,1,128]{0,2,1:T(8,128)(2,1)S(1)} %get-tuple-element.49), channel_id=1, source_target_pairs={{0,2},{2,4},{4,6},{6,8},{8,10},{10,12},{12,14},{1,3},{3,5},{5,7},{... | collective-permute-start | bytes 786440 | tf_op jit(solution)/shard_map/ppermute | solution.py:19
  186.8 2.9 %collective-permute-done.30 = bf16[32,1152]{1,0:T(8,128)(2,1)S(1)} collective-permute-done((bf16[32,1152]{1,0:T(8,128)(2,1)S(1)}, bf16[32,1152]{1,0:T(8,128)(2,1)S(1)}, u32[]{:S(2)}, u32[]{:S(2)}) %collective-permute-start.30) | collective-permute-done | bytes 73760 | tf_op jit(solution)/shard_map/ppermute | solution.py:93
  190.2 1.9 collective-permute-done.17
  192.1 2.5 %collective-permute-start.18 = (bf16[32,1152]{1,0:T(8,128)(2,1)S(1)}, bf16[32,1152]{1,0:T(8,128)(2,1)S(1)}, u32[]{:S(2)}, u32[]{:S(2)}) collective-permute-start(bf16[32,1152]{1,0:T(8,128)(2,1)S(1)} %collective-permute-done.17), channel_id=1, source_target_pairs={{0,2},{2,6},{6,10},{10,14},{14,12},{12,8},{8,4},{4,0},{1,3},{3,7},... | collective-permute-start | bytes 221192 | tf_op jit(solution)/shard_map/ppermute | solution.py:93
  194.7 2.0 collective-permute-done.18
  196.7 2.5 %collective-permute-start.19 = (bf16[32,1152]{1,0:T(8,128)(2,1)S(1)}, bf16[32,1152]{1,0:T(8,128)(2,1)S(1)}, u32[]{:S(2)}, u32[]{:S(2)}) collective-permute-start(bf16[32,1152]{1,0:T(8,128)(2,1)S(1)} %collective-permute-done.18), channel_id=1, source_target_pairs={{0,2},{2,6},{6,10},{10,14},{14,12},{12,8},{8,4},{4,0},{1,3},{3,7},... | collective-permute-start | bytes 221192 | tf_op jit(solution)/shard_map/ppermute | solution.py:93
  206.1 2.1 collective-permute-start.20
  208.2 2.2 collective-permute-done.33
  210.5 2.0 collective-permute-start.21
  212.5 2.2 collective-permute-done.34
  214.9 2.0 collective-permute-start.22
  216.9 2.2 collective-permute-done.35
  (170 shorter events, 57.6 us)
Async XLA Ops:
  7.2 77.8 %all-gather.2.cloned.1.call-start = ((), (), s32[]{:S(2)}) async-start(), calls=%async_computation.1 | async-start | bytes 4478976 | tf_op jit(solution)/shard_map/all_gather | solution.py:114
  7.9 93.4 %reduce-scatter.2.cloned.1.call-start = ((), (), s32[]{:S(2)}) async-start(), calls=%async_computation.2 | async-start | bytes 3145728 | tf_op jit(solution)/shard_map/reduce_scatter | solution.py:123
  9.2 7.3 %collective-permute-start = (bf16[212,1,128]{2,1,0:T(2,128)(2,1)S(1)}, bf16[212,1,128]{2,1,0:T(2,128)(2,1)S(1)}, u32[]{:S(2)}, u32[]{:S(2)}) collective-permute-start(bf16[212,1,128]{2,1,0:T(2,128)(2,1)S(1)} %get-tuple-element.60), channel_id=1, source_target_pairs={{0,2},{2,4},{4,6},{6,8},{8,10},{10,12},{12,14},{1,3},{3,5},{5,7},{... | collective-permute-start | bytes 162824 | tf_op jit(solution)/shard_map/ppermute | solution.py:19
  14.1 6.6 %collective-permute-start.1 = (bf16[212,1,128]{2,1,0:T(2,128)(2,1)S(1)}, bf16[212,1,128]{2,1,0:T(2,128)(2,1)S(1)}, u32[]{:S(2)}, u32[]{:S(2)}) collective-permute-start(bf16[212,1,128]{2,1,0:T(2,128)(2,1)S(1)} %get-tuple-element.61), channel_id=1, source_target_pairs={{2,0},{4,2},{6,4},{8,6},{10,8},{12,10},{14,12},{3,1},{5,3},{7,5},{... | collective-permute-start | bytes 162824 | tf_op jit(solution)/shard_map/ppermute | solution.py:20
  103.4 10.0 %collective-permute-start.2 = (bf16[512,512]{0,1:T(8,128)(2,1)}, bf16[512,512]{0,1:T(8,128)(2,1)}, u32[]{:S(2)}, u32[]{:S(2)}) collective-permute-start(bf16[512,512]{0,1:T(8,128)(2,1)} %multiply_convert_fusion), channel_id=1, source_target_pairs={{0,1},{1,0},{2,3},{3,2},{4,5},{5,4},{6,7},{7,6},{8,9},{9,8},{10,11... | collective-permute-start | bytes 1572872 | tf_op jit(solution)/shard_map/ppermute | solution.py:26
  104.9 49.3 %collective-permute-start.5 = (bf16[512,512]{1,0:T(8,128)(2,1)}, bf16[512,512]{1,0:T(8,128)(2,1)}, u32[]{:S(2)}, u32[]{:S(2)}) collective-permute-start(bf16[512,512]{1,0:T(8,128)(2,1)} %get-tuple-element.50), channel_id=1, source_target_pairs={{0,1},{1,0},{2,3},{3,2},{4,5},{5,4},{6,7},{7,6},{8,9},{9,8},{10,11... | collective-permute-start | bytes 1572872 | tf_op jit(solution)/shard_map/ppermute | solution.py:134
  119.5 6.1 %collective-permute-start.3 = (f32[32,1152]{1,0:T(8,128)S(1)}, f32[32,1152]{1,0:T(8,128)S(1)}, u32[]{:S(2)}, u32[]{:S(2)}) collective-permute-start(f32[32,1152]{1,0:T(8,128)S(1)} %select_bitcast_fusion.1), channel_id=1, source_target_pairs={{0,2},{2,6},{6,10},{10,14},{14,12},{12,8},{8,4},{4,0},{1,3},{3,7},... | collective-permute-start | bytes 442376 | tf_op jit(solution)/shard_map/ppermute | solution.py:85
  121.4 5.7 %collective-permute-start.4 = (f32[32,1152]{1,0:T(8,128)S(1)}, f32[32,1152]{1,0:T(8,128)S(1)}, u32[]{:S(2)}, u32[]{:S(2)}) collective-permute-start(f32[32,1152]{1,0:T(8,128)S(1)} %select_bitcast_fusion), channel_id=1, source_target_pairs={{2,0},{6,2},{10,6},{14,10},{12,14},{8,12},{4,8},{0,4},{3,1},{7,3},... | collective-permute-start | bytes 442376 | tf_op jit(solution)/shard_map/ppermute | solution.py:85
  127.8 14.6 %collective-permute-start.23 = (f32[32,1152]{1,0:T(8,128)}, f32[32,1152]{1,0:T(8,128)}, u32[]{:S(2)}, u32[]{:S(2)}) collective-permute-start(f32[32,1152]{1,0:T(8,128)} %bitcast_add_fusion.17), channel_id=1, source_target_pairs={{2,0},{6,2},{10,6},{14,10},{12,14},{8,12},{4,8},{0,4},{3,1},{7,3},... | collective-permute-start | bytes 442376 | tf_op jit(solution)/shard_map/ppermute | solution.py:85
  138.6 15.6 %collective-permute-start.6 = (bf16[512,512]{0,1:T(8,128)(2,1)}, bf16[512,512]{0,1:T(8,128)(2,1)}, u32[]{:S(2)}, u32[]{:S(2)}) collective-permute-start(bf16[512,512]{0,1:T(8,128)(2,1)} %copy-done.5), channel_id=1, source_target_pairs={{0,1},{1,0},{2,3},{3,2},{4,5},{5,4},{6,7},{7,6},{8,9},{9,8},{10,11... | collective-permute-start | bytes 1572872 | tf_op jit(solution)/shard_map/ppermute | solution.py:26
  140.7 6.3 %collective-permute-start.10 = (f32[32,1152]{1,0:T(8,128)S(1)}, f32[32,1152]{1,0:T(8,128)S(1)}, u32[]{:S(2)}, u32[]{:S(2)}) collective-permute-start(f32[32,1152]{1,0:T(8,128)S(1)} %bitcast_add_fusion.18), channel_id=1, source_target_pairs={{0,2},{2,6},{6,10},{10,14},{14,12},{12,8},{8,4},{4,0},{1,3},{3,7},... | collective-permute-start | bytes 442376 | tf_op jit(solution)/shard_map/ppermute | solution.py:85
  143.3 6.0 %collective-permute-start.24 = (f32[32,1152]{1,0:T(8,128)S(1)}, f32[32,1152]{1,0:T(8,128)S(1)}, u32[]{:S(2)}, u32[]{:S(2)}) collective-permute-start(f32[32,1152]{1,0:T(8,128)S(1)} %bitcast_add_fusion.10), channel_id=1, source_target_pairs={{2,0},{6,2},{10,6},{14,10},{12,14},{8,12},{4,8},{0,4},{3,1},{7,3},... | collective-permute-start | bytes 442376 | tf_op jit(solution)/shard_map/ppermute | solution.py:85
  146.9 5.5 %collective-permute-start.11 = (f32[32,1152]{1,0:T(8,128)S(1)}, f32[32,1152]{1,0:T(8,128)S(1)}, u32[]{:S(2)}, u32[]{:S(2)}) collective-permute-start(f32[32,1152]{1,0:T(8,128)S(1)} %bitcast_add_fusion.16), channel_id=1, source_target_pairs={{0,2},{2,6},{6,10},{10,14},{14,12},{12,8},{8,4},{4,0},{1,3},{3,7},... | collective-permute-start | bytes 442376 | tf_op jit(solution)/shard_map/ppermute | solution.py:85
  149.3 8.6 %collective-permute-start.25 = (f32[32,1152]{1,0:T(8,128)S(1)}, f32[32,1152]{1,0:T(8,128)S(1)}, u32[]{:S(2)}, u32[]{:S(2)}) collective-permute-start(f32[32,1152]{1,0:T(8,128)S(1)} %bitcast_add_fusion.9), channel_id=1, source_target_pairs={{2,0},{6,2},{10,6},{14,10},{12,14},{8,12},{4,8},{0,4},{3,1},{7,3},... | collective-permute-start | bytes 442376 | tf_op jit(solution)/shard_map/ppermute | solution.py:85
  152.4 5.9 %collective-permute-start.12 = (f32[32,1152]{1,0:T(8,128)S(1)}, f32[32,1152]{1,0:T(8,128)S(1)}, u32[]{:S(2)}, u32[]{:S(2)}) collective-permute-start(f32[32,1152]{1,0:T(8,128)S(1)} %bitcast_add_fusion.15), channel_id=1, source_target_pairs={{0,2},{2,6},{6,10},{10,14},{14,12},{12,8},{8,4},{4,0},{1,3},{3,7},... | collective-permute-start | bytes 442376 | tf_op jit(solution)/shard_map/ppermute | solution.py:85
  157.8 19.3 %collective-permute-start.7 = (bf16[512,4,128]{0,2,1:T(8,128)(2,1)S(1)}, bf16[512,4,128]{0,2,1:T(8,128)(2,1)S(1)}, u32[]{:S(2)}, u32[]{:S(2)}) collective-permute-start(bf16[512,4,128]{0,2,1:T(8,128)(2,1)S(1)} %bitcast.249), channel_id=1, source_target_pairs={{0,1},{1,0},{2,3},{3,2},{4,5},{5,4},{6,7},{7,6},{8,9},{9,8},{10,11... | collective-permute-start | bytes 1572872 | tf_op jit(solution)/shard_map/ppermute | solution.py:26
  158.0 6.3 %collective-permute-start.26 = (f32[32,1152]{1,0:T(8,128)S(1)}, f32[32,1152]{1,0:T(8,128)S(1)}, u32[]{:S(2)}, u32[]{:S(2)}) collective-permute-start(f32[32,1152]{1,0:T(8,128)S(1)} %bitcast_add_fusion.8), channel_id=1, source_target_pairs={{2,0},{6,2},{10,6},{14,10},{12,14},{8,12},{4,8},{0,4},{3,1},{7,3},... | collective-permute-start | bytes 442376 | tf_op jit(solution)/shard_map/ppermute | solution.py:85
  158.4 6.3 %collective-permute-start.13 = (f32[32,1152]{1,0:T(8,128)S(1)}, f32[32,1152]{1,0:T(8,128)S(1)}, u32[]{:S(2)}, u32[]{:S(2)}) collective-permute-start(f32[32,1152]{1,0:T(8,128)S(1)} %bitcast_add_fusion.14), channel_id=1, source_target_pairs={{0,2},{2,6},{6,10},{10,14},{14,12},{12,8},{8,4},{4,0},{1,3},{3,7},... | collective-permute-start | bytes 442376 | tf_op jit(solution)/shard_map/ppermute | solution.py:85
  164.3 5.4 %collective-permute-start.27 = (f32[32,1152]{1,0:T(8,128)S(1)}, f32[32,1152]{1,0:T(8,128)S(1)}, u32[]{:S(2)}, u32[]{:S(2)}) collective-permute-start(f32[32,1152]{1,0:T(8,128)S(1)} %bitcast_add_fusion.7), channel_id=1, source_target_pairs={{2,0},{6,2},{10,6},{14,10},{12,14},{8,12},{4,8},{0,4},{3,1},{7,3},... | collective-permute-start | bytes 442376 | tf_op jit(solution)/shard_map/ppermute | solution.py:85
  164.7 5.4 %collective-permute-start.14 = (f32[32,1152]{1,0:T(8,128)S(1)}, f32[32,1152]{1,0:T(8,128)S(1)}, u32[]{:S(2)}, u32[]{:S(2)}) collective-permute-start(f32[32,1152]{1,0:T(8,128)S(1)} %bitcast_add_fusion.13), channel_id=1, source_target_pairs={{0,2},{2,6},{6,10},{10,14},{14,12},{12,8},{8,4},{4,0},{1,3},{3,7},... | collective-permute-start | bytes 442376 | tf_op jit(solution)/shard_map/ppermute | solution.py:85
  169.7 5.2 %collective-permute-start.28 = (f32[32,1152]{1,0:T(8,128)S(1)}, f32[32,1152]{1,0:T(8,128)S(1)}, u32[]{:S(2)}, u32[]{:S(2)}) collective-permute-start(f32[32,1152]{1,0:T(8,128)S(1)} %bitcast_add_fusion.6), channel_id=1, source_target_pairs={{2,0},{6,2},{10,6},{14,10},{12,14},{8,12},{4,8},{0,4},{3,1},{7,3},... | collective-permute-start | bytes 442376 | tf_op jit(solution)/shard_map/ppermute | solution.py:85
  170.2 5.2 %collective-permute-start.15 = (f32[32,1152]{1,0:T(8,128)S(1)}, f32[32,1152]{1,0:T(8,128)S(1)}, u32[]{:S(2)}, u32[]{:S(2)}) collective-permute-start(f32[32,1152]{1,0:T(8,128)S(1)} %bitcast_add_fusion.12), channel_id=1, source_target_pairs={{0,2},{2,6},{6,10},{10,14},{14,12},{12,8},{8,4},{4,0},{1,3},{3,7},... | collective-permute-start | bytes 442376 | tf_op jit(solution)/shard_map/ppermute | solution.py:85
  174.9 9.3 %collective-permute-start.29 = (bf16[32,1152]{1,0:T(8,128)(2,1)S(1)}, bf16[32,1152]{1,0:T(8,128)(2,1)S(1)}, u32[]{:S(2)}, u32[]{:S(2)}) collective-permute-start(bf16[32,1152]{1,0:T(8,128)(2,1)S(1)} %get-tuple-element.35), channel_id=1, source_target_pairs={{2,0},{6,2},{10,6},{14,10},{12,14},{8,12},{4,8},{0,4},{3,1},{7,3},... | collective-permute-start | bytes 221192 | tf_op jit(solution)/shard_map/ppermute | solution.py:93
  175.4 9.9 %collective-permute-start.16 = (bf16[32,1152]{1,0:T(8,128)(2,1)S(1)}, bf16[32,1152]{1,0:T(8,128)(2,1)S(1)}, u32[]{:S(2)}, u32[]{:S(2)}) collective-permute-start(bf16[32,1152]{1,0:T(8,128)(2,1)S(1)} %get-tuple-element.33), channel_id=1, source_target_pairs={{0,2},{2,6},{6,10},{10,14},{14,12},{12,8},{8,4},{4,0},{1,3},{3,7},... | collective-permute-start | bytes 221192 | tf_op jit(solution)/shard_map/ppermute | solution.py:93
  177.9 21.3 %collective-permute-start.9 = (bf16[1024,1,128]{0,2,1:T(8,128)(2,1)S(1)}, bf16[1024,1,128]{0,2,1:T(8,128)(2,1)S(1)}, u32[]{:S(2)}, u32[]{:S(2)}) collective-permute-start(bf16[1024,1,128]{0,2,1:T(8,128)(2,1)S(1)} %get-tuple-element.48), channel_id=1, source_target_pairs={{2,0},{4,2},{6,4},{8,6},{10,8},{12,10},{14,12},{3,1},{5,3},{7,5},{... | collective-permute-start | bytes 786440 | tf_op jit(solution)/shard_map/ppermute | solution.py:20
  179.2 20.0 %collective-permute-start.8 = (bf16[1024,1,128]{0,2,1:T(8,128)(2,1)S(1)}, bf16[1024,1,128]{0,2,1:T(8,128)(2,1)S(1)}, u32[]{:S(2)}, u32[]{:S(2)}) collective-permute-start(bf16[1024,1,128]{0,2,1:T(8,128)(2,1)S(1)} %get-tuple-element.49), channel_id=1, source_target_pairs={{0,2},{2,4},{4,6},{6,8},{8,10},{10,12},{12,14},{1,3},{3,5},{5,7},{... | collective-permute-start | bytes 786440 | tf_op jit(solution)/shard_map/ppermute | solution.py:19
  184.3 5.4 %collective-permute-start.30 = (bf16[32,1152]{1,0:T(8,128)(2,1)S(1)}, bf16[32,1152]{1,0:T(8,128)(2,1)S(1)}, u32[]{:S(2)}, u32[]{:S(2)}) collective-permute-start(bf16[32,1152]{1,0:T(8,128)(2,1)S(1)} %collective-permute-done.29), channel_id=1, source_target_pairs={{2,0},{6,2},{10,6},{14,10},{12,14},{8,12},{4,8},{0,4},{3,1},{7,3},... | collective-permute-start | bytes 221192 | tf_op jit(solution)/shard_map/ppermute | solution.py:93
  185.3 6.8 %collective-permute-start.17 = (bf16[32,1152]{1,0:T(8,128)(2,1)S(1)}, bf16[32,1152]{1,0:T(8,128)(2,1)S(1)}, u32[]{:S(2)}, u32[]{:S(2)}) collective-permute-start(bf16[32,1152]{1,0:T(8,128)(2,1)S(1)} %collective-permute-done.16), channel_id=1, source_target_pairs={{0,2},{2,6},{6,10},{10,14},{14,12},{12,8},{8,4},{4,0},{1,3},{3,7},... | collective-permute-start | bytes 221192 | tf_op jit(solution)/shard_map/ppermute | solution.py:93
  189.7 4.9 %collective-permute-start.31 = (bf16[32,1152]{1,0:T(8,128)(2,1)S(1)}, bf16[32,1152]{1,0:T(8,128)(2,1)S(1)}, u32[]{:S(2)}, u32[]{:S(2)}) collective-permute-start(bf16[32,1152]{1,0:T(8,128)(2,1)S(1)} %collective-permute-done.30), channel_id=1, source_target_pairs={{2,0},{6,2},{10,6},{14,10},{12,14},{8,12},{4,8},{0,4},{3,1},{7,3},... | collective-permute-start | bytes 221192 | tf_op jit(solution)/shard_map/ppermute | solution.py:93
  194.6 11.4 %collective-permute-start.32 = (bf16[32,1152]{1,0:T(8,128)(2,1)S(1)}, bf16[32,1152]{1,0:T(8,128)(2,1)S(1)}, u32[]{:S(2)}, u32[]{:S(2)}) collective-permute-start(bf16[32,1152]{1,0:T(8,128)(2,1)S(1)} %collective-permute-done.31), channel_id=1, source_target_pairs={{2,0},{6,2},{10,6},{14,10},{12,14},{8,12},{4,8},{0,4},{3,1},{7,3},... | collective-permute-start | bytes 221192 | tf_op jit(solution)/shard_map/ppermute | solution.py:93
  196.7 9.4 %collective-permute-start.19 = (bf16[32,1152]{1,0:T(8,128)(2,1)S(1)}, bf16[32,1152]{1,0:T(8,128)(2,1)S(1)}, u32[]{:S(2)}, u32[]{:S(2)}) collective-permute-start(bf16[32,1152]{1,0:T(8,128)(2,1)S(1)} %collective-permute-done.18), channel_id=1, source_target_pairs={{0,2},{2,6},{6,10},{10,14},{14,12},{12,8},{8,4},{4,0},{1,3},{3,7},... | collective-permute-start | bytes 221192 | tf_op jit(solution)/shard_map/ppermute | solution.py:93
  214.9 5.2 %collective-permute-start.22 = (bf16[32,1152]{1,0:T(8,128)(2,1)S(1)}, bf16[32,1152]{1,0:T(8,128)(2,1)S(1)}, u32[]{:S(2)}, u32[]{:S(2)}) collective-permute-start(bf16[32,1152]{1,0:T(8,128)(2,1)S(1)} %collective-permute-done.21), channel_id=1, source_target_pairs={{0,2},{2,6},{6,10},{10,14},{14,12},{12,8},{8,4},{4,0},{1,3},{3,7},... | collective-permute-start | bytes 221192 | tf_op jit(solution)/shard_map/ppermute | solution.py:93
  (18 other events, 131.8 us)
Sparse Core Ops, SparseCore 0:
  10.0 74.9 all-gather.1
  93.4 7.8 reduce-scatter.1

commit v10 on v7

--- a/solution.py
+++ b/solution.py
@@ -26,11 +26,6 @@
     other = lax.ppermute(x, "chan", SWAP)
     both = jnp.concatenate([x, other], 0)
     return jnp.roll(both, lax.axis_index("chan") * x.shape[0], axis=0)
-
-
-def chan_gather_into(mine, other):
-    both = jnp.concatenate([mine, other], 0)
-    return jnp.roll(both, lax.axis_index("chan") * mine.shape[0], axis=0)
 
 
 def chan_scatter_sum(x):
@@ -119,18 +114,19 @@
                 shard_piece[:, tap_index, :], window, preferred_element_type=jnp.float32
             )
         pre = lax.psum_scatter(partial_value, "chan", scatter_dimension=0, tiled=True)
+        index = lax.axis_index("chan")
+        gamma_mine = lax.dynamic_slice_in_dim(gdn_gamma, index * lat_local, lat_local, 1)
+        gamma_theirs = lax.dynamic_slice_in_dim(gdn_gamma, (1 - index) * lat_local, lat_local, 1)
+        gamma_local = jnp.concatenate([gamma_mine, gamma_theirs], 1)
         squares_own = (pre * pre).astype(jnp.bfloat16)
-        squares = chan_gather(squares_own)
-        norm_value = gdn_beta[:, None] + jnp.dot(gdn_gamma, squares, preferred_element_type=jnp.float32)
+        squares = jnp.concatenate([squares_own, lax.ppermute(squares_own, "chan", SWAP)], 0)
+        norm_value = gdn_beta[:, None] + jnp.dot(gamma_local, squares, preferred_element_type=jnp.float32)
         inverse = lax.rsqrt(norm_value)
         latent = (pre * inverse).astype(jnp.bfloat16)
         upstream = cotangent.reshape(lat_local, pixels).astype(jnp.float32)
         shares = (-0.5 * upstream * pre * inverse * inverse * inverse).astype(jnp.bfloat16)
-        index = lax.axis_index("chan")
-        gamma_mine = lax.dynamic_slice_in_dim(gdn_gamma, index * lat_local, lat_local, 1)
-        gamma_theirs = lax.dynamic_slice_in_dim(gdn_gamma, (1 - index) * lat_local, lat_local, 1)
-        gamma_cols = chan_gather_into(gamma_mine, lax.ppermute(gamma_theirs, "chan", SWAP))
-        shares_all = chan_gather(shares)
+        gamma_cols = jnp.concatenate([gamma_mine, lax.ppermute(gamma_theirs, "chan", SWAP)], 0)
+        shares_all = jnp.concatenate([shares, lax.ppermute(shares, "chan", SWAP)], 0)
         back_sum = lax.dot_general(
             gamma_cols, shares_all, (((0,), (0,)), ((), ())), preferred_element_type=jnp.float32
         )
@@ -144,7 +140,7 @@
             (joined_total,) = ring_sum([joined], ring)
         else:
             joined_total = lax.psum(joined, "row")
-        gamma_total = joined_total[:, :lat_all]
+        gamma_total = jnp.roll(joined_total[:, :lat_all], index * lat_local, axis=1)
         beta_total = joined_total[:, lat_all]
         scale_factor = 1.0 / math.sqrt(pixels * lax.axis_size("row"))
         grad_gamma = gamma_total * scale_factor

time: 215 us -> 218 us (1.014)
  other arithmetic: 11.9 us -> 15.7 us
    unnamed x51 -> x57, local copies, waits for them, and re-layouts: 5.53 us -> 5.87 us
  transfers between devices with their start and end apart: 38 -> 38, of which waited for: 15 -> 17; matrix products, arithmetic and copies ran while one was open for 15% -> 17% of each run, Pallas kernels for 0% -> 0%
where the time goes in v10:
time: 218 us; the launch traced here: 217 us
  waiting for transfers between devices  98.5 us (45%)
  starting transfers between devices  43.2 us (20%)
  between operations  25.6 us (12%)
  matrix products  20.6 us (9%)
  other arithmetic  15.7 us (7%)
  local copies, waits for them, and re-layouts  13.8 us (6%)
    all_gather x1, waiting for transfers between devices, per_device(): shard_piece = lax.all_gather(conv_weight, 'row', axis=0, tiled=True)  59.5 us
    ppermute x14, waiting for transfers between devices, ring_sum(): got = lax.ppermute(carry[part], 'row', moves[part])  18.8 us
    ppermute x14, starting transfers between devices, ring_sum(): gathered[part].append(lax.ppermute(gathered[part][-1], 'row', moves[part]))  16.6 us
    ppermute x14, waiting for transfers between devices, ring_sum(): gathered[part].append(lax.ppermute(gathered[part][-1], 'row', moves[part]))  15.3 us
    ppermute x14, starting transfers between devices, ring_sum(): got = lax.ppermute(carry[part], 'row', moves[part])  15 us
    dot_general x9, matrix products, per_device(): jnp.dot(shard_piece[:, tap_index, :], window, preferred_element_type=jnp....  8.28 us
    ppermute x2, starting transfers between devices, extended(): before = lax.ppermute(last, axis, up)  8.24 us
    unnamed x57, local copies, waits for them, and re-layouts  5.87 us
  transfers between devices with their start and end apart: 38, of which 17 were waited for; matrix products, arithmetic and copies ran while one was open for 17% of the time, Pallas kernels for 0%

profile of v10, /device:TPU:0, one launch (start us, length us, event | category | flops | bytes accessed | tf_op | source)
XLA Modules:
  0.0 217.3 jit_solution(12563974429160119011)
XLA Ops:
  9.2 4.9 %collective-permute-start = (bf16[212,1,128]{2,1,0:T(2,128)(2,1)S(1)}, bf16[212,1,128]{2,1,0:T(2,128)(2,1)S(1)}, u32[]{:S(2)}, u32[]{:S(2)}) collective-permute-start(bf16[212,1,128]{2,1,0:T(2,128)(2,1)S(1)} %get-tuple-element.54), channel_id=1, source_target_pairs={{0,2},{2,4},{4,6},{6,8},{8,10},{10,12},{12,14},{1,3},{3,5},{5,7},{... | collective-permute-start | bytes 162824 | tf_op jit(solution)/shard_map/ppermute | solution.py:19
  16.4 4.2 %collective-permute-done.1 = bf16[212,1,128]{2,1,0:T(2,128)(2,1)S(1)} collective-permute-done((bf16[212,1,128]{2,1,0:T(2,128)(2,1)S(1)}, bf16[212,1,128]{2,1,0:T(2,128)(2,1)S(1)}, u32[]{:S(2)}, u32[]{:S(2)}) %collective-permute-start.1) | collective-permute-done | bytes 54304 | tf_op jit(solution)/shard_map/ppermute | solution.py:20
  20.7 2.1 fusion.38
  25.5 59.5 %all-gather.2.cloned.1.call-done = bf16[1024,9,212]{0,2,1:T(8,128)(2,1)} async-done(((bf16[128,9,212]{0,2,1:T(8,128)(2,1)}), bf16[1024,9,212]{0,2,1:T(8,128)(2,1)}) %all-gather.2.cloned.1.call-update) | async-done | bytes 3907600 | tf_op jit(solution)/shard_map/all_gather | solution.py:107
  85.0 1.6 fusion.41
  91.0 2.3 %bitcast_add_fusion = f32[1024,512]{0,1:T(8,128)} fusion(f32[512,1024]{1,0:T(8,128)S(1)} %fusion.55, f32[512,1024]{1,0:T(8,128)S(1)} %fusion.53, f32[512,1024]{1,0:T(8,128)S(1)} %fusion.51, f32[1024,512]{0,1:T(8,128)S(1)} %fusion.49, f32[512,1024]{1,0:T(8,128)S(1)} %fusion.47, f32[512,1024]{1,0:T(8,128)S(1)} %fusion.45, f32[512,1024]{1,0:T(8,128)S(1)} %fusion.41, ...), kind=kOutput, calls=%fused_computation.15 | convolution fusion | flops 226492416 | bytes 19537920 | tf_op jit(solution)/shard_map/dot_general | solution.py:113
  114.1 3.7 %fusion.17 = (bf16[512,512]{0,1:T(8,128)(2,1)}, f32[512,512]{0,1:T(8,128)}, bf16[512,512]{0,1:T(8,128)(2,1)}) fusion(f32[512,512]{0,1:T(8,128)} %reduce-scatter.2.cloned.1.call-done, f32[512,4,128]{0,2,1:T(8,128)S(1)} %copy.14, bf16[512,512]{0,1:T(8,128)(2,1)S(1)} %collective-permute-done.2, bf16[512,512]{0,1:T(8,128)(2,1)S(1)} %multiply_convert_fusion.1, ...), kind=kOutput, calls=%fused_computation.38 | convolution fusion | flops 543686656 | bytes 6293504 | tf_op jit(solution)/shard_map/dot_general | solution.py:123
  117.9 1.9 fusion.12
  123.4 2.1 copy.15
  125.5 1.7 collective-permute-done.8
  130.4 3.0 %collective-permute-done.9 = f32[32,1152]{1,0:T(8,128)S(1)} collective-permute-done((f32[32,1152]{1,0:T(8,128)S(1)}, f32[32,1152]{1,0:T(8,128)S(1)}, u32[]{:S(2)}, u32[]{:S(2)}) %collective-permute-start.9) | collective-permute-done | bytes 147488 | tf_op jit(solution)/shard_map/ppermute | solution.py:80
  133.5 1.5 collective-permute-start.10
  135.6 3.0 %collective-permute-done.10 = f32[32,1152]{1,0:T(8,128)S(1)} collective-permute-done((f32[32,1152]{1,0:T(8,128)S(1)}, f32[32,1152]{1,0:T(8,128)S(1)}, u32[]{:S(2)}, u32[]{:S(2)}) %collective-permute-start.10) | collective-permute-done | bytes 147488 | tf_op jit(solution)/shard_map/ppermute | solution.py:80
  138.7 1.5 collective-permute-start.11
  140.9 2.1 fusion.11
  143.9 1.5 collective-permute-start.12
  146.1 3.3 %collective-permute-done.12 = f32[32,1152]{1,0:T(8,128)S(1)} collective-permute-done((f32[32,1152]{1,0:T(8,128)S(1)}, f32[32,1152]{1,0:T(8,128)S(1)}, u32[]{:S(2)}, u32[]{:S(2)}) %collective-permute-start.12) | collective-permute-done | bytes 147488 | tf_op jit(solution)/shard_map/ppermute | solution.py:80
  151.6 3.0 %collective-permute-done.13 = f32[32,1152]{1,0:T(8,128)S(1)} collective-permute-done((f32[32,1152]{1,0:T(8,128)S(1)}, f32[32,1152]{1,0:T(8,128)S(1)}, u32[]{:S(2)}, u32[]{:S(2)}) %collective-permute-start.13) | collective-permute-done | bytes 147488 | tf_op jit(solution)/shard_map/ppermute | solution.py:80
  156.8 3.8 %collective-permute-done.14 = f32[32,1152]{1,0:T(8,128)S(1)} collective-permute-done((f32[32,1152]{1,0:T(8,128)S(1)}, f32[32,1152]{1,0:T(8,128)S(1)}, u32[]{:S(2)}, u32[]{:S(2)}) %collective-permute-start.14) | collective-permute-done | bytes 147488 | tf_op jit(solution)/shard_map/ppermute | solution.py:80
  163.6 3.4 %collective-permute-start.6 = (bf16[1024,1,128]{0,2,1:T(8,128)(2,1)S(1)}, bf16[1024,1,128]{0,2,1:T(8,128)(2,1)S(1)}, u32[]{:S(2)}, u32[]{:S(2)}) collective-permute-start(bf16[1024,1,128]{0,2,1:T(8,128)(2,1)S(1)} %get-tuple-element.43), channel_id=1, source_target_pairs={{0,2},{2,4},{4,6},{6,8},{8,10},{10,12},{12,14},{1,3},{3,5},{5,7},{... | collective-permute-start | bytes 786440 | tf_op jit(solution)/shard_map/ppermute | solution.py:19
  168.8 2.7 %collective-permute-start.16 = (bf16[32,1152]{1,0:T(8,128)(2,1)S(1)}, bf16[32,1152]{1,0:T(8,128)(2,1)S(1)}, u32[]{:S(2)}, u32[]{:S(2)}) collective-permute-start(bf16[32,1152]{1,0:T(8,128)(2,1)S(1)} %collective-permute-done.15), channel_id=1, source_target_pairs={{0,2},{2,6},{6,10},{10,14},{14,12},{12,8},{8,4},{4,0},{1,3},{3,7},... | collective-permute-start | bytes 221192 | tf_op jit(solution)/shard_map/ppermute | solution.py:86
  171.6 5.3 %collective-permute-done.16 = bf16[32,1152]{1,0:T(8,128)(2,1)S(1)} collective-permute-done((bf16[32,1152]{1,0:T(8,128)(2,1)S(1)}, bf16[32,1152]{1,0:T(8,128)(2,1)S(1)}, u32[]{:S(2)}, u32[]{:S(2)}) %collective-permute-start.16) | collective-permute-done | bytes 73760 | tf_op jit(solution)/shard_map/ppermute | solution.py:86
  176.9 2.5 %collective-permute-start.17 = (bf16[32,1152]{1,0:T(8,128)(2,1)S(1)}, bf16[32,1152]{1,0:T(8,128)(2,1)S(1)}, u32[]{:S(2)}, u32[]{:S(2)}) collective-permute-start(bf16[32,1152]{1,0:T(8,128)(2,1)S(1)} %collective-permute-done.16), channel_id=1, source_target_pairs={{0,2},{2,6},{6,10},{10,14},{14,12},{12,8},{8,4},{4,0},{1,3},{3,7},... | collective-permute-start | bytes 221192 | tf_op jit(solution)/shard_map/ppermute | solution.py:86
  179.5 1.9 collective-permute-done.17
  181.3 2.4 %collective-permute-start.18 = (bf16[32,1152]{1,0:T(8,128)(2,1)S(1)}, bf16[32,1152]{1,0:T(8,128)(2,1)S(1)}, u32[]{:S(2)}, u32[]{:S(2)}) collective-permute-start(bf16[32,1152]{1,0:T(8,128)(2,1)S(1)} %collective-permute-done.17), channel_id=1, source_target_pairs={{0,2},{2,6},{6,10},{10,14},{14,12},{12,8},{8,4},{4,0},{1,3},{3,7},... | collective-permute-start | bytes 221192 | tf_op jit(solution)/shard_map/ppermute | solution.py:86
  190.7 2.0 collective-permute-start.19
  192.8 2.6 %collective-permute-done.19 = bf16[32,1152]{1,0:T(8,128)(2,1)S(1)} collective-permute-done((bf16[32,1152]{1,0:T(8,128)(2,1)S(1)}, bf16[32,1152]{1,0:T(8,128)(2,1)S(1)}, u32[]{:S(2)}, u32[]{:S(2)}) %collective-permute-start.19) | collective-permute-done | bytes 73760 | tf_op jit(solution)/shard_map/ppermute | solution.py:86
  195.5 2.3 %collective-permute-start.20 = (bf16[32,1152]{1,0:T(8,128)(2,1)S(1)}, bf16[32,1152]{1,0:T(8,128)(2,1)S(1)}, u32[]{:S(2)}, u32[]{:S(2)}) collective-permute-start(bf16[32,1152]{1,0:T(8,128)(2,1)S(1)} %collective-permute-done.19), channel_id=1, source_target_pairs={{0,2},{2,6},{6,10},{10,14},{14,12},{12,8},{8,4},{4,0},{1,3},{3,7},... | collective-permute-start | bytes 221192 | tf_op jit(solution)/shard_map/ppermute | solution.py:86
  197.9 1.9 collective-permute-done.20
  199.8 2.3 %collective-permute-start.21 = (bf16[32,1152]{1,0:T(8,128)(2,1)S(1)}, bf16[32,1152]{1,0:T(8,128)(2,1)S(1)}, u32[]{:S(2)}, u32[]{:S(2)}) collective-permute-start(bf16[32,1152]{1,0:T(8,128)(2,1)S(1)} %collective-permute-done.20), channel_id=1, source_target_pairs={{0,2},{2,6},{6,10},{10,14},{14,12},{12,8},{8,4},{4,0},{1,3},{3,7},... | collective-permute-start | bytes 221192 | tf_op jit(solution)/shard_map/ppermute | solution.py:86
  202.2 1.9 collective-permute-done.21
  208.7 1.8 fusion.2
  (173 shorter events, 51.8 us)
Async XLA Ops:
  7.2 77.8 %all-gather.2.cloned.1.call-start = ((), (), s32[]{:S(2)}) async-start(), calls=%async_computation.1 | async-start | bytes 4478976 | tf_op jit(solution)/shard_map/all_gather | solution.py:107
  7.9 100.1 %reduce-scatter.2.cloned.1.call-start = ((), (), s32[]{:S(2)}) async-start(), calls=%async_computation.2 | async-start | bytes 3145728 | tf_op jit(solution)/shard_map/reduce_scatter | solution.py:116
  9.2 7.3 %collective-permute-start = (bf16[212,1,128]{2,1,0:T(2,128)(2,1)S(1)}, bf16[212,1,128]{2,1,0:T(2,128)(2,1)S(1)}, u32[]{:S(2)}, u32[]{:S(2)}) collective-permute-start(bf16[212,1,128]{2,1,0:T(2,128)(2,1)S(1)} %get-tuple-element.54), channel_id=1, source_target_pairs={{0,2},{2,4},{4,6},{6,8},{8,10},{10,12},{12,14},{1,3},{3,5},{5,7},{... | collective-permute-start | bytes 162824 | tf_op jit(solution)/shard_map/ppermute | solution.py:19
  14.1 6.6 %collective-permute-start.1 = (bf16[212,1,128]{2,1,0:T(2,128)(2,1)S(1)}, bf16[212,1,128]{2,1,0:T(2,128)(2,1)S(1)}, u32[]{:S(2)}, u32[]{:S(2)}) collective-permute-start(bf16[212,1,128]{2,1,0:T(2,128)(2,1)S(1)} %get-tuple-element.55), channel_id=1, source_target_pairs={{2,0},{4,2},{6,4},{8,6},{10,8},{12,10},{14,12},{3,1},{5,3},{7,5},{... | collective-permute-start | bytes 162824 | tf_op jit(solution)/shard_map/ppermute | solution.py:20
  95.4 45.4 %collective-permute-start.3 = (bf16[512,512]{1,0:T(8,128)(2,1)}, bf16[512,512]{1,0:T(8,128)(2,1)}, u32[]{:S(2)}, u32[]{:S(2)}) collective-permute-start(bf16[512,512]{1,0:T(8,128)(2,1)} %get-tuple-element.45), channel_id=1, source_target_pairs={{0,1},{1,0},{2,3},{3,2},{4,5},{5,4},{6,7},{7,6},{8,9},{9,8},{10,11... | collective-permute-start | bytes 1572872 | tf_op jit(solution)/shard_map/ppermute | solution.py:128
  109.4 4.7 %collective-permute-start.2 = (bf16[512,512]{0,1:T(8,128)(2,1)S(1)}, bf16[512,512]{0,1:T(8,128)(2,1)S(1)}, u32[]{:S(2)}, u32[]{:S(2)}) collective-permute-start(bf16[512,512]{0,1:T(8,128)(2,1)S(1)} %multiply_convert_fusion.1), channel_id=1, source_target_pairs={{0,1},{1,0},{2,3},{3,2},{4,5},{5,4},{6,7},{7,6},{8,9},{9,8},{10,11... | collective-permute-start | bytes 1572872 | tf_op jit(solution)/shard_map/ppermute | solution.py:122
  117.8 23.1 %collective-permute-start.4 = (bf16[512,512]{0,1:T(8,128)(2,1)}, bf16[512,512]{0,1:T(8,128)(2,1)}, u32[]{:S(2)}, u32[]{:S(2)}) collective-permute-start(bf16[512,512]{0,1:T(8,128)(2,1)} %get-tuple-element.31), channel_id=1, source_target_pairs={{0,1},{1,0},{2,3},{3,2},{4,5},{5,4},{6,7},{7,6},{8,9},{9,8},{10,11... | collective-permute-start | bytes 1572872 | tf_op jit(solution)/shard_map/ppermute | solution.py:129
  120.7 6.5 %collective-permute-start.8 = (f32[32,1152]{1,0:T(8,128)}, f32[32,1152]{1,0:T(8,128)}, u32[]{:S(2)}, u32[]{:S(2)}) collective-permute-start(f32[32,1152]{1,0:T(8,128)} %select_bitcast_fusion.1), channel_id=1, source_target_pairs={{0,2},{2,6},{6,10},{10,14},{14,12},{12,8},{8,4},{4,0},{1,3},{3,7},... | collective-permute-start | bytes 442376 | tf_op jit(solution)/shard_map/ppermute | solution.py:80
  122.8 6.8 %collective-permute-start.22 = (f32[32,1152]{1,0:T(8,128)}, f32[32,1152]{1,0:T(8,128)S(1)}, u32[]{:S(2)}, u32[]{:S(2)}) collective-permute-start(f32[32,1152]{1,0:T(8,128)} %select_bitcast_fusion), channel_id=1, source_target_pairs={{2,0},{6,2},{10,6},{14,10},{12,14},{8,12},{4,8},{0,4},{3,1},{7,3},... | collective-permute-start | bytes 442376 | tf_op jit(solution)/shard_map/ppermute | solution.py:80
  128.1 5.4 %collective-permute-start.9 = (f32[32,1152]{1,0:T(8,128)S(1)}, f32[32,1152]{1,0:T(8,128)S(1)}, u32[]{:S(2)}, u32[]{:S(2)}) collective-permute-start(f32[32,1152]{1,0:T(8,128)S(1)} %bitcast_add_fusion.18), channel_id=1, source_target_pairs={{0,2},{2,6},{6,10},{10,14},{14,12},{12,8},{8,4},{4,0},{1,3},{3,7},... | collective-permute-start | bytes 442376 | tf_op jit(solution)/shard_map/ppermute | solution.py:80
  129.6 5.4 %collective-permute-start.23 = (f32[32,1152]{1,0:T(8,128)S(1)}, f32[32,1152]{1,0:T(8,128)S(1)}, u32[]{:S(2)}, u32[]{:S(2)}) collective-permute-start(f32[32,1152]{1,0:T(8,128)S(1)} %bitcast_add_fusion.11), channel_id=1, source_target_pairs={{2,0},{6,2},{10,6},{14,10},{12,14},{8,12},{4,8},{0,4},{3,1},{7,3},... | collective-permute-start | bytes 442376 | tf_op jit(solution)/shard_map/ppermute | solution.py:80
  133.5 5.2 %collective-permute-start.10 = (f32[32,1152]{1,0:T(8,128)S(1)}, f32[32,1152]{1,0:T(8,128)S(1)}, u32[]{:S(2)}, u32[]{:S(2)}) collective-permute-start(f32[32,1152]{1,0:T(8,128)S(1)} %bitcast_add_fusion.17), channel_id=1, source_target_pairs={{0,2},{2,6},{6,10},{10,14},{14,12},{12,8},{8,4},{4,0},{1,3},{3,7},... | collective-permute-start | bytes 442376 | tf_op jit(solution)/shard_map/ppermute | solution.py:80
  135.0 5.2 %collective-permute-start.24 = (f32[32,1152]{1,0:T(8,128)S(1)}, f32[32,1152]{1,0:T(8,128)S(1)}, u32[]{:S(2)}, u32[]{:S(2)}) collective-permute-start(f32[32,1152]{1,0:T(8,128)S(1)} %bitcast_add_fusion.10), channel_id=1, source_target_pairs={{2,0},{6,2},{10,6},{14,10},{12,14},{8,12},{4,8},{0,4},{3,1},{7,3},... | collective-permute-start | bytes 442376 | tf_op jit(solution)/shard_map/ppermute | solution.py:80
  138.7 5.2 %collective-permute-start.11 = (f32[32,1152]{1,0:T(8,128)S(1)}, f32[32,1152]{1,0:T(8,128)S(1)}, u32[]{:S(2)}, u32[]{:S(2)}) collective-permute-start(f32[32,1152]{1,0:T(8,128)S(1)} %bitcast_add_fusion.16), channel_id=1, source_target_pairs={{0,2},{2,6},{6,10},{10,14},{14,12},{12,8},{8,4},{4,0},{1,3},{3,7},... | collective-permute-start | bytes 442376 | tf_op jit(solution)/shard_map/ppermute | solution.py:80
  140.2 5.2 %collective-permute-start.25 = (f32[32,1152]{1,0:T(8,128)S(1)}, f32[32,1152]{1,0:T(8,128)S(1)}, u32[]{:S(2)}, u32[]{:S(2)}) collective-permute-start(f32[32,1152]{1,0:T(8,128)S(1)} %bitcast_add_fusion.9), channel_id=1, source_target_pairs={{2,0},{6,2},{10,6},{14,10},{12,14},{8,12},{4,8},{0,4},{3,1},{7,3},... | collective-permute-start | bytes 442376 | tf_op jit(solution)/shard_map/ppermute | solution.py:80
  143.0 19.8 %collective-permute-start.5 = (bf16[512,4,128]{0,2,1:T(8,128)(2,1)S(1)}, bf16[512,4,128]{0,2,1:T(8,128)(2,1)S(1)}, u32[]{:S(2)}, u32[]{:S(2)}) collective-permute-start(bf16[512,4,128]{0,2,1:T(8,128)(2,1)S(1)} %bitcast.244), channel_id=1, source_target_pairs={{0,1},{1,0},{2,3},{3,2},{4,5},{5,4},{6,7},{7,6},{8,9},{9,8},{10,11... | collective-permute-start | bytes 1572872 | tf_op jit(solution)/shard_map/ppermute | solution.py:26
  143.9 5.5 %collective-permute-start.12 = (f32[32,1152]{1,0:T(8,128)S(1)}, f32[32,1152]{1,0:T(8,128)S(1)}, u32[]{:S(2)}, u32[]{:S(2)}) collective-permute-start(f32[32,1152]{1,0:T(8,128)S(1)} %bitcast_add_fusion.15), channel_id=1, source_target_pairs={{0,2},{2,6},{6,10},{10,14},{14,12},{12,8},{8,4},{4,0},{1,3},{3,7},... | collective-permute-start | bytes 442376 | tf_op jit(solution)/shard_map/ppermute | solution.py:80
  145.4 5.5 %collective-permute-start.26 = (f32[32,1152]{1,0:T(8,128)S(1)}, f32[32,1152]{1,0:T(8,128)S(1)}, u32[]{:S(2)}, u32[]{:S(2)}) collective-permute-start(f32[32,1152]{1,0:T(8,128)S(1)} %bitcast_add_fusion.8), channel_id=1, source_target_pairs={{2,0},{6,2},{10,6},{14,10},{12,14},{8,12},{4,8},{0,4},{3,1},{7,3},... | collective-permute-start | bytes 442376 | tf_op jit(solution)/shard_map/ppermute | solution.py:80
  149.4 5.2 %collective-permute-start.13 = (f32[32,1152]{1,0:T(8,128)S(1)}, f32[32,1152]{1,0:T(8,128)S(1)}, u32[]{:S(2)}, u32[]{:S(2)}) collective-permute-start(f32[32,1152]{1,0:T(8,128)S(1)} %bitcast_add_fusion.14), channel_id=1, source_target_pairs={{0,2},{2,6},{6,10},{10,14},{14,12},{12,8},{8,4},{4,0},{1,3},{3,7},... | collective-permute-start | bytes 442376 | tf_op jit(solution)/shard_map/ppermute | solution.py:80
  150.9 5.2 %collective-permute-start.27 = (f32[32,1152]{1,0:T(8,128)S(1)}, f32[32,1152]{1,0:T(8,128)S(1)}, u32[]{:S(2)}, u32[]{:S(2)}) collective-permute-start(f32[32,1152]{1,0:T(8,128)S(1)} %bitcast_add_fusion.7), channel_id=1, source_target_pairs={{2,0},{6,2},{10,6},{14,10},{12,14},{8,12},{4,8},{0,4},{3,1},{7,3},... | collective-permute-start | bytes 442376 | tf_op jit(solution)/shard_map/ppermute | solution.py:80
  154.6 6.0 %collective-permute-start.14 = (f32[32,1152]{1,0:T(8,128)S(1)}, f32[32,1152]{1,0:T(8,128)S(1)}, u32[]{:S(2)}, u32[]{:S(2)}) collective-permute-start(f32[32,1152]{1,0:T(8,128)S(1)} %bitcast_add_fusion.13), channel_id=1, source_target_pairs={{0,2},{2,6},{6,10},{10,14},{14,12},{12,8},{8,4},{4,0},{1,3},{3,7},... | collective-permute-start | bytes 442376 | tf_op jit(solution)/shard_map/ppermute | solution.py:80
  156.2 6.0 %collective-permute-start.28 = (f32[32,1152]{1,0:T(8,128)S(1)}, f32[32,1152]{1,0:T(8,128)S(1)}, u32[]{:S(2)}, u32[]{:S(2)}) collective-permute-start(f32[32,1152]{1,0:T(8,128)S(1)} %bitcast_add_fusion.6), channel_id=1, source_target_pairs={{2,0},{6,2},{10,6},{14,10},{12,14},{8,12},{4,8},{0,4},{3,1},{7,3},... | collective-permute-start | bytes 442376 | tf_op jit(solution)/shard_map/ppermute | solution.py:80
  160.6 8.1 %collective-permute-start.15 = (bf16[32,1152]{1,0:T(8,128)(2,1)S(1)}, bf16[32,1152]{1,0:T(8,128)(2,1)S(1)}, u32[]{:S(2)}, u32[]{:S(2)}) collective-permute-start(bf16[32,1152]{1,0:T(8,128)(2,1)S(1)} %get-tuple-element.26), channel_id=1, source_target_pairs={{0,2},{2,6},{6,10},{10,14},{14,12},{12,8},{8,4},{4,0},{1,3},{3,7},... | collective-permute-start | bytes 221192 | tf_op jit(solution)/shard_map/ppermute | solution.py:86
  162.2 9.3 %collective-permute-start.29 = (bf16[32,1152]{1,0:T(8,128)(2,1)S(1)}, bf16[32,1152]{1,0:T(8,128)(2,1)S(1)}, u32[]{:S(2)}, u32[]{:S(2)}) collective-permute-start(bf16[32,1152]{1,0:T(8,128)(2,1)S(1)} %get-tuple-element.28), channel_id=1, source_target_pairs={{2,0},{6,2},{10,6},{14,10},{12,14},{8,12},{4,8},{0,4},{3,1},{7,3},... | collective-permute-start | bytes 221192 | tf_op jit(solution)/shard_map/ppermute | solution.py:86
  163.6 20.3 %collective-permute-start.6 = (bf16[1024,1,128]{0,2,1:T(8,128)(2,1)S(1)}, bf16[1024,1,128]{0,2,1:T(8,128)(2,1)S(1)}, u32[]{:S(2)}, u32[]{:S(2)}) collective-permute-start(bf16[1024,1,128]{0,2,1:T(8,128)(2,1)S(1)} %get-tuple-element.43), channel_id=1, source_target_pairs={{0,2},{2,4},{4,6},{6,8},{8,10},{10,12},{12,14},{1,3},{3,5},{5,7},{... | collective-permute-start | bytes 786440 | tf_op jit(solution)/shard_map/ppermute | solution.py:19
  166.9 16.9 %collective-permute-start.7 = (bf16[1024,1,128]{0,2,1:T(8,128)(2,1)S(1)}, bf16[1024,1,128]{0,2,1:T(8,128)(2,1)S(1)}, u32[]{:S(2)}, u32[]{:S(2)}) collective-permute-start(bf16[1024,1,128]{0,2,1:T(8,128)(2,1)S(1)} %get-tuple-element.42), channel_id=1, source_target_pairs={{2,0},{4,2},{6,4},{8,6},{10,8},{12,10},{14,12},{3,1},{5,3},{7,5},{... | collective-permute-start | bytes 786440 | tf_op jit(solution)/shard_map/ppermute | solution.py:20
  168.8 8.1 %collective-permute-start.16 = (bf16[32,1152]{1,0:T(8,128)(2,1)S(1)}, bf16[32,1152]{1,0:T(8,128)(2,1)S(1)}, u32[]{:S(2)}, u32[]{:S(2)}) collective-permute-start(bf16[32,1152]{1,0:T(8,128)(2,1)S(1)} %collective-permute-done.15), channel_id=1, source_target_pairs={{0,2},{2,6},{6,10},{10,14},{14,12},{12,8},{8,4},{4,0},{1,3},{3,7},... | collective-permute-start | bytes 221192 | tf_op jit(solution)/shard_map/ppermute | solution.py:86
  171.5 7.9 %collective-permute-start.30 = (bf16[32,1152]{1,0:T(8,128)(2,1)S(1)}, bf16[32,1152]{1,0:T(8,128)(2,1)S(1)}, u32[]{:S(2)}, u32[]{:S(2)}) collective-permute-start(bf16[32,1152]{1,0:T(8,128)(2,1)S(1)} %collective-permute-done.29), channel_id=1, source_target_pairs={{2,0},{6,2},{10,6},{14,10},{12,14},{8,12},{4,8},{0,4},{3,1},{7,3},... | collective-permute-start | bytes 221192 | tf_op jit(solution)/shard_map/ppermute | solution.py:86
  181.3 9.4 %collective-permute-start.18 = (bf16[32,1152]{1,0:T(8,128)(2,1)S(1)}, bf16[32,1152]{1,0:T(8,128)(2,1)S(1)}, u32[]{:S(2)}, u32[]{:S(2)}) collective-permute-start(bf16[32,1152]{1,0:T(8,128)(2,1)S(1)} %collective-permute-done.17), channel_id=1, source_target_pairs={{0,2},{2,6},{6,10},{10,14},{14,12},{12,8},{8,4},{4,0},{1,3},{3,7},... | collective-permute-start | bytes 221192 | tf_op jit(solution)/shard_map/ppermute | solution.py:86
  183.8 9.0 %collective-permute-start.32 = (bf16[32,1152]{1,0:T(8,128)(2,1)S(1)}, bf16[32,1152]{1,0:T(8,128)(2,1)S(1)}, u32[]{:S(2)}, u32[]{:S(2)}) collective-permute-start(bf16[32,1152]{1,0:T(8,128)(2,1)S(1)} %collective-permute-done.31), channel_id=1, source_target_pairs={{2,0},{6,2},{10,6},{14,10},{12,14},{8,12},{4,8},{0,4},{3,1},{7,3},... | collective-permute-start | bytes 221192 | tf_op jit(solution)/shard_map/ppermute | solution.py:86
  190.7 4.7 %collective-permute-start.19 = (bf16[32,1152]{1,0:T(8,128)(2,1)S(1)}, bf16[32,1152]{1,0:T(8,128)(2,1)S(1)}, u32[]{:S(2)}, u32[]{:S(2)}) collective-permute-start(bf16[32,1152]{1,0:T(8,128)(2,1)S(1)} %collective-permute-done.18), channel_id=1, source_target_pairs={{0,2},{2,6},{6,10},{10,14},{14,12},{12,8},{8,4},{4,0},{1,3},{3,7},... | collective-permute-start | bytes 221192 | tf_op jit(solution)/shard_map/ppermute | solution.py:86
  192.8 5.0 %collective-permute-start.33 = (bf16[32,1152]{1,0:T(8,128)(2,1)S(1)}, bf16[32,1152]{1,0:T(8,128)(2,1)S(1)}, u32[]{:S(2)}, u32[]{:S(2)}) collective-permute-start(bf16[32,1152]{1,0:T(8,128)(2,1)S(1)} %collective-permute-done.32), channel_id=1, source_target_pairs={{2,0},{6,2},{10,6},{14,10},{12,14},{8,12},{4,8},{0,4},{3,1},{7,3},... | collective-permute-start | bytes 221192 | tf_op jit(solution)/shard_map/ppermute | solution.py:86
  (19 other events, 176.7 us)
Sparse Core Ops, SparseCore 0:
  10.0 74.9 all-gather.1
  93.5 7.7 reduce-scatter.1

commit v11 on v7

--- a/solution.py
+++ b/solution.py
@@ -150,20 +150,36 @@
         grad_gamma = gamma_total * scale_factor
         grad_beta = beta_total * scale_factor
         grad_all = chan_gather(latent_grad.reshape(lat_local, row_count, col_count))
-        grad_rimmed = extended(grad_all, (("row", 1),), 1)
-        grad_padded = jnp.pad(grad_rimmed, ((0, 0), (0, 0), (1, 1)))
+        grad_padded = jnp.pad(grad_all, ((0, 0), (1, 1), (1, 1)))
         running = jnp.zeros((in_local, pixels), jnp.float32)
         count_rows = shard_piece.shape[0]
+        to_next = jnp.zeros((in_local, col_count), jnp.float32)
+        to_prev = jnp.zeros((in_local, col_count), jnp.float32)
         for tap_index, (row_shift, col_shift) in enumerate(TAPS):
             window = grad_padded[
                 :, 1 - row_shift : 1 - row_shift + row_count, 1 - col_shift : 1 - col_shift + col_count
             ].reshape(count_rows, pixels)
+            weights = shard_piece[:, tap_index, :]
+            contract = (((0,), (0,)), ((), ()))
             running = running + lax.dot_general(
-                shard_piece[:, tap_index, :],
-                window,
-                (((0,), (0,)), ((), ())),
-                preferred_element_type=jnp.float32,
+                weights, window, contract, preferred_element_type=jnp.float32
             )
+            if row_shift != 0:
+                edge = row_count if row_shift == 1 else 1
+                line = grad_padded[:, edge, 1 - col_shift : 1 - col_shift + col_count]
+                part = lax.dot_general(weights, line, contract, preferred_element_type=jnp.float32)
+                if row_shift == 1:
+                    to_next = to_next + part
+                else:
+                    to_prev = to_prev + part
+        count = lax.axis_size("row")
+        up = [(i, i + 1) for i in range(count - 1)]
+        down = [(j, i) for i, j in up]
+        from_prev = lax.ppermute(to_next, "row", up)
+        from_next = lax.ppermute(to_prev, "row", down)
+        running = running.reshape(in_local, row_count, col_count)
+        running = running.at[:, 0].add(from_prev).at[:, row_count - 1].add(from_next)
+        running = running.reshape(in_local, pixels)
         return (
             latent.reshape(lat_local, row_count, col_count),
             running.reshape(in_local, row_count, col_count),

time: 215 us -> 223 us (1.037)
  matrix products: 20.2 us -> 28.1 us
  starting transfers between devices: 44.3 us -> 41.5 us
    dot_general x9 -> x15, matrix products: 4.53 us -> 12.3 us  [the longest x6 7.85 us: per_device(): lax.dot_general(weights, line, contract, preferred_element_type=jnp.float32)]
    ppermute x0 -> x2, starting transfers between devices: none -> 4.66 us  [the longest x1 3.37 us: per_device(): from_prev = lax.ppermute(to_next, 'row', up)]
    ppermute x2 -> x1, starting transfers between devices: 9.44 us -> 4.88 us  [extended(): before = lax.ppermute(last, axis, up)]
    ppermute x0 -> x2, waiting for transfers between devices: none -> 3.05 us  [the longest x1 3.05 us: per_device(): from_next = lax.ppermute(to_prev, 'row', down)]
    unnamed x51 -> x52, local copies, waits for them, and re-layouts: 5.53 us -> 6.4 us
  transfers between devices with their start and end apart: 38 -> 38, of which waited for: 15 -> 19; matrix products, arithmetic and copies ran while one was open for 15% -> 19% of each run, Pallas kernels for 0% -> 0%
where the time goes in v11:
time: 223 us; the launch traced here: 222 us
  waiting for transfers between devices  101 us (45%)
  starting transfers between devices  41.5 us (19%)
  matrix products  28.1 us (13%)
  between operations  25.6 us (11%)
  local copies, waits for them, and re-layouts  14.9 us (7%)
  other arithmetic  11.3 us (5%)
    all_gather x1, waiting for transfers between devices, per_device(): shard_piece = lax.all_gather(conv_weight, 'row', axis=0, tiled=True)  59.7 us
    ppermute x14, waiting for transfers between devices, ring_sum(): got = lax.ppermute(carry[part], 'row', moves[part])  20.9 us
    ppermute x14, starting transfers between devices, ring_sum(): got = lax.ppermute(carry[part], 'row', moves[part])  15.1 us
    ppermute x14, starting transfers between devices, ring_sum(): gathered[part].append(lax.ppermute(gathered[part][-1], 'row', moves[part]))  14.9 us
    ppermute x14, waiting for transfers between devices, ring_sum(): gathered[part].append(lax.ppermute(gathered[part][-1], 'row', moves[part]))  12.2 us
    dot_general x9, matrix products, per_device(): jnp.dot(shard_piece[:, tap_index, :], window, preferred_element_type=jnp....  8.27 us
    dot_general x6, matrix products, per_device(): lax.dot_general(weights, line, contract, preferred_element_type=jnp.float32)  7.85 us
    unnamed x52, local copies, waits for them, and re-layouts  6.4 us
  transfers between devices with their start and end apart: 38, of which 19 were waited for; matrix products, arithmetic and copies ran while one was open for 19% of the time, Pallas kernels for 0%

profile of v11, /device:TPU:0, one launch (start us, length us, event | category | flops | bytes accessed | tf_op | source)
XLA Modules:
  0.0 222.2 jit_solution(3726464767236511245)
XLA Ops:
  9.2 4.9 %collective-permute-start = (bf16[212,1,128]{2,1,0:T(2,128)(2,1)S(1)}, bf16[212,1,128]{2,1,0:T(2,128)(2,1)S(1)}, u32[]{:S(2)}, u32[]{:S(2)}) collective-permute-start(bf16[212,1,128]{2,1,0:T(2,128)(2,1)S(1)} %get-tuple-element.77), channel_id=1, source_target_pairs={{0,2},{2,4},{4,6},{6,8},{8,10},{10,12},{12,14},{1,3},{3,5},{5,7},{... | collective-permute-start | bytes 162824 | tf_op jit(solution)/shard_map/ppermute | solution.py:19
  16.5 4.2 %collective-permute-done.1 = bf16[212,1,128]{2,1,0:T(2,128)(2,1)S(1)} collective-permute-done((bf16[212,1,128]{2,1,0:T(2,128)(2,1)S(1)}, bf16[212,1,128]{2,1,0:T(2,128)(2,1)S(1)}, u32[]{:S(2)}, u32[]{:S(2)}) %collective-permute-start.1) | collective-permute-done | bytes 54304 | tf_op jit(solution)/shard_map/ppermute | solution.py:20
  25.3 59.7 %all-gather.2.cloned.1.call-done = bf16[1024,9,212]{0,2,1:T(8,128)(2,1)} async-done(((bf16[128,9,212]{0,2,1:T(8,128)(2,1)}), bf16[1024,9,212]{0,2,1:T(8,128)(2,1)}) %all-gather.2.cloned.1.call-update) | async-done | bytes 3907600 | tf_op jit(solution)/shard_map/all_gather | solution.py:112
  85.0 1.6 fusion.45
  91.0 2.3 %bitcast_add_fusion = f32[1024,512]{0,1:T(8,128)} fusion(f32[512,1024]{1,0:T(8,128)S(1)} %fusion.45, f32[512,1024]{1,0:T(8,128)S(1)} %fusion.43, f32[512,1024]{1,0:T(8,128)S(1)} %fusion.37, f32[1024,512]{0,1:T(8,128)S(1)} %fusion.35, f32[512,1024]{1,0:T(8,128)S(1)} %fusion.34, f32[512,1024]{1,0:T(8,128)S(1)} %fusion.42, f32[512,1024]{1,0:T(8,128)S(1)} %fusion.38, ...), kind=kOutput, calls=%fused_computation.33 | convolution fusion | flops 226492416 | bytes 19537920 | tf_op jit(solution)/shard_map/dot_general | solution.py:118
  112.9 2.3 %fusion.11 = (bf16[512,512]{0,1:T(8,128)(2,1)}, f32[512,512]{0,1:T(8,128)}, bf16[512,512]{0,1:T(8,128)(2,1)}) fusion(f32[512,512]{0,1:T(8,128)S(1)} %copy-done.2, f32[512,4,128]{0,2,1:T(8,128)S(1)} %copy.17, bf16[1024,512]{0,1:T(8,128)(2,1)S(1)} %fusion.26, bf16[512,1024]{1,0:T(8,128)(2,1)S(1)} %copy-done.3, f32[512]{0:T(512)S(1)} %copy-done.8), kind=kOutput, calls=%fused_computation.64 | convolution fusion | flops 539492352 | bytes 6293504 | tf_op jit(solution)/shard_map/dot_general | solution.py:124
  115.2 1.9 fusion.7
  117.1 2.1 copy.20
  119.5 2.1 collective-permute-start.8
  121.5 4.2 %collective-permute-done.22 = f32[32,1152]{1,0:T(8,128)S(1)} collective-permute-done((f32[32,1152]{1,0:T(8,128)S(1)}, f32[32,1152]{1,0:T(8,128)S(1)}, u32[]{:S(2)}, u32[]{:S(2)}) %collective-permute-start.22) | collective-permute-done | bytes 147488 | tf_op jit(solution)/shard_map/ppermute | solution.py:85
  126.3 1.8 collective-permute-start.9
  128.1 3.3 %collective-permute-done.23 = f32[32,1152]{1,0:T(8,128)S(1)} collective-permute-done((f32[32,1152]{1,0:T(8,128)S(1)}, f32[32,1152]{1,0:T(8,128)S(1)}, u32[]{:S(2)}, u32[]{:S(2)}) %collective-permute-start.23) | collective-permute-done | bytes 147488 | tf_op jit(solution)/shard_map/ppermute | solution.py:85
  133.5 3.0 %collective-permute-done.24 = f32[32,1152]{1,0:T(8,128)S(1)} collective-permute-done((f32[32,1152]{1,0:T(8,128)S(1)}, f32[32,1152]{1,0:T(8,128)S(1)}, u32[]{:S(2)}, u32[]{:S(2)}) %collective-permute-start.24) | collective-permute-done | bytes 147488 | tf_op jit(solution)/shard_map/ppermute | solution.py:85
  138.8 3.3 %fusion.4 = bf16[512,512]{0,1:T(8,128)(2,1)S(1)} fusion(f32[512,512]{0,1:T(8,128)S(1)} %copy-done.5, s32[]{:T(128)S(6)} %select_n.194, bf16[512,512]{1,0:T(8,128)(2,1)S(1)} %copy-done.7, bf16[512,512]{1,0:T(8,128)(2,1)} %collective-permute-done.3, bf16[512,512]{0,1:T(8,128)(2,1)} %get-tuple-element.56, bf16[512,512]{0,1:T(8,128)(2,1)} %collective-permute-done.4, ...), kind=kOutput, calls=%fused_computation.45 | convolution fusion | flops 546308096 | bytes 4719616 | tf_op jit(solution)/shard_map/dot_general | solution.py:134
  144.3 4.1 %collective-permute-done.26 = f32[32,1152]{1,0:T(8,128)S(1)} collective-permute-done((f32[32,1152]{1,0:T(8,128)S(1)}, f32[32,1152]{1,0:T(8,128)S(1)}, u32[]{:S(2)}, u32[]{:S(2)}) %collective-permute-start.26) | collective-permute-done | bytes 147488 | tf_op jit(solution)/shard_map/ppermute | solution.py:85
  150.6 3.3 %collective-permute-done.27 = f32[32,1152]{1,0:T(8,128)S(1)} collective-permute-done((f32[32,1152]{1,0:T(8,128)S(1)}, f32[32,1152]{1,0:T(8,128)S(1)}, u32[]{:S(2)}, u32[]{:S(2)}) %collective-permute-start.27) | collective-permute-done | bytes 147488 | tf_op jit(solution)/shard_map/ppermute | solution.py:85
  156.1 3.0 %collective-permute-done.28 = f32[32,1152]{1,0:T(8,128)S(1)} collective-permute-done((f32[32,1152]{1,0:T(8,128)S(1)}, f32[32,1152]{1,0:T(8,128)S(1)}, u32[]{:S(2)}, u32[]{:S(2)}) %collective-permute-start.28) | collective-permute-done | bytes 147488 | tf_op jit(solution)/shard_map/ppermute | solution.py:85
  162.0 2.8 %pad_slice_fusion.4 = (bf16[1024,4,128]{0,2,1:T(8,128)(2,1)S(1)}, bf16[1024,4,128]{0,2,1:T(8,128)(2,1)S(1)}, bf16[1024,4,128]{0,2,1:T(8,128)(2,1)S(1)}, bf16[102...) fusion(bf16[1024,4,128]{0,2,1:T(8,128)(2,1)S(1)} %fusion.14), kind=kLoop, calls=%fused_computation.6 | loop fusion | bytes 9437184 | tf_op jit(solution)/shard_map/slice | solution.py:159
  173.5 3.4 %collective-permute-start.6 = (f32[212,128]{1,0:T(8,128)S(1)}, f32[212,128]{1,0:T(8,128)S(1)}, u32[]{:S(2)}, u32[]{:S(2)}) collective-permute-start(f32[212,128]{1,0:T(8,128)S(1)} %fusion.10), channel_id=1, source_target_pairs={{0,2},{2,4},{4,6},{6,8},{8,10},{10,12},{12,14},{1,3},{3,5},{5,7},{... | collective-permute-start | bytes 325640 | tf_op jit(solution)/shard_map/ppermute | solution.py:178
  182.2 2.7 %collective-permute-start.30 = (bf16[32,1152]{1,0:T(8,128)(2,1)S(1)}, bf16[32,1152]{1,0:T(8,128)(2,1)S(1)}, u32[]{:S(2)}, u32[]{:S(2)}) collective-permute-start(bf16[32,1152]{1,0:T(8,128)(2,1)S(1)} %collective-permute-done.29), channel_id=1, source_target_pairs={{2,0},{6,2},{10,6},{14,10},{12,14},{8,12},{4,8},{0,4},{3,1},{7,3},... | collective-permute-start | bytes 221192 | tf_op jit(solution)/shard_map/ppermute | solution.py:91
  185.0 3.0 %collective-permute-done.7 = f32[212,128]{1,0:T(8,128)S(1)} collective-permute-done((f32[212,128]{1,0:T(8,128)S(1)}, f32[212,128]{1,0:T(8,128)S(1)}, u32[]{:S(2)}, u32[]{:S(2)}) %collective-permute-start.7) | collective-permute-done | bytes 108576 | tf_op jit(solution)/shard_map/ppermute | solution.py:179
  189.3 1.9 collective-permute-start.17
  191.2 2.2 %collective-permute-done.31 = bf16[32,1152]{1,0:T(8,128)(2,1)S(1)} collective-permute-done((bf16[32,1152]{1,0:T(8,128)(2,1)S(1)}, bf16[32,1152]{1,0:T(8,128)(2,1)S(1)}, u32[]{:S(2)}, u32[]{:S(2)}) %collective-permute-start.31) | collective-permute-done | bytes 73760 | tf_op jit(solution)/shard_map/ppermute | solution.py:91
  193.6 1.9 collective-permute-start.18
  195.5 2.4 %collective-permute-done.32 = bf16[32,1152]{1,0:T(8,128)(2,1)S(1)} collective-permute-done((bf16[32,1152]{1,0:T(8,128)(2,1)S(1)}, bf16[32,1152]{1,0:T(8,128)(2,1)S(1)}, u32[]{:S(2)}, u32[]{:S(2)}) %collective-permute-start.32) | collective-permute-done | bytes 73760 | tf_op jit(solution)/shard_map/ppermute | solution.py:91
  198.2 1.8 collective-permute-start.19
  200.1 2.5 %collective-permute-done.33 = bf16[32,1152]{1,0:T(8,128)(2,1)S(1)} collective-permute-done((bf16[32,1152]{1,0:T(8,128)(2,1)S(1)}, bf16[32,1152]{1,0:T(8,128)(2,1)S(1)}, u32[]{:S(2)}, u32[]{:S(2)}) %collective-permute-start.33) | collective-permute-done | bytes 73760 | tf_op jit(solution)/shard_map/ppermute | solution.py:91
  203.0 1.6 collective-permute-start.20
  204.7 2.2 %collective-permute-done.34 = bf16[32,1152]{1,0:T(8,128)(2,1)S(1)} collective-permute-done((bf16[32,1152]{1,0:T(8,128)(2,1)S(1)}, bf16[32,1152]{1,0:T(8,128)(2,1)S(1)}, u32[]{:S(2)}, u32[]{:S(2)}) %collective-permute-start.34) | collective-permute-done | bytes 73760 | tf_op jit(solution)/shard_map/ppermute | solution.py:91
  207.4 1.6 collective-permute-start.21
  209.0 2.2 %collective-permute-done.35 = bf16[32,1152]{1,0:T(8,128)(2,1)S(1)} collective-permute-done((bf16[32,1152]{1,0:T(8,128)(2,1)S(1)}, bf16[32,1152]{1,0:T(8,128)(2,1)S(1)}, u32[]{:S(2)}, u32[]{:S(2)}) %collective-permute-start.35) | collective-permute-done | bytes 73760 | tf_op jit(solution)/shard_map/ppermute | solution.py:91
  213.8 1.6 slice_multiply_fusion
  (172 shorter events, 55.6 us)
Async XLA Ops:
  7.2 77.8 %all-gather.2.cloned.1.call-start = ((), (), s32[]{:S(2)}) async-start(), calls=%async_computation.1 | async-start | bytes 4478976 | tf_op jit(solution)/shard_map/all_gather | solution.py:112
  7.9 100.2 %reduce-scatter.2.cloned.1.call-start = ((), (), s32[]{:S(2)}) async-start(), calls=%async_computation.2 | async-start | bytes 3145728 | tf_op jit(solution)/shard_map/reduce_scatter | solution.py:121
  9.2 7.3 %collective-permute-start = (bf16[212,1,128]{2,1,0:T(2,128)(2,1)S(1)}, bf16[212,1,128]{2,1,0:T(2,128)(2,1)S(1)}, u32[]{:S(2)}, u32[]{:S(2)}) collective-permute-start(bf16[212,1,128]{2,1,0:T(2,128)(2,1)S(1)} %get-tuple-element.77), channel_id=1, source_target_pairs={{0,2},{2,4},{4,6},{6,8},{8,10},{10,12},{12,14},{1,3},{3,5},{5,7},{... | collective-permute-start | bytes 162824 | tf_op jit(solution)/shard_map/ppermute | solution.py:19
  14.1 6.6 %collective-permute-start.1 = (bf16[212,1,128]{2,1,0:T(2,128)(2,1)S(1)}, bf16[212,1,128]{2,1,0:T(2,128)(2,1)S(1)}, u32[]{:S(2)}, u32[]{:S(2)}) collective-permute-start(bf16[212,1,128]{2,1,0:T(2,128)(2,1)S(1)} %get-tuple-element.78), channel_id=1, source_target_pairs={{2,0},{4,2},{6,4},{8,6},{10,8},{12,10},{14,12},{3,1},{5,3},{7,5},{... | collective-permute-start | bytes 162824 | tf_op jit(solution)/shard_map/ppermute | solution.py:20
  95.6 43.1 %collective-permute-start.3 = (bf16[512,512]{1,0:T(8,128)(2,1)}, bf16[512,512]{1,0:T(8,128)(2,1)}, u32[]{:S(2)}, u32[]{:S(2)}) collective-permute-start(bf16[512,512]{1,0:T(8,128)(2,1)} %get-tuple-element.67), channel_id=1, source_target_pairs={{0,1},{1,0},{2,3},{3,2},{4,5},{5,4},{6,7},{7,6},{8,9},{9,8},{10,11... | collective-permute-start | bytes 1572872 | tf_op jit(solution)/shard_map/ppermute | solution.py:132
  115.1 23.6 %collective-permute-start.4 = (bf16[512,512]{0,1:T(8,128)(2,1)}, bf16[512,512]{0,1:T(8,128)(2,1)}, u32[]{:S(2)}, u32[]{:S(2)}) collective-permute-start(bf16[512,512]{0,1:T(8,128)(2,1)} %get-tuple-element.56), channel_id=1, source_target_pairs={{0,1},{1,0},{2,3},{3,2},{4,5},{5,4},{6,7},{7,6},{8,9},{9,8},{10,11... | collective-permute-start | bytes 1572872 | tf_op jit(solution)/shard_map/ppermute | solution.py:26
  119.4 6.3 %collective-permute-start.22 = (f32[32,1152]{1,0:T(8,128)S(1)}, f32[32,1152]{1,0:T(8,128)S(1)}, u32[]{:S(2)}, u32[]{:S(2)}) collective-permute-start(f32[32,1152]{1,0:T(8,128)S(1)} %select_bitcast_fusion), channel_id=1, source_target_pairs={{2,0},{6,2},{10,6},{14,10},{12,14},{8,12},{4,8},{0,4},{3,1},{7,3},... | collective-permute-start | bytes 442376 | tf_op jit(solution)/shard_map/ppermute | solution.py:85
  119.5 6.8 %collective-permute-start.8 = (f32[32,1152]{1,0:T(8,128)S(1)}, f32[32,1152]{1,0:T(8,128)S(1)}, u32[]{:S(2)}, u32[]{:S(2)}) collective-permute-start(f32[32,1152]{1,0:T(8,128)S(1)} %select_bitcast_fusion.1), channel_id=1, source_target_pairs={{0,2},{2,6},{6,10},{10,14},{14,12},{12,8},{8,4},{4,0},{1,3},{3,7},... | collective-permute-start | bytes 442376 | tf_op jit(solution)/shard_map/ppermute | solution.py:85
  125.7 5.6 %collective-permute-start.23 = (f32[32,1152]{1,0:T(8,128)S(1)}, f32[32,1152]{1,0:T(8,128)S(1)}, u32[]{:S(2)}, u32[]{:S(2)}) collective-permute-start(f32[32,1152]{1,0:T(8,128)S(1)} %bitcast_add_fusion.11), channel_id=1, source_target_pairs={{2,0},{6,2},{10,6},{14,10},{12,14},{8,12},{4,8},{0,4},{3,1},{7,3},... | collective-permute-start | bytes 442376 | tf_op jit(solution)/shard_map/ppermute | solution.py:85
  126.3 5.7 %collective-permute-start.9 = (f32[32,1152]{1,0:T(8,128)S(1)}, f32[32,1152]{1,0:T(8,128)S(1)}, u32[]{:S(2)}, u32[]{:S(2)}) collective-permute-start(f32[32,1152]{1,0:T(8,128)S(1)} %bitcast_add_fusion.18), channel_id=1, source_target_pairs={{0,2},{2,6},{6,10},{10,14},{14,12},{12,8},{8,4},{4,0},{1,3},{3,7},... | collective-permute-start | bytes 442376 | tf_op jit(solution)/shard_map/ppermute | solution.py:85
  131.4 5.2 %collective-permute-start.24 = (f32[32,1152]{1,0:T(8,128)S(1)}, f32[32,1152]{1,0:T(8,128)S(1)}, u32[]{:S(2)}, u32[]{:S(2)}) collective-permute-start(f32[32,1152]{1,0:T(8,128)S(1)} %bitcast_add_fusion.10), channel_id=1, source_target_pairs={{2,0},{6,2},{10,6},{14,10},{12,14},{8,12},{4,8},{0,4},{3,1},{7,3},... | collective-permute-start | bytes 442376 | tf_op jit(solution)/shard_map/ppermute | solution.py:85
  132.0 5.2 %collective-permute-start.10 = (f32[32,1152]{1,0:T(8,128)S(1)}, f32[32,1152]{1,0:T(8,128)S(1)}, u32[]{:S(2)}, u32[]{:S(2)}) collective-permute-start(f32[32,1152]{1,0:T(8,128)S(1)} %bitcast_add_fusion.17), channel_id=1, source_target_pairs={{0,2},{2,6},{6,10},{10,14},{14,12},{12,8},{8,4},{4,0},{1,3},{3,7},... | collective-permute-start | bytes 442376 | tf_op jit(solution)/shard_map/ppermute | solution.py:85
  136.6 5.5 %collective-permute-start.25 = (f32[32,1152]{1,0:T(8,128)S(1)}, f32[32,1152]{1,0:T(8,128)S(1)}, u32[]{:S(2)}, u32[]{:S(2)}) collective-permute-start(f32[32,1152]{1,0:T(8,128)S(1)} %bitcast_add_fusion.9), channel_id=1, source_target_pairs={{2,0},{6,2},{10,6},{14,10},{12,14},{8,12},{4,8},{0,4},{3,1},{7,3},... | collective-permute-start | bytes 442376 | tf_op jit(solution)/shard_map/ppermute | solution.py:85
  137.2 5.5 %collective-permute-start.11 = (f32[32,1152]{1,0:T(8,128)S(1)}, f32[32,1152]{1,0:T(8,128)S(1)}, u32[]{:S(2)}, u32[]{:S(2)}) collective-permute-start(f32[32,1152]{1,0:T(8,128)S(1)} %bitcast_add_fusion.16), channel_id=1, source_target_pairs={{0,2},{2,6},{6,10},{10,14},{14,12},{12,8},{8,4},{4,0},{1,3},{3,7},... | collective-permute-start | bytes 442376 | tf_op jit(solution)/shard_map/ppermute | solution.py:85
  142.0 19.3 %collective-permute-start.5 = (bf16[512,4,128]{0,2,1:T(8,128)(2,1)S(1)}, bf16[512,4,128]{0,2,1:T(8,128)(2,1)S(1)}, u32[]{:S(2)}, u32[]{:S(2)}) collective-permute-start(bf16[512,4,128]{0,2,1:T(8,128)(2,1)S(1)} %bitcast.279), channel_id=1, source_target_pairs={{0,1},{1,0},{2,3},{3,2},{4,5},{5,4},{6,7},{7,6},{8,9},{9,8},{10,11... | collective-permute-start | bytes 1572872 | tf_op jit(solution)/shard_map/ppermute | solution.py:26
  142.1 6.3 %collective-permute-start.26 = (f32[32,1152]{1,0:T(8,128)S(1)}, f32[32,1152]{1,0:T(8,128)S(1)}, u32[]{:S(2)}, u32[]{:S(2)}) collective-permute-start(f32[32,1152]{1,0:T(8,128)S(1)} %bitcast_add_fusion.8), channel_id=1, source_target_pairs={{2,0},{6,2},{10,6},{14,10},{12,14},{8,12},{4,8},{0,4},{3,1},{7,3},... | collective-permute-start | bytes 442376 | tf_op jit(solution)/shard_map/ppermute | solution.py:85
  142.8 6.3 %collective-permute-start.12 = (f32[32,1152]{1,0:T(8,128)S(1)}, f32[32,1152]{1,0:T(8,128)S(1)}, u32[]{:S(2)}, u32[]{:S(2)}) collective-permute-start(f32[32,1152]{1,0:T(8,128)S(1)} %bitcast_add_fusion.15), channel_id=1, source_target_pairs={{0,2},{2,6},{6,10},{10,14},{14,12},{12,8},{8,4},{4,0},{1,3},{3,7},... | collective-permute-start | bytes 442376 | tf_op jit(solution)/shard_map/ppermute | solution.py:85
  148.4 5.4 %collective-permute-start.27 = (f32[32,1152]{1,0:T(8,128)S(1)}, f32[32,1152]{1,0:T(8,128)S(1)}, u32[]{:S(2)}, u32[]{:S(2)}) collective-permute-start(f32[32,1152]{1,0:T(8,128)S(1)} %bitcast_add_fusion.7), channel_id=1, source_target_pairs={{2,0},{6,2},{10,6},{14,10},{12,14},{8,12},{4,8},{0,4},{3,1},{7,3},... | collective-permute-start | bytes 442376 | tf_op jit(solution)/shard_map/ppermute | solution.py:85
  149.1 5.4 %collective-permute-start.13 = (f32[32,1152]{1,0:T(8,128)S(1)}, f32[32,1152]{1,0:T(8,128)S(1)}, u32[]{:S(2)}, u32[]{:S(2)}) collective-permute-start(f32[32,1152]{1,0:T(8,128)S(1)} %bitcast_add_fusion.14), channel_id=1, source_target_pairs={{0,2},{2,6},{6,10},{10,14},{14,12},{12,8},{8,4},{4,0},{1,3},{3,7},... | collective-permute-start | bytes 442376 | tf_op jit(solution)/shard_map/ppermute | solution.py:85
  153.9 5.2 %collective-permute-start.28 = (f32[32,1152]{1,0:T(8,128)S(1)}, f32[32,1152]{1,0:T(8,128)S(1)}, u32[]{:S(2)}, u32[]{:S(2)}) collective-permute-start(f32[32,1152]{1,0:T(8,128)S(1)} %bitcast_add_fusion.6), channel_id=1, source_target_pairs={{2,0},{6,2},{10,6},{14,10},{12,14},{8,12},{4,8},{0,4},{3,1},{7,3},... | collective-permute-start | bytes 442376 | tf_op jit(solution)/shard_map/ppermute | solution.py:85
  154.5 5.2 %collective-permute-start.14 = (f32[32,1152]{1,0:T(8,128)S(1)}, f32[32,1152]{1,0:T(8,128)S(1)}, u32[]{:S(2)}, u32[]{:S(2)}) collective-permute-start(f32[32,1152]{1,0:T(8,128)S(1)} %bitcast_add_fusion.13), channel_id=1, source_target_pairs={{0,2},{2,6},{6,10},{10,14},{14,12},{12,8},{8,4},{4,0},{1,3},{3,7},... | collective-permute-start | bytes 442376 | tf_op jit(solution)/shard_map/ppermute | solution.py:85
  159.1 23.0 %collective-permute-start.29 = (bf16[32,1152]{1,0:T(8,128)(2,1)S(1)}, bf16[32,1152]{1,0:T(8,128)(2,1)S(1)}, u32[]{:S(2)}, u32[]{:S(2)}) collective-permute-start(bf16[32,1152]{1,0:T(8,128)(2,1)S(1)} %get-tuple-element.53), channel_id=1, source_target_pairs={{2,0},{6,2},{10,6},{14,10},{12,14},{8,12},{4,8},{0,4},{3,1},{7,3},... | collective-permute-start | bytes 221192 | tf_op jit(solution)/shard_map/ppermute | solution.py:91
  159.8 25.1 %collective-permute-start.15 = (bf16[32,1152]{1,0:T(8,128)(2,1)S(1)}, bf16[32,1152]{1,0:T(8,128)(2,1)S(1)}, u32[]{:S(2)}, u32[]{:S(2)}) collective-permute-start(bf16[32,1152]{1,0:T(8,128)(2,1)S(1)} %get-tuple-element.51), channel_id=1, source_target_pairs={{0,2},{2,6},{6,10},{10,14},{14,12},{12,8},{8,4},{4,0},{1,3},{3,7},... | collective-permute-start | bytes 221192 | tf_op jit(solution)/shard_map/ppermute | solution.py:91
  173.5 11.4 %collective-permute-start.6 = (f32[212,128]{1,0:T(8,128)S(1)}, f32[212,128]{1,0:T(8,128)S(1)}, u32[]{:S(2)}, u32[]{:S(2)}) collective-permute-start(f32[212,128]{1,0:T(8,128)S(1)} %fusion.10), channel_id=1, source_target_pairs={{0,2},{2,4},{4,6},{6,8},{8,10},{10,12},{12,14},{1,3},{3,5},{5,7},{... | collective-permute-start | bytes 325640 | tf_op jit(solution)/shard_map/ppermute | solution.py:178
  180.9 7.2 %collective-permute-start.7 = (f32[212,128]{1,0:T(8,128)S(1)}, f32[212,128]{1,0:T(8,128)S(1)}, u32[]{:S(2)}, u32[]{:S(2)}) collective-permute-start(f32[212,128]{1,0:T(8,128)S(1)} %fusion.9), channel_id=1, source_target_pairs={{2,0},{4,2},{6,4},{8,6},{10,8},{12,10},{14,12},{3,1},{5,3},{7,5},{... | collective-permute-start | bytes 325640 | tf_op jit(solution)/shard_map/ppermute | solution.py:179
  182.2 6.9 %collective-permute-start.30 = (bf16[32,1152]{1,0:T(8,128)(2,1)S(1)}, bf16[32,1152]{1,0:T(8,128)(2,1)S(1)}, u32[]{:S(2)}, u32[]{:S(2)}) collective-permute-start(bf16[32,1152]{1,0:T(8,128)(2,1)S(1)} %collective-permute-done.29), channel_id=1, source_target_pairs={{2,0},{6,2},{10,6},{14,10},{12,14},{8,12},{4,8},{0,4},{3,1},{7,3},... | collective-permute-start | bytes 221192 | tf_op jit(solution)/shard_map/ppermute | solution.py:91
  184.9 4.4 %collective-permute-start.16 = (bf16[32,1152]{1,0:T(8,128)(2,1)S(1)}, bf16[32,1152]{1,0:T(8,128)(2,1)S(1)}, u32[]{:S(2)}, u32[]{:S(2)}) collective-permute-start(bf16[32,1152]{1,0:T(8,128)(2,1)S(1)} %collective-permute-done.15), channel_id=1, source_target_pairs={{0,2},{2,6},{6,10},{10,14},{14,12},{12,8},{8,4},{4,0},{1,3},{3,7},... | collective-permute-start | bytes 221192 | tf_op jit(solution)/shard_map/ppermute | solution.py:91
  193.4 4.5 %collective-permute-start.32 = (bf16[32,1152]{1,0:T(8,128)(2,1)S(1)}, bf16[32,1152]{1,0:T(8,128)(2,1)S(1)}, u32[]{:S(2)}, u32[]{:S(2)}) collective-permute-start(bf16[32,1152]{1,0:T(8,128)(2,1)S(1)} %collective-permute-done.31), channel_id=1, source_target_pairs={{2,0},{6,2},{10,6},{14,10},{12,14},{8,12},{4,8},{0,4},{3,1},{7,3},... | collective-permute-start | bytes 221192 | tf_op jit(solution)/shard_map/ppermute | solution.py:91
  193.6 4.6 %collective-permute-start.18 = (bf16[32,1152]{1,0:T(8,128)(2,1)S(1)}, bf16[32,1152]{1,0:T(8,128)(2,1)S(1)}, u32[]{:S(2)}, u32[]{:S(2)}) collective-permute-start(bf16[32,1152]{1,0:T(8,128)(2,1)S(1)} %collective-permute-done.17), channel_id=1, source_target_pairs={{0,2},{2,6},{6,10},{10,14},{14,12},{12,8},{8,4},{4,0},{1,3},{3,7},... | collective-permute-start | bytes 221192 | tf_op jit(solution)/shard_map/ppermute | solution.py:91
  197.9 4.6 %collective-permute-start.33 = (bf16[32,1152]{1,0:T(8,128)(2,1)S(1)}, bf16[32,1152]{1,0:T(8,128)(2,1)S(1)}, u32[]{:S(2)}, u32[]{:S(2)}) collective-permute-start(bf16[32,1152]{1,0:T(8,128)(2,1)S(1)} %collective-permute-done.32), channel_id=1, source_target_pairs={{2,0},{6,2},{10,6},{14,10},{12,14},{8,12},{4,8},{0,4},{3,1},{7,3},... | collective-permute-start | bytes 221192 | tf_op jit(solution)/shard_map/ppermute | solution.py:91
  198.2 4.8 %collective-permute-start.19 = (bf16[32,1152]{1,0:T(8,128)(2,1)S(1)}, bf16[32,1152]{1,0:T(8,128)(2,1)S(1)}, u32[]{:S(2)}, u32[]{:S(2)}) collective-permute-start(bf16[32,1152]{1,0:T(8,128)(2,1)S(1)} %collective-permute-done.18), channel_id=1, source_target_pairs={{0,2},{2,6},{6,10},{10,14},{14,12},{12,8},{8,4},{4,0},{1,3},{3,7},... | collective-permute-start | bytes 221192 | tf_op jit(solution)/shard_map/ppermute | solution.py:91
  207.4 4.6 %collective-permute-start.21 = (bf16[32,1152]{1,0:T(8,128)(2,1)S(1)}, bf16[32,1152]{1,0:T(8,128)(2,1)S(1)}, u32[]{:S(2)}, u32[]{:S(2)}) collective-permute-start(bf16[32,1152]{1,0:T(8,128)(2,1)S(1)} %collective-permute-done.20), channel_id=1, source_target_pairs={{0,2},{2,6},{6,10},{10,14},{14,12},{12,8},{8,4},{4,0},{1,3},{3,7},... | collective-permute-start | bytes 221192 | tf_op jit(solution)/shard_map/ppermute | solution.py:91
  (16 other events, 112.0 us)
Sparse Core Ops, SparseCore 0:
  10.0 74.9 all-gather.1
  93.5 7.7 reduce-scatter.1

commit v12 on v8

--- a/solution.py
+++ b/solution.py
@@ -60,27 +60,33 @@
     return path if len(set(path)) == count else list(range(count))
 
 
-def ring_sum(x, ring):
+def ring_sum(halves, ring):
     count = len(ring)
     forward = [(ring[i], ring[(i + 1) % count]) for i in range(count)]
     backward = [(b, a) for a, b in forward]
-    ring_index = jnp.asarray(ring, jnp.int32)
     position = jnp.asarray([ring.index(i) for i in range(count)], jnp.int32)[lax.axis_index("row")]
-    rows = x.shape[0] // (2 * count)
-    blocks = x.reshape((count, 2, rows) + x.shape[1:])
+    split = [x.reshape((count, x.shape[0] // count) + x.shape[1:]) for x in halves]
     moves = (forward, backward)
     signs = (1, -1)
 
     def pick(part, step):
-        index = ring_index[(position - signs[part] * (1 + step)) % count]
-        return lax.dynamic_index_in_dim(blocks, index, 0, keepdims=False)[part]
+        index = (position - signs[part] * (1 + step)) % count
+        return jnp.take(split[part], index, axis=0)
 
     carry = [pick(part, 0) for part in range(2)]
     for step in range(1, count):
         for part in range(2):
             carry[part] = lax.ppermute(carry[part], "row", moves[part]) + pick(part, step)
-    own = jnp.concatenate(carry, 0).astype(jnp.bfloat16)
-    return lax.all_gather(own, "row", axis=0, tiled=True).astype(jnp.float32)
+    gathered = [[c.astype(jnp.bfloat16)] for c in carry]
+    for step in range(1, count):
+        for part in range(2):
+            gathered[part].append(lax.ppermute(gathered[part][-1], "row", moves[part]))
+    results = []
+    for part in range(2):
+        stacked = jnp.stack(gathered[part], 0)
+        order = (signs[part] * (position - jnp.arange(count))) % count
+        results.append(jnp.take(stacked, order, axis=0).reshape((-1,) + stacked.shape[2:]))
+    return [r.astype(jnp.float32) for r in results]
 
 
 def make_per_device(ring):
@@ -124,11 +130,16 @@
             shares, squares_ones, (((1,), (1,)), ((), ())), preferred_element_type=jnp.float32
         )
         if len(ring) <= 16:
-            joined_total = ring_sum(joined, ring)
+            half = lat_local // 2
+            first = joined[:half, :lat_all]
+            second = joined[half:].at[:, lat_all + 1].set(joined[:half, lat_all])
+            first_total, second_total = ring_sum([first, second], ring)
+            gamma_total = jnp.concatenate([first_total, second_total[:, :lat_all]], 0)
+            beta_total = jnp.concatenate([second_total[:, lat_all + 1], second_total[:, lat_all]], 0)
         else:
             joined_total = lax.psum(joined, "row")
-        gamma_total = joined_total[:, :lat_all]
-        beta_total = joined_total[:, lat_all]
+            gamma_total = joined_total[:, :lat_all]
+            beta_total = joined_total[:, lat_all]
         scale_factor = 1.0 / math.sqrt(pixels * lax.axis_size("row"))
         grad_gamma = gamma_total * scale_factor
         grad_beta = beta_total * scale_factor

time: 251 us -> 231 us (0.920)
  between operations: 55.2 us -> 25.6 us
  starting transfers between devices: 27.3 us -> 42.6 us
  other arithmetic: 23.2 us -> 17.9 us
    ppermute x0 -> x14, waiting for transfers between devices: none -> 22.7 us  [ring_sum(): gathered[part].append(lax.ppermute(gathered[part][-1], 'row', moves[part]))]
    all_gather x1 -> x0, waiting for transfers between devices: 19 us -> none  [ring_sum(): return lax.all_gather(own, 'row', axis=0, tiled=True).astype(jnp.float32)]
    ppermute x14, waiting for transfers between devices: 4.9 us -> 20.4 us  [ring_sum(): lax.ppermute(carry[part], 'row', moves[part]) + pick(part, step)]
    ppermute x0 -> x14, starting transfers between devices: none -> 14 us  [ring_sum(): gathered[part].append(lax.ppermute(gathered[part][-1], 'row', moves[part]))]
    reduce_scatter x1, waiting for transfers between devices: 7.93 us -> 0.02 us  [per_device(): lax.psum_scatter(partial_value, 'chan', scatter_dimension=0, tiled=True)]
    add x6 -> x12, other arithmetic: 9.38 us -> 2.06 us  [ring_sum(): lax.ppermute(carry[part], 'row', moves[part]) + pick(part, step)]
    ppermute x2, waiting for transfers between devices: 4.84 us -> 0.01 us  [extended(): before = lax.ppermute(last, axis, up)]
    ppermute x2, waiting for transfers between devices: 8.64 us -> 4.24 us  [extended(): after = lax.ppermute(leading, axis, down)]
  transfers between devices with their start and end apart: 25 -> 38, of which waited for: 13 -> 21; matrix products, arithmetic and copies ran while one was open for 12% -> 18% of each run, Pallas kernels for 0% -> 0%
where the time goes in v12:
time: 231 us; the launch traced here: 230 us
  waiting for transfers between devices  108 us (47%)
  starting transfers between devices  42.6 us (18%)
  between operations  25.6 us (11%)
  matrix products  20.3 us (9%)
  other arithmetic  17.9 us (8%)
  local copies, waits for them, and re-layouts  16.1 us (7%)
    all_gather x1, waiting for transfers between devices, per_device(): shard_piece = lax.all_gather(conv_weight, 'row', axis=0, tiled=True)  59.7 us
    ppermute x14, waiting for transfers between devices, ring_sum(): gathered[part].append(lax.ppermute(gathered[part][-1], 'row', moves[part]))  22.7 us
    ppermute x14, waiting for transfers between devices, ring_sum(): lax.ppermute(carry[part], 'row', moves[part]) + pick(part, step)  20.4 us
    ppermute x14, starting transfers between devices, ring_sum(): lax.ppermute(carry[part], 'row', moves[part]) + pick(part, step)  16 us
    ppermute x14, starting transfers between devices, ring_sum(): gathered[part].append(lax.ppermute(gathered[part][-1], 'row', moves[part]))  14 us
    ppermute x2, starting transfers between devices, extended(): before = lax.ppermute(last, axis, up)  9.44 us
    dot_general x9, matrix products, per_device(): jnp.dot(shard_piece[:, tap_index, :], window, preferred_element_type=jnp....  8.27 us
    unnamed x55, local copies, waits for them, and re-layouts  5.5 us
  transfers between devices with their start and end apart: 38, of which 21 were waited for; matrix products, arithmetic and copies ran while one was open for 18% of the time, Pallas kernels for 0%

profile of v12, /device:TPU:0, one launch (start us, length us, event | category | flops | bytes accessed | tf_op | source)
XLA Modules:
  0.0 230.2 jit_solution(18377444468440101445)
XLA Ops:
  9.2 4.9 %collective-permute-start = (bf16[212,1,128]{2,1,0:T(2,128)(2,1)S(1)}, bf16[212,1,128]{2,1,0:T(2,128)(2,1)S(1)}, u32[]{:S(2)}, u32[]{:S(2)}) collective-permute-start(bf16[212,1,128]{2,1,0:T(2,128)(2,1)S(1)} %get-tuple-element.78), channel_id=1, source_target_pairs={{0,2},{2,4},{4,6},{6,8},{8,10},{10,12},{12,14},{1,3},{3,5},{5,7},{... | collective-permute-start | bytes 162824 | tf_op jit(solution)/shard_map/ppermute | solution.py:19
  16.5 4.2 %collective-permute-done.1 = bf16[212,1,128]{2,1,0:T(2,128)(2,1)S(1)} collective-permute-done((bf16[212,1,128]{2,1,0:T(2,128)(2,1)S(1)}, bf16[212,1,128]{2,1,0:T(2,128)(2,1)S(1)}, u32[]{:S(2)}, u32[]{:S(2)}) %collective-permute-start.1) | collective-permute-done | bytes 54304 | tf_op jit(solution)/shard_map/ppermute | solution.py:20
  25.3 59.7 %all-gather.2.cloned.1.call-done = bf16[1024,9,212]{0,2,1:T(8,128)(2,1)} async-done(((bf16[128,9,212]{0,2,1:T(8,128)(2,1)}), bf16[1024,9,212]{0,2,1:T(8,128)(2,1)}) %all-gather.2.cloned.1.call-update) | async-done | bytes 3907600 | tf_op jit(solution)/shard_map/all_gather | solution.py:101
  91.0 2.3 bitcast_add_fusion
  107.4 2.2 multiply_convert_fusion.1
  113.1 2.0 fusion.28
  115.2 2.3 %fusion.13 = (bf16[512,512]{0,1:T(8,128)(2,1)}, f32[512,512]{0,1:T(8,128)}, bf16[512,512]{0,1:T(8,128)(2,1)}) fusion(f32[512,512]{0,1:T(8,128)S(1)} %copy-done.3, f32[512,4,128]{0,2,1:T(8,128)S(1)} %copy.14, bf16[1024,512]{0,1:T(8,128)(2,1)S(1)} %fusion.28, bf16[512,1024]{1,0:T(8,128)(2,1)S(1)} %copy-done.5, f32[512]{0:T(512)S(1)} %copy-done.10), kind=kOutput, calls=%fused_computation.44 | convolution fusion | flops 539492352 | bytes 6293504 | tf_op jit(solution)/shard_map/dot_general | solution.py:113
  117.5 1.9 fusion.11
  120.6 2.1 copy.15
  125.2 1.7 collective-permute-start.8
  129.0 2.3 %collective-permute-done.8 = f32[32,1024]{1,0:T(8,128)S(1)} collective-permute-done((f32[32,1024]{1,0:T(8,128)S(1)}, f32[32,1024]{1,0:T(8,128)S(1)}, u32[]{:S(2)}, u32[]{:S(2)}) %collective-permute-start.8) | collective-permute-done | bytes 131104 | tf_op jit(solution)/shard_map/ppermute | solution.py:79
  135.1 2.3 collective-permute-done.9
  140.4 2.9 %collective-permute-done.10 = f32[32,1024]{1,0:T(8,128)S(1)} collective-permute-done((f32[32,1024]{1,0:T(8,128)S(1)}, f32[32,1024]{1,0:T(8,128)S(1)}, u32[]{:S(2)}, u32[]{:S(2)}) %collective-permute-start.10) | collective-permute-done | bytes 131104 | tf_op jit(solution)/shard_map/ppermute | solution.py:79
  145.7 3.2 %collective-permute-done.11 = f32[32,1024]{1,0:T(8,128)S(1)} collective-permute-done((f32[32,1024]{1,0:T(8,128)S(1)}, f32[32,1024]{1,0:T(8,128)S(1)}, u32[]{:S(2)}, u32[]{:S(2)}) %collective-permute-start.11) | collective-permute-done | bytes 131104 | tf_op jit(solution)/shard_map/ppermute | solution.py:79
  148.9 1.8 collective-permute-start.12
  150.8 3.3 %fusion.10 = bf16[512,512]{0,1:T(8,128)(2,1)S(1)} fusion(f32[512,512]{0,1:T(8,128)S(1)} %copy-done.7, s32[]{:T(128)S(6)} %select_n.260, bf16[512,512]{1,0:T(8,128)(2,1)S(1)} %copy-done.9, bf16[512,512]{1,0:T(8,128)(2,1)} %collective-permute-done.3, bf16[512,512]{0,1:T(8,128)(2,1)} %get-tuple-element.55, bf16[512,512]{0,1:T(8,128)(2,1)} %collective-permute-done.4, ...), kind=kOutput, calls=%fused_computation.41 | convolution fusion | flops 546308096 | bytes 4719616 | tf_op jit(solution)/shard_map/dot_general | solution.py:123
  156.3 3.8 %collective-permute-done.13 = f32[32,1024]{1,0:T(8,128)S(1)} collective-permute-done((f32[32,1024]{1,0:T(8,128)S(1)}, f32[32,1024]{1,0:T(8,128)S(1)}, u32[]{:S(2)}, u32[]{:S(2)}) %collective-permute-start.13) | collective-permute-done | bytes 131104 | tf_op jit(solution)/shard_map/ppermute | solution.py:79
  162.3 2.8 %collective-permute-done.14 = f32[32,1024]{1,0:T(8,128)S(1)} collective-permute-done((f32[32,1024]{1,0:T(8,128)S(1)}, f32[32,1024]{1,0:T(8,128)S(1)}, u32[]{:S(2)}, u32[]{:S(2)}) %collective-permute-start.14) | collective-permute-done | bytes 131104 | tf_op jit(solution)/shard_map/ppermute | solution.py:79
  167.6 2.0 collective-permute-done.15
  170.2 1.7 collective-permute-done.28
  175.0 4.6 %collective-permute-start.6 = (bf16[1024,1,128]{0,2,1:T(8,128)(2,1)S(1)}, bf16[1024,1,128]{0,2,1:T(8,128)(2,1)S(1)}, u32[]{:S(2)}, u32[]{:S(2)}) collective-permute-start(bf16[1024,1,128]{0,2,1:T(8,128)(2,1)S(1)} %get-tuple-element.67), channel_id=1, source_target_pairs={{0,2},{2,4},{4,6},{6,8},{8,10},{10,12},{12,14},{1,3},{3,5},{5,7},{... | collective-permute-start | bytes 786440 | tf_op jit(solution)/shard_map/ppermute | solution.py:19
  180.1 2.0 collective-permute-start.17
  182.2 4.1 %collective-permute-done.17 = bf16[32,1024]{1,0:T(8,128)(2,1)S(1)} collective-permute-done((bf16[32,1024]{1,0:T(8,128)(2,1)S(1)}, bf16[32,1024]{1,0:T(8,128)(2,1)S(1)}, u32[]{:S(2)}, u32[]{:S(2)}) %collective-permute-start.17) | collective-permute-done | bytes 65568 | tf_op jit(solution)/shard_map/ppermute | solution.py:83
  186.4 2.5 %collective-permute-start.18 = (bf16[32,1024]{1,0:T(8,128)(2,1)S(1)}, bf16[32,1024]{1,0:T(8,128)(2,1)S(1)}, u32[]{:S(2)}, u32[]{:S(2)}) collective-permute-start(bf16[32,1024]{1,0:T(8,128)(2,1)S(1)} %collective-permute-done.17), channel_id=1, source_target_pairs={{0,2},{2,6},{6,10},{10,14},{14,12},{12,8},{8,4},{4,0},{1,3},{3,7},... | collective-permute-start | bytes 196616 | tf_op jit(solution)/shard_map/ppermute | solution.py:83
  188.9 2.3 %collective-permute-done.18 = bf16[32,1024]{1,0:T(8,128)(2,1)S(1)} collective-permute-done((bf16[32,1024]{1,0:T(8,128)(2,1)S(1)}, bf16[32,1024]{1,0:T(8,128)(2,1)S(1)}, u32[]{:S(2)}, u32[]{:S(2)}) %collective-permute-start.18) | collective-permute-done | bytes 65568 | tf_op jit(solution)/shard_map/ppermute | solution.py:83
  191.3 2.5 %collective-permute-start.19 = (bf16[32,1024]{1,0:T(8,128)(2,1)S(1)}, bf16[32,1024]{1,0:T(8,128)(2,1)S(1)}, u32[]{:S(2)}, u32[]{:S(2)}) collective-permute-start(bf16[32,1024]{1,0:T(8,128)(2,1)S(1)} %collective-permute-done.18), channel_id=1, source_target_pairs={{0,2},{2,6},{6,10},{10,14},{14,12},{12,8},{8,4},{4,0},{1,3},{3,7},... | collective-permute-start | bytes 196616 | tf_op jit(solution)/shard_map/ppermute | solution.py:83
  193.8 1.9 collective-permute-done.19
  195.7 2.4 %collective-permute-start.20 = (bf16[32,1024]{1,0:T(8,128)(2,1)S(1)}, bf16[32,1024]{1,0:T(8,128)(2,1)S(1)}, u32[]{:S(2)}, u32[]{:S(2)}) collective-permute-start(bf16[32,1024]{1,0:T(8,128)(2,1)S(1)} %collective-permute-done.19), channel_id=1, source_target_pairs={{0,2},{2,6},{6,10},{10,14},{14,12},{12,8},{8,4},{4,0},{1,3},{3,7},... | collective-permute-start | bytes 196616 | tf_op jit(solution)/shard_map/ppermute | solution.py:83
  204.9 2.0 collective-permute-start.21
  207.1 2.1 collective-permute-done.21
  211.4 4.3 %collective-permute-done.34 = bf16[32,1152]{1,0:T(8,128)(2,1)S(1)} collective-permute-done((bf16[32,1152]{1,0:T(8,128)(2,1)S(1)}, bf16[32,1152]{1,0:T(8,128)(2,1)S(1)}, u32[]{:S(2)}, u32[]{:S(2)}) %collective-permute-start.34) | collective-permute-done | bytes 73760 | tf_op jit(solution)/shard_map/ppermute | solution.py:83
  215.8 4.3 %collective-permute-done.35 = bf16[32,1152]{1,0:T(8,128)(2,1)S(1)} collective-permute-done((bf16[32,1152]{1,0:T(8,128)(2,1)S(1)}, bf16[32,1152]{1,0:T(8,128)(2,1)S(1)}, u32[]{:S(2)}, u32[]{:S(2)}) %collective-permute-start.35) | collective-permute-done | bytes 73760 | tf_op jit(solution)/shard_map/ppermute | solution.py:83
  (177 shorter events, 60.1 us)
Async XLA Ops:
  7.2 77.8 %all-gather.2.cloned.1.call-start = ((), (), s32[]{:S(2)}) async-start(), calls=%async_computation.1 | async-start | bytes 4478976 | tf_op jit(solution)/shard_map/all_gather | solution.py:101
  7.9 99.5 %reduce-scatter.2.cloned.1.call-start = ((), (), s32[]{:S(2)}) async-start(), calls=%async_computation.2 | async-start | bytes 3145728 | tf_op jit(solution)/shard_map/reduce_scatter | solution.py:110
  9.2 7.3 %collective-permute-start = (bf16[212,1,128]{2,1,0:T(2,128)(2,1)S(1)}, bf16[212,1,128]{2,1,0:T(2,128)(2,1)S(1)}, u32[]{:S(2)}, u32[]{:S(2)}) collective-permute-start(bf16[212,1,128]{2,1,0:T(2,128)(2,1)S(1)} %get-tuple-element.78), channel_id=1, source_target_pairs={{0,2},{2,4},{4,6},{6,8},{8,10},{10,12},{12,14},{1,3},{3,5},{5,7},{... | collective-permute-start | bytes 162824 | tf_op jit(solution)/shard_map/ppermute | solution.py:19
  14.1 6.6 %collective-permute-start.1 = (bf16[212,1,128]{2,1,0:T(2,128)(2,1)S(1)}, bf16[212,1,128]{2,1,0:T(2,128)(2,1)S(1)}, u32[]{:S(2)}, u32[]{:S(2)}) collective-permute-start(bf16[212,1,128]{2,1,0:T(2,128)(2,1)S(1)} %get-tuple-element.79), channel_id=1, source_target_pairs={{2,0},{4,2},{6,4},{8,6},{10,8},{12,10},{14,12},{3,1},{5,3},{7,5},{... | collective-permute-start | bytes 162824 | tf_op jit(solution)/shard_map/ppermute | solution.py:20
  95.6 55.1 %collective-permute-start.3 = (bf16[512,512]{1,0:T(8,128)(2,1)}, bf16[512,512]{1,0:T(8,128)(2,1)}, u32[]{:S(2)}, u32[]{:S(2)}) collective-permute-start(bf16[512,512]{1,0:T(8,128)(2,1)} %get-tuple-element.68), channel_id=1, source_target_pairs={{0,1},{1,0},{2,3},{3,2},{4,5},{5,4},{6,7},{7,6},{8,9},{9,8},{10,11... | collective-permute-start | bytes 1572872 | tf_op jit(solution)/shard_map/ppermute | solution.py:121
  117.5 33.2 %collective-permute-start.4 = (bf16[512,512]{0,1:T(8,128)(2,1)}, bf16[512,512]{0,1:T(8,128)(2,1)}, u32[]{:S(2)}, u32[]{:S(2)}) collective-permute-start(bf16[512,512]{0,1:T(8,128)(2,1)} %get-tuple-element.55), channel_id=1, source_target_pairs={{0,1},{1,0},{2,3},{3,2},{4,5},{5,4},{6,7},{7,6},{8,9},{9,8},{10,11... | collective-permute-start | bytes 1572872 | tf_op jit(solution)/shard_map/ppermute | solution.py:26
  125.2 6.1 %collective-permute-start.8 = (f32[32,1024]{1,0:T(8,128)S(1)}, f32[32,1024]{1,0:T(8,128)S(1)}, u32[]{:S(2)}, u32[]{:S(2)}) collective-permute-start(f32[32,1024]{1,0:T(8,128)S(1)} %select_bitcast_fusion.1), channel_id=1, source_target_pairs={{0,2},{2,6},{6,10},{10,14},{14,12},{12,8},{8,4},{4,0},{1,3},{3,7},... | collective-permute-start | bytes 393224 | tf_op jit(solution)/shard_map/ppermute | solution.py:79
  128.4 6.0 %collective-permute-start.22 = (f32[32,1152]{1,0:T(8,128)S(1)}, f32[32,1152]{1,0:T(8,128)S(1)}, u32[]{:S(2)}, u32[]{:S(2)}) collective-permute-start(f32[32,1152]{1,0:T(8,128)S(1)} %select_bitcast_fusion), channel_id=1, source_target_pairs={{2,0},{6,2},{10,6},{14,10},{12,14},{8,12},{4,8},{0,4},{3,1},{7,3},... | collective-permute-start | bytes 442376 | tf_op jit(solution)/shard_map/ppermute | solution.py:79
  132.3 5.1 %collective-permute-start.9 = (f32[32,1024]{1,0:T(8,128)S(1)}, f32[32,1024]{1,0:T(8,128)S(1)}, u32[]{:S(2)}, u32[]{:S(2)}) collective-permute-start(f32[32,1024]{1,0:T(8,128)S(1)} %bitcast_add_fusion.18), channel_id=1, source_target_pairs={{0,2},{2,6},{6,10},{10,14},{14,12},{12,8},{8,4},{4,0},{1,3},{3,7},... | collective-permute-start | bytes 393224 | tf_op jit(solution)/shard_map/ppermute | solution.py:79
  134.5 5.4 %collective-permute-start.23 = (f32[32,1152]{1,0:T(8,128)S(1)}, f32[32,1152]{1,0:T(8,128)S(1)}, u32[]{:S(2)}, u32[]{:S(2)}) collective-permute-start(f32[32,1152]{1,0:T(8,128)S(1)} %bitcast_add_fusion.11), channel_id=1, source_target_pairs={{2,0},{6,2},{10,6},{14,10},{12,14},{8,12},{4,8},{0,4},{3,1},{7,3},... | collective-permute-start | bytes 442376 | tf_op jit(solution)/shard_map/ppermute | solution.py:79
  138.3 5.0 %collective-permute-start.10 = (f32[32,1024]{1,0:T(8,128)S(1)}, f32[32,1024]{1,0:T(8,128)S(1)}, u32[]{:S(2)}, u32[]{:S(2)}) collective-permute-start(f32[32,1024]{1,0:T(8,128)S(1)} %bitcast_add_fusion.17), channel_id=1, source_target_pairs={{0,2},{2,6},{6,10},{10,14},{14,12},{12,8},{8,4},{4,0},{1,3},{3,7},... | collective-permute-start | bytes 393224 | tf_op jit(solution)/shard_map/ppermute | solution.py:79
  139.8 5.2 %collective-permute-start.24 = (f32[32,1152]{1,0:T(8,128)S(1)}, f32[32,1152]{1,0:T(8,128)S(1)}, u32[]{:S(2)}, u32[]{:S(2)}) collective-permute-start(f32[32,1152]{1,0:T(8,128)S(1)} %bitcast_add_fusion.10), channel_id=1, source_target_pairs={{2,0},{6,2},{10,6},{14,10},{12,14},{8,12},{4,8},{0,4},{3,1},{7,3},... | collective-permute-start | bytes 442376 | tf_op jit(solution)/shard_map/ppermute | solution.py:79
  143.3 5.6 %collective-permute-start.11 = (f32[32,1024]{1,0:T(8,128)S(1)}, f32[32,1024]{1,0:T(8,128)S(1)}, u32[]{:S(2)}, u32[]{:S(2)}) collective-permute-start(f32[32,1024]{1,0:T(8,128)S(1)} %bitcast_add_fusion.16), channel_id=1, source_target_pairs={{0,2},{2,6},{6,10},{10,14},{14,12},{12,8},{8,4},{4,0},{1,3},{3,7},... | collective-permute-start | bytes 393224 | tf_op jit(solution)/shard_map/ppermute | solution.py:79
  145.0 10.7 %collective-permute-start.25 = (f32[32,1152]{1,0:T(8,128)S(1)}, f32[32,1152]{1,0:T(8,128)S(1)}, u32[]{:S(2)}, u32[]{:S(2)}) collective-permute-start(f32[32,1152]{1,0:T(8,128)S(1)} %bitcast_add_fusion.9), channel_id=1, source_target_pairs={{2,0},{6,2},{10,6},{14,10},{12,14},{8,12},{4,8},{0,4},{3,1},{7,3},... | collective-permute-start | bytes 442376 | tf_op jit(solution)/shard_map/ppermute | solution.py:79
  148.9 5.2 %collective-permute-start.12 = (f32[32,1024]{1,0:T(8,128)S(1)}, f32[32,1024]{1,0:T(8,128)S(1)}, u32[]{:S(2)}, u32[]{:S(2)}) collective-permute-start(f32[32,1024]{1,0:T(8,128)S(1)} %bitcast_add_fusion.15), channel_id=1, source_target_pairs={{0,2},{2,6},{6,10},{10,14},{14,12},{12,8},{8,4},{4,0},{1,3},{3,7},... | collective-permute-start | bytes 393224 | tf_op jit(solution)/shard_map/ppermute | solution.py:79
  154.0 18.9 %collective-permute-start.5 = (bf16[512,4,128]{0,2,1:T(8,128)(2,1)S(1)}, bf16[512,4,128]{0,2,1:T(8,128)(2,1)S(1)}, u32[]{:S(2)}, u32[]{:S(2)}) collective-permute-start(bf16[512,4,128]{0,2,1:T(8,128)(2,1)S(1)} %bitcast.255), channel_id=1, source_target_pairs={{0,1},{1,0},{2,3},{3,2},{4,5},{5,4},{6,7},{7,6},{8,9},{9,8},{10,11... | collective-permute-start | bytes 1572872 | tf_op jit(solution)/shard_map/ppermute | solution.py:26
  154.1 5.9 %collective-permute-start.13 = (f32[32,1024]{1,0:T(8,128)S(1)}, f32[32,1024]{1,0:T(8,128)S(1)}, u32[]{:S(2)}, u32[]{:S(2)}) collective-permute-start(f32[32,1024]{1,0:T(8,128)S(1)} %bitcast_add_fusion.14), channel_id=1, source_target_pairs={{0,2},{2,6},{6,10},{10,14},{14,12},{12,8},{8,4},{4,0},{1,3},{3,7},... | collective-permute-start | bytes 393224 | tf_op jit(solution)/shard_map/ppermute | solution.py:79
  155.8 5.2 %collective-permute-start.26 = (f32[32,1152]{1,0:T(8,128)S(1)}, f32[32,1152]{1,0:T(8,128)S(1)}, u32[]{:S(2)}, u32[]{:S(2)}) collective-permute-start(f32[32,1152]{1,0:T(8,128)S(1)} %bitcast_add_fusion.8), channel_id=1, source_target_pairs={{2,0},{6,2},{10,6},{14,10},{12,14},{8,12},{4,8},{0,4},{3,1},{7,3},... | collective-permute-start | bytes 442376 | tf_op jit(solution)/shard_map/ppermute | solution.py:79
  160.1 5.1 %collective-permute-start.14 = (f32[32,1024]{1,0:T(8,128)S(1)}, f32[32,1024]{1,0:T(8,128)S(1)}, u32[]{:S(2)}, u32[]{:S(2)}) collective-permute-start(f32[32,1024]{1,0:T(8,128)S(1)} %bitcast_add_fusion.13), channel_id=1, source_target_pairs={{0,2},{2,6},{6,10},{10,14},{14,12},{12,8},{8,4},{4,0},{1,3},{3,7},... | collective-permute-start | bytes 393224 | tf_op jit(solution)/shard_map/ppermute | solution.py:79
  161.0 5.2 %collective-permute-start.27 = (f32[32,1152]{1,0:T(8,128)S(1)}, f32[32,1152]{1,0:T(8,128)S(1)}, u32[]{:S(2)}, u32[]{:S(2)}) collective-permute-start(f32[32,1152]{1,0:T(8,128)S(1)} %bitcast_add_fusion.7), channel_id=1, source_target_pairs={{2,0},{6,2},{10,6},{14,10},{12,14},{8,12},{4,8},{0,4},{3,1},{7,3},... | collective-permute-start | bytes 442376 | tf_op jit(solution)/shard_map/ppermute | solution.py:79
  166.2 5.7 %collective-permute-start.28 = (f32[32,1152]{1,0:T(8,128)S(1)}, f32[32,1152]{1,0:T(8,128)S(1)}, u32[]{:S(2)}, u32[]{:S(2)}) collective-permute-start(f32[32,1152]{1,0:T(8,128)S(1)} %bitcast_add_fusion.6), channel_id=1, source_target_pairs={{2,0},{6,2},{10,6},{14,10},{12,14},{8,12},{4,8},{0,4},{3,1},{7,3},... | collective-permute-start | bytes 442376 | tf_op jit(solution)/shard_map/ppermute | solution.py:79
  169.5 10.6 %collective-permute-start.16 = (bf16[32,1024]{1,0:T(8,128)(2,1)S(1)}, bf16[32,1024]{1,0:T(8,128)(2,1)S(1)}, u32[]{:S(2)}, u32[]{:S(2)}) collective-permute-start(bf16[32,1024]{1,0:T(8,128)(2,1)S(1)} %collective-permute-done.15), channel_id=1, source_target_pairs={{0,2},{2,6},{6,10},{10,14},{14,12},{12,8},{8,4},{4,0},{1,3},{3,7},... | collective-permute-start | bytes 196616 | tf_op jit(solution)/shard_map/ppermute | solution.py:83
  171.9 10.2 %collective-permute-start.29 = (bf16[32,1152]{1,0:T(8,128)(2,1)S(1)}, bf16[32,1152]{1,0:T(8,128)(2,1)S(1)}, u32[]{:S(2)}, u32[]{:S(2)}) collective-permute-start(bf16[32,1152]{1,0:T(8,128)(2,1)S(1)} %get-tuple-element.54), channel_id=1, source_target_pairs={{2,0},{6,2},{10,6},{14,10},{12,14},{8,12},{4,8},{0,4},{3,1},{7,3},... | collective-permute-start | bytes 221192 | tf_op jit(solution)/shard_map/ppermute | solution.py:83
  173.7 24.4 %collective-permute-start.7 = (bf16[1024,1,128]{0,2,1:T(8,128)(2,1)S(1)}, bf16[1024,1,128]{0,2,1:T(8,128)(2,1)S(1)}, u32[]{:S(2)}, u32[]{:S(2)}) collective-permute-start(bf16[1024,1,128]{0,2,1:T(8,128)(2,1)S(1)} %get-tuple-element.66), channel_id=1, source_target_pairs={{2,0},{4,2},{6,4},{8,6},{10,8},{12,10},{14,12},{3,1},{5,3},{7,5},{... | collective-permute-start | bytes 786440 | tf_op jit(solution)/shard_map/ppermute | solution.py:20
  175.0 23.2 %collective-permute-start.6 = (bf16[1024,1,128]{0,2,1:T(8,128)(2,1)S(1)}, bf16[1024,1,128]{0,2,1:T(8,128)(2,1)S(1)}, u32[]{:S(2)}, u32[]{:S(2)}) collective-permute-start(bf16[1024,1,128]{0,2,1:T(8,128)(2,1)S(1)} %get-tuple-element.67), channel_id=1, source_target_pairs={{0,2},{2,4},{4,6},{6,8},{8,10},{10,12},{12,14},{1,3},{3,5},{5,7},{... | collective-permute-start | bytes 786440 | tf_op jit(solution)/shard_map/ppermute | solution.py:19
  180.1 6.3 %collective-permute-start.17 = (bf16[32,1024]{1,0:T(8,128)(2,1)S(1)}, bf16[32,1024]{1,0:T(8,128)(2,1)S(1)}, u32[]{:S(2)}, u32[]{:S(2)}) collective-permute-start(bf16[32,1024]{1,0:T(8,128)(2,1)S(1)} %collective-permute-done.16), channel_id=1, source_target_pairs={{0,2},{2,6},{6,10},{10,14},{14,12},{12,8},{8,4},{4,0},{1,3},{3,7},... | collective-permute-start | bytes 196616 | tf_op jit(solution)/shard_map/ppermute | solution.py:83
  182.1 6.7 %collective-permute-start.30 = (bf16[32,1152]{1,0:T(8,128)(2,1)S(1)}, bf16[32,1152]{1,0:T(8,128)(2,1)S(1)}, u32[]{:S(2)}, u32[]{:S(2)}) collective-permute-start(bf16[32,1152]{1,0:T(8,128)(2,1)S(1)} %collective-permute-done.29), channel_id=1, source_target_pairs={{2,0},{6,2},{10,6},{14,10},{12,14},{8,12},{4,8},{0,4},{3,1},{7,3},... | collective-permute-start | bytes 221192 | tf_op jit(solution)/shard_map/ppermute | solution.py:83
  186.4 4.9 %collective-permute-start.18 = (bf16[32,1024]{1,0:T(8,128)(2,1)S(1)}, bf16[32,1024]{1,0:T(8,128)(2,1)S(1)}, u32[]{:S(2)}, u32[]{:S(2)}) collective-permute-start(bf16[32,1024]{1,0:T(8,128)(2,1)S(1)} %collective-permute-done.17), channel_id=1, source_target_pairs={{0,2},{2,6},{6,10},{10,14},{14,12},{12,8},{8,4},{4,0},{1,3},{3,7},... | collective-permute-start | bytes 196616 | tf_op jit(solution)/shard_map/ppermute | solution.py:83
  188.9 9.2 %collective-permute-start.31 = (bf16[32,1152]{1,0:T(8,128)(2,1)S(1)}, bf16[32,1152]{1,0:T(8,128)(2,1)S(1)}, u32[]{:S(2)}, u32[]{:S(2)}) collective-permute-start(bf16[32,1152]{1,0:T(8,128)(2,1)S(1)} %collective-permute-done.30), channel_id=1, source_target_pairs={{2,0},{6,2},{10,6},{14,10},{12,14},{8,12},{4,8},{0,4},{3,1},{7,3},... | collective-permute-start | bytes 221192 | tf_op jit(solution)/shard_map/ppermute | solution.py:83
  195.7 9.3 %collective-permute-start.20 = (bf16[32,1024]{1,0:T(8,128)(2,1)S(1)}, bf16[32,1024]{1,0:T(8,128)(2,1)S(1)}, u32[]{:S(2)}, u32[]{:S(2)}) collective-permute-start(bf16[32,1024]{1,0:T(8,128)(2,1)S(1)} %collective-permute-done.19), channel_id=1, source_target_pairs={{0,2},{2,6},{6,10},{10,14},{14,12},{12,8},{8,4},{4,0},{1,3},{3,7},... | collective-permute-start | bytes 196616 | tf_op jit(solution)/shard_map/ppermute | solution.py:83
  198.0 8.9 %collective-permute-start.32 = (bf16[32,1152]{1,0:T(8,128)(2,1)S(1)}, bf16[32,1152]{1,0:T(8,128)(2,1)S(1)}, u32[]{:S(2)}, u32[]{:S(2)}) collective-permute-start(bf16[32,1152]{1,0:T(8,128)(2,1)S(1)} %collective-permute-done.31), channel_id=1, source_target_pairs={{2,0},{6,2},{10,6},{14,10},{12,14},{8,12},{4,8},{0,4},{3,1},{7,3},... | collective-permute-start | bytes 221192 | tf_op jit(solution)/shard_map/ppermute | solution.py:83
  207.0 4.4 %collective-permute-start.33 = (bf16[32,1152]{1,0:T(8,128)(2,1)S(1)}, bf16[32,1152]{1,0:T(8,128)(2,1)S(1)}, u32[]{:S(2)}, u32[]{:S(2)}) collective-permute-start(bf16[32,1152]{1,0:T(8,128)(2,1)S(1)} %collective-permute-done.32), channel_id=1, source_target_pairs={{2,0},{6,2},{10,6},{14,10},{12,14},{8,12},{4,8},{0,4},{3,1},{7,3},... | collective-permute-start | bytes 221192 | tf_op jit(solution)/shard_map/ppermute | solution.py:83
  (18 other events, 181.3 us)
Sparse Core Ops, SparseCore 0:
  10.0 74.9 all-gather.1
  93.5 7.7 reduce-scatter.1

commit v13 on v7

--- a/solution.py
+++ b/solution.py
@@ -96,7 +96,7 @@
             stacked = jnp.stack([g[leaf] for g in gathered[part]], 0)
             order = (signs[part] * (position - jnp.arange(count))) % count
             halves.append(jnp.take(stacked, order, axis=0).reshape((-1,) + stacked.shape[2:]))
-        results.append(jnp.concatenate(halves, 0).astype(jnp.float32))
+        results.append(halves)
     return results
 
 
@@ -140,15 +140,17 @@
         joined = lax.dot_general(
             shares, squares_ones, (((1,), (1,)), ((), ())), preferred_element_type=jnp.float32
         )
+        scale_factor = 1.0 / math.sqrt(pixels * lax.axis_size("row"))
         if len(ring) <= 16:
-            (joined_total,) = ring_sum([joined], ring)
+            (halves,) = ring_sum([joined], ring)
+            gamma_total = jnp.concatenate([h[:, :lat_all] for h in halves], 0)
+            beta_total = jnp.concatenate([h[:, lat_all] for h in halves], 0)
         else:
             joined_total = lax.psum(joined, "row")
-        gamma_total = joined_total[:, :lat_all]
-        beta_total = joined_total[:, lat_all]
-        scale_factor = 1.0 / math.sqrt(pixels * lax.axis_size("row"))
-        grad_gamma = gamma_total * scale_factor
-        grad_beta = beta_total * scale_factor
+            gamma_total = joined_total[:, :lat_all]
+            beta_total = joined_total[:, lat_all]
+        grad_gamma = gamma_total.astype(jnp.float32) * scale_factor
+        grad_beta = beta_total.astype(jnp.float32) * scale_factor
         grad_all = chan_gather(latent_grad.reshape(lat_local, row_count, col_count))
         grad_rimmed = extended(grad_all, (("row", 1),), 1)
         grad_padded = jnp.pad(grad_rimmed, ((0, 0), (0, 0), (1, 1)))

time: 215 us -> 215 us (level)
  no operation moved by 1% of the time
where the time goes in v13:
time: 215 us
  waiting for transfers between devices  99.4 us (46%)
  starting transfers between devices  44.4 us (21%)
  between operations  25.6 us (12%)
  matrix products  20.2 us (9%)
  local copies, waits for them, and re-layouts  13.3 us (6%)
  other arithmetic  11.6 us (5%)
    all_gather x1, waiting for transfers between devices, per_device(): shard_piece = lax.all_gather(conv_weight, 'row', axis=0, tiled=True)  59.7 us
    ppermute x14, waiting for transfers between devices, ring_sum(): got = lax.ppermute(carry[part], 'row', moves[part])  20.9 us
    ppermute x14, starting transfers between devices, ring_sum(): gathered[part].append(lax.ppermute(gathered[part][-1], 'row', moves[part]))  16.5 us
    ppermute x14, starting transfers between devices, ring_sum(): got = lax.ppermute(carry[part], 'row', moves[part])  15.1 us
    ppermute x14, waiting for transfers between devices, ring_sum(): gathered[part].append(lax.ppermute(gathered[part][-1], 'row', moves[part]))  13.8 us
    ppermute x2, starting transfers between devices, extended(): before = lax.ppermute(last, axis, up)  9.44 us
    dot_general x9, matrix products, per_device(): jnp.dot(shard_piece[:, tap_index, :], window, preferred_element_type=jnp....  8.27 us
    unnamed x51, local copies, waits for them, and re-layouts  5.53 us
  transfers between devices with their start and end apart: 38, of which 15 were waited for; matrix products, arithmetic and copies ran while one was open for 15% of the time, Pallas kernels for 0%

profile of v13, /device:TPU:0, one launch (start us, length us, event | category | flops | bytes accessed | tf_op | source)
XLA Modules:
  0.0 214.5 jit_solution(288428517567403523)
XLA Ops:
  9.2 4.9 %collective-permute-start = (bf16[212,1,128]{2,1,0:T(2,128)(2,1)S(1)}, bf16[212,1,128]{2,1,0:T(2,128)(2,1)S(1)}, u32[]{:S(2)}, u32[]{:S(2)}) collective-permute-start(bf16[212,1,128]{2,1,0:T(2,128)(2,1)S(1)} %get-tuple-element.55), channel_id=1, source_target_pairs={{0,2},{2,4},{4,6},{6,8},{8,10},{10,12},{12,14},{1,3},{3,5},{5,7},{... | collective-permute-start | bytes 162824 | tf_op jit(solution)/shard_map/ppermute | solution.py:19
  16.5 4.2 %collective-permute-done.1 = bf16[212,1,128]{2,1,0:T(2,128)(2,1)S(1)} collective-permute-done((bf16[212,1,128]{2,1,0:T(2,128)(2,1)S(1)}, bf16[212,1,128]{2,1,0:T(2,128)(2,1)S(1)}, u32[]{:S(2)}, u32[]{:S(2)}) %collective-permute-start.1) | collective-permute-done | bytes 54304 | tf_op jit(solution)/shard_map/ppermute | solution.py:20
  20.7 1.6 pad_maximum_fusion.3
  25.3 59.7 %all-gather.2.cloned.1.call-done = bf16[1024,9,212]{0,2,1:T(8,128)(2,1)} async-done(((bf16[128,9,212]{0,2,1:T(8,128)(2,1)}), bf16[1024,9,212]{0,2,1:T(8,128)(2,1)}) %all-gather.2.cloned.1.call-update) | async-done | bytes 3907600 | tf_op jit(solution)/shard_map/all_gather | solution.py:112
  85.0 1.6 fusion.51
  91.0 2.3 %bitcast_add_fusion = f32[1024,512]{0,1:T(8,128)} fusion(f32[512,1024]{1,0:T(8,128)S(1)} %fusion.51, f32[512,1024]{1,0:T(8,128)S(1)} %fusion.49, f32[512,1024]{1,0:T(8,128)S(1)} %fusion.47, f32[1024,512]{0,1:T(8,128)S(1)} %fusion.45, f32[512,1024]{1,0:T(8,128)S(1)} %fusion.43, f32[512,1024]{1,0:T(8,128)S(1)} %fusion.41, f32[512,1024]{1,0:T(8,128)S(1)} %fusion.37, ...), kind=kOutput, calls=%fused_computation.23 | convolution fusion | flops 226492416 | bytes 19537920 | tf_op jit(solution)/shard_map/dot_general | solution.py:118
  112.9 2.3 %fusion.13 = (bf16[512,512]{0,1:T(8,128)(2,1)}, f32[512,512]{0,1:T(8,128)}, bf16[512,512]{0,1:T(8,128)(2,1)}) fusion(f32[512,512]{0,1:T(8,128)S(1)} %copy-done.2, f32[512,4,128]{0,2,1:T(8,128)S(1)} %copy.14, bf16[1024,512]{0,1:T(8,128)(2,1)S(1)} %fusion.28, bf16[512,1024]{1,0:T(8,128)(2,1)S(1)} %copy-done.3, f32[512]{0:T(512)S(1)} %copy-done.8), kind=kOutput, calls=%fused_computation.44 | convolution fusion | flops 539492352 | bytes 6293504 | tf_op jit(solution)/shard_map/dot_general | solution.py:124
  115.2 1.9 fusion.11
  117.1 2.1 copy.15
  119.5 2.1 collective-permute-start.8
  121.5 4.2 %collective-permute-done.22 = f32[32,1152]{1,0:T(8,128)S(1)} collective-permute-done((f32[32,1152]{1,0:T(8,128)S(1)}, f32[32,1152]{1,0:T(8,128)S(1)}, u32[]{:S(2)}, u32[]{:S(2)}) %collective-permute-start.22) | collective-permute-done | bytes 147488 | tf_op jit(solution)/shard_map/ppermute | solution.py:85
  126.3 1.8 collective-permute-start.9
  128.1 3.3 %collective-permute-done.23 = f32[32,1152]{1,0:T(8,128)S(1)} collective-permute-done((f32[32,1152]{1,0:T(8,128)S(1)}, f32[32,1152]{1,0:T(8,128)S(1)}, u32[]{:S(2)}, u32[]{:S(2)}) %collective-permute-start.23) | collective-permute-done | bytes 147488 | tf_op jit(solution)/shard_map/ppermute | solution.py:85
  133.5 3.0 %collective-permute-done.24 = f32[32,1152]{1,0:T(8,128)S(1)} collective-permute-done((f32[32,1152]{1,0:T(8,128)S(1)}, f32[32,1152]{1,0:T(8,128)S(1)}, u32[]{:S(2)}, u32[]{:S(2)}) %collective-permute-start.24) | collective-permute-done | bytes 147488 | tf_op jit(solution)/shard_map/ppermute | solution.py:85
  138.8 3.3 %fusion.10 = bf16[512,512]{0,1:T(8,128)(2,1)S(1)} fusion(f32[512,512]{0,1:T(8,128)S(1)} %copy-done.5, s32[]{:T(128)S(6)} %select_n.194, bf16[512,512]{1,0:T(8,128)(2,1)S(1)} %copy-done.7, bf16[512,512]{1,0:T(8,128)(2,1)} %collective-permute-done.3, bf16[512,512]{0,1:T(8,128)(2,1)} %get-tuple-element.32, bf16[512,512]{0,1:T(8,128)(2,1)} %collective-permute-done.4, ...), kind=kOutput, calls=%fused_computation.41 | convolution fusion | flops 546308096 | bytes 4719616 | tf_op jit(solution)/shard_map/dot_general | solution.py:134
  144.3 4.1 %collective-permute-done.26 = f32[32,1152]{1,0:T(8,128)S(1)} collective-permute-done((f32[32,1152]{1,0:T(8,128)S(1)}, f32[32,1152]{1,0:T(8,128)S(1)}, u32[]{:S(2)}, u32[]{:S(2)}) %collective-permute-start.26) | collective-permute-done | bytes 147488 | tf_op jit(solution)/shard_map/ppermute | solution.py:85
  150.6 3.3 %collective-permute-done.27 = f32[32,1152]{1,0:T(8,128)S(1)} collective-permute-done((f32[32,1152]{1,0:T(8,128)S(1)}, f32[32,1152]{1,0:T(8,128)S(1)}, u32[]{:S(2)}, u32[]{:S(2)}) %collective-permute-start.27) | collective-permute-done | bytes 147488 | tf_op jit(solution)/shard_map/ppermute | solution.py:85
  156.1 3.0 %collective-permute-done.28 = f32[32,1152]{1,0:T(8,128)S(1)} collective-permute-done((f32[32,1152]{1,0:T(8,128)S(1)}, f32[32,1152]{1,0:T(8,128)S(1)}, u32[]{:S(2)}, u32[]{:S(2)}) %collective-permute-start.28) | collective-permute-done | bytes 147488 | tf_op jit(solution)/shard_map/ppermute | solution.py:85
  163.3 4.6 %collective-permute-start.6 = (bf16[1024,1,128]{0,2,1:T(8,128)(2,1)S(1)}, bf16[1024,1,128]{0,2,1:T(8,128)(2,1)S(1)}, u32[]{:S(2)}, u32[]{:S(2)}) collective-permute-start(bf16[1024,1,128]{0,2,1:T(8,128)(2,1)S(1)} %get-tuple-element.44), channel_id=1, source_target_pairs={{0,2},{2,4},{4,6},{6,8},{8,10},{10,12},{12,14},{1,3},{3,5},{5,7},{... | collective-permute-start | bytes 786440 | tf_op jit(solution)/shard_map/ppermute | solution.py:19
  169.4 1.5 collective-permute-start.16
  170.9 2.6 %collective-permute-done.30 = bf16[32,1152]{1,0:T(8,128)(2,1)S(1)} collective-permute-done((bf16[32,1152]{1,0:T(8,128)(2,1)S(1)}, bf16[32,1152]{1,0:T(8,128)(2,1)S(1)}, u32[]{:S(2)}, u32[]{:S(2)}) %collective-permute-start.30) | collective-permute-done | bytes 73760 | tf_op jit(solution)/shard_map/ppermute | solution.py:91
  174.4 2.1 %collective-permute-done.16 = bf16[32,1152]{1,0:T(8,128)(2,1)S(1)} collective-permute-done((bf16[32,1152]{1,0:T(8,128)(2,1)S(1)}, bf16[32,1152]{1,0:T(8,128)(2,1)S(1)}, u32[]{:S(2)}, u32[]{:S(2)}) %collective-permute-start.16) | collective-permute-done | bytes 73760 | tf_op jit(solution)/shard_map/ppermute | solution.py:91
  176.6 2.5 %collective-permute-start.17 = (bf16[32,1152]{1,0:T(8,128)(2,1)S(1)}, bf16[32,1152]{1,0:T(8,128)(2,1)S(1)}, u32[]{:S(2)}, u32[]{:S(2)}) collective-permute-start(bf16[32,1152]{1,0:T(8,128)(2,1)S(1)} %collective-permute-done.16), channel_id=1, source_target_pairs={{0,2},{2,6},{6,10},{10,14},{14,12},{12,8},{8,4},{4,0},{1,3},{3,7},... | collective-permute-start | bytes 221192 | tf_op jit(solution)/shard_map/ppermute | solution.py:91
  179.2 1.9 collective-permute-done.17
  181.0 2.4 %collective-permute-start.18 = (bf16[32,1152]{1,0:T(8,128)(2,1)S(1)}, bf16[32,1152]{1,0:T(8,128)(2,1)S(1)}, u32[]{:S(2)}, u32[]{:S(2)}) collective-permute-start(bf16[32,1152]{1,0:T(8,128)(2,1)S(1)} %collective-permute-done.17), channel_id=1, source_target_pairs={{0,2},{2,6},{6,10},{10,14},{14,12},{12,8},{8,4},{4,0},{1,3},{3,7},... | collective-permute-start | bytes 221192 | tf_op jit(solution)/shard_map/ppermute | solution.py:91
  190.3 2.1 collective-permute-start.19
  192.4 2.6 %collective-permute-done.33 = bf16[32,1152]{1,0:T(8,128)(2,1)S(1)} collective-permute-done((bf16[32,1152]{1,0:T(8,128)(2,1)S(1)}, bf16[32,1152]{1,0:T(8,128)(2,1)S(1)}, u32[]{:S(2)}, u32[]{:S(2)}) %collective-permute-start.33) | collective-permute-done | bytes 73760 | tf_op jit(solution)/shard_map/ppermute | solution.py:91
  195.2 1.8 collective-permute-start.20
  197.0 2.2 %collective-permute-done.34 = bf16[32,1152]{1,0:T(8,128)(2,1)S(1)} collective-permute-done((bf16[32,1152]{1,0:T(8,128)(2,1)S(1)}, bf16[32,1152]{1,0:T(8,128)(2,1)S(1)}, u32[]{:S(2)}, u32[]{:S(2)}) %collective-permute-start.34) | collective-permute-done | bytes 73760 | tf_op jit(solution)/shard_map/ppermute | solution.py:91
  199.6 1.7 collective-permute-start.21
  201.4 2.2 %collective-permute-done.35 = bf16[32,1152]{1,0:T(8,128)(2,1)S(1)} collective-permute-done((bf16[32,1152]{1,0:T(8,128)(2,1)S(1)}, bf16[32,1152]{1,0:T(8,128)(2,1)S(1)}, u32[]{:S(2)}, u32[]{:S(2)}) %collective-permute-start.35) | collective-permute-done | bytes 73760 | tf_op jit(solution)/shard_map/ppermute | solution.py:91
  205.5 1.6 convert_multiply_fusion
  (167 shorter events, 48.4 us)
Async XLA Ops:
  7.2 77.8 %all-gather.2.cloned.1.call-start = ((), (), s32[]{:S(2)}) async-start(), calls=%async_computation.1 | async-start | bytes 4478976 | tf_op jit(solution)/shard_map/all_gather | solution.py:112
  7.9 100.2 %reduce-scatter.2.cloned.1.call-start = ((), (), s32[]{:S(2)}) async-start(), calls=%async_computation.2 | async-start | bytes 3145728 | tf_op jit(solution)/shard_map/reduce_scatter | solution.py:121
  9.2 7.3 %collective-permute-start = (bf16[212,1,128]{2,1,0:T(2,128)(2,1)S(1)}, bf16[212,1,128]{2,1,0:T(2,128)(2,1)S(1)}, u32[]{:S(2)}, u32[]{:S(2)}) collective-permute-start(bf16[212,1,128]{2,1,0:T(2,128)(2,1)S(1)} %get-tuple-element.55), channel_id=1, source_target_pairs={{0,2},{2,4},{4,6},{6,8},{8,10},{10,12},{12,14},{1,3},{3,5},{5,7},{... | collective-permute-start | bytes 162824 | tf_op jit(solution)/shard_map/ppermute | solution.py:19
  14.1 6.6 %collective-permute-start.1 = (bf16[212,1,128]{2,1,0:T(2,128)(2,1)S(1)}, bf16[212,1,128]{2,1,0:T(2,128)(2,1)S(1)}, u32[]{:S(2)}, u32[]{:S(2)}) collective-permute-start(bf16[212,1,128]{2,1,0:T(2,128)(2,1)S(1)} %get-tuple-element.56), channel_id=1, source_target_pairs={{2,0},{4,2},{6,4},{8,6},{10,8},{12,10},{14,12},{3,1},{5,3},{7,5},{... | collective-permute-start | bytes 162824 | tf_op jit(solution)/shard_map/ppermute | solution.py:20
  95.6 43.1 %collective-permute-start.3 = (bf16[512,512]{1,0:T(8,128)(2,1)}, bf16[512,512]{1,0:T(8,128)(2,1)}, u32[]{:S(2)}, u32[]{:S(2)}) collective-permute-start(bf16[512,512]{1,0:T(8,128)(2,1)} %get-tuple-element.45), channel_id=1, source_target_pairs={{0,1},{1,0},{2,3},{3,2},{4,5},{5,4},{6,7},{7,6},{8,9},{9,8},{10,11... | collective-permute-start | bytes 1572872 | tf_op jit(solution)/shard_map/ppermute | solution.py:132
  115.1 23.6 %collective-permute-start.4 = (bf16[512,512]{0,1:T(8,128)(2,1)}, bf16[512,512]{0,1:T(8,128)(2,1)}, u32[]{:S(2)}, u32[]{:S(2)}) collective-permute-start(bf16[512,512]{0,1:T(8,128)(2,1)} %get-tuple-element.32), channel_id=1, source_target_pairs={{0,1},{1,0},{2,3},{3,2},{4,5},{5,4},{6,7},{7,6},{8,9},{9,8},{10,11... | collective-permute-start | bytes 1572872 | tf_op jit(solution)/shard_map/ppermute | solution.py:26
  119.4 6.3 %collective-permute-start.22 = (f32[32,1152]{1,0:T(8,128)S(1)}, f32[32,1152]{1,0:T(8,128)S(1)}, u32[]{:S(2)}, u32[]{:S(2)}) collective-permute-start(f32[32,1152]{1,0:T(8,128)S(1)} %select_bitcast_fusion), channel_id=1, source_target_pairs={{2,0},{6,2},{10,6},{14,10},{12,14},{8,12},{4,8},{0,4},{3,1},{7,3},... | collective-permute-start | bytes 442376 | tf_op jit(solution)/shard_map/ppermute | solution.py:85
  119.5 6.8 %collective-permute-start.8 = (f32[32,1152]{1,0:T(8,128)S(1)}, f32[32,1152]{1,0:T(8,128)S(1)}, u32[]{:S(2)}, u32[]{:S(2)}) collective-permute-start(f32[32,1152]{1,0:T(8,128)S(1)} %select_bitcast_fusion.1), channel_id=1, source_target_pairs={{0,2},{2,6},{6,10},{10,14},{14,12},{12,8},{8,4},{4,0},{1,3},{3,7},... | collective-permute-start | bytes 442376 | tf_op jit(solution)/shard_map/ppermute | solution.py:85
  125.7 5.6 %collective-permute-start.23 = (f32[32,1152]{1,0:T(8,128)S(1)}, f32[32,1152]{1,0:T(8,128)S(1)}, u32[]{:S(2)}, u32[]{:S(2)}) collective-permute-start(f32[32,1152]{1,0:T(8,128)S(1)} %bitcast_add_fusion.11), channel_id=1, source_target_pairs={{2,0},{6,2},{10,6},{14,10},{12,14},{8,12},{4,8},{0,4},{3,1},{7,3},... | collective-permute-start | bytes 442376 | tf_op jit(solution)/shard_map/ppermute | solution.py:85
  126.3 5.7 %collective-permute-start.9 = (f32[32,1152]{1,0:T(8,128)S(1)}, f32[32,1152]{1,0:T(8,128)S(1)}, u32[]{:S(2)}, u32[]{:S(2)}) collective-permute-start(f32[32,1152]{1,0:T(8,128)S(1)} %bitcast_add_fusion.18), channel_id=1, source_target_pairs={{0,2},{2,6},{6,10},{10,14},{14,12},{12,8},{8,4},{4,0},{1,3},{3,7},... | collective-permute-start | bytes 442376 | tf_op jit(solution)/shard_map/ppermute | solution.py:85
  131.4 5.2 %collective-permute-start.24 = (f32[32,1152]{1,0:T(8,128)S(1)}, f32[32,1152]{1,0:T(8,128)S(1)}, u32[]{:S(2)}, u32[]{:S(2)}) collective-permute-start(f32[32,1152]{1,0:T(8,128)S(1)} %bitcast_add_fusion.10), channel_id=1, source_target_pairs={{2,0},{6,2},{10,6},{14,10},{12,14},{8,12},{4,8},{0,4},{3,1},{7,3},... | collective-permute-start | bytes 442376 | tf_op jit(solution)/shard_map/ppermute | solution.py:85
  132.0 5.2 %collective-permute-start.10 = (f32[32,1152]{1,0:T(8,128)S(1)}, f32[32,1152]{1,0:T(8,128)S(1)}, u32[]{:S(2)}, u32[]{:S(2)}) collective-permute-start(f32[32,1152]{1,0:T(8,128)S(1)} %bitcast_add_fusion.17), channel_id=1, source_target_pairs={{0,2},{2,6},{6,10},{10,14},{14,12},{12,8},{8,4},{4,0},{1,3},{3,7},... | collective-permute-start | bytes 442376 | tf_op jit(solution)/shard_map/ppermute | solution.py:85
  136.6 5.5 %collective-permute-start.25 = (f32[32,1152]{1,0:T(8,128)S(1)}, f32[32,1152]{1,0:T(8,128)S(1)}, u32[]{:S(2)}, u32[]{:S(2)}) collective-permute-start(f32[32,1152]{1,0:T(8,128)S(1)} %bitcast_add_fusion.9), channel_id=1, source_target_pairs={{2,0},{6,2},{10,6},{14,10},{12,14},{8,12},{4,8},{0,4},{3,1},{7,3},... | collective-permute-start | bytes 442376 | tf_op jit(solution)/shard_map/ppermute | solution.py:85
  137.2 5.5 %collective-permute-start.11 = (f32[32,1152]{1,0:T(8,128)S(1)}, f32[32,1152]{1,0:T(8,128)S(1)}, u32[]{:S(2)}, u32[]{:S(2)}) collective-permute-start(f32[32,1152]{1,0:T(8,128)S(1)} %bitcast_add_fusion.16), channel_id=1, source_target_pairs={{0,2},{2,6},{6,10},{10,14},{14,12},{12,8},{8,4},{4,0},{1,3},{3,7},... | collective-permute-start | bytes 442376 | tf_op jit(solution)/shard_map/ppermute | solution.py:85
  142.0 19.3 %collective-permute-start.5 = (bf16[512,4,128]{0,2,1:T(8,128)(2,1)S(1)}, bf16[512,4,128]{0,2,1:T(8,128)(2,1)S(1)}, u32[]{:S(2)}, u32[]{:S(2)}) collective-permute-start(bf16[512,4,128]{0,2,1:T(8,128)(2,1)S(1)} %bitcast.249), channel_id=1, source_target_pairs={{0,1},{1,0},{2,3},{3,2},{4,5},{5,4},{6,7},{7,6},{8,9},{9,8},{10,11... | collective-permute-start | bytes 1572872 | tf_op jit(solution)/shard_map/ppermute | solution.py:26
  142.2 6.3 %collective-permute-start.26 = (f32[32,1152]{1,0:T(8,128)S(1)}, f32[32,1152]{1,0:T(8,128)S(1)}, u32[]{:S(2)}, u32[]{:S(2)}) collective-permute-start(f32[32,1152]{1,0:T(8,128)S(1)} %bitcast_add_fusion.8), channel_id=1, source_target_pairs={{2,0},{6,2},{10,6},{14,10},{12,14},{8,12},{4,8},{0,4},{3,1},{7,3},... | collective-permute-start | bytes 442376 | tf_op jit(solution)/shard_map/ppermute | solution.py:85
  142.8 6.3 %collective-permute-start.12 = (f32[32,1152]{1,0:T(8,128)S(1)}, f32[32,1152]{1,0:T(8,128)S(1)}, u32[]{:S(2)}, u32[]{:S(2)}) collective-permute-start(f32[32,1152]{1,0:T(8,128)S(1)} %bitcast_add_fusion.15), channel_id=1, source_target_pairs={{0,2},{2,6},{6,10},{10,14},{14,12},{12,8},{8,4},{4,0},{1,3},{3,7},... | collective-permute-start | bytes 442376 | tf_op jit(solution)/shard_map/ppermute | solution.py:85
  148.5 5.4 %collective-permute-start.27 = (f32[32,1152]{1,0:T(8,128)S(1)}, f32[32,1152]{1,0:T(8,128)S(1)}, u32[]{:S(2)}, u32[]{:S(2)}) collective-permute-start(f32[32,1152]{1,0:T(8,128)S(1)} %bitcast_add_fusion.7), channel_id=1, source_target_pairs={{2,0},{6,2},{10,6},{14,10},{12,14},{8,12},{4,8},{0,4},{3,1},{7,3},... | collective-permute-start | bytes 442376 | tf_op jit(solution)/shard_map/ppermute | solution.py:85
  149.1 5.4 %collective-permute-start.13 = (f32[32,1152]{1,0:T(8,128)S(1)}, f32[32,1152]{1,0:T(8,128)S(1)}, u32[]{:S(2)}, u32[]{:S(2)}) collective-permute-start(f32[32,1152]{1,0:T(8,128)S(1)} %bitcast_add_fusion.14), channel_id=1, source_target_pairs={{0,2},{2,6},{6,10},{10,14},{14,12},{12,8},{8,4},{4,0},{1,3},{3,7},... | collective-permute-start | bytes 442376 | tf_op jit(solution)/shard_map/ppermute | solution.py:85
  153.9 5.2 %collective-permute-start.28 = (f32[32,1152]{1,0:T(8,128)S(1)}, f32[32,1152]{1,0:T(8,128)S(1)}, u32[]{:S(2)}, u32[]{:S(2)}) collective-permute-start(f32[32,1152]{1,0:T(8,128)S(1)} %bitcast_add_fusion.6), channel_id=1, source_target_pairs={{2,0},{6,2},{10,6},{14,10},{12,14},{8,12},{4,8},{0,4},{3,1},{7,3},... | collective-permute-start | bytes 442376 | tf_op jit(solution)/shard_map/ppermute | solution.py:85
  154.6 5.2 %collective-permute-start.14 = (f32[32,1152]{1,0:T(8,128)S(1)}, f32[32,1152]{1,0:T(8,128)S(1)}, u32[]{:S(2)}, u32[]{:S(2)}) collective-permute-start(f32[32,1152]{1,0:T(8,128)S(1)} %bitcast_add_fusion.13), channel_id=1, source_target_pairs={{0,2},{2,6},{6,10},{10,14},{14,12},{12,8},{8,4},{4,0},{1,3},{3,7},... | collective-permute-start | bytes 442376 | tf_op jit(solution)/shard_map/ppermute | solution.py:85
  159.1 9.3 %collective-permute-start.29 = (bf16[32,1152]{1,0:T(8,128)(2,1)S(1)}, bf16[32,1152]{1,0:T(8,128)(2,1)S(1)}, u32[]{:S(2)}, u32[]{:S(2)}) collective-permute-start(bf16[32,1152]{1,0:T(8,128)(2,1)S(1)} %get-tuple-element.29), channel_id=1, source_target_pairs={{2,0},{6,2},{10,6},{14,10},{12,14},{8,12},{4,8},{0,4},{3,1},{7,3},... | collective-permute-start | bytes 221192 | tf_op jit(solution)/shard_map/ppermute | solution.py:91
  159.8 9.6 %collective-permute-start.15 = (bf16[32,1152]{1,0:T(8,128)(2,1)S(1)}, bf16[32,1152]{1,0:T(8,128)(2,1)S(1)}, u32[]{:S(2)}, u32[]{:S(2)}) collective-permute-start(bf16[32,1152]{1,0:T(8,128)(2,1)S(1)} %get-tuple-element.27), channel_id=1, source_target_pairs={{0,2},{2,6},{6,10},{10,14},{14,12},{12,8},{8,4},{4,0},{1,3},{3,7},... | collective-permute-start | bytes 221192 | tf_op jit(solution)/shard_map/ppermute | solution.py:91
  162.0 21.4 %collective-permute-start.7 = (bf16[1024,1,128]{0,2,1:T(8,128)(2,1)S(1)}, bf16[1024,1,128]{0,2,1:T(8,128)(2,1)S(1)}, u32[]{:S(2)}, u32[]{:S(2)}) collective-permute-start(bf16[1024,1,128]{0,2,1:T(8,128)(2,1)S(1)} %get-tuple-element.43), channel_id=1, source_target_pairs={{2,0},{4,2},{6,4},{8,6},{10,8},{12,10},{14,12},{3,1},{5,3},{7,5},{... | collective-permute-start | bytes 786440 | tf_op jit(solution)/shard_map/ppermute | solution.py:20
  163.3 20.1 %collective-permute-start.6 = (bf16[1024,1,128]{0,2,1:T(8,128)(2,1)S(1)}, bf16[1024,1,128]{0,2,1:T(8,128)(2,1)S(1)}, u32[]{:S(2)}, u32[]{:S(2)}) collective-permute-start(bf16[1024,1,128]{0,2,1:T(8,128)(2,1)S(1)} %get-tuple-element.44), channel_id=1, source_target_pairs={{0,2},{2,4},{4,6},{6,8},{8,10},{10,12},{12,14},{1,3},{3,5},{5,7},{... | collective-permute-start | bytes 786440 | tf_op jit(solution)/shard_map/ppermute | solution.py:19
  168.4 5.1 %collective-permute-start.30 = (bf16[32,1152]{1,0:T(8,128)(2,1)S(1)}, bf16[32,1152]{1,0:T(8,128)(2,1)S(1)}, u32[]{:S(2)}, u32[]{:S(2)}) collective-permute-start(bf16[32,1152]{1,0:T(8,128)(2,1)S(1)} %collective-permute-done.29), channel_id=1, source_target_pairs={{2,0},{6,2},{10,6},{14,10},{12,14},{8,12},{4,8},{0,4},{3,1},{7,3},... | collective-permute-start | bytes 221192 | tf_op jit(solution)/shard_map/ppermute | solution.py:91
  169.4 7.2 %collective-permute-start.16 = (bf16[32,1152]{1,0:T(8,128)(2,1)S(1)}, bf16[32,1152]{1,0:T(8,128)(2,1)S(1)}, u32[]{:S(2)}, u32[]{:S(2)}) collective-permute-start(bf16[32,1152]{1,0:T(8,128)(2,1)S(1)} %collective-permute-done.15), channel_id=1, source_target_pairs={{0,2},{2,6},{6,10},{10,14},{14,12},{12,8},{8,4},{4,0},{1,3},{3,7},... | collective-permute-start | bytes 221192 | tf_op jit(solution)/shard_map/ppermute | solution.py:91
  173.6 5.5 %collective-permute-start.31 = (bf16[32,1152]{1,0:T(8,128)(2,1)S(1)}, bf16[32,1152]{1,0:T(8,128)(2,1)S(1)}, u32[]{:S(2)}, u32[]{:S(2)}) collective-permute-start(bf16[32,1152]{1,0:T(8,128)(2,1)S(1)} %collective-permute-done.30), channel_id=1, source_target_pairs={{2,0},{6,2},{10,6},{14,10},{12,14},{8,12},{4,8},{0,4},{3,1},{7,3},... | collective-permute-start | bytes 221192 | tf_op jit(solution)/shard_map/ppermute | solution.py:91
  179.1 11.2 %collective-permute-start.32 = (bf16[32,1152]{1,0:T(8,128)(2,1)S(1)}, bf16[32,1152]{1,0:T(8,128)(2,1)S(1)}, u32[]{:S(2)}, u32[]{:S(2)}) collective-permute-start(bf16[32,1152]{1,0:T(8,128)(2,1)S(1)} %collective-permute-done.31), channel_id=1, source_target_pairs={{2,0},{6,2},{10,6},{14,10},{12,14},{8,12},{4,8},{0,4},{3,1},{7,3},... | collective-permute-start | bytes 221192 | tf_op jit(solution)/shard_map/ppermute | solution.py:91
  181.0 9.2 %collective-permute-start.18 = (bf16[32,1152]{1,0:T(8,128)(2,1)S(1)}, bf16[32,1152]{1,0:T(8,128)(2,1)S(1)}, u32[]{:S(2)}, u32[]{:S(2)}) collective-permute-start(bf16[32,1152]{1,0:T(8,128)(2,1)S(1)} %collective-permute-done.17), channel_id=1, source_target_pairs={{0,2},{2,6},{6,10},{10,14},{14,12},{12,8},{8,4},{4,0},{1,3},{3,7},... | collective-permute-start | bytes 221192 | tf_op jit(solution)/shard_map/ppermute | solution.py:91
  190.3 5.0 %collective-permute-start.19 = (bf16[32,1152]{1,0:T(8,128)(2,1)S(1)}, bf16[32,1152]{1,0:T(8,128)(2,1)S(1)}, u32[]{:S(2)}, u32[]{:S(2)}) collective-permute-start(bf16[32,1152]{1,0:T(8,128)(2,1)S(1)} %collective-permute-done.18), channel_id=1, source_target_pairs={{0,2},{2,6},{6,10},{10,14},{14,12},{12,8},{8,4},{4,0},{1,3},{3,7},... | collective-permute-start | bytes 221192 | tf_op jit(solution)/shard_map/ppermute | solution.py:91
  199.6 4.9 %collective-permute-start.21 = (bf16[32,1152]{1,0:T(8,128)(2,1)S(1)}, bf16[32,1152]{1,0:T(8,128)(2,1)S(1)}, u32[]{:S(2)}, u32[]{:S(2)}) collective-permute-start(bf16[32,1152]{1,0:T(8,128)(2,1)S(1)} %collective-permute-done.20), channel_id=1, source_target_pairs={{0,2},{2,6},{6,10},{10,14},{14,12},{12,8},{8,4},{4,0},{1,3},{3,7},... | collective-permute-start | bytes 221192 | tf_op jit(solution)/shard_map/ppermute | solution.py:91
  (16 other events, 122.9 us)
Sparse Core Ops, SparseCore 0:
  10.0 74.9 all-gather.1
  93.5 7.7 reduce-scatter.1

commit v14 on v7

--- a/solution.py
+++ b/solution.py
@@ -110,15 +110,25 @@
         rimmed = extended(band_strip, (("row", 1),), 1)
         strip_padded = jnp.pad(rimmed, ((0, 0), (0, 0), (1, 1)))
         shard_piece = lax.all_gather(conv_weight, "row", axis=0, tiled=True)
-        partial_value = jnp.zeros((shard_piece.shape[0], pixels), jnp.float32)
-        for tap_index, (row_shift, col_shift) in enumerate(TAPS):
-            window = strip_padded[
+        index = lax.axis_index("chan")
+        windows = [
+            strip_padded[
                 :, 1 + row_shift : 1 + row_shift + row_count, 1 + col_shift : 1 + col_shift + col_count
             ].reshape(in_local, pixels)
-            partial_value = partial_value + jnp.dot(
-                shard_piece[:, tap_index, :], window, preferred_element_type=jnp.float32
-            )
-        pre = lax.psum_scatter(partial_value, "chan", scatter_dimension=0, tiled=True)
+            for row_shift, col_shift in TAPS
+        ]
+
+        def half_conv(start):
+            rows = lax.dynamic_slice_in_dim(shard_piece, start, lat_local, 0)
+            total = jnp.zeros((lat_local, pixels), jnp.float32)
+            for tap_index in range(len(TAPS)):
+                total = total + jnp.dot(
+                    rows[:, tap_index, :], windows[tap_index], preferred_element_type=jnp.float32
+                )
+            return total
+
+        sent = lax.ppermute(half_conv((1 - index) * lat_local), "chan", SWAP)
+        pre = half_conv(index * lat_local) + sent
         squares_own = (pre * pre).astype(jnp.bfloat16)
         squares = chan_gather(squares_own)
         norm_value = gdn_beta[:, None] + jnp.dot(gdn_gamma, squares, preferred_element_type=jnp.float32)

time: 215 us -> 199 us (0.926)
  waiting for transfers between devices: 99.4 us -> 86 us
  other arithmetic: 11.9 us -> 9.41 us
    all_gather x1, waiting for transfers between devices: 59.7 us -> 50.6 us  [per_device(): shard_piece = lax.all_gather(conv_weight, 'row', axis=0, tiled=True)]
    ppermute x2, waiting for transfers between devices: 4.24 us -> 0.01 us  [extended(): after = lax.ppermute(leading, axis, down)]
    unnamed x51 -> x57, local copies, waits for them, and re-layouts: 5.53 us -> 3.61 us
    dot_general x9 -> x18, matrix products: 8.27 us -> 8.28 us  [half_conv(): jnp.dot(rows[:, tap_index, :], windows[tap_index], preferred_element_type...]
  transfers between devices with their start and end apart: 38 -> 38, of which waited for: 15 -> 14; matrix products, arithmetic and copies ran while one was open for 15% -> 19% of each run, Pallas kernels for 0% -> 0%
where the time goes in v14:
time: 199 us
  waiting for transfers between devices  86 us (43%)
  starting transfers between devices  44.9 us (23%)
  between operations  25.8 us (13%)
  matrix products  20.5 us (10%)
  local copies, waits for them, and re-layouts  12.3 us (6%)
  other arithmetic  9.41 us (5%)
    all_gather x1, waiting for transfers between devices, per_device(): shard_piece = lax.all_gather(conv_weight, 'row', axis=0, tiled=True)  50.6 us
    ppermute x14, waiting for transfers between devices, ring_sum(): got = lax.ppermute(carry[part], 'row', moves[part])  20.9 us
    ppermute x14, starting transfers between devices, ring_sum(): gathered[part].append(lax.ppermute(gathered[part][-1], 'row', moves[part]))  16.6 us
    ppermute x14, starting transfers between devices, ring_sum(): got = lax.ppermute(carry[part], 'row', moves[part])  14.9 us
    ppermute x14, waiting for transfers between devices, ring_sum(): gathered[part].append(lax.ppermute(gathered[part][-1], 'row', moves[part]))  13.7 us
    ppermute x2, starting transfers between devices, extended(): before = lax.ppermute(last, axis, up)  10.1 us
    dot_general x18, matrix products, half_conv(): jnp.dot(rows[:, tap_index, :], windows[tap_index], preferred_element_type...  8.28 us
    dot_general x9, matrix products, per_device(): lax.dot_general(shard_piece[:, tap_index, :], window, (((0,), (0,)), ((),...  4.58 us
  transfers between devices with their start and end apart: 38, of which 14 were waited for; matrix products, arithmetic and copies ran while one was open for 19% of the time, Pallas kernels for 0%

profile of v14, /device:TPU:0, one launch (start us, length us, event | category | flops | bytes accessed | tf_op | source)
XLA Modules:
  0.0 198.9 jit_solution(7891969795449861967)
XLA Ops:
  10.5 5.5 %collective-permute-start = (bf16[212,1,128]{2,1,0:T(2,128)(2,1)S(1)}, bf16[212,1,128]{2,1,0:T(2,128)(2,1)S(1)}, u32[]{:S(2)}, u32[]{:S(2)}) collective-permute-start(bf16[212,1,128]{2,1,0:T(2,128)(2,1)S(1)} %get-tuple-element.54), channel_id=1, source_target_pairs={{0,2},{2,4},{4,6},{6,8},{8,10},{10,12},{12,14},{1,3},{3,5},{5,7},{... | collective-permute-start | bytes 162824 | tf_op jit(solution)/shard_map/ppermute | solution.py:19
  16.0 2.3 %constant_dynamic-slice_fusion = (bf16[512,512]{1,0:T(8,128)(2,1)}, bf16[512,512]{1,0:T(8,128)(2,1)}) fusion(bf16[512,1024]{1,0:T(8,128)(2,1)} %param.14, s32[]{:T(128)S(6)} %select_n.121, s32[]{:T(128)S(6)} %select_n.120), kind=kLoop, calls=%fused_computation.186 | loop fusion | bytes 2097160 | tf_op jit(solution)/shard_map/dynamic_slice | solution.py:141
  34.4 50.6 %all-gather.2.cloned.1.call-done = bf16[1024,9,212]{0,2,1:T(8,128)(2,1)} async-done(((bf16[128,9,212]{0,2,1:T(8,128)(2,1)}), bf16[1024,9,212]{0,2,1:T(8,128)(2,1)}) %all-gather.2.cloned.1.call-update) | async-done | bytes 3907600 | tf_op jit(solution)/shard_map/all_gather | solution.py:112
  97.1 2.5 %fusion.12 = (bf16[512,512]{0,1:T(8,128)(2,1)}, bf16[512,512]{0,1:T(8,128)(2,1)}, f32[512,512]{0,1:T(8,128)}) fusion(f32[512,512]{0,1:T(8,128)S(1)} %get-tuple-element.57, f32[512,4,128]{0,2,1:T(8,128)S(1)} %copy.30, bf16[1024,512]{0,1:T(8,128)(2,1)S(1)} %fusion.28, bf16[512,1024]{1,0:T(8,128)(2,1)S(1)} %copy-done.4, f32[512]{0:T(512)S(1)} %copy-done.11), kind=kOutput, calls=%fused_computation.54 | convolution fusion | flops 539230208 | bytes 6293504 | tf_op jit(solution)/shard_map/dot_general | solution.py:134
  99.6 1.9 fusion.10
  101.5 2.1 %copy.31 = bf16[512,4,128]{2,1,0:T(4,128)(2,1)} copy(bf16[512,4,128]{0,2,1:T(8,128)(2,1)} %bitcast.288) | data formatting | bytes 1048576
  103.9 2.1 %collective-permute-start.9 = (f32[32,1152]{1,0:T(8,128)S(1)}, f32[32,1152]{1,0:T(8,128)S(1)}, u32[]{:S(2)}, u32[]{:S(2)}) collective-permute-start(f32[32,1152]{1,0:T(8,128)S(1)} %select_bitcast_fusion.1), channel_id=1, source_target_pairs={{0,2},{2,6},{6,10},{10,14},{14,12},{12,8},{8,4},{4,0},{1,3},{3,7},... | collective-permute-start | bytes 442376 | tf_op jit(solution)/shard_map/ppermute | solution.py:85
  106.0 4.1 %collective-permute-done.23 = f32[32,1152]{1,0:T(8,128)S(1)} collective-permute-done((f32[32,1152]{1,0:T(8,128)S(1)}, f32[32,1152]{1,0:T(8,128)S(1)}, u32[]{:S(2)}, u32[]{:S(2)}) %collective-permute-start.23) | collective-permute-done | bytes 147488 | tf_op jit(solution)/shard_map/ppermute | solution.py:85
  110.5 1.8 collective-permute-start.10
  112.3 3.3 %collective-permute-done.24 = f32[32,1152]{1,0:T(8,128)S(1)} collective-permute-done((f32[32,1152]{1,0:T(8,128)S(1)}, f32[32,1152]{1,0:T(8,128)S(1)}, u32[]{:S(2)}, u32[]{:S(2)}) %collective-permute-start.24) | collective-permute-done | bytes 147488 | tf_op jit(solution)/shard_map/ppermute | solution.py:85
  116.2 1.5 collective-permute-start.11
  117.8 3.0 %collective-permute-done.25 = f32[32,1152]{1,0:T(8,128)S(1)} collective-permute-done((f32[32,1152]{1,0:T(8,128)S(1)}, f32[32,1152]{1,0:T(8,128)S(1)}, u32[]{:S(2)}, u32[]{:S(2)}) %collective-permute-start.25) | collective-permute-done | bytes 147488 | tf_op jit(solution)/shard_map/ppermute | solution.py:85
  121.5 1.5 collective-permute-start.12
  123.0 3.3 %fusion.31 = bf16[512,512]{0,1:T(8,128)(2,1)S(1)} fusion(f32[512,512]{0,1:T(8,128)S(1)} %copy-done.8, f32[512,4,128]{0,2,1:T(8,128)S(1)} %copy-done.3, f32[512,512]{0,1:T(8,128)S(1)} %get-tuple-element.57, s32[]{:T(128)S(6)} %select_n.196, bf16[512,512]{1,0:T(8,128)(2,1)S(1)} %copy-done.10, bf16[512,512]{1,0:T(8,128)(2,1)} %collective-permute-done.4, ...), kind=kOutput, calls=%fused_computation.73 | convolution fusion | flops 546570240 | bytes 5768192 | tf_op jit(solution)/shard_map/dot_general | solution.py:144
  127.1 1.5 collective-permute-start.13
  128.6 4.1 %collective-permute-done.27 = f32[32,1152]{1,0:T(8,128)S(1)} collective-permute-done((f32[32,1152]{1,0:T(8,128)S(1)}, f32[32,1152]{1,0:T(8,128)S(1)}, u32[]{:S(2)}, u32[]{:S(2)}) %collective-permute-start.27) | collective-permute-done | bytes 147488 | tf_op jit(solution)/shard_map/ppermute | solution.py:85
  134.9 3.3 %collective-permute-done.28 = f32[32,1152]{1,0:T(8,128)S(1)} collective-permute-done((f32[32,1152]{1,0:T(8,128)S(1)}, f32[32,1152]{1,0:T(8,128)S(1)}, u32[]{:S(2)}, u32[]{:S(2)}) %collective-permute-start.28) | collective-permute-done | bytes 147488 | tf_op jit(solution)/shard_map/ppermute | solution.py:85
  140.4 3.0 %collective-permute-done.29 = f32[32,1152]{1,0:T(8,128)S(1)} collective-permute-done((f32[32,1152]{1,0:T(8,128)S(1)}, f32[32,1152]{1,0:T(8,128)S(1)}, u32[]{:S(2)}, u32[]{:S(2)}) %collective-permute-start.29) | collective-permute-done | bytes 147488 | tf_op jit(solution)/shard_map/ppermute | solution.py:85
  147.6 4.6 %collective-permute-start.7 = (bf16[1024,1,128]{0,2,1:T(8,128)(2,1)S(1)}, bf16[1024,1,128]{0,2,1:T(8,128)(2,1)S(1)}, u32[]{:S(2)}, u32[]{:S(2)}) collective-permute-start(bf16[1024,1,128]{0,2,1:T(8,128)(2,1)S(1)} %get-tuple-element.42), channel_id=1, source_target_pairs={{0,2},{2,4},{4,6},{6,8},{8,10},{10,12},{12,14},{1,3},{3,5},{5,7},{... | collective-permute-start | bytes 786440 | tf_op jit(solution)/shard_map/ppermute | solution.py:19
  153.7 1.5 collective-permute-start.17
  155.2 2.6 %collective-permute-done.31 = bf16[32,1152]{1,0:T(8,128)(2,1)S(1)} collective-permute-done((bf16[32,1152]{1,0:T(8,128)(2,1)S(1)}, bf16[32,1152]{1,0:T(8,128)(2,1)S(1)}, u32[]{:S(2)}, u32[]{:S(2)}) %collective-permute-start.31) | collective-permute-done | bytes 73760 | tf_op jit(solution)/shard_map/ppermute | solution.py:91
  158.7 2.1 %collective-permute-done.17 = bf16[32,1152]{1,0:T(8,128)(2,1)S(1)} collective-permute-done((bf16[32,1152]{1,0:T(8,128)(2,1)S(1)}, bf16[32,1152]{1,0:T(8,128)(2,1)S(1)}, u32[]{:S(2)}, u32[]{:S(2)}) %collective-permute-start.17) | collective-permute-done | bytes 73760 | tf_op jit(solution)/shard_map/ppermute | solution.py:91
  160.9 2.5 %collective-permute-start.18 = (bf16[32,1152]{1,0:T(8,128)(2,1)S(1)}, bf16[32,1152]{1,0:T(8,128)(2,1)S(1)}, u32[]{:S(2)}, u32[]{:S(2)}) collective-permute-start(bf16[32,1152]{1,0:T(8,128)(2,1)S(1)} %collective-permute-done.17), channel_id=1, source_target_pairs={{0,2},{2,6},{6,10},{10,14},{14,12},{12,8},{8,4},{4,0},{1,3},{3,7},... | collective-permute-start | bytes 221192 | tf_op jit(solution)/shard_map/ppermute | solution.py:91
  163.4 1.9 collective-permute-done.18
  165.3 2.4 %collective-permute-start.19 = (bf16[32,1152]{1,0:T(8,128)(2,1)S(1)}, bf16[32,1152]{1,0:T(8,128)(2,1)S(1)}, u32[]{:S(2)}, u32[]{:S(2)}) collective-permute-start(bf16[32,1152]{1,0:T(8,128)(2,1)S(1)} %collective-permute-done.18), channel_id=1, source_target_pairs={{0,2},{2,6},{6,10},{10,14},{14,12},{12,8},{8,4},{4,0},{1,3},{3,7},... | collective-permute-start | bytes 221192 | tf_op jit(solution)/shard_map/ppermute | solution.py:91
  174.6 2.1 %collective-permute-start.20 = (bf16[32,1152]{1,0:T(8,128)(2,1)S(1)}, bf16[32,1152]{1,0:T(8,128)(2,1)S(1)}, u32[]{:S(2)}, u32[]{:S(2)}) collective-permute-start(bf16[32,1152]{1,0:T(8,128)(2,1)S(1)} %collective-permute-done.19), channel_id=1, source_target_pairs={{0,2},{2,6},{6,10},{10,14},{14,12},{12,8},{8,4},{4,0},{1,3},{3,7},... | collective-permute-start | bytes 221192 | tf_op jit(solution)/shard_map/ppermute | solution.py:91
  176.7 2.6 %collective-permute-done.34 = bf16[32,1152]{1,0:T(8,128)(2,1)S(1)} collective-permute-done((bf16[32,1152]{1,0:T(8,128)(2,1)S(1)}, bf16[32,1152]{1,0:T(8,128)(2,1)S(1)}, u32[]{:S(2)}, u32[]{:S(2)}) %collective-permute-start.34) | collective-permute-done | bytes 73760 | tf_op jit(solution)/shard_map/ppermute | solution.py:91
  179.6 1.8 collective-permute-start.21
  181.4 2.2 %collective-permute-done.35 = bf16[32,1152]{1,0:T(8,128)(2,1)S(1)} collective-permute-done((bf16[32,1152]{1,0:T(8,128)(2,1)S(1)}, bf16[32,1152]{1,0:T(8,128)(2,1)S(1)}, u32[]{:S(2)}, u32[]{:S(2)}) %collective-permute-start.35) | collective-permute-done | bytes 73760 | tf_op jit(solution)/shard_map/ppermute | solution.py:91
  184.0 1.7 collective-permute-start.22
  185.7 2.2 %collective-permute-done.36 = bf16[32,1152]{1,0:T(8,128)(2,1)S(1)} collective-permute-done((bf16[32,1152]{1,0:T(8,128)(2,1)S(1)}, bf16[32,1152]{1,0:T(8,128)(2,1)S(1)}, u32[]{:S(2)}, u32[]{:S(2)}) %collective-permute-start.36) | collective-permute-done | bytes 73760 | tf_op jit(solution)/shard_map/ppermute | solution.py:91
  190.5 1.6 slice_multiply_fusion
  (178 shorter events, 43.8 us)
Async XLA Ops:
  7.2 77.8 %all-gather.2.cloned.1.call-start = ((), (), s32[]{:S(2)}) async-start(), calls=%async_computation | async-start | bytes 4478976 | tf_op jit(solution)/shard_map/all_gather | solution.py:112
  9.2 21.7 %collective-permute-start.1 = (bf16[212,1,128]{2,1,0:T(2,128)(2,1)S(1)}, bf16[212,1,128]{2,1,0:T(2,128)(2,1)S(1)}, u32[]{:S(2)}, u32[]{:S(2)}) collective-permute-start(bf16[212,1,128]{2,1,0:T(2,128)(2,1)S(1)} %get-tuple-element.55), channel_id=1, source_target_pairs={{2,0},{4,2},{6,4},{8,6},{10,8},{12,10},{14,12},{3,1},{5,3},{7,5},{... | collective-permute-start | bytes 162824 | tf_op jit(solution)/shard_map/ppermute | solution.py:20
  10.5 20.4 %collective-permute-start = (bf16[212,1,128]{2,1,0:T(2,128)(2,1)S(1)}, bf16[212,1,128]{2,1,0:T(2,128)(2,1)S(1)}, u32[]{:S(2)}, u32[]{:S(2)}) collective-permute-start(bf16[212,1,128]{2,1,0:T(2,128)(2,1)S(1)} %get-tuple-element.54), channel_id=1, source_target_pairs={{0,2},{2,4},{4,6},{6,8},{8,10},{10,12},{12,14},{1,3},{3,5},{5,7},{... | collective-permute-start | bytes 162824 | tf_op jit(solution)/shard_map/ppermute | solution.py:19
  18.3 104.7 %collective-permute-start.4 = (bf16[512,512]{1,0:T(8,128)(2,1)}, bf16[512,512]{1,0:T(8,128)(2,1)}, u32[]{:S(2)}, u32[]{:S(2)}) collective-permute-start(bf16[512,512]{1,0:T(8,128)(2,1)} %get-tuple-element.44), channel_id=1, source_target_pairs={{0,1},{1,0},{2,3},{3,2},{4,5},{5,4},{6,7},{7,6},{8,9},{9,8},{10,11... | collective-permute-start | bytes 1572872 | tf_op jit(solution)/shard_map/ppermute | solution.py:142
  99.6 23.4 %collective-permute-start.5 = (bf16[512,512]{0,1:T(8,128)(2,1)}, bf16[512,512]{0,1:T(8,128)(2,1)}, u32[]{:S(2)}, u32[]{:S(2)}) collective-permute-start(bf16[512,512]{0,1:T(8,128)(2,1)} %get-tuple-element.32), channel_id=1, source_target_pairs={{0,1},{1,0},{2,3},{3,2},{4,5},{5,4},{6,7},{7,6},{8,9},{9,8},{10,11... | collective-permute-start | bytes 1572872 | tf_op jit(solution)/shard_map/ppermute | solution.py:26
  103.8 6.3 %collective-permute-start.23 = (f32[32,1152]{1,0:T(8,128)S(1)}, f32[32,1152]{1,0:T(8,128)S(1)}, u32[]{:S(2)}, u32[]{:S(2)}) collective-permute-start(f32[32,1152]{1,0:T(8,128)S(1)} %select_bitcast_fusion), channel_id=1, source_target_pairs={{2,0},{6,2},{10,6},{14,10},{12,14},{8,12},{4,8},{0,4},{3,1},{7,3},... | collective-permute-start | bytes 442376 | tf_op jit(solution)/shard_map/ppermute | solution.py:85
  103.9 6.6 %collective-permute-start.9 = (f32[32,1152]{1,0:T(8,128)S(1)}, f32[32,1152]{1,0:T(8,128)S(1)}, u32[]{:S(2)}, u32[]{:S(2)}) collective-permute-start(f32[32,1152]{1,0:T(8,128)S(1)} %select_bitcast_fusion.1), channel_id=1, source_target_pairs={{0,2},{2,6},{6,10},{10,14},{14,12},{12,8},{8,4},{4,0},{1,3},{3,7},... | collective-permute-start | bytes 442376 | tf_op jit(solution)/shard_map/ppermute | solution.py:85
  110.1 5.4 %collective-permute-start.24 = (f32[32,1152]{1,0:T(8,128)S(1)}, f32[32,1152]{1,0:T(8,128)S(1)}, u32[]{:S(2)}, u32[]{:S(2)}) collective-permute-start(f32[32,1152]{1,0:T(8,128)S(1)} %bitcast_add_fusion.6), channel_id=1, source_target_pairs={{2,0},{6,2},{10,6},{14,10},{12,14},{8,12},{4,8},{0,4},{3,1},{7,3},... | collective-permute-start | bytes 442376 | tf_op jit(solution)/shard_map/ppermute | solution.py:85
  110.5 5.7 %collective-permute-start.10 = (f32[32,1152]{1,0:T(8,128)S(1)}, f32[32,1152]{1,0:T(8,128)S(1)}, u32[]{:S(2)}, u32[]{:S(2)}) collective-permute-start(f32[32,1152]{1,0:T(8,128)S(1)} %bitcast_add_fusion.13), channel_id=1, source_target_pairs={{0,2},{2,6},{6,10},{10,14},{14,12},{12,8},{8,4},{4,0},{1,3},{3,7},... | collective-permute-start | bytes 442376 | tf_op jit(solution)/shard_map/ppermute | solution.py:85
  115.6 5.2 %collective-permute-start.25 = (f32[32,1152]{1,0:T(8,128)S(1)}, f32[32,1152]{1,0:T(8,128)S(1)}, u32[]{:S(2)}, u32[]{:S(2)}) collective-permute-start(f32[32,1152]{1,0:T(8,128)S(1)} %bitcast_add_fusion.5), channel_id=1, source_target_pairs={{2,0},{6,2},{10,6},{14,10},{12,14},{8,12},{4,8},{0,4},{3,1},{7,3},... | collective-permute-start | bytes 442376 | tf_op jit(solution)/shard_map/ppermute | solution.py:85
  116.2 5.2 %collective-permute-start.11 = (f32[32,1152]{1,0:T(8,128)S(1)}, f32[32,1152]{1,0:T(8,128)S(1)}, u32[]{:S(2)}, u32[]{:S(2)}) collective-permute-start(f32[32,1152]{1,0:T(8,128)S(1)} %bitcast_add_fusion.12), channel_id=1, source_target_pairs={{0,2},{2,6},{6,10},{10,14},{14,12},{12,8},{8,4},{4,0},{1,3},{3,7},... | collective-permute-start | bytes 442376 | tf_op jit(solution)/shard_map/ppermute | solution.py:85
  120.8 5.6 %collective-permute-start.26 = (f32[32,1152]{1,0:T(8,128)S(1)}, f32[32,1152]{1,0:T(8,128)S(1)}, u32[]{:S(2)}, u32[]{:S(2)}) collective-permute-start(f32[32,1152]{1,0:T(8,128)S(1)} %bitcast_add_fusion.4), channel_id=1, source_target_pairs={{2,0},{6,2},{10,6},{14,10},{12,14},{8,12},{4,8},{0,4},{3,1},{7,3},... | collective-permute-start | bytes 442376 | tf_op jit(solution)/shard_map/ppermute | solution.py:85
  121.5 5.6 %collective-permute-start.12 = (f32[32,1152]{1,0:T(8,128)S(1)}, f32[32,1152]{1,0:T(8,128)S(1)}, u32[]{:S(2)}, u32[]{:S(2)}) collective-permute-start(f32[32,1152]{1,0:T(8,128)S(1)} %bitcast_add_fusion.11), channel_id=1, source_target_pairs={{0,2},{2,6},{6,10},{10,14},{14,12},{12,8},{8,4},{4,0},{1,3},{3,7},... | collective-permute-start | bytes 442376 | tf_op jit(solution)/shard_map/ppermute | solution.py:85
  126.3 19.3 %collective-permute-start.6 = (bf16[512,4,128]{0,2,1:T(8,128)(2,1)S(1)}, bf16[512,4,128]{0,2,1:T(8,128)(2,1)S(1)}, u32[]{:S(2)}, u32[]{:S(2)}) collective-permute-start(bf16[512,4,128]{0,2,1:T(8,128)(2,1)S(1)} %bitcast.316), channel_id=1, source_target_pairs={{0,1},{1,0},{2,3},{3,2},{4,5},{5,4},{6,7},{7,6},{8,9},{9,8},{10,11... | collective-permute-start | bytes 1572872 | tf_op jit(solution)/shard_map/ppermute | solution.py:26
  126.4 6.3 %collective-permute-start.27 = (f32[32,1152]{1,0:T(8,128)S(1)}, f32[32,1152]{1,0:T(8,128)S(1)}, u32[]{:S(2)}, u32[]{:S(2)}) collective-permute-start(f32[32,1152]{1,0:T(8,128)S(1)} %bitcast_add_fusion.3), channel_id=1, source_target_pairs={{2,0},{6,2},{10,6},{14,10},{12,14},{8,12},{4,8},{0,4},{3,1},{7,3},... | collective-permute-start | bytes 442376 | tf_op jit(solution)/shard_map/ppermute | solution.py:85
  127.1 6.3 %collective-permute-start.13 = (f32[32,1152]{1,0:T(8,128)S(1)}, f32[32,1152]{1,0:T(8,128)S(1)}, u32[]{:S(2)}, u32[]{:S(2)}) collective-permute-start(f32[32,1152]{1,0:T(8,128)S(1)} %bitcast_add_fusion.10), channel_id=1, source_target_pairs={{0,2},{2,6},{6,10},{10,14},{14,12},{12,8},{8,4},{4,0},{1,3},{3,7},... | collective-permute-start | bytes 442376 | tf_op jit(solution)/shard_map/ppermute | solution.py:85
  132.7 5.4 %collective-permute-start.28 = (f32[32,1152]{1,0:T(8,128)S(1)}, f32[32,1152]{1,0:T(8,128)S(1)}, u32[]{:S(2)}, u32[]{:S(2)}) collective-permute-start(f32[32,1152]{1,0:T(8,128)S(1)} %bitcast_add_fusion.2), channel_id=1, source_target_pairs={{2,0},{6,2},{10,6},{14,10},{12,14},{8,12},{4,8},{0,4},{3,1},{7,3},... | collective-permute-start | bytes 442376 | tf_op jit(solution)/shard_map/ppermute | solution.py:85
  133.4 5.4 %collective-permute-start.14 = (f32[32,1152]{1,0:T(8,128)S(1)}, f32[32,1152]{1,0:T(8,128)S(1)}, u32[]{:S(2)}, u32[]{:S(2)}) collective-permute-start(f32[32,1152]{1,0:T(8,128)S(1)} %bitcast_add_fusion.9), channel_id=1, source_target_pairs={{0,2},{2,6},{6,10},{10,14},{14,12},{12,8},{8,4},{4,0},{1,3},{3,7},... | collective-permute-start | bytes 442376 | tf_op jit(solution)/shard_map/ppermute | solution.py:85
  138.2 5.2 %collective-permute-start.29 = (f32[32,1152]{1,0:T(8,128)S(1)}, f32[32,1152]{1,0:T(8,128)S(1)}, u32[]{:S(2)}, u32[]{:S(2)}) collective-permute-start(f32[32,1152]{1,0:T(8,128)S(1)} %bitcast_add_fusion.1), channel_id=1, source_target_pairs={{2,0},{6,2},{10,6},{14,10},{12,14},{8,12},{4,8},{0,4},{3,1},{7,3},... | collective-permute-start | bytes 442376 | tf_op jit(solution)/shard_map/ppermute | solution.py:85
  138.9 5.2 %collective-permute-start.15 = (f32[32,1152]{1,0:T(8,128)S(1)}, f32[32,1152]{1,0:T(8,128)S(1)}, u32[]{:S(2)}, u32[]{:S(2)}) collective-permute-start(f32[32,1152]{1,0:T(8,128)S(1)} %bitcast_add_fusion.8), channel_id=1, source_target_pairs={{0,2},{2,6},{6,10},{10,14},{14,12},{12,8},{8,4},{4,0},{1,3},{3,7},... | collective-permute-start | bytes 442376 | tf_op jit(solution)/shard_map/ppermute | solution.py:85
  143.4 9.3 %collective-permute-start.30 = (bf16[32,1152]{1,0:T(8,128)(2,1)S(1)}, bf16[32,1152]{1,0:T(8,128)(2,1)S(1)}, u32[]{:S(2)}, u32[]{:S(2)}) collective-permute-start(bf16[32,1152]{1,0:T(8,128)(2,1)S(1)} %get-tuple-element.29), channel_id=1, source_target_pairs={{2,0},{6,2},{10,6},{14,10},{12,14},{8,12},{4,8},{0,4},{3,1},{7,3},... | collective-permute-start | bytes 221192 | tf_op jit(solution)/shard_map/ppermute | solution.py:91
  144.1 9.6 %collective-permute-start.16 = (bf16[32,1152]{1,0:T(8,128)(2,1)S(1)}, bf16[32,1152]{1,0:T(8,128)(2,1)S(1)}, u32[]{:S(2)}, u32[]{:S(2)}) collective-permute-start(bf16[32,1152]{1,0:T(8,128)(2,1)S(1)} %get-tuple-element.27), channel_id=1, source_target_pairs={{0,2},{2,6},{6,10},{10,14},{14,12},{12,8},{8,4},{4,0},{1,3},{3,7},... | collective-permute-start | bytes 221192 | tf_op jit(solution)/shard_map/ppermute | solution.py:91
  146.3 21.4 %collective-permute-start.8 = (bf16[1024,1,128]{0,2,1:T(8,128)(2,1)S(1)}, bf16[1024,1,128]{0,2,1:T(8,128)(2,1)S(1)}, u32[]{:S(2)}, u32[]{:S(2)}) collective-permute-start(bf16[1024,1,128]{0,2,1:T(8,128)(2,1)S(1)} %get-tuple-element.43), channel_id=1, source_target_pairs={{2,0},{4,2},{6,4},{8,6},{10,8},{12,10},{14,12},{3,1},{5,3},{7,5},{... | collective-permute-start | bytes 786440 | tf_op jit(solution)/shard_map/ppermute | solution.py:20
  147.6 20.1 %collective-permute-start.7 = (bf16[1024,1,128]{0,2,1:T(8,128)(2,1)S(1)}, bf16[1024,1,128]{0,2,1:T(8,128)(2,1)S(1)}, u32[]{:S(2)}, u32[]{:S(2)}) collective-permute-start(bf16[1024,1,128]{0,2,1:T(8,128)(2,1)S(1)} %get-tuple-element.42), channel_id=1, source_target_pairs={{0,2},{2,4},{4,6},{6,8},{8,10},{10,12},{12,14},{1,3},{3,5},{5,7},{... | collective-permute-start | bytes 786440 | tf_op jit(solution)/shard_map/ppermute | solution.py:19
  152.7 5.1 %collective-permute-start.31 = (bf16[32,1152]{1,0:T(8,128)(2,1)S(1)}, bf16[32,1152]{1,0:T(8,128)(2,1)S(1)}, u32[]{:S(2)}, u32[]{:S(2)}) collective-permute-start(bf16[32,1152]{1,0:T(8,128)(2,1)S(1)} %collective-permute-done.30), channel_id=1, source_target_pairs={{2,0},{6,2},{10,6},{14,10},{12,14},{8,12},{4,8},{0,4},{3,1},{7,3},... | collective-permute-start | bytes 221192 | tf_op jit(solution)/shard_map/ppermute | solution.py:91
  153.7 7.2 %collective-permute-start.17 = (bf16[32,1152]{1,0:T(8,128)(2,1)S(1)}, bf16[32,1152]{1,0:T(8,128)(2,1)S(1)}, u32[]{:S(2)}, u32[]{:S(2)}) collective-permute-start(bf16[32,1152]{1,0:T(8,128)(2,1)S(1)} %collective-permute-done.16), channel_id=1, source_target_pairs={{0,2},{2,6},{6,10},{10,14},{14,12},{12,8},{8,4},{4,0},{1,3},{3,7},... | collective-permute-start | bytes 221192 | tf_op jit(solution)/shard_map/ppermute | solution.py:91
  157.9 5.5 %collective-permute-start.32 = (bf16[32,1152]{1,0:T(8,128)(2,1)S(1)}, bf16[32,1152]{1,0:T(8,128)(2,1)S(1)}, u32[]{:S(2)}, u32[]{:S(2)}) collective-permute-start(bf16[32,1152]{1,0:T(8,128)(2,1)S(1)} %collective-permute-done.31), channel_id=1, source_target_pairs={{2,0},{6,2},{10,6},{14,10},{12,14},{8,12},{4,8},{0,4},{3,1},{7,3},... | collective-permute-start | bytes 221192 | tf_op jit(solution)/shard_map/ppermute | solution.py:91
  163.4 11.2 %collective-permute-start.33 = (bf16[32,1152]{1,0:T(8,128)(2,1)S(1)}, bf16[32,1152]{1,0:T(8,128)(2,1)S(1)}, u32[]{:S(2)}, u32[]{:S(2)}) collective-permute-start(bf16[32,1152]{1,0:T(8,128)(2,1)S(1)} %collective-permute-done.32), channel_id=1, source_target_pairs={{2,0},{6,2},{10,6},{14,10},{12,14},{8,12},{4,8},{0,4},{3,1},{7,3},... | collective-permute-start | bytes 221192 | tf_op jit(solution)/shard_map/ppermute | solution.py:91
  165.3 9.3 %collective-permute-start.19 = (bf16[32,1152]{1,0:T(8,128)(2,1)S(1)}, bf16[32,1152]{1,0:T(8,128)(2,1)S(1)}, u32[]{:S(2)}, u32[]{:S(2)}) collective-permute-start(bf16[32,1152]{1,0:T(8,128)(2,1)S(1)} %collective-permute-done.18), channel_id=1, source_target_pairs={{0,2},{2,6},{6,10},{10,14},{14,12},{12,8},{8,4},{4,0},{1,3},{3,7},... | collective-permute-start | bytes 221192 | tf_op jit(solution)/shard_map/ppermute | solution.py:91
  174.6 4.7 %collective-permute-start.34 = (bf16[32,1152]{1,0:T(8,128)(2,1)S(1)}, bf16[32,1152]{1,0:T(8,128)(2,1)S(1)}, u32[]{:S(2)}, u32[]{:S(2)}) collective-permute-start(bf16[32,1152]{1,0:T(8,128)(2,1)S(1)} %collective-permute-done.33), channel_id=1, source_target_pairs={{2,0},{6,2},{10,6},{14,10},{12,14},{8,12},{4,8},{0,4},{3,1},{7,3},... | collective-permute-start | bytes 221192 | tf_op jit(solution)/shard_map/ppermute | solution.py:91
  174.6 5.0 %collective-permute-start.20 = (bf16[32,1152]{1,0:T(8,128)(2,1)S(1)}, bf16[32,1152]{1,0:T(8,128)(2,1)S(1)}, u32[]{:S(2)}, u32[]{:S(2)}) collective-permute-start(bf16[32,1152]{1,0:T(8,128)(2,1)S(1)} %collective-permute-done.19), channel_id=1, source_target_pairs={{0,2},{2,6},{6,10},{10,14},{14,12},{12,8},{8,4},{4,0},{1,3},{3,7},... | collective-permute-start | bytes 221192 | tf_op jit(solution)/shard_map/ppermute | solution.py:91
  184.0 4.8 %collective-permute-start.22 = (bf16[32,1152]{1,0:T(8,128)(2,1)S(1)}, bf16[32,1152]{1,0:T(8,128)(2,1)S(1)}, u32[]{:S(2)}, u32[]{:S(2)}) collective-permute-start(bf16[32,1152]{1,0:T(8,128)(2,1)S(1)} %collective-permute-done.21), channel_id=1, source_target_pairs={{0,2},{2,6},{6,10},{10,14},{14,12},{12,8},{8,4},{4,0},{1,3},{3,7},... | collective-permute-start | bytes 221192 | tf_op jit(solution)/shard_map/ppermute | solution.py:91
  (19 other events, 284.2 us)
Sparse Core Ops, SparseCore 0:
  10.0 74.9 all-gather.1

commit v15 on v14

--- a/solution.py
+++ b/solution.py
@@ -130,8 +130,19 @@
         sent = lax.ppermute(half_conv((1 - index) * lat_local), "chan", SWAP)
         pre = half_conv(index * lat_local) + sent
         squares_own = (pre * pre).astype(jnp.bfloat16)
-        squares = chan_gather(squares_own)
-        norm_value = gdn_beta[:, None] + jnp.dot(gdn_gamma, squares, preferred_element_type=jnp.float32)
+        squares_other = lax.ppermute(squares_own, "chan", SWAP)
+        squares = jnp.roll(jnp.concatenate([squares_own, squares_other], 0), index * lat_local, axis=0)
+        norm_own = jnp.dot(
+            lax.dynamic_slice_in_dim(gdn_gamma, index * lat_local, lat_local, 1),
+            squares_own,
+            preferred_element_type=jnp.float32,
+        )
+        norm_other = jnp.dot(
+            lax.dynamic_slice_in_dim(gdn_gamma, (1 - index) * lat_local, lat_local, 1),
+            squares_other,
+            preferred_element_type=jnp.float32,
+        )
+        norm_value = gdn_beta[:, None] + (norm_own + norm_other)
         inverse = lax.rsqrt(norm_value)
         latent = (pre * inverse).astype(jnp.bfloat16)
         upstream = cotangent.reshape(lat_local, pixels).astype(jnp.float32)

time: 199 us -> 201 us (1.010)
  transfers between devices with their start and end apart: 38 -> 38, of which waited for: 14 -> 14; matrix products, arithmetic and copies ran while one was open for 19% -> 20% of each run, Pallas kernels for 0% -> 0%
where the time goes in v15:
time: 201 us; the launch traced here: 200 us
  waiting for transfers between devices  86.1 us (43%)
  starting transfers between devices  44.8 us (22%)
  between operations  25.8 us (13%)
  matrix products  20.3 us (10%)
  local copies, waits for them, and re-layouts  12.3 us (6%)
  other arithmetic  10.7 us (5%)
    all_gather x1, waiting for transfers between devices, per_device(): shard_piece = lax.all_gather(conv_weight, 'row', axis=0, tiled=True)  50.6 us
    ppermute x14, waiting for transfers between devices, ring_sum(): got = lax.ppermute(carry[part], 'row', moves[part])  21 us
    ppermute x14, starting transfers between devices, ring_sum(): gathered[part].append(lax.ppermute(gathered[part][-1], 'row', moves[part]))  16.6 us
    ppermute x14, starting transfers between devices, ring_sum(): got = lax.ppermute(carry[part], 'row', moves[part])  14.9 us
    ppermute x14, waiting for transfers between devices, ring_sum(): gathered[part].append(lax.ppermute(gathered[part][-1], 'row', moves[part]))  13.8 us
    ppermute x2, starting transfers between devices, extended(): before = lax.ppermute(last, axis, up)  10.1 us
    dot_general x18, matrix products, half_conv(): jnp.dot(rows[:, tap_index, :], windows[tap_index], preferred_element_type...  8.27 us
    dot_general x9, matrix products, per_device(): lax.dot_general(shard_piece[:, tap_index, :], window, (((0,), (0,)), ((),...  4.6 us
  transfers between devices with their start and end apart: 38, of which 14 were waited for; matrix products, arithmetic and copies ran while one was open for 20% of the time, Pallas kernels for 0%

profile of v15, /device:TPU:0, one launch (start us, length us, event | category | flops | bytes accessed | tf_op | source)
XLA Modules:
  0.0 200.0 jit_solution(893821153963654699)
XLA Ops:
  10.5 5.5 %collective-permute-start = (bf16[212,1,128]{2,1,0:T(2,128)(2,1)S(1)}, bf16[212,1,128]{2,1,0:T(2,128)(2,1)S(1)}, u32[]{:S(2)}, u32[]{:S(2)}) collective-permute-start(bf16[212,1,128]{2,1,0:T(2,128)(2,1)S(1)} %get-tuple-element.54), channel_id=1, source_target_pairs={{0,2},{2,4},{4,6},{6,8},{8,10},{10,12},{12,14},{1,3},{3,5},{5,7},{... | collective-permute-start | bytes 162824 | tf_op jit(solution)/shard_map/ppermute | solution.py:19
  16.0 2.3 %constant_dynamic-slice_fusion.1 = (bf16[512,512]{1,0:T(8,128)(2,1)}, bf16[512,512]{1,0:T(8,128)(2,1)}) fusion(bf16[512,1024]{1,0:T(8,128)(2,1)} %param.14, s32[]{:T(128)S(6)} %select_n.122, s32[]{:T(128)S(6)} %select_n.123), kind=kLoop, calls=%fused_computation.187 | loop fusion | bytes 2097160 | tf_op jit(solution)/shard_map/dynamic_slice | solution.py:136
  34.4 50.6 %all-gather.2.cloned.1.call-done = bf16[1024,9,212]{0,2,1:T(8,128)(2,1)} async-done(((bf16[128,9,212]{0,2,1:T(8,128)(2,1)}), bf16[1024,9,212]{0,2,1:T(8,128)(2,1)}) %all-gather.2.cloned.1.call-update) | async-done | bytes 3907600 | tf_op jit(solution)/shard_map/all_gather | solution.py:112
  96.4 1.7 fusion.95
  98.1 1.8 fusion.12
  99.9 2.1 %copy.31 = bf16[512,4,128]{2,1,0:T(4,128)(2,1)} copy(bf16[512,4,128]{0,2,1:T(8,128)(2,1)} %bitcast.288) | data formatting | bytes 1048576
  102.1 1.9 fusion.14
  105.2 2.1 %collective-permute-start.9 = (f32[32,1152]{1,0:T(8,128)S(1)}, f32[32,1152]{1,0:T(8,128)S(1)}, u32[]{:S(2)}, u32[]{:S(2)}) collective-permute-start(f32[32,1152]{1,0:T(8,128)S(1)} %select_bitcast_fusion.1), channel_id=1, source_target_pairs={{0,2},{2,6},{6,10},{10,14},{14,12},{12,8},{8,4},{4,0},{1,3},{3,7},... | collective-permute-start | bytes 442376 | tf_op jit(solution)/shard_map/ppermute | solution.py:85
  107.2 4.2 %collective-permute-done.23 = f32[32,1152]{1,0:T(8,128)S(1)} collective-permute-done((f32[32,1152]{1,0:T(8,128)S(1)}, f32[32,1152]{1,0:T(8,128)S(1)}, u32[]{:S(2)}, u32[]{:S(2)}) %collective-permute-start.23) | collective-permute-done | bytes 147488 | tf_op jit(solution)/shard_map/ppermute | solution.py:85
  111.8 1.8 collective-permute-start.10
  113.6 3.3 %collective-permute-done.24 = f32[32,1152]{1,0:T(8,128)S(1)} collective-permute-done((f32[32,1152]{1,0:T(8,128)S(1)}, f32[32,1152]{1,0:T(8,128)S(1)}, u32[]{:S(2)}, u32[]{:S(2)}) %collective-permute-start.24) | collective-permute-done | bytes 147488 | tf_op jit(solution)/shard_map/ppermute | solution.py:85
  117.6 1.5 collective-permute-start.11
  119.1 3.0 %collective-permute-done.25 = f32[32,1152]{1,0:T(8,128)S(1)} collective-permute-done((f32[32,1152]{1,0:T(8,128)S(1)}, f32[32,1152]{1,0:T(8,128)S(1)}, u32[]{:S(2)}, u32[]{:S(2)}) %collective-permute-start.25) | collective-permute-done | bytes 147488 | tf_op jit(solution)/shard_map/ppermute | solution.py:85
  122.8 1.5 collective-permute-start.12
  124.3 3.0 %fusion.31 = bf16[512,512]{0,1:T(8,128)(2,1)S(1)} fusion(f32[512,512]{0,1:T(8,128)S(1)} %copy-done.8, f32[512,4,128]{0,2,1:T(8,128)S(1)} %copy.30, f32[512,512]{0,1:T(8,128)S(1)} %get-tuple-element.57, s32[]{:T(128)S(6)} %select_n.198, bf16[512,512]{1,0:T(8,128)(2,1)S(1)} %copy-done.4, bf16[512,512]{1,0:T(8,128)(2,1)} %collective-permute-done.4, ...), kind=kOutput, calls=%fused_computation.73 | convolution fusion | flops 546570240 | bytes 5768192 | tf_op jit(solution)/shard_map/dot_general | solution.py:155
  129.6 4.1 %collective-permute-done.27 = f32[32,1152]{1,0:T(8,128)S(1)} collective-permute-done((f32[32,1152]{1,0:T(8,128)S(1)}, f32[32,1152]{1,0:T(8,128)S(1)}, u32[]{:S(2)}, u32[]{:S(2)}) %collective-permute-start.27) | collective-permute-done | bytes 147488 | tf_op jit(solution)/shard_map/ppermute | solution.py:85
  135.9 3.3 %collective-permute-done.28 = f32[32,1152]{1,0:T(8,128)S(1)} collective-permute-done((f32[32,1152]{1,0:T(8,128)S(1)}, f32[32,1152]{1,0:T(8,128)S(1)}, u32[]{:S(2)}, u32[]{:S(2)}) %collective-permute-start.28) | collective-permute-done | bytes 147488 | tf_op jit(solution)/shard_map/ppermute | solution.py:85
  141.4 3.0 %collective-permute-done.29 = f32[32,1152]{1,0:T(8,128)S(1)} collective-permute-done((f32[32,1152]{1,0:T(8,128)S(1)}, f32[32,1152]{1,0:T(8,128)S(1)}, u32[]{:S(2)}, u32[]{:S(2)}) %collective-permute-start.29) | collective-permute-done | bytes 147488 | tf_op jit(solution)/shard_map/ppermute | solution.py:85
  148.7 4.6 %collective-permute-start.7 = (bf16[1024,1,128]{0,2,1:T(8,128)(2,1)S(1)}, bf16[1024,1,128]{0,2,1:T(8,128)(2,1)S(1)}, u32[]{:S(2)}, u32[]{:S(2)}) collective-permute-start(bf16[1024,1,128]{0,2,1:T(8,128)(2,1)S(1)} %get-tuple-element.42), channel_id=1, source_target_pairs={{0,2},{2,4},{4,6},{6,8},{8,10},{10,12},{12,14},{1,3},{3,5},{5,7},{... | collective-permute-start | bytes 786440 | tf_op jit(solution)/shard_map/ppermute | solution.py:19
  154.7 1.5 collective-permute-start.17
  156.3 2.6 %collective-permute-done.31 = bf16[32,1152]{1,0:T(8,128)(2,1)S(1)} collective-permute-done((bf16[32,1152]{1,0:T(8,128)(2,1)S(1)}, bf16[32,1152]{1,0:T(8,128)(2,1)S(1)}, u32[]{:S(2)}, u32[]{:S(2)}) %collective-permute-start.31) | collective-permute-done | bytes 73760 | tf_op jit(solution)/shard_map/ppermute | solution.py:91
  159.8 2.1 %collective-permute-done.17 = bf16[32,1152]{1,0:T(8,128)(2,1)S(1)} collective-permute-done((bf16[32,1152]{1,0:T(8,128)(2,1)S(1)}, bf16[32,1152]{1,0:T(8,128)(2,1)S(1)}, u32[]{:S(2)}, u32[]{:S(2)}) %collective-permute-start.17) | collective-permute-done | bytes 73760 | tf_op jit(solution)/shard_map/ppermute | solution.py:91
  161.9 2.5 %collective-permute-start.18 = (bf16[32,1152]{1,0:T(8,128)(2,1)S(1)}, bf16[32,1152]{1,0:T(8,128)(2,1)S(1)}, u32[]{:S(2)}, u32[]{:S(2)}) collective-permute-start(bf16[32,1152]{1,0:T(8,128)(2,1)S(1)} %collective-permute-done.17), channel_id=1, source_target_pairs={{0,2},{2,6},{6,10},{10,14},{14,12},{12,8},{8,4},{4,0},{1,3},{3,7},... | collective-permute-start | bytes 221192 | tf_op jit(solution)/shard_map/ppermute | solution.py:91
  164.5 1.9 collective-permute-done.18
  166.4 2.4 %collective-permute-start.19 = (bf16[32,1152]{1,0:T(8,128)(2,1)S(1)}, bf16[32,1152]{1,0:T(8,128)(2,1)S(1)}, u32[]{:S(2)}, u32[]{:S(2)}) collective-permute-start(bf16[32,1152]{1,0:T(8,128)(2,1)S(1)} %collective-permute-done.18), channel_id=1, source_target_pairs={{0,2},{2,6},{6,10},{10,14},{14,12},{12,8},{8,4},{4,0},{1,3},{3,7},... | collective-permute-start | bytes 221192 | tf_op jit(solution)/shard_map/ppermute | solution.py:91
  175.7 2.1 %collective-permute-start.20 = (bf16[32,1152]{1,0:T(8,128)(2,1)S(1)}, bf16[32,1152]{1,0:T(8,128)(2,1)S(1)}, u32[]{:S(2)}, u32[]{:S(2)}) collective-permute-start(bf16[32,1152]{1,0:T(8,128)(2,1)S(1)} %collective-permute-done.19), channel_id=1, source_target_pairs={{0,2},{2,6},{6,10},{10,14},{14,12},{12,8},{8,4},{4,0},{1,3},{3,7},... | collective-permute-start | bytes 221192 | tf_op jit(solution)/shard_map/ppermute | solution.py:91
  177.8 2.6 %collective-permute-done.34 = bf16[32,1152]{1,0:T(8,128)(2,1)S(1)} collective-permute-done((bf16[32,1152]{1,0:T(8,128)(2,1)S(1)}, bf16[32,1152]{1,0:T(8,128)(2,1)S(1)}, u32[]{:S(2)}, u32[]{:S(2)}) %collective-permute-start.34) | collective-permute-done | bytes 73760 | tf_op jit(solution)/shard_map/ppermute | solution.py:91
  180.7 1.8 collective-permute-start.21
  182.5 2.2 %collective-permute-done.35 = bf16[32,1152]{1,0:T(8,128)(2,1)S(1)} collective-permute-done((bf16[32,1152]{1,0:T(8,128)(2,1)S(1)}, bf16[32,1152]{1,0:T(8,128)(2,1)S(1)}, u32[]{:S(2)}, u32[]{:S(2)}) %collective-permute-start.35) | collective-permute-done | bytes 73760 | tf_op jit(solution)/shard_map/ppermute | solution.py:91
  185.1 1.7 collective-permute-start.22
  186.8 2.2 %collective-permute-done.36 = bf16[32,1152]{1,0:T(8,128)(2,1)S(1)} collective-permute-done((bf16[32,1152]{1,0:T(8,128)(2,1)S(1)}, bf16[32,1152]{1,0:T(8,128)(2,1)S(1)}, u32[]{:S(2)}, u32[]{:S(2)}) %collective-permute-start.36) | collective-permute-done | bytes 73760 | tf_op jit(solution)/shard_map/ppermute | solution.py:91
  191.6 1.6 slice_multiply_fusion
  (177 shorter events, 45.6 us)
Async XLA Ops:
  7.2 77.8 %all-gather.2.cloned.1.call-start = ((), (), s32[]{:S(2)}) async-start(), calls=%async_computation | async-start | bytes 4478976 | tf_op jit(solution)/shard_map/all_gather | solution.py:112
  9.2 21.6 %collective-permute-start.1 = (bf16[212,1,128]{2,1,0:T(2,128)(2,1)S(1)}, bf16[212,1,128]{2,1,0:T(2,128)(2,1)S(1)}, u32[]{:S(2)}, u32[]{:S(2)}) collective-permute-start(bf16[212,1,128]{2,1,0:T(2,128)(2,1)S(1)} %get-tuple-element.55), channel_id=1, source_target_pairs={{2,0},{4,2},{6,4},{8,6},{10,8},{12,10},{14,12},{3,1},{5,3},{7,5},{... | collective-permute-start | bytes 162824 | tf_op jit(solution)/shard_map/ppermute | solution.py:20
  10.5 20.4 %collective-permute-start = (bf16[212,1,128]{2,1,0:T(2,128)(2,1)S(1)}, bf16[212,1,128]{2,1,0:T(2,128)(2,1)S(1)}, u32[]{:S(2)}, u32[]{:S(2)}) collective-permute-start(bf16[212,1,128]{2,1,0:T(2,128)(2,1)S(1)} %get-tuple-element.54), channel_id=1, source_target_pairs={{0,2},{2,4},{4,6},{6,8},{8,10},{10,12},{12,14},{1,3},{3,5},{5,7},{... | collective-permute-start | bytes 162824 | tf_op jit(solution)/shard_map/ppermute | solution.py:19
  18.3 106.0 %collective-permute-start.4 = (bf16[512,512]{1,0:T(8,128)(2,1)}, bf16[512,512]{1,0:T(8,128)(2,1)}, u32[]{:S(2)}, u32[]{:S(2)}) collective-permute-start(bf16[512,512]{1,0:T(8,128)(2,1)} %get-tuple-element.45), channel_id=1, source_target_pairs={{0,1},{1,0},{2,3},{3,2},{4,5},{5,4},{6,7},{7,6},{8,9},{9,8},{10,11... | collective-permute-start | bytes 1572872 | tf_op jit(solution)/shard_map/ppermute | solution.py:153
  102.0 22.3 %collective-permute-start.5 = (bf16[512,512]{0,1:T(8,128)(2,1)S(1)}, bf16[512,512]{0,1:T(8,128)(2,1)S(1)}, u32[]{:S(2)}, u32[]{:S(2)}) collective-permute-start(bf16[512,512]{0,1:T(8,128)(2,1)S(1)} %get-tuple-element.32), channel_id=1, source_target_pairs={{0,1},{1,0},{2,3},{3,2},{4,5},{5,4},{6,7},{7,6},{8,9},{9,8},{10,11... | collective-permute-start | bytes 1572872 | tf_op jit(solution)/shard_map/ppermute | solution.py:26
  105.1 6.3 %collective-permute-start.23 = (f32[32,1152]{1,0:T(8,128)S(1)}, f32[32,1152]{1,0:T(8,128)S(1)}, u32[]{:S(2)}, u32[]{:S(2)}) collective-permute-start(f32[32,1152]{1,0:T(8,128)S(1)} %select_bitcast_fusion), channel_id=1, source_target_pairs={{2,0},{6,2},{10,6},{14,10},{12,14},{8,12},{4,8},{0,4},{3,1},{7,3},... | collective-permute-start | bytes 442376 | tf_op jit(solution)/shard_map/ppermute | solution.py:85
  105.2 6.6 %collective-permute-start.9 = (f32[32,1152]{1,0:T(8,128)S(1)}, f32[32,1152]{1,0:T(8,128)S(1)}, u32[]{:S(2)}, u32[]{:S(2)}) collective-permute-start(f32[32,1152]{1,0:T(8,128)S(1)} %select_bitcast_fusion.1), channel_id=1, source_target_pairs={{0,2},{2,6},{6,10},{10,14},{14,12},{12,8},{8,4},{4,0},{1,3},{3,7},... | collective-permute-start | bytes 442376 | tf_op jit(solution)/shard_map/ppermute | solution.py:85
  111.4 5.5 %collective-permute-start.24 = (f32[32,1152]{1,0:T(8,128)S(1)}, f32[32,1152]{1,0:T(8,128)S(1)}, u32[]{:S(2)}, u32[]{:S(2)}) collective-permute-start(f32[32,1152]{1,0:T(8,128)S(1)} %bitcast_add_fusion.6), channel_id=1, source_target_pairs={{2,0},{6,2},{10,6},{14,10},{12,14},{8,12},{4,8},{0,4},{3,1},{7,3},... | collective-permute-start | bytes 442376 | tf_op jit(solution)/shard_map/ppermute | solution.py:85
  111.8 5.7 %collective-permute-start.10 = (f32[32,1152]{1,0:T(8,128)S(1)}, f32[32,1152]{1,0:T(8,128)S(1)}, u32[]{:S(2)}, u32[]{:S(2)}) collective-permute-start(f32[32,1152]{1,0:T(8,128)S(1)} %bitcast_add_fusion.13), channel_id=1, source_target_pairs={{0,2},{2,6},{6,10},{10,14},{14,12},{12,8},{8,4},{4,0},{1,3},{3,7},... | collective-permute-start | bytes 442376 | tf_op jit(solution)/shard_map/ppermute | solution.py:85
  116.9 5.2 %collective-permute-start.25 = (f32[32,1152]{1,0:T(8,128)S(1)}, f32[32,1152]{1,0:T(8,128)S(1)}, u32[]{:S(2)}, u32[]{:S(2)}) collective-permute-start(f32[32,1152]{1,0:T(8,128)S(1)} %bitcast_add_fusion.5), channel_id=1, source_target_pairs={{2,0},{6,2},{10,6},{14,10},{12,14},{8,12},{4,8},{0,4},{3,1},{7,3},... | collective-permute-start | bytes 442376 | tf_op jit(solution)/shard_map/ppermute | solution.py:85
  117.6 5.2 %collective-permute-start.11 = (f32[32,1152]{1,0:T(8,128)S(1)}, f32[32,1152]{1,0:T(8,128)S(1)}, u32[]{:S(2)}, u32[]{:S(2)}) collective-permute-start(f32[32,1152]{1,0:T(8,128)S(1)} %bitcast_add_fusion.12), channel_id=1, source_target_pairs={{0,2},{2,6},{6,10},{10,14},{14,12},{12,8},{8,4},{4,0},{1,3},{3,7},... | collective-permute-start | bytes 442376 | tf_op jit(solution)/shard_map/ppermute | solution.py:85
  122.1 5.3 %collective-permute-start.26 = (f32[32,1152]{1,0:T(8,128)S(1)}, f32[32,1152]{1,0:T(8,128)S(1)}, u32[]{:S(2)}, u32[]{:S(2)}) collective-permute-start(f32[32,1152]{1,0:T(8,128)S(1)} %bitcast_add_fusion.4), channel_id=1, source_target_pairs={{2,0},{6,2},{10,6},{14,10},{12,14},{8,12},{4,8},{0,4},{3,1},{7,3},... | collective-permute-start | bytes 442376 | tf_op jit(solution)/shard_map/ppermute | solution.py:85
  122.8 5.3 %collective-permute-start.12 = (f32[32,1152]{1,0:T(8,128)S(1)}, f32[32,1152]{1,0:T(8,128)S(1)}, u32[]{:S(2)}, u32[]{:S(2)}) collective-permute-start(f32[32,1152]{1,0:T(8,128)S(1)} %bitcast_add_fusion.11), channel_id=1, source_target_pairs={{0,2},{2,6},{6,10},{10,14},{14,12},{12,8},{8,4},{4,0},{1,3},{3,7},... | collective-permute-start | bytes 442376 | tf_op jit(solution)/shard_map/ppermute | solution.py:85
  127.4 19.3 %collective-permute-start.6 = (bf16[512,4,128]{0,2,1:T(8,128)(2,1)S(1)}, bf16[512,4,128]{0,2,1:T(8,128)(2,1)S(1)}, u32[]{:S(2)}, u32[]{:S(2)}) collective-permute-start(bf16[512,4,128]{0,2,1:T(8,128)(2,1)S(1)} %bitcast.316), channel_id=1, source_target_pairs={{0,1},{1,0},{2,3},{3,2},{4,5},{5,4},{6,7},{7,6},{8,9},{9,8},{10,11... | collective-permute-start | bytes 1572872 | tf_op jit(solution)/shard_map/ppermute | solution.py:26
  127.5 6.3 %collective-permute-start.27 = (f32[32,1152]{1,0:T(8,128)S(1)}, f32[32,1152]{1,0:T(8,128)S(1)}, u32[]{:S(2)}, u32[]{:S(2)}) collective-permute-start(f32[32,1152]{1,0:T(8,128)S(1)} %bitcast_add_fusion.3), channel_id=1, source_target_pairs={{2,0},{6,2},{10,6},{14,10},{12,14},{8,12},{4,8},{0,4},{3,1},{7,3},... | collective-permute-start | bytes 442376 | tf_op jit(solution)/shard_map/ppermute | solution.py:85
  128.1 6.3 %collective-permute-start.13 = (f32[32,1152]{1,0:T(8,128)S(1)}, f32[32,1152]{1,0:T(8,128)S(1)}, u32[]{:S(2)}, u32[]{:S(2)}) collective-permute-start(f32[32,1152]{1,0:T(8,128)S(1)} %bitcast_add_fusion.10), channel_id=1, source_target_pairs={{0,2},{2,6},{6,10},{10,14},{14,12},{12,8},{8,4},{4,0},{1,3},{3,7},... | collective-permute-start | bytes 442376 | tf_op jit(solution)/shard_map/ppermute | solution.py:85
  133.8 5.4 %collective-permute-start.28 = (f32[32,1152]{1,0:T(8,128)S(1)}, f32[32,1152]{1,0:T(8,128)S(1)}, u32[]{:S(2)}, u32[]{:S(2)}) collective-permute-start(f32[32,1152]{1,0:T(8,128)S(1)} %bitcast_add_fusion.2), channel_id=1, source_target_pairs={{2,0},{6,2},{10,6},{14,10},{12,14},{8,12},{4,8},{0,4},{3,1},{7,3},... | collective-permute-start | bytes 442376 | tf_op jit(solution)/shard_map/ppermute | solution.py:85
  134.4 5.4 %collective-permute-start.14 = (f32[32,1152]{1,0:T(8,128)S(1)}, f32[32,1152]{1,0:T(8,128)S(1)}, u32[]{:S(2)}, u32[]{:S(2)}) collective-permute-start(f32[32,1152]{1,0:T(8,128)S(1)} %bitcast_add_fusion.9), channel_id=1, source_target_pairs={{0,2},{2,6},{6,10},{10,14},{14,12},{12,8},{8,4},{4,0},{1,3},{3,7},... | collective-permute-start | bytes 442376 | tf_op jit(solution)/shard_map/ppermute | solution.py:85
  139.2 5.2 %collective-permute-start.29 = (f32[32,1152]{1,0:T(8,128)S(1)}, f32[32,1152]{1,0:T(8,128)S(1)}, u32[]{:S(2)}, u32[]{:S(2)}) collective-permute-start(f32[32,1152]{1,0:T(8,128)S(1)} %bitcast_add_fusion.1), channel_id=1, source_target_pairs={{2,0},{6,2},{10,6},{14,10},{12,14},{8,12},{4,8},{0,4},{3,1},{7,3},... | collective-permute-start | bytes 442376 | tf_op jit(solution)/shard_map/ppermute | solution.py:85
  139.9 5.2 %collective-permute-start.15 = (f32[32,1152]{1,0:T(8,128)S(1)}, f32[32,1152]{1,0:T(8,128)S(1)}, u32[]{:S(2)}, u32[]{:S(2)}) collective-permute-start(f32[32,1152]{1,0:T(8,128)S(1)} %bitcast_add_fusion.8), channel_id=1, source_target_pairs={{0,2},{2,6},{6,10},{10,14},{14,12},{12,8},{8,4},{4,0},{1,3},{3,7},... | collective-permute-start | bytes 442376 | tf_op jit(solution)/shard_map/ppermute | solution.py:85
  144.5 9.3 %collective-permute-start.30 = (bf16[32,1152]{1,0:T(8,128)(2,1)S(1)}, bf16[32,1152]{1,0:T(8,128)(2,1)S(1)}, u32[]{:S(2)}, u32[]{:S(2)}) collective-permute-start(bf16[32,1152]{1,0:T(8,128)(2,1)S(1)} %get-tuple-element.29), channel_id=1, source_target_pairs={{2,0},{6,2},{10,6},{14,10},{12,14},{8,12},{4,8},{0,4},{3,1},{7,3},... | collective-permute-start | bytes 221192 | tf_op jit(solution)/shard_map/ppermute | solution.py:91
  145.1 9.6 %collective-permute-start.16 = (bf16[32,1152]{1,0:T(8,128)(2,1)S(1)}, bf16[32,1152]{1,0:T(8,128)(2,1)S(1)}, u32[]{:S(2)}, u32[]{:S(2)}) collective-permute-start(bf16[32,1152]{1,0:T(8,128)(2,1)S(1)} %get-tuple-element.27), channel_id=1, source_target_pairs={{0,2},{2,6},{6,10},{10,14},{14,12},{12,8},{8,4},{4,0},{1,3},{3,7},... | collective-permute-start | bytes 221192 | tf_op jit(solution)/shard_map/ppermute | solution.py:91
  147.4 21.4 %collective-permute-start.8 = (bf16[1024,1,128]{0,2,1:T(8,128)(2,1)S(1)}, bf16[1024,1,128]{0,2,1:T(8,128)(2,1)S(1)}, u32[]{:S(2)}, u32[]{:S(2)}) collective-permute-start(bf16[1024,1,128]{0,2,1:T(8,128)(2,1)S(1)} %get-tuple-element.43), channel_id=1, source_target_pairs={{2,0},{4,2},{6,4},{8,6},{10,8},{12,10},{14,12},{3,1},{5,3},{7,5},{... | collective-permute-start | bytes 786440 | tf_op jit(solution)/shard_map/ppermute | solution.py:20
  148.7 20.1 %collective-permute-start.7 = (bf16[1024,1,128]{0,2,1:T(8,128)(2,1)S(1)}, bf16[1024,1,128]{0,2,1:T(8,128)(2,1)S(1)}, u32[]{:S(2)}, u32[]{:S(2)}) collective-permute-start(bf16[1024,1,128]{0,2,1:T(8,128)(2,1)S(1)} %get-tuple-element.42), channel_id=1, source_target_pairs={{0,2},{2,4},{4,6},{6,8},{8,10},{10,12},{12,14},{1,3},{3,5},{5,7},{... | collective-permute-start | bytes 786440 | tf_op jit(solution)/shard_map/ppermute | solution.py:19
  153.8 5.1 %collective-permute-start.31 = (bf16[32,1152]{1,0:T(8,128)(2,1)S(1)}, bf16[32,1152]{1,0:T(8,128)(2,1)S(1)}, u32[]{:S(2)}, u32[]{:S(2)}) collective-permute-start(bf16[32,1152]{1,0:T(8,128)(2,1)S(1)} %collective-permute-done.30), channel_id=1, source_target_pairs={{2,0},{6,2},{10,6},{14,10},{12,14},{8,12},{4,8},{0,4},{3,1},{7,3},... | collective-permute-start | bytes 221192 | tf_op jit(solution)/shard_map/ppermute | solution.py:91
  154.7 7.2 %collective-permute-start.17 = (bf16[32,1152]{1,0:T(8,128)(2,1)S(1)}, bf16[32,1152]{1,0:T(8,128)(2,1)S(1)}, u32[]{:S(2)}, u32[]{:S(2)}) collective-permute-start(bf16[32,1152]{1,0:T(8,128)(2,1)S(1)} %collective-permute-done.16), channel_id=1, source_target_pairs={{0,2},{2,6},{6,10},{10,14},{14,12},{12,8},{8,4},{4,0},{1,3},{3,7},... | collective-permute-start | bytes 221192 | tf_op jit(solution)/shard_map/ppermute | solution.py:91
  158.9 5.5 %collective-permute-start.32 = (bf16[32,1152]{1,0:T(8,128)(2,1)S(1)}, bf16[32,1152]{1,0:T(8,128)(2,1)S(1)}, u32[]{:S(2)}, u32[]{:S(2)}) collective-permute-start(bf16[32,1152]{1,0:T(8,128)(2,1)S(1)} %collective-permute-done.31), channel_id=1, source_target_pairs={{2,0},{6,2},{10,6},{14,10},{12,14},{8,12},{4,8},{0,4},{3,1},{7,3},... | collective-permute-start | bytes 221192 | tf_op jit(solution)/shard_map/ppermute | solution.py:91
  164.4 11.2 %collective-permute-start.33 = (bf16[32,1152]{1,0:T(8,128)(2,1)S(1)}, bf16[32,1152]{1,0:T(8,128)(2,1)S(1)}, u32[]{:S(2)}, u32[]{:S(2)}) collective-permute-start(bf16[32,1152]{1,0:T(8,128)(2,1)S(1)} %collective-permute-done.32), channel_id=1, source_target_pairs={{2,0},{6,2},{10,6},{14,10},{12,14},{8,12},{4,8},{0,4},{3,1},{7,3},... | collective-permute-start | bytes 221192 | tf_op jit(solution)/shard_map/ppermute | solution.py:91
  166.4 9.3 %collective-permute-start.19 = (bf16[32,1152]{1,0:T(8,128)(2,1)S(1)}, bf16[32,1152]{1,0:T(8,128)(2,1)S(1)}, u32[]{:S(2)}, u32[]{:S(2)}) collective-permute-start(bf16[32,1152]{1,0:T(8,128)(2,1)S(1)} %collective-permute-done.18), channel_id=1, source_target_pairs={{0,2},{2,6},{6,10},{10,14},{14,12},{12,8},{8,4},{4,0},{1,3},{3,7},... | collective-permute-start | bytes 221192 | tf_op jit(solution)/shard_map/ppermute | solution.py:91
  175.7 4.7 %collective-permute-start.34 = (bf16[32,1152]{1,0:T(8,128)(2,1)S(1)}, bf16[32,1152]{1,0:T(8,128)(2,1)S(1)}, u32[]{:S(2)}, u32[]{:S(2)}) collective-permute-start(bf16[32,1152]{1,0:T(8,128)(2,1)S(1)} %collective-permute-done.33), channel_id=1, source_target_pairs={{2,0},{6,2},{10,6},{14,10},{12,14},{8,12},{4,8},{0,4},{3,1},{7,3},... | collective-permute-start | bytes 221192 | tf_op jit(solution)/shard_map/ppermute | solution.py:91
  175.7 5.0 %collective-permute-start.20 = (bf16[32,1152]{1,0:T(8,128)(2,1)S(1)}, bf16[32,1152]{1,0:T(8,128)(2,1)S(1)}, u32[]{:S(2)}, u32[]{:S(2)}) collective-permute-start(bf16[32,1152]{1,0:T(8,128)(2,1)S(1)} %collective-permute-done.19), channel_id=1, source_target_pairs={{0,2},{2,6},{6,10},{10,14},{14,12},{12,8},{8,4},{4,0},{1,3},{3,7},... | collective-permute-start | bytes 221192 | tf_op jit(solution)/shard_map/ppermute | solution.py:91
  185.1 4.8 %collective-permute-start.22 = (bf16[32,1152]{1,0:T(8,128)(2,1)S(1)}, bf16[32,1152]{1,0:T(8,128)(2,1)S(1)}, u32[]{:S(2)}, u32[]{:S(2)}) collective-permute-start(bf16[32,1152]{1,0:T(8,128)(2,1)S(1)} %collective-permute-done.21), channel_id=1, source_target_pairs={{0,2},{2,6},{6,10},{10,14},{14,12},{12,8},{8,4},{4,0},{1,3},{3,7},... | collective-permute-start | bytes 221192 | tf_op jit(solution)/shard_map/ppermute | solution.py:91
  (18 other events, 202.5 us)
Sparse Core Ops, SparseCore 0:
  10.0 74.9 all-gather.1

commit v16 on v14

--- a/solution.py
+++ b/solution.py
@@ -118,16 +118,23 @@
             for row_shift, col_shift in TAPS
         ]
 
-        def half_conv(start):
-            rows = lax.dynamic_slice_in_dim(shard_piece, start, lat_local, 0)
-            total = jnp.zeros((lat_local, pixels), jnp.float32)
+        def half_conv(start, size=lat_local):
+            rows = lax.dynamic_slice_in_dim(shard_piece, start, size, 0)
+            total = jnp.zeros((size, pixels), jnp.float32)
             for tap_index in range(len(TAPS)):
                 total = total + jnp.dot(
                     rows[:, tap_index, :], windows[tap_index], preferred_element_type=jnp.float32
                 )
             return total
 
-        sent = lax.ppermute(half_conv((1 - index) * lat_local), "chan", SWAP)
+        quarter = lat_local // 2
+        sent = jnp.concatenate(
+            [
+                lax.ppermute(half_conv((1 - index) * lat_local + k * quarter, quarter), "chan", SWAP)
+                for k in range(2)
+            ],
+            0,
+        )
         pre = half_conv(index * lat_local) + sent
         squares_own = (pre * pre).astype(jnp.bfloat16)
         squares = chan_gather(squares_own)

time: 199 us -> 203 us (1.020)
  matrix products: 20.5 us -> 24.1 us
    dot_general x18 -> x27, matrix products: 8.28 us -> 12 us  [half_conv(): jnp.dot(rows[:, tap_index, :], windows[tap_index], preferred_element_type...]
  transfers between devices with their start and end apart: 38 -> 39, of which waited for: 14 -> 14; matrix products, arithmetic and copies ran while one was open for 19% -> 21% of each run, Pallas kernels for 0% -> 0%
where the time goes in v16:
time: 203 us
  waiting for transfers between devices  85.8 us (42%)
  starting transfers between devices  45.4 us (22%)
  between operations  25.8 us (13%)
  matrix products  24.1 us (12%)
  local copies, waits for them, and re-layouts  12.2 us (6%)
  other arithmetic  9.59 us (5%)
    all_gather x1, waiting for transfers between devices, per_device(): shard_piece = lax.all_gather(conv_weight, 'row', axis=0, tiled=True)  50.7 us
    ppermute x14, waiting for transfers between devices, ring_sum(): got = lax.ppermute(carry[part], 'row', moves[part])  20.7 us
    ppermute x14, starting transfers between devices, ring_sum(): gathered[part].append(lax.ppermute(gathered[part][-1], 'row', moves[part]))  16.6 us
    ppermute x14, starting transfers between devices, ring_sum(): got = lax.ppermute(carry[part], 'row', moves[part])  14.9 us
    ppermute x14, waiting for transfers between devices, ring_sum(): gathered[part].append(lax.ppermute(gathered[part][-1], 'row', moves[part]))  13.7 us
    dot_general x27, matrix products, half_conv(): jnp.dot(rows[:, tap_index, :], windows[tap_index], preferred_element_type...  12 us
    ppermute x2, starting transfers between devices, extended(): before = lax.ppermute(last, axis, up)  10.1 us
    dot_general x9, matrix products, per_device(): lax.dot_general(shard_piece[:, tap_index, :], window, (((0,), (0,)), ((),...  4.6 us
  transfers between devices with their start and end apart: 39, of which 14 were waited for; matrix products, arithmetic and copies ran while one was open for 21% of the time, Pallas kernels for 0%

profile of v16, /device:TPU:0, one launch (start us, length us, event | category | flops | bytes accessed | tf_op | source)
XLA Modules:
  0.0 202.9 jit_solution(4612198256366583191)
XLA Ops:
  10.5 5.5 %collective-permute-start = (bf16[212,1,128]{2,1,0:T(2,128)(2,1)S(1)}, bf16[212,1,128]{2,1,0:T(2,128)(2,1)S(1)}, u32[]{:S(2)}, u32[]{:S(2)}) collective-permute-start(bf16[212,1,128]{2,1,0:T(2,128)(2,1)S(1)} %get-tuple-element.54), channel_id=1, source_target_pairs={{0,2},{2,4},{4,6},{6,8},{8,10},{10,12},{12,14},{1,3},{3,5},{5,7},{... | collective-permute-start | bytes 162824 | tf_op jit(solution)/shard_map/ppermute | solution.py:19
  16.0 2.3 %constant_dynamic-slice_fusion = (bf16[512,512]{1,0:T(8,128)(2,1)}, bf16[512,512]{1,0:T(8,128)(2,1)}) fusion(bf16[512,1024]{1,0:T(8,128)(2,1)} %param.14, s32[]{:T(128)S(6)} %select_n.124, s32[]{:T(128)S(6)} %select_n.123), kind=kLoop, calls=%fused_computation.212 | loop fusion | bytes 2097160 | tf_op jit(solution)/shard_map/dynamic_slice | solution.py:148
  34.4 50.7 %all-gather.2.cloned.1.call-done = bf16[1024,9,212]{0,2,1:T(8,128)(2,1)} async-done(((bf16[128,9,212]{0,2,1:T(8,128)(2,1)}), bf16[1024,9,212]{0,2,1:T(8,128)(2,1)}) %all-gather.2.cloned.1.call-update) | async-done | bytes 3907600 | tf_op jit(solution)/shard_map/all_gather | solution.py:112
  101.0 2.3 %fusion.11 = (bf16[512,512]{0,1:T(8,128)(2,1)}, bf16[512,512]{0,1:T(8,128)(2,1)}, f32[512,512]{0,1:T(8,128)}) fusion(f32[512,512]{0,1:T(8,128)S(1)} %get-tuple-element.57, f32[512,4,128]{0,2,1:T(8,128)S(1)} %copy.48, bf16[1024,512]{0,1:T(8,128)(2,1)S(1)} %fusion.27, bf16[512,1024]{1,0:T(8,128)(2,1)S(1)} %copy-done.4, f32[512]{0:T(512)S(1)} %copy-done.11), kind=kOutput, calls=%fused_computation.61 | convolution fusion | flops 539230208 | bytes 6293504 | tf_op jit(solution)/shard_map/dot_general | solution.py:141
  103.8 1.9 fusion.9
  105.7 2.1 %copy.49 = bf16[512,4,128]{2,1,0:T(4,128)(2,1)} copy(bf16[512,4,128]{0,2,1:T(8,128)(2,1)} %bitcast.353) | data formatting | bytes 1048576
  108.1 2.1 %collective-permute-start.10 = (f32[32,1152]{1,0:T(8,128)S(1)}, f32[32,1152]{1,0:T(8,128)S(1)}, u32[]{:S(2)}, u32[]{:S(2)}) collective-permute-start(f32[32,1152]{1,0:T(8,128)S(1)} %select_bitcast_fusion.1), channel_id=1, source_target_pairs={{0,2},{2,6},{6,10},{10,14},{14,12},{12,8},{8,4},{4,0},{1,3},{3,7},... | collective-permute-start | bytes 442376 | tf_op jit(solution)/shard_map/ppermute | solution.py:85
  110.2 3.7 %collective-permute-done.24 = f32[32,1152]{1,0:T(8,128)S(1)} collective-permute-done((f32[32,1152]{1,0:T(8,128)S(1)}, f32[32,1152]{1,0:T(8,128)S(1)}, u32[]{:S(2)}, u32[]{:S(2)}) %collective-permute-start.24) | collective-permute-done | bytes 147488 | tf_op jit(solution)/shard_map/ppermute | solution.py:85
  114.2 1.8 collective-permute-start.11
  116.0 3.0 %collective-permute-done.25 = f32[32,1152]{1,0:T(8,128)S(1)} collective-permute-done((f32[32,1152]{1,0:T(8,128)S(1)}, f32[32,1152]{1,0:T(8,128)S(1)}, u32[]{:S(2)}, u32[]{:S(2)}) %collective-permute-start.25) | collective-permute-done | bytes 147488 | tf_op jit(solution)/shard_map/ppermute | solution.py:85
  119.5 1.7 collective-permute-start.12
  121.2 3.5 %collective-permute-done.26 = f32[32,1152]{1,0:T(8,128)S(1)} collective-permute-done((f32[32,1152]{1,0:T(8,128)S(1)}, f32[32,1152]{1,0:T(8,128)S(1)}, u32[]{:S(2)}, u32[]{:S(2)}) %collective-permute-start.26) | collective-permute-done | bytes 147488 | tf_op jit(solution)/shard_map/ppermute | solution.py:85
  124.9 2.0 %collective-permute-start.13 = (f32[32,1152]{1,0:T(8,128)S(1)}, f32[32,1152]{1,0:T(8,128)S(1)}, u32[]{:S(2)}, u32[]{:S(2)}) collective-permute-start(f32[32,1152]{1,0:T(8,128)S(1)} %bitcast_add_fusion.11), channel_id=1, source_target_pairs={{0,2},{2,6},{6,10},{10,14},{14,12},{12,8},{8,4},{4,0},{1,3},{3,7},... | collective-permute-start | bytes 442376 | tf_op jit(solution)/shard_map/ppermute | solution.py:85
  126.9 3.3 %fusion.30 = bf16[512,512]{0,1:T(8,128)(2,1)S(1)} fusion(f32[512,512]{0,1:T(8,128)S(1)} %copy-done.8, f32[512,4,128]{0,2,1:T(8,128)S(1)} %copy-done.3, f32[512,512]{0,1:T(8,128)S(1)} %get-tuple-element.57, s32[]{:T(128)S(6)} %select_n.200, bf16[512,512]{1,0:T(8,128)(2,1)S(1)} %copy-done.10, bf16[512,512]{1,0:T(8,128)(2,1)} %collective-permute-done.5, ...), kind=kOutput, calls=%fused_computation.81 | convolution fusion | flops 546570240 | bytes 5768192 | tf_op jit(solution)/shard_map/dot_general | solution.py:151
  130.5 2.0 collective-permute-start.14
  132.5 4.1 %collective-permute-done.28 = f32[32,1152]{1,0:T(8,128)S(1)} collective-permute-done((f32[32,1152]{1,0:T(8,128)S(1)}, f32[32,1152]{1,0:T(8,128)S(1)}, u32[]{:S(2)}, u32[]{:S(2)}) %collective-permute-start.28) | collective-permute-done | bytes 147488 | tf_op jit(solution)/shard_map/ppermute | solution.py:85
  137.1 1.8 collective-permute-start.15
  138.9 3.3 %collective-permute-done.29 = f32[32,1152]{1,0:T(8,128)S(1)} collective-permute-done((f32[32,1152]{1,0:T(8,128)S(1)}, f32[32,1152]{1,0:T(8,128)S(1)}, u32[]{:S(2)}, u32[]{:S(2)}) %collective-permute-start.29) | collective-permute-done | bytes 147488 | tf_op jit(solution)/shard_map/ppermute | solution.py:85
  144.3 3.0 %collective-permute-done.30 = f32[32,1152]{1,0:T(8,128)S(1)} collective-permute-done((f32[32,1152]{1,0:T(8,128)S(1)}, f32[32,1152]{1,0:T(8,128)S(1)}, u32[]{:S(2)}, u32[]{:S(2)}) %collective-permute-start.30) | collective-permute-done | bytes 147488 | tf_op jit(solution)/shard_map/ppermute | solution.py:85
  151.6 4.6 %collective-permute-start.8 = (bf16[1024,1,128]{0,2,1:T(8,128)(2,1)S(1)}, bf16[1024,1,128]{0,2,1:T(8,128)(2,1)S(1)}, u32[]{:S(2)}, u32[]{:S(2)}) collective-permute-start(bf16[1024,1,128]{0,2,1:T(8,128)(2,1)S(1)} %get-tuple-element.42), channel_id=1, source_target_pairs={{0,2},{2,4},{4,6},{6,8},{8,10},{10,12},{12,14},{1,3},{3,5},{5,7},{... | collective-permute-start | bytes 786440 | tf_op jit(solution)/shard_map/ppermute | solution.py:19
  159.2 2.6 %collective-permute-done.32 = bf16[32,1152]{1,0:T(8,128)(2,1)S(1)} collective-permute-done((bf16[32,1152]{1,0:T(8,128)(2,1)S(1)}, bf16[32,1152]{1,0:T(8,128)(2,1)S(1)}, u32[]{:S(2)}, u32[]{:S(2)}) %collective-permute-start.32) | collective-permute-done | bytes 73760 | tf_op jit(solution)/shard_map/ppermute | solution.py:91
  162.7 2.1 %collective-permute-done.18 = bf16[32,1152]{1,0:T(8,128)(2,1)S(1)} collective-permute-done((bf16[32,1152]{1,0:T(8,128)(2,1)S(1)}, bf16[32,1152]{1,0:T(8,128)(2,1)S(1)}, u32[]{:S(2)}, u32[]{:S(2)}) %collective-permute-start.18) | collective-permute-done | bytes 73760 | tf_op jit(solution)/shard_map/ppermute | solution.py:91
  164.8 2.5 %collective-permute-start.19 = (bf16[32,1152]{1,0:T(8,128)(2,1)S(1)}, bf16[32,1152]{1,0:T(8,128)(2,1)S(1)}, u32[]{:S(2)}, u32[]{:S(2)}) collective-permute-start(bf16[32,1152]{1,0:T(8,128)(2,1)S(1)} %collective-permute-done.18), channel_id=1, source_target_pairs={{0,2},{2,6},{6,10},{10,14},{14,12},{12,8},{8,4},{4,0},{1,3},{3,7},... | collective-permute-start | bytes 221192 | tf_op jit(solution)/shard_map/ppermute | solution.py:91
  167.4 1.9 collective-permute-done.19
  169.3 2.4 %collective-permute-start.20 = (bf16[32,1152]{1,0:T(8,128)(2,1)S(1)}, bf16[32,1152]{1,0:T(8,128)(2,1)S(1)}, u32[]{:S(2)}, u32[]{:S(2)}) collective-permute-start(bf16[32,1152]{1,0:T(8,128)(2,1)S(1)} %collective-permute-done.19), channel_id=1, source_target_pairs={{0,2},{2,6},{6,10},{10,14},{14,12},{12,8},{8,4},{4,0},{1,3},{3,7},... | collective-permute-start | bytes 221192 | tf_op jit(solution)/shard_map/ppermute | solution.py:91
  178.6 2.1 %collective-permute-start.21 = (bf16[32,1152]{1,0:T(8,128)(2,1)S(1)}, bf16[32,1152]{1,0:T(8,128)(2,1)S(1)}, u32[]{:S(2)}, u32[]{:S(2)}) collective-permute-start(bf16[32,1152]{1,0:T(8,128)(2,1)S(1)} %collective-permute-done.20), channel_id=1, source_target_pairs={{0,2},{2,6},{6,10},{10,14},{14,12},{12,8},{8,4},{4,0},{1,3},{3,7},... | collective-permute-start | bytes 221192 | tf_op jit(solution)/shard_map/ppermute | solution.py:91
  180.6 2.5 %collective-permute-done.35 = bf16[32,1152]{1,0:T(8,128)(2,1)S(1)} collective-permute-done((bf16[32,1152]{1,0:T(8,128)(2,1)S(1)}, bf16[32,1152]{1,0:T(8,128)(2,1)S(1)}, u32[]{:S(2)}, u32[]{:S(2)}) %collective-permute-start.35) | collective-permute-done | bytes 73760 | tf_op jit(solution)/shard_map/ppermute | solution.py:91
  183.5 1.8 collective-permute-start.22
  185.3 2.2 %collective-permute-done.36 = bf16[32,1152]{1,0:T(8,128)(2,1)S(1)} collective-permute-done((bf16[32,1152]{1,0:T(8,128)(2,1)S(1)}, bf16[32,1152]{1,0:T(8,128)(2,1)S(1)}, u32[]{:S(2)}, u32[]{:S(2)}) %collective-permute-start.36) | collective-permute-done | bytes 73760 | tf_op jit(solution)/shard_map/ppermute | solution.py:91
  187.9 1.7 collective-permute-start.23
  189.7 2.2 %collective-permute-done.37 = bf16[32,1152]{1,0:T(8,128)(2,1)S(1)} collective-permute-done((bf16[32,1152]{1,0:T(8,128)(2,1)S(1)}, bf16[32,1152]{1,0:T(8,128)(2,1)S(1)}, u32[]{:S(2)}, u32[]{:S(2)}) %collective-permute-start.37) | collective-permute-done | bytes 73760 | tf_op jit(solution)/shard_map/ppermute | solution.py:91
  194.4 1.6 slice_multiply_fusion
  (189 shorter events, 46.7 us)
Async XLA Ops:
  7.2 77.8 %all-gather.2.cloned.1.call-start = ((), (), s32[]{:S(2)}) async-start(), calls=%async_computation | async-start | bytes 4478976 | tf_op jit(solution)/shard_map/all_gather | solution.py:112
  9.2 21.7 %collective-permute-start.1 = (bf16[212,1,128]{2,1,0:T(2,128)(2,1)S(1)}, bf16[212,1,128]{2,1,0:T(2,128)(2,1)S(1)}, u32[]{:S(2)}, u32[]{:S(2)}) collective-permute-start(bf16[212,1,128]{2,1,0:T(2,128)(2,1)S(1)} %get-tuple-element.55), channel_id=1, source_target_pairs={{2,0},{4,2},{6,4},{8,6},{10,8},{12,10},{14,12},{3,1},{5,3},{7,5},{... | collective-permute-start | bytes 162824 | tf_op jit(solution)/shard_map/ppermute | solution.py:20
  10.5 20.4 %collective-permute-start = (bf16[212,1,128]{2,1,0:T(2,128)(2,1)S(1)}, bf16[212,1,128]{2,1,0:T(2,128)(2,1)S(1)}, u32[]{:S(2)}, u32[]{:S(2)}) collective-permute-start(bf16[212,1,128]{2,1,0:T(2,128)(2,1)S(1)} %get-tuple-element.54), channel_id=1, source_target_pairs={{0,2},{2,4},{4,6},{6,8},{8,10},{10,12},{12,14},{1,3},{3,5},{5,7},{... | collective-permute-start | bytes 162824 | tf_op jit(solution)/shard_map/ppermute | solution.py:19
  18.2 108.7 %collective-permute-start.5 = (bf16[512,512]{1,0:T(8,128)(2,1)}, bf16[512,512]{1,0:T(8,128)(2,1)}, u32[]{:S(2)}, u32[]{:S(2)}) collective-permute-start(bf16[512,512]{1,0:T(8,128)(2,1)} %get-tuple-element.44), channel_id=1, source_target_pairs={{0,1},{1,0},{2,3},{3,2},{4,5},{5,4},{6,7},{7,6},{8,9},{9,8},{10,11... | collective-permute-start | bytes 1572872 | tf_op jit(solution)/shard_map/ppermute | solution.py:149
  91.3 6.1 %collective-permute-start.3 = (f32[256,512]{0,1:T(8,128)S(1)}, f32[256,512]{0,1:T(8,128)S(1)}, u32[]{:S(2)}, u32[]{:S(2)}) collective-permute-start(f32[256,512]{0,1:T(8,128)S(1)} %convolution_add_fusion.9), channel_id=1, source_target_pairs={{0,1},{1,0},{2,3},{3,2},{4,5},{5,4},{6,7},{7,6},{8,9},{9,8},{10,11... | collective-permute-start | bytes 1572872 | tf_op jit(solution)/shard_map/ppermute | solution.py:133
  103.3 23.6 %collective-permute-start.6 = (bf16[512,512]{0,1:T(8,128)(2,1)}, bf16[512,512]{0,1:T(8,128)(2,1)}, u32[]{:S(2)}, u32[]{:S(2)}) collective-permute-start(bf16[512,512]{0,1:T(8,128)(2,1)} %get-tuple-element.32), channel_id=1, source_target_pairs={{0,1},{1,0},{2,3},{3,2},{4,5},{5,4},{6,7},{7,6},{8,9},{9,8},{10,11... | collective-permute-start | bytes 1572872 | tf_op jit(solution)/shard_map/ppermute | solution.py:26
  108.0 5.8 %collective-permute-start.24 = (f32[32,1152]{1,0:T(8,128)S(1)}, f32[32,1152]{1,0:T(8,128)S(1)}, u32[]{:S(2)}, u32[]{:S(2)}) collective-permute-start(f32[32,1152]{1,0:T(8,128)S(1)} %select_bitcast_fusion), channel_id=1, source_target_pairs={{2,0},{6,2},{10,6},{14,10},{12,14},{8,12},{4,8},{0,4},{3,1},{7,3},... | collective-permute-start | bytes 442376 | tf_op jit(solution)/shard_map/ppermute | solution.py:85
  108.1 6.1 %collective-permute-start.10 = (f32[32,1152]{1,0:T(8,128)S(1)}, f32[32,1152]{1,0:T(8,128)S(1)}, u32[]{:S(2)}, u32[]{:S(2)}) collective-permute-start(f32[32,1152]{1,0:T(8,128)S(1)} %select_bitcast_fusion.1), channel_id=1, source_target_pairs={{0,2},{2,6},{6,10},{10,14},{14,12},{12,8},{8,4},{4,0},{1,3},{3,7},... | collective-permute-start | bytes 442376 | tf_op jit(solution)/shard_map/ppermute | solution.py:85
  113.9 5.2 %collective-permute-start.25 = (f32[32,1152]{1,0:T(8,128)S(1)}, f32[32,1152]{1,0:T(8,128)S(1)}, u32[]{:S(2)}, u32[]{:S(2)}) collective-permute-start(f32[32,1152]{1,0:T(8,128)S(1)} %bitcast_add_fusion.6), channel_id=1, source_target_pairs={{2,0},{6,2},{10,6},{14,10},{12,14},{8,12},{4,8},{0,4},{3,1},{7,3},... | collective-permute-start | bytes 442376 | tf_op jit(solution)/shard_map/ppermute | solution.py:85
  114.2 5.3 %collective-permute-start.11 = (f32[32,1152]{1,0:T(8,128)S(1)}, f32[32,1152]{1,0:T(8,128)S(1)}, u32[]{:S(2)}, u32[]{:S(2)}) collective-permute-start(f32[32,1152]{1,0:T(8,128)S(1)} %bitcast_add_fusion.13), channel_id=1, source_target_pairs={{0,2},{2,6},{6,10},{10,14},{14,12},{12,8},{8,4},{4,0},{1,3},{3,7},... | collective-permute-start | bytes 442376 | tf_op jit(solution)/shard_map/ppermute | solution.py:85
  119.1 5.7 %collective-permute-start.26 = (f32[32,1152]{1,0:T(8,128)S(1)}, f32[32,1152]{1,0:T(8,128)S(1)}, u32[]{:S(2)}, u32[]{:S(2)}) collective-permute-start(f32[32,1152]{1,0:T(8,128)S(1)} %bitcast_add_fusion.5), channel_id=1, source_target_pairs={{2,0},{6,2},{10,6},{14,10},{12,14},{8,12},{4,8},{0,4},{3,1},{7,3},... | collective-permute-start | bytes 442376 | tf_op jit(solution)/shard_map/ppermute | solution.py:85
  119.5 5.4 %collective-permute-start.12 = (f32[32,1152]{1,0:T(8,128)S(1)}, f32[32,1152]{1,0:T(8,128)S(1)}, u32[]{:S(2)}, u32[]{:S(2)}) collective-permute-start(f32[32,1152]{1,0:T(8,128)S(1)} %bitcast_add_fusion.12), channel_id=1, source_target_pairs={{0,2},{2,6},{6,10},{10,14},{14,12},{12,8},{8,4},{4,0},{1,3},{3,7},... | collective-permute-start | bytes 442376 | tf_op jit(solution)/shard_map/ppermute | solution.py:85
  124.8 5.6 %collective-permute-start.27 = (f32[32,1152]{1,0:T(8,128)S(1)}, f32[32,1152]{1,0:T(8,128)S(1)}, u32[]{:S(2)}, u32[]{:S(2)}) collective-permute-start(f32[32,1152]{1,0:T(8,128)S(1)} %bitcast_add_fusion.4), channel_id=1, source_target_pairs={{2,0},{6,2},{10,6},{14,10},{12,14},{8,12},{4,8},{0,4},{3,1},{7,3},... | collective-permute-start | bytes 442376 | tf_op jit(solution)/shard_map/ppermute | solution.py:85
  124.9 5.7 %collective-permute-start.13 = (f32[32,1152]{1,0:T(8,128)S(1)}, f32[32,1152]{1,0:T(8,128)S(1)}, u32[]{:S(2)}, u32[]{:S(2)}) collective-permute-start(f32[32,1152]{1,0:T(8,128)S(1)} %bitcast_add_fusion.11), channel_id=1, source_target_pairs={{0,2},{2,6},{6,10},{10,14},{14,12},{12,8},{8,4},{4,0},{1,3},{3,7},... | collective-permute-start | bytes 442376 | tf_op jit(solution)/shard_map/ppermute | solution.py:85
  130.3 19.3 %collective-permute-start.7 = (bf16[512,4,128]{0,2,1:T(8,128)(2,1)S(1)}, bf16[512,4,128]{0,2,1:T(8,128)(2,1)S(1)}, u32[]{:S(2)}, u32[]{:S(2)}) collective-permute-start(bf16[512,4,128]{0,2,1:T(8,128)(2,1)S(1)} %bitcast.363), channel_id=1, source_target_pairs={{0,1},{1,0},{2,3},{3,2},{4,5},{5,4},{6,7},{7,6},{8,9},{9,8},{10,11... | collective-permute-start | bytes 1572872 | tf_op jit(solution)/shard_map/ppermute | solution.py:26
  130.4 6.3 %collective-permute-start.28 = (f32[32,1152]{1,0:T(8,128)S(1)}, f32[32,1152]{1,0:T(8,128)S(1)}, u32[]{:S(2)}, u32[]{:S(2)}) collective-permute-start(f32[32,1152]{1,0:T(8,128)S(1)} %bitcast_add_fusion.3), channel_id=1, source_target_pairs={{2,0},{6,2},{10,6},{14,10},{12,14},{8,12},{4,8},{0,4},{3,1},{7,3},... | collective-permute-start | bytes 442376 | tf_op jit(solution)/shard_map/ppermute | solution.py:85
  130.5 6.5 %collective-permute-start.14 = (f32[32,1152]{1,0:T(8,128)S(1)}, f32[32,1152]{1,0:T(8,128)S(1)}, u32[]{:S(2)}, u32[]{:S(2)}) collective-permute-start(f32[32,1152]{1,0:T(8,128)S(1)} %bitcast_add_fusion.10), channel_id=1, source_target_pairs={{0,2},{2,6},{6,10},{10,14},{14,12},{12,8},{8,4},{4,0},{1,3},{3,7},... | collective-permute-start | bytes 442376 | tf_op jit(solution)/shard_map/ppermute | solution.py:85
  136.7 5.4 %collective-permute-start.29 = (f32[32,1152]{1,0:T(8,128)S(1)}, f32[32,1152]{1,0:T(8,128)S(1)}, u32[]{:S(2)}, u32[]{:S(2)}) collective-permute-start(f32[32,1152]{1,0:T(8,128)S(1)} %bitcast_add_fusion.2), channel_id=1, source_target_pairs={{2,0},{6,2},{10,6},{14,10},{12,14},{8,12},{4,8},{0,4},{3,1},{7,3},... | collective-permute-start | bytes 442376 | tf_op jit(solution)/shard_map/ppermute | solution.py:85
  137.1 5.6 %collective-permute-start.15 = (f32[32,1152]{1,0:T(8,128)S(1)}, f32[32,1152]{1,0:T(8,128)S(1)}, u32[]{:S(2)}, u32[]{:S(2)}) collective-permute-start(f32[32,1152]{1,0:T(8,128)S(1)} %bitcast_add_fusion.9), channel_id=1, source_target_pairs={{0,2},{2,6},{6,10},{10,14},{14,12},{12,8},{8,4},{4,0},{1,3},{3,7},... | collective-permute-start | bytes 442376 | tf_op jit(solution)/shard_map/ppermute | solution.py:85
  142.1 5.2 %collective-permute-start.30 = (f32[32,1152]{1,0:T(8,128)S(1)}, f32[32,1152]{1,0:T(8,128)S(1)}, u32[]{:S(2)}, u32[]{:S(2)}) collective-permute-start(f32[32,1152]{1,0:T(8,128)S(1)} %bitcast_add_fusion.1), channel_id=1, source_target_pairs={{2,0},{6,2},{10,6},{14,10},{12,14},{8,12},{4,8},{0,4},{3,1},{7,3},... | collective-permute-start | bytes 442376 | tf_op jit(solution)/shard_map/ppermute | solution.py:85
  142.7 5.2 %collective-permute-start.16 = (f32[32,1152]{1,0:T(8,128)S(1)}, f32[32,1152]{1,0:T(8,128)S(1)}, u32[]{:S(2)}, u32[]{:S(2)}) collective-permute-start(f32[32,1152]{1,0:T(8,128)S(1)} %bitcast_add_fusion.8), channel_id=1, source_target_pairs={{0,2},{2,6},{6,10},{10,14},{14,12},{12,8},{8,4},{4,0},{1,3},{3,7},... | collective-permute-start | bytes 442376 | tf_op jit(solution)/shard_map/ppermute | solution.py:85
  147.4 9.3 %collective-permute-start.31 = (bf16[32,1152]{1,0:T(8,128)(2,1)S(1)}, bf16[32,1152]{1,0:T(8,128)(2,1)S(1)}, u32[]{:S(2)}, u32[]{:S(2)}) collective-permute-start(bf16[32,1152]{1,0:T(8,128)(2,1)S(1)} %get-tuple-element.29), channel_id=1, source_target_pairs={{2,0},{6,2},{10,6},{14,10},{12,14},{8,12},{4,8},{0,4},{3,1},{7,3},... | collective-permute-start | bytes 221192 | tf_op jit(solution)/shard_map/ppermute | solution.py:91
  147.9 9.7 %collective-permute-start.17 = (bf16[32,1152]{1,0:T(8,128)(2,1)S(1)}, bf16[32,1152]{1,0:T(8,128)(2,1)S(1)}, u32[]{:S(2)}, u32[]{:S(2)}) collective-permute-start(bf16[32,1152]{1,0:T(8,128)(2,1)S(1)} %get-tuple-element.27), channel_id=1, source_target_pairs={{0,2},{2,6},{6,10},{10,14},{14,12},{12,8},{8,4},{4,0},{1,3},{3,7},... | collective-permute-start | bytes 221192 | tf_op jit(solution)/shard_map/ppermute | solution.py:91
  150.3 21.4 %collective-permute-start.9 = (bf16[1024,1,128]{0,2,1:T(8,128)(2,1)S(1)}, bf16[1024,1,128]{0,2,1:T(8,128)(2,1)S(1)}, u32[]{:S(2)}, u32[]{:S(2)}) collective-permute-start(bf16[1024,1,128]{0,2,1:T(8,128)(2,1)S(1)} %get-tuple-element.43), channel_id=1, source_target_pairs={{2,0},{4,2},{6,4},{8,6},{10,8},{12,10},{14,12},{3,1},{5,3},{7,5},{... | collective-permute-start | bytes 786440 | tf_op jit(solution)/shard_map/ppermute | solution.py:20
  151.6 20.1 %collective-permute-start.8 = (bf16[1024,1,128]{0,2,1:T(8,128)(2,1)S(1)}, bf16[1024,1,128]{0,2,1:T(8,128)(2,1)S(1)}, u32[]{:S(2)}, u32[]{:S(2)}) collective-permute-start(bf16[1024,1,128]{0,2,1:T(8,128)(2,1)S(1)} %get-tuple-element.42), channel_id=1, source_target_pairs={{0,2},{2,4},{4,6},{6,8},{8,10},{10,12},{12,14},{1,3},{3,5},{5,7},{... | collective-permute-start | bytes 786440 | tf_op jit(solution)/shard_map/ppermute | solution.py:19
  156.7 5.2 %collective-permute-start.32 = (bf16[32,1152]{1,0:T(8,128)(2,1)S(1)}, bf16[32,1152]{1,0:T(8,128)(2,1)S(1)}, u32[]{:S(2)}, u32[]{:S(2)}) collective-permute-start(bf16[32,1152]{1,0:T(8,128)(2,1)S(1)} %collective-permute-done.31), channel_id=1, source_target_pairs={{2,0},{6,2},{10,6},{14,10},{12,14},{8,12},{4,8},{0,4},{3,1},{7,3},... | collective-permute-start | bytes 221192 | tf_op jit(solution)/shard_map/ppermute | solution.py:91
  157.6 7.2 %collective-permute-start.18 = (bf16[32,1152]{1,0:T(8,128)(2,1)S(1)}, bf16[32,1152]{1,0:T(8,128)(2,1)S(1)}, u32[]{:S(2)}, u32[]{:S(2)}) collective-permute-start(bf16[32,1152]{1,0:T(8,128)(2,1)S(1)} %collective-permute-done.17), channel_id=1, source_target_pairs={{0,2},{2,6},{6,10},{10,14},{14,12},{12,8},{8,4},{4,0},{1,3},{3,7},... | collective-permute-start | bytes 221192 | tf_op jit(solution)/shard_map/ppermute | solution.py:91
  161.8 5.5 %collective-permute-start.33 = (bf16[32,1152]{1,0:T(8,128)(2,1)S(1)}, bf16[32,1152]{1,0:T(8,128)(2,1)S(1)}, u32[]{:S(2)}, u32[]{:S(2)}) collective-permute-start(bf16[32,1152]{1,0:T(8,128)(2,1)S(1)} %collective-permute-done.32), channel_id=1, source_target_pairs={{2,0},{6,2},{10,6},{14,10},{12,14},{8,12},{4,8},{0,4},{3,1},{7,3},... | collective-permute-start | bytes 221192 | tf_op jit(solution)/shard_map/ppermute | solution.py:91
  167.3 11.2 %collective-permute-start.34 = (bf16[32,1152]{1,0:T(8,128)(2,1)S(1)}, bf16[32,1152]{1,0:T(8,128)(2,1)S(1)}, u32[]{:S(2)}, u32[]{:S(2)}) collective-permute-start(bf16[32,1152]{1,0:T(8,128)(2,1)S(1)} %collective-permute-done.33), channel_id=1, source_target_pairs={{2,0},{6,2},{10,6},{14,10},{12,14},{8,12},{4,8},{0,4},{3,1},{7,3},... | collective-permute-start | bytes 221192 | tf_op jit(solution)/shard_map/ppermute | solution.py:91
  169.3 9.3 %collective-permute-start.20 = (bf16[32,1152]{1,0:T(8,128)(2,1)S(1)}, bf16[32,1152]{1,0:T(8,128)(2,1)S(1)}, u32[]{:S(2)}, u32[]{:S(2)}) collective-permute-start(bf16[32,1152]{1,0:T(8,128)(2,1)S(1)} %collective-permute-done.19), channel_id=1, source_target_pairs={{0,2},{2,6},{6,10},{10,14},{14,12},{12,8},{8,4},{4,0},{1,3},{3,7},... | collective-permute-start | bytes 221192 | tf_op jit(solution)/shard_map/ppermute | solution.py:91
  178.6 4.9 %collective-permute-start.21 = (bf16[32,1152]{1,0:T(8,128)(2,1)S(1)}, bf16[32,1152]{1,0:T(8,128)(2,1)S(1)}, u32[]{:S(2)}, u32[]{:S(2)}) collective-permute-start(bf16[32,1152]{1,0:T(8,128)(2,1)S(1)} %collective-permute-done.20), channel_id=1, source_target_pairs={{0,2},{2,6},{6,10},{10,14},{14,12},{12,8},{8,4},{4,0},{1,3},{3,7},... | collective-permute-start | bytes 221192 | tf_op jit(solution)/shard_map/ppermute | solution.py:91
  187.9 4.8 %collective-permute-start.23 = (bf16[32,1152]{1,0:T(8,128)(2,1)S(1)}, bf16[32,1152]{1,0:T(8,128)(2,1)S(1)}, u32[]{:S(2)}, u32[]{:S(2)}) collective-permute-start(bf16[32,1152]{1,0:T(8,128)(2,1)S(1)} %collective-permute-done.22), channel_id=1, source_target_pairs={{0,2},{2,6},{6,10},{10,14},{14,12},{12,8},{8,4},{4,0},{1,3},{3,7},... | collective-permute-start | bytes 221192 | tf_op jit(solution)/shard_map/ppermute | solution.py:91
  (20 other events, 303.8 us)
Sparse Core Ops, SparseCore 0:
  10.0 74.9 all-gather.1
